TPU v7x, 128 devices: a whole 4x4x4 slice. The times are simulated.
128 devices in a mesh: gy: 8 (over x, core), gx: 16 (over z, y).
Axes of the slice: x: 4, y: 4, z: 4, core: 2. Of those that a mesh axis runs over, the one named last changes fastest.
Arguments:
- water_depth: float32 [4096, 8192], P('gy', 'gx'), may hold values from 1 to 3
- flux_east: float32 [4096, 8192], P('gy', 'gx'), may hold values from -1.5 to 1.5
- flux_south: float32 [4096, 8192], P('gy', 'gx'), may hold values from -1.5 to 1.5
- bed_level: float32 [4096, 8192], P('gy', 'gx'), may hold values from -3 to 3
- roughness: float32 [4096, 8192], P('gy', 'gx'), may hold values from 0.5 to 5
- land_mask: int32 [4096, 8192], P('gy', 'gx'), may hold values 0 or 1
- tile_block: int32 [32768], P(('gy', 'gx')), may hold values from 0 to 2047, as said below
- storage: float32 [2048, 128], P(('gy', 'gx')), may hold values from 0.5 to 2
- reach_rate: float32 [2048, 128], P(('gy', 'gx')), may hold values from 0.1 to 0.5
- downstream: int32 [2048], P(('gy', 'gx')), may hold values from 1 to 2048, as said below
Outputs:
- new_depth: float32 [4096, 8192], P('gy', 'gx')
- new_flux_east: float32 [4096, 8192], P('gy', 'gx')
- new_flux_south: float32 [4096, 8192], P('gy', 'gx')
- new_storage: float32 [2048, 128], P(('gy', 'gx'))
Inputs may be any that keep to these rules, and one draw needn't show every extreme that they name: downstream[r] = min(r + k, 2048) with 1 <= k <= 8; in every device's 16 blocks the first has k = 8. `tile_block`: among the 256 tiles of one device, at most 4 drain into blocks held by one device (16 consecutive blocks from a multiple of 16); on every device some such owner receives exactly 4.
All inputs are finite; a program needn't handle non-finite values. No bound on the sum of `land_mask` on one device may be relied on, other than what follows from the above.
Results may differ from a plain program's by a relative error of at most 0.0001.
Values sent between devices are 32-bit elements; how exact they have to be, the bound alone decides.
No kernel may reach another device: no remote copies, remote signals or barrier semaphores. Data moves between devices by JAX's collectives and lax.ppermute only.
A program may use at most 64 MiB of HBM per device.

v0:
```python
import jax
import jax.numpy as jnp
from jax import lax
from jax.sharding import PartitionSpec as P

STRIP = 8
STEPS = 2


rim_depth = 0.1
slope_gain = 0.1
friction_gain = 1.0
mass_gain = 0.05
drain_rate = 0.05
lateral_gain = 0.125


def shifted(value, axis, steps):
    count = lax.axis_size(axis)
    first, last = (max(0, -steps), min(count, count - steps))
    return lax.ppermute(value, axis, [(source, source + steps) for source in range(first, last)])


def in_blocks(value, dim, length):
    before, after = (value.shape[:dim], value.shape[dim + 1 :])
    return jnp.moveaxis(value.reshape(*before, length, -1, *after), dim, 0)


def sum_at_owner(value, axis, dim):
    length = lax.axis_size(axis)
    parts = lax.all_to_all(in_blocks(value, dim, length), axis, 0, 0, tiled=True)
    return jnp.sum(parts, axis=0)


def face_update(flux, level, level_next, depth, depth_next, roughness, active):
    face_depth = rim_depth + 0.5 * (jnp.abs(depth) + jnp.abs(depth_next))
    drive = flux - slope_gain * face_depth * (level_next - level)
    damping = 1.0 + friction_gain * roughness * jnp.abs(flux) / jnp.power(face_depth, 7.0 / 3.0)
    return active * drive / damping


def block_term(target_ids, values, start, count):
    targets = start + lax.iota(jnp.int32, count)
    onehot = (target_ids[:, None] == targets[None, :]).astype(jnp.float32)
    return jnp.einsum("tb,tc->bc", onehot, values, precision=lax.Precision.HIGHEST)


def body(
    water_depth,
    flux_east,
    flux_south,
    bed_level,
    roughness,
    land_mask,
    tile_block,
    storage,
    reach_rate,
    downstream,
):
    cell_rows, cell_cols = water_depth.shape
    block_rows, reach_width = storage.shape
    row_count = lax.axis_size("gy")
    col_count = lax.axis_size("gx")
    row_index = lax.axis_index("gy")
    col_index = lax.axis_index("gx")
    device_count = row_count * col_count
    total_blocks = block_rows * device_count
    tile_count = tile_block.shape[0]
    slot_cap = max(2, 2 * tile_count // device_count)
    land_float = land_mask.astype(jnp.float32)
    global_cols = col_index * cell_cols + lax.iota(jnp.int32, cell_cols)
    global_rows = row_index * cell_rows + lax.iota(jnp.int32, cell_rows)
    east_open = land_float * (global_cols < cell_cols * col_count - 1).astype(jnp.float32)[None, :]
    south_open = land_float * (global_rows < cell_rows * row_count - 1).astype(jnp.float32)[:, None]
    device_index = row_index * col_count + col_index
    first_block = device_index * block_rows
    tile_owner = tile_block // block_rows
    owner_hits = (tile_owner[:, None] == lax.iota(jnp.int32, device_count)[None, :]).astype(
        jnp.int32
    )
    earlier = jnp.sum((jnp.cumsum(owner_hits, axis=0) - owner_hits) * owner_hits, axis=1)
    send_slot = tile_owner * slot_cap + earlier
    local_ids = (tile_block - tile_owner * block_rows).astype(jnp.float32)
    send_ids = jnp.full((device_count * slot_cap,), -1.0, jnp.float32).at[send_slot].set(local_ids)
    send_ids = send_ids.reshape(device_count, slot_cap)
    depth = water_depth
    for _ in range(STEPS):
        level = bed_level + depth
        east_level, east_depth = shifted((level[:, 0], depth[:, 0]), "gx", -1)
        south_level, south_depth = shifted((level[0, :], depth[0, :]), "gy", -1)
        level_east = jnp.concatenate([level[:, 1:], east_level[:, None]], axis=1)
        depth_east = jnp.concatenate([depth[:, 1:], east_depth[:, None]], axis=1)
        level_south = jnp.concatenate([level[1:], south_level[None, :]], axis=0)
        depth_south = jnp.concatenate([depth[1:], south_depth[None, :]], axis=0)
        flux_east = face_update(
            flux_east, level, level_east, depth, depth_east, roughness, east_open
        )
        flux_south = face_update(
            flux_south, level, level_south, depth, depth_south, roughness, south_open
        )
        west_edge = shifted(flux_east[:, -1], "gx", 1)
        north_edge = shifted(flux_south[-1, :], "gy", 1)
        west_flux = jnp.concatenate([west_edge[:, None], flux_east[:, :-1]], axis=1)
        north_flux = jnp.concatenate([north_edge[None, :], flux_south[:-1]], axis=0)
        drained = drain_rate * land_float * jnp.abs(depth)
        depth = depth - mass_gain * (flux_east - west_flux + (flux_south - north_flux)) - drained
        tile_sums = drained.reshape(
            cell_rows // STRIP, STRIP, cell_cols // reach_width, reach_width
        ).sum(axis=1)
        tile_sums = tile_sums.reshape(-1, reach_width)
        every_block = block_term(tile_block, tile_sums, 0, total_blocks).reshape(
            row_count, col_count, block_rows, reach_width
        )
        by_column = sum_at_owner(every_block, "gx", 1)
        lateral = sum_at_owner(by_column, "gy", 0).reshape(block_rows, reach_width)
        ratio = reach_rate * jnp.power(storage, 2.0 / 3.0)
        outflow = storage * ratio / (1.0 + ratio)
        own_part = block_term(downstream, outflow, first_block, block_rows)
        ahead_part = block_term(downstream, outflow, first_block + block_rows, block_rows)
        upstream = own_part + shifted(ahead_part, ("gy", "gx"), 1)
        storage = storage - outflow + upstream + lateral_gain * lateral
    return (depth, flux_east, flux_south, storage)


def solution(mesh):
    placed = (
        P("gy", "gx"),
        P("gy", "gx"),
        P("gy", "gx"),
        P("gy", "gx"),
        P("gy", "gx"),
        P("gy", "gx"),
        P(("gy", "gx")),
        P(("gy", "gx"), None),
        P(("gy", "gx"), None),
        P(("gy", "gx")),
    )
    return jax.shard_map(
        body,
        mesh=mesh,
        in_specs=placed,
        out_specs=(P("gy", "gx"), P("gy", "gx"), P("gy", "gx"), P(("gy", "gx"), None)),
        check_vma=False,
    )
```

profile of v0, /device:TPU:1, one launch (start us, length us, event | category | flops | bytes accessed | tf_op | source)
XLA Modules:
  0.0 122.6 jit_solution(14846101160106319228)
XLA Ops:
  1.4 3.3 %collective-permute-start.3 = (f32[512]{0:T(512)S(1)}, f32[512]{0:T(512)S(1)}, u32[]{:S(2)}, u32[]{:S(2)}) collective-permute-start(f32[512]{0:T(512)S(1)} %bitcast.62), channel_id=1, source_target_pairs={{16,0},{32,16},{48,32},{64,48},{80,64},{96,80},{112,96},{17,1},{33... | collective-permute-start | bytes 6152 | tf_op jit(solution)/shard_map/ppermute | solution.py:21
  5.7 1.3 %collective-permute-start = (f32[512]{0:T(512)S(1)}, f32[512]{0:T(512)S(1)}, u32[]{:S(2)}, u32[]{:S(2)}) collective-permute-start(f32[512]{0:T(512)S(1)} %slice_reduce_fusion.5), channel_id=1, source_target_pairs={{1,0},{2,1},{3,2},{4,3},{5,4},{6,5},{7,6},{8,7},{9,8},{10,9},{11,1... | collective-permute-start | bytes 6152 | tf_op jit(solution)/shard_map/ppermute | solution.py:21
  7.0 1.8 %add.135 = f32[512,512]{1,0:T(8,128)S(1)} add(f32[512,512]{1,0:T(8,128)} %param.13, f32[512,512]{1,0:T(8,128)} %param.10) | non-fusion elementwise | flops 262144 | bytes 3145728 | tf_op jit(solution)/shard_map/add | solution.py:88
  8.9 1.3 %collective-permute-start.1 = (f32[512]{0:T(512)S(1)}, f32[512]{0:T(512)S(1)}, u32[]{:S(2)}, u32[]{:S(2)}) collective-permute-start(f32[512]{0:T(512)S(1)} %slice_reduce_fusion.4), channel_id=1, source_target_pairs={{1,0},{2,1},{3,2},{4,3},{5,4},{6,5},{7,6},{8,7},{9,8},{10,9},{11,1... | collective-permute-start | bytes 6152 | tf_op jit(solution)/shard_map/ppermute | solution.py:21
  10.3 1.9 %collective-permute-start.4 = (f32[512]{0:T(512)S(1)}, f32[512]{0:T(512)S(1)}, u32[]{:S(2)}, u32[]{:S(2)}) collective-permute-start(f32[512]{0:T(512)S(1)} %bitcast.64), channel_id=1, source_target_pairs={{16,0},{32,16},{48,32},{64,48},{80,64},{96,80},{112,96},{17,1},{33... | collective-permute-start | bytes 6152 | tf_op jit(solution)/shard_map/ppermute | solution.py:21
  13.3 1.3 %slice.96 = f32[512,511]{1,0:T(8,128)} slice(f32[512,512]{1,0:T(8,128)S(1)} %add.135), slice={[0:512], [1:512]} | slice | bytes 2093056 | tf_op jit(solution)/shard_map/slice | solution.py:91
  15.7 1.3 %slice.72 = f32[512,511]{1,0:T(8,128)} slice(f32[512,512]{1,0:T(8,128)S(1)} %copy-done), slice={[0:512], [1:512]} | slice | bytes 2093056 | tf_op jit(solution)/shard_map/slice | solution.py:92
  18.0 5.4 %fusion.18 = (f32[512,512]{1,0:T(8,128)S(1)}, f32[512,512]{1,0:T(8,128)S(1)}) fusion(f32[512,512]{1,0:T(8,128)} %param.11, f32[512,512]{1,0:T(8,128)S(1)} %add.135, f32[512,1]{1,0:T(8,128)} %copy.21, f32[512,511]{1,0:T(8,128)} %slice.96, f32[512,512]{1,0:T(8,128)} %param.14, f32[512,1]{1,0:T(8,128)S(1)} %copy.20, f32[512,511]{1,0:T(8,128)} %slice.72, ...), kind=kLoop, calls=%fused_computation.18 | loop fusion | flops 9437184 | bytes 12587008 | tf_op jit(solution)/shard_map/div | solution.py:39
  24.4 3.6 %collective-permute-start.5 = (f32[512]{0:T(512)S(1)}, f32[512]{0:T(512)S(1)}, u32[]{:S(2)}, u32[]{:S(2)}) collective-permute-start(f32[512]{0:T(512)S(1)} %bitcast.67), channel_id=1, source_target_pairs={{0,16},{16,32},{32,48},{48,64},{64,80},{80,96},{96,112},{1,17},{17... | collective-permute-start | bytes 6152 | tf_op jit(solution)/shard_map/ppermute | solution.py:21
  28.0 4.6 %collective-permute-start.2 = (f32[512]{0:T(512)S(1)}, f32[512]{0:T(512)S(1)}, u32[]{:S(2)}, u32[]{:S(2)}) collective-permute-start(f32[512]{0:T(512)S(1)} %slice_reduce_fusion.3), channel_id=1, source_target_pairs={{0,1},{1,2},{2,3},{3,4},{4,5},{5,6},{6,7},{7,8},{8,9},{9,10},{10,1... | collective-permute-start | bytes 6152 | tf_op jit(solution)/shard_map/ppermute | solution.py:21
  33.5 3.8 %bitcast_reduce_fusion.1 = (f32[64,4,128]{2,1,0:T(4,128)S(1)}, f32[64,4,128]{2,1,0:T(4,128)}, f32[512,512]{1,0:T(8,128)S(1)}) fusion(f32[512,512]{1,0:T(8,128)S(1)} %copy-done, s32[512,512]{1,0:T(8,128)} %param.15, f32[512,512]{1,0:T(8,128)} %copy-done.1, f32[511,512]{1,0:T(8,128)} %bitcast.49, f32[1,512]{1,0:T(1,128)S(1)} %bitcast.60, ...), kind=kLoop, calls=%fused_computation.59 | loop fusion | flops 4128768 | bytes 7602176 | tf_op jit(solution)/shard_map/reduce_sum | solution.py:109
  39.4 10.7 %all-to-all-start = ((f32[16,8,1,16,128]{4,3,1,2,0:T(8,128)}), f32[16,8,1,16,128]{4,3,1,2,0:T(8,128)}, u32[]{:S(2)}, u32[]{:S(2)}) async-start(f32[16,8,1,16,128]{4,3,1,2,0:T(8,128)} %copy.26), calls=%async_computation | async-start | bytes 2097152 | tf_op jit(solution)/shard_map/all_to_all | solution.py:31
  50.1 1.5 %add.145 = f32[512,512]{1,0:T(8,128)S(1)} add(f32[512,512]{1,0:T(8,128)} %param.13, f32[512,512]{1,0:T(8,128)S(1)} %get-tuple-element.6) | non-fusion elementwise | flops 262144 | bytes 3145728 | tf_op jit(solution)/shard_map/add | solution.py:88
  51.8 1.3 %collective-permute-start.6 = (f32[512]{0:T(512)S(1)}, f32[512]{0:T(512)S(1)}, u32[]{:S(2)}, u32[]{:S(2)}) collective-permute-start(f32[512]{0:T(512)S(1)} %slice_reduce_fusion.2), channel_id=1, source_target_pairs={{1,0},{2,1},{3,2},{4,3},{5,4},{6,5},{7,6},{8,7},{9,8},{10,9},{11,1... | collective-permute-start | bytes 6152 | tf_op jit(solution)/shard_map/ppermute | solution.py:21
  53.1 2.1 %collective-permute-start.9 = (f32[512]{0:T(512)S(1)}, f32[512]{0:T(512)S(1)}, u32[]{:S(2)}, u32[]{:S(2)}) collective-permute-start(f32[512]{0:T(512)S(1)} %bitcast.63), channel_id=1, source_target_pairs={{16,0},{32,16},{48,32},{64,48},{80,64},{96,80},{112,96},{17,1},{33... | collective-permute-start | bytes 6152 | tf_op jit(solution)/shard_map/ppermute | solution.py:21
  57.5 1.3 %collective-permute-start.7 = (f32[512]{0:T(512)S(1)}, f32[512]{0:T(512)S(1)}, u32[]{:S(2)}, u32[]{:S(2)}) collective-permute-start(f32[512]{0:T(512)S(1)} %slice_reduce_fusion.1), channel_id=1, source_target_pairs={{1,0},{2,1},{3,2},{4,3},{5,4},{6,5},{7,6},{8,7},{9,8},{10,9},{11,1... | collective-permute-start | bytes 6152 | tf_op jit(solution)/shard_map/ppermute | solution.py:21
  58.9 2.1 %collective-permute-start.10 = (f32[512]{0:T(512)S(1)}, f32[512]{0:T(512)S(1)}, u32[]{:S(2)}, u32[]{:S(2)}) collective-permute-start(f32[512]{0:T(512)S(1)} %bitcast.65), channel_id=1, source_target_pairs={{16,0},{32,16},{48,32},{64,48},{80,64},{96,80},{112,96},{17,1},{33... | collective-permute-start | bytes 6152 | tf_op jit(solution)/shard_map/ppermute | solution.py:21
  60.9 7.4 %all-to-all-done = f32[16,8,1,16,128]{4,3,1,2,0:T(8,128)} async-done(((f32[16,8,1,16,128]{4,3,1,2,0:T(8,128)}), f32[16,8,1,16,128]{4,3,1,2,0:T(8,128)}, u32[]{:S(2)}, u32[]{:S(2)}) %all-to-all-start) | async-done | bytes 1048608 | tf_op jit(solution)/shard_map/all_to_all | solution.py:31
  68.3 4.3 %all-to-all-start.2 = ((f32[16,8,1,16,128]{4,3,1,2,0:T(8,128)}), f32[16,8,1,16,128]{4,3,1,2,0:T(8,128)}, u32[]{:S(2)}, u32[]{:S(2)}) async-start(f32[16,8,1,16,128]{4,3,1,2,0:T(8,128)} %copy.27), calls=%async_computation.2 | async-start | bytes 2097152 | tf_op jit(solution)/shard_map/all_to_all | solution.py:31
  73.6 3.1 %collective-permute-start.12 = (f32[16,128]{1,0:T(8,128)}, f32[16,128]{1,0:T(8,128)}, u32[]{:S(2)}, u32[]{:S(2)}) collective-permute-start(f32[16,128]{1,0:T(8,128)} %fusion.56), channel_id=1, source_target_pairs={{0,1},{1,2},{2,3},{3,4},{4,5},{5,6},{6,7},{7,8},{8,9},{9,10},{10,1... | collective-permute-start | bytes 24584 | tf_op jit(solution)/shard_map/ppermute | solution.py:21
  77.8 1.3 %slice.106 = f32[512,511]{1,0:T(8,128)} slice(f32[512,512]{1,0:T(8,128)S(1)} %add.145), slice={[0:512], [1:512]} | slice | bytes 2093056 | tf_op jit(solution)/shard_map/slice | solution.py:91
  80.2 1.3 %slice.104 = f32[512,511]{1,0:T(8,128)} slice(f32[512,512]{1,0:T(8,128)S(1)} %get-tuple-element.6), slice={[0:512], [1:512]} | slice | bytes 2093056 | tf_op jit(solution)/shard_map/slice | solution.py:92
  82.6 6.0 %fusion.47 = (f32[512,512]{1,0:T(8,128)}, f32[512,512]{1,0:T(8,128)S(1)}) fusion(f32[512,512]{1,0:T(8,128)} %copy-done.1, f32[512,512]{1,0:T(8,128)S(1)} %add.145, f32[1,512]{1,0:T(1,128)S(1)} %bitcast.71, f32[511,512]{1,0:T(8,128)} %slice.112, f32[512,512]{1,0:T(8,128)} %param.14, f32[1,512]{1,0:T(1,128)S(1)} %bitcast.69, f32[511,512]{1,0:T(8,128)} %slice.110, ...), kind=kLoop, calls=%fused_computation.56 | loop fusion | flops 9437184 | bytes 12587008 | tf_op jit(solution)/shard_map/div | solution.py:39
  89.7 3.1 %collective-permute-start.8 = (f32[512]{0:T(512)S(1)}, f32[512]{0:T(512)S(1)}, u32[]{:S(2)}, u32[]{:S(2)}) collective-permute-start(f32[512]{0:T(512)S(1)} %slice_reduce_fusion), channel_id=1, source_target_pairs={{0,1},{1,2},{2,3},{3,4},{4,5},{5,6},{6,7},{7,8},{8,9},{9,10},{10,1... | collective-permute-start | bytes 6152 | tf_op jit(solution)/shard_map/ppermute | solution.py:21
  92.9 2.0 %reduce_sum.55 = f32[8,16,128]{2,1,0:T(8,128)} reduce(f32[16,8,1,16,128]{4,3,1,2,0:T(8,128)} %all-to-all-done, f32[]{:T(128)} %constant.39.clone.1), dimensions={0,2}, to_apply=%region_1.0 | reduce | flops 245760 | bytes 1114116 | tf_op jit(solution)/shard_map/reduce_sum | solution.py:32
  94.9 5.6 %all-to-all-start.1 = ((f32[8,1,1,16,128]{4,3,2,1,0:T(8,128)}), f32[8,1,1,16,128]{4,3,2,1,0:T(8,128)S(1)}, u32[]{:S(2)}, u32[]{:S(2)}) async-start(f32[8,1,1,16,128]{4,3,2,1,0:T(8,128)} %bitcast.24), calls=%async_computation.1 | async-start | bytes 131072 | tf_op jit(solution)/shard_map/all_to_all | solution.py:31
  101.7 3.5 %collective-permute-start.11 = (f32[512]{0:T(512)S(1)}, f32[512]{0:T(512)S(1)}, u32[]{:S(2)}, u32[]{:S(2)}) collective-permute-start(f32[512]{0:T(512)S(1)} %bitcast.66), channel_id=1, source_target_pairs={{0,16},{16,32},{32,48},{48,64},{64,80},{80,96},{96,112},{1,17},{17... | collective-permute-start | bytes 6152 | tf_op jit(solution)/shard_map/ppermute | solution.py:21
  105.4 1.9 %reduce_sum.58 = f32[8,16,128]{2,1,0:T(8,128)} reduce(f32[16,8,1,16,128]{4,3,1,2,0:T(8,128)} %all-to-all-done.2, f32[]{:T(128)} %constant.39.clone.1), dimensions={0,2}, to_apply=%region_4.0 | reduce | flops 245760 | bytes 1114116 | tf_op jit(solution)/shard_map/reduce_sum | solution.py:32
  107.4 4.1 %all-to-all-start.3 = ((f32[8,1,1,16,128]{4,3,2,1,0:T(8,128)}), f32[8,1,1,16,128]{4,3,2,1,0:T(8,128)S(1)}, u32[]{:S(2)}, u32[]{:S(2)}) async-start(f32[8,1,1,16,128]{4,3,2,1,0:T(8,128)} %bitcast.31), calls=%async_computation.3 | async-start | bytes 131072 | tf_op jit(solution)/shard_map/all_to_all | solution.py:31
  113.5 2.8 %collective-permute-start.13 = (f32[16,128]{1,0:T(8,128)S(1)}, f32[16,128]{1,0:T(8,128)S(1)}, u32[]{:S(2)}, u32[]{:S(2)}) collective-permute-start(f32[16,128]{1,0:T(8,128)S(1)} %fusion.54), channel_id=1, source_target_pairs={{0,1},{1,2},{2,3},{3,4},{4,5},{5,6},{6,7},{7,8},{8,9},{9,10},{10,1... | collective-permute-start | bytes 24584 | tf_op jit(solution)/shard_map/ppermute | solution.py:21
  116.3 3.4 %fusion.40 = f32[512,512]{1,0:T(8,128)} fusion(f32[512,512]{1,0:T(8,128)S(1)} %get-tuple-element.6, f32[512,512]{1,0:T(8,128)S(1)} %copy-done.4, f32[512,511]{1,0:T(8,128)S(1)} %bitcast.50, f32[512,1]{1,0:T(8,128)S(1)} %copy.25, f32[512,512]{1,0:T(8,128)} %get-tuple-element.7, f32[511,512]{1,0:T(8,128)} %bitcast.51, f32[1,512]{1,0:T(1,128)S(1)} %bitcast.57, ...), kind=kLoop, calls=%fused_computation.47 | loop fusion | flops 3145728 | bytes 7340032 | tf_op jit(solution)/shard_map/sub | solution.py:106
  119.7 2.0 %collective-permute-done.13 = f32[16,128]{1,0:T(8,128)S(1)} collective-permute-done((f32[16,128]{1,0:T(8,128)S(1)}, f32[16,128]{1,0:T(8,128)S(1)}, u32[]{:S(2)}, u32[]{:S(2)}) %collective-permute-start.13) | collective-permute-done | bytes 8224 | tf_op jit(solution)/shard_map/ppermute | solution.py:21
  (80 shorter events, 21.2 us)
Async XLA Ops:
  1.4 16.7 %collective-permute-start.3 = (f32[512]{0:T(512)S(1)}, f32[512]{0:T(512)S(1)}, u32[]{:S(2)}, u32[]{:S(2)}) collective-permute-start(f32[512]{0:T(512)S(1)} %bitcast.62), channel_id=1, source_target_pairs={{16,0},{32,16},{48,32},{64,48},{80,64},{96,80},{112,96},{17,1},{33... | collective-permute-start | bytes 6152 | tf_op jit(solution)/shard_map/ppermute | solution.py:21
  5.7 11.3 %collective-permute-start = (f32[512]{0:T(512)S(1)}, f32[512]{0:T(512)S(1)}, u32[]{:S(2)}, u32[]{:S(2)}) collective-permute-start(f32[512]{0:T(512)S(1)} %slice_reduce_fusion.5), channel_id=1, source_target_pairs={{1,0},{2,1},{3,2},{4,3},{5,4},{6,5},{7,6},{8,7},{9,8},{10,9},{11,1... | collective-permute-start | bytes 6152 | tf_op jit(solution)/shard_map/ppermute | solution.py:21
  8.9 8.2 %collective-permute-start.1 = (f32[512]{0:T(512)S(1)}, f32[512]{0:T(512)S(1)}, u32[]{:S(2)}, u32[]{:S(2)}) collective-permute-start(f32[512]{0:T(512)S(1)} %slice_reduce_fusion.4), channel_id=1, source_target_pairs={{1,0},{2,1},{3,2},{4,3},{5,4},{6,5},{7,6},{8,7},{9,8},{10,9},{11,1... | collective-permute-start | bytes 6152 | tf_op jit(solution)/shard_map/ppermute | solution.py:21
  10.3 7.8 %collective-permute-start.4 = (f32[512]{0:T(512)S(1)}, f32[512]{0:T(512)S(1)}, u32[]{:S(2)}, u32[]{:S(2)}) collective-permute-start(f32[512]{0:T(512)S(1)} %bitcast.64), channel_id=1, source_target_pairs={{16,0},{32,16},{48,32},{64,48},{80,64},{96,80},{112,96},{17,1},{33... | collective-permute-start | bytes 6152 | tf_op jit(solution)/shard_map/ppermute | solution.py:21
  13.3 1.3 %copy-start = (f32[512,512]{1,0:T(8,128)S(1)}, f32[512,512]{1,0:T(8,128)}, u32[]{:S(2)}) copy-start(f32[512,512]{1,0:T(8,128)} %param.10) | copy-start | bytes 3145732
  23.4 1.0 copy-start.1
  24.4 9.1 %collective-permute-start.5 = (f32[512]{0:T(512)S(1)}, f32[512]{0:T(512)S(1)}, u32[]{:S(2)}, u32[]{:S(2)}) collective-permute-start(f32[512]{0:T(512)S(1)} %bitcast.67), channel_id=1, source_target_pairs={{0,16},{16,32},{32,48},{48,64},{64,80},{80,96},{96,112},{1,17},{17... | collective-permute-start | bytes 6152 | tf_op jit(solution)/shard_map/ppermute | solution.py:21
  28.0 5.3 %collective-permute-start.2 = (f32[512]{0:T(512)S(1)}, f32[512]{0:T(512)S(1)}, u32[]{:S(2)}, u32[]{:S(2)}) collective-permute-start(f32[512]{0:T(512)S(1)} %slice_reduce_fusion.3), channel_id=1, source_target_pairs={{0,1},{1,2},{2,3},{3,4},{4,5},{5,6},{6,7},{7,8},{8,9},{9,10},{10,1... | collective-permute-start | bytes 6152 | tf_op jit(solution)/shard_map/ppermute | solution.py:21
  33.5 3.8 %copy-start.6 = (s32[256]{0:T(256)S(1)}, s32[256]{0:T(256)}, u32[]{:S(2)}) copy-start(s32[256]{0:T(256)} %param.16) | copy-start | bytes 3076
  39.4 28.9 %all-to-all-start = ((f32[16,8,1,16,128]{4,3,1,2,0:T(8,128)}), f32[16,8,1,16,128]{4,3,1,2,0:T(8,128)}, u32[]{:S(2)}, u32[]{:S(2)}) async-start(f32[16,8,1,16,128]{4,3,1,2,0:T(8,128)} %copy.26), calls=%async_computation | async-start | bytes 2097152 | tf_op jit(solution)/shard_map/all_to_all | solution.py:31
  50.1 22.6 %copy-start.12 = (s32[16]{0:T(128)}, s32[16]{0:T(128)S(1)}, u32[]{:S(2)}) copy-start(s32[16]{0:T(128)S(1)} %iota_add_fusion) | copy-start | bytes 196
  50.1 5.1 %copy-start.5 = (f32[64,4,128]{2,1,0:T(4,128)S(1)}, f32[64,4,128]{2,1,0:T(4,128)}, u32[]{:S(2)}) copy-start(f32[64,4,128]{2,1,0:T(4,128)} %get-tuple-element.5) | copy-start | bytes 393220
  51.8 29.8 %collective-permute-start.6 = (f32[512]{0:T(512)S(1)}, f32[512]{0:T(512)S(1)}, u32[]{:S(2)}, u32[]{:S(2)}) collective-permute-start(f32[512]{0:T(512)S(1)} %slice_reduce_fusion.2), channel_id=1, source_target_pairs={{1,0},{2,1},{3,2},{4,3},{5,4},{6,5},{7,6},{8,7},{9,8},{10,9},{11,1... | collective-permute-start | bytes 6152 | tf_op jit(solution)/shard_map/ppermute | solution.py:21
  53.1 29.5 %collective-permute-start.9 = (f32[512]{0:T(512)S(1)}, f32[512]{0:T(512)S(1)}, u32[]{:S(2)}, u32[]{:S(2)}) collective-permute-start(f32[512]{0:T(512)S(1)} %bitcast.63), channel_id=1, source_target_pairs={{16,0},{32,16},{48,32},{64,48},{80,64},{96,80},{112,96},{17,1},{33... | collective-permute-start | bytes 6152 | tf_op jit(solution)/shard_map/ppermute | solution.py:21
  57.5 24.2 %collective-permute-start.7 = (f32[512]{0:T(512)S(1)}, f32[512]{0:T(512)S(1)}, u32[]{:S(2)}, u32[]{:S(2)}) collective-permute-start(f32[512]{0:T(512)S(1)} %slice_reduce_fusion.1), channel_id=1, source_target_pairs={{1,0},{2,1},{3,2},{4,3},{5,4},{6,5},{7,6},{8,7},{9,8},{10,9},{11,1... | collective-permute-start | bytes 6152 | tf_op jit(solution)/shard_map/ppermute | solution.py:21
  58.8 13.9 %copy-start.7 = (f32[16,128]{1,0:T(8,128)S(1)}, f32[16,128]{1,0:T(8,128)}, u32[]{:S(2)}) copy-start(f32[16,128]{1,0:T(8,128)} %param.17) | copy-start | bytes 24580
  58.8 13.9 %copy-start.8 = (f32[16,128]{1,0:T(8,128)S(1)}, f32[16,128]{1,0:T(8,128)}, u32[]{:S(2)}) copy-start(f32[16,128]{1,0:T(8,128)} %param.18) | copy-start | bytes 24580
  58.8 13.9 %copy-start.10 = (s32[16]{0:T(128)S(1)}, s32[16]{0:T(128)}, u32[]{:S(2)}) copy-start(s32[16]{0:T(128)} %param.19) | copy-start | bytes 196
  58.9 23.7 %collective-permute-start.10 = (f32[512]{0:T(512)S(1)}, f32[512]{0:T(512)S(1)}, u32[]{:S(2)}, u32[]{:S(2)}) collective-permute-start(f32[512]{0:T(512)S(1)} %bitcast.65), channel_id=1, source_target_pairs={{16,0},{32,16},{48,32},{64,48},{80,64},{96,80},{112,96},{17,1},{33... | collective-permute-start | bytes 6152 | tf_op jit(solution)/shard_map/ppermute | solution.py:21
  68.3 26.5 %all-to-all-start.2 = ((f32[16,8,1,16,128]{4,3,1,2,0:T(8,128)}), f32[16,8,1,16,128]{4,3,1,2,0:T(8,128)}, u32[]{:S(2)}, u32[]{:S(2)}) async-start(f32[16,8,1,16,128]{4,3,1,2,0:T(8,128)} %copy.27), calls=%async_computation.2 | async-start | bytes 2097152 | tf_op jit(solution)/shard_map/all_to_all | solution.py:31
  73.6 37.9 %collective-permute-start.12 = (f32[16,128]{1,0:T(8,128)}, f32[16,128]{1,0:T(8,128)}, u32[]{:S(2)}, u32[]{:S(2)}) collective-permute-start(f32[16,128]{1,0:T(8,128)} %fusion.56), channel_id=1, source_target_pairs={{0,1},{1,2},{2,3},{3,4},{4,5},{5,6},{6,7},{7,8},{8,9},{9,10},{10,1... | collective-permute-start | bytes 24584 | tf_op jit(solution)/shard_map/ppermute | solution.py:21
  88.5 1.0 copy-start.3
  89.7 15.5 %collective-permute-start.8 = (f32[512]{0:T(512)S(1)}, f32[512]{0:T(512)S(1)}, u32[]{:S(2)}, u32[]{:S(2)}) collective-permute-start(f32[512]{0:T(512)S(1)} %slice_reduce_fusion), channel_id=1, source_target_pairs={{0,1},{1,2},{2,3},{3,4},{4,5},{5,6},{6,7},{7,8},{8,9},{9,10},{10,1... | collective-permute-start | bytes 6152 | tf_op jit(solution)/shard_map/ppermute | solution.py:21
  92.8 23.5 %copy-start.4 = (f32[512,512]{1,0:T(8,128)S(1)}, f32[512,512]{1,0:T(8,128)}, u32[]{:S(2)}) copy-start(f32[512,512]{1,0:T(8,128)} %copy-done.3) | copy-start | bytes 3145732
  94.9 21.4 %copy-start.2 = (s32[512,512]{1,0:T(8,128)S(1)}, s32[512,512]{1,0:T(8,128)}, u32[]{:S(2)}) copy-start(s32[512,512]{1,0:T(8,128)} %param.15) | copy-start | bytes 3145732
  94.9 12.5 %all-to-all-start.1 = ((f32[8,1,1,16,128]{4,3,2,1,0:T(8,128)}), f32[8,1,1,16,128]{4,3,2,1,0:T(8,128)S(1)}, u32[]{:S(2)}, u32[]{:S(2)}) async-start(f32[8,1,1,16,128]{4,3,2,1,0:T(8,128)} %bitcast.24), calls=%async_computation.1 | async-start | bytes 131072 | tf_op jit(solution)/shard_map/all_to_all | solution.py:31
  101.7 14.5 %collective-permute-start.11 = (f32[512]{0:T(512)S(1)}, f32[512]{0:T(512)S(1)}, u32[]{:S(2)}, u32[]{:S(2)}) collective-permute-start(f32[512]{0:T(512)S(1)} %bitcast.66), channel_id=1, source_target_pairs={{0,16},{16,32},{32,48},{48,64},{64,80},{80,96},{96,112},{1,17},{17... | collective-permute-start | bytes 6152 | tf_op jit(solution)/shard_map/ppermute | solution.py:21
  107.4 12.3 %all-to-all-start.3 = ((f32[8,1,1,16,128]{4,3,2,1,0:T(8,128)}), f32[8,1,1,16,128]{4,3,2,1,0:T(8,128)S(1)}, u32[]{:S(2)}, u32[]{:S(2)}) async-start(f32[8,1,1,16,128]{4,3,2,1,0:T(8,128)} %bitcast.31), calls=%async_computation.3 | async-start | bytes 131072 | tf_op jit(solution)/shard_map/all_to_all | solution.py:31
  113.5 8.3 %collective-permute-start.13 = (f32[16,128]{1,0:T(8,128)S(1)}, f32[16,128]{1,0:T(8,128)S(1)}, u32[]{:S(2)}, u32[]{:S(2)}) collective-permute-start(f32[16,128]{1,0:T(8,128)S(1)} %fusion.54), channel_id=1, source_target_pairs={{0,1},{1,2},{2,3},{3,4},{4,5},{5,6},{6,7},{7,8},{8,9},{9,10},{10,1... | collective-permute-start | bytes 24584 | tf_op jit(solution)/shard_map/ppermute | solution.py:21
  116.3 5.4 %copy-start.9 = (f32[16,128]{1,0:T(8,128)S(1)}, f32[16,128]{1,0:T(8,128)}, u32[]{:S(2)}) copy-start(f32[16,128]{1,0:T(8,128)} %param.18) | copy-start | bytes 24580
  116.3 5.4 %copy-start.11 = (s32[16]{0:T(128)S(1)}, s32[16]{0:T(128)}, u32[]{:S(2)}) copy-start(s32[16]{0:T(128)} %param.19) | copy-start | bytes 196
  116.3 5.4 %copy-start.13 = (s32[16]{0:T(128)S(1)}, s32[16]{0:T(128)}, u32[]{:S(2)}) copy-start(s32[16]{0:T(128)} %iota_add_fusion.1) | copy-start | bytes 196
where the time goes:
time: 124 us; the launch traced here: 123 us
  starting transfers between devices  60 us (48%)
  other arithmetic  26.1 us (21%)
  local copies, waits for them, and re-layouts  19.4 us (16%)
  waiting for transfers between devices  10.2 us (8%)
  matrix products  5.8 us (5%)
    ppermute x14, starting transfers between devices, shifted(): lax.ppermute(value, axis, [(source, source + steps) for source in range(f...  35.3 us
    all_to_all x4, starting transfers between devices, sum_at_owner(): lax.all_to_all(in_blocks(value, dim, length), axis, 0, 0, tiled=True)  24.7 us
    div x2, other arithmetic, face_update(): return active * drive / damping  11.3 us
    all_to_all x4, waiting for transfers between devices, sum_at_owner(): lax.all_to_all(in_blocks(value, dim, length), axis, 0, 0, tiled=True)  7.44 us
    dot_general x6, matrix products, block_term(): jnp.einsum('tb,tc->bc', onehot, values, precision=lax.Precision.HIGHEST)  5.8 us
    reduce_sum x4, other arithmetic, sum_at_owner(): return jnp.sum(parts, axis=0)  3.95 us
    reduce_sum x1, other arithmetic, body(): tile_sums = drained.reshape(cell_rows // STRIP, STRIP, cell_cols // reach...  3.76 us
    sub x1, other arithmetic, body(): depth - mass_gain * (flux_east - west_flux + (flux_south - north_flux))  3.35 us
  transfers between devices with their start and end apart: 18, of which 3 were waited for; matrix products, arithmetic and copies ran while one was open for 30% of the time, Pallas kernels for 0%

commit v1 on v0

v1 whole, which is shorter than its diff:
```python
import jax
import jax.numpy as jnp
from jax import lax
from jax.sharding import PartitionSpec as P

STRIP = 8
STEPS = 2


rim_depth = 0.1
slope_gain = 0.1
friction_gain = 1.0
mass_gain = 0.05
drain_rate = 0.05
lateral_gain = 0.125


def shifted(value, axis, steps):
    count = lax.axis_size(axis)
    first, last = (max(0, -steps), min(count, count - steps))
    return lax.ppermute(value, axis, [(source, source + steps) for source in range(first, last)])


def face_update(flux, level, level_next, depth, depth_next, roughness, active):
    face_depth = rim_depth + 0.5 * (jnp.abs(depth) + jnp.abs(depth_next))
    drive = flux - slope_gain * face_depth * (level_next - level)
    damping = 1.0 + friction_gain * roughness * jnp.abs(flux) / jnp.power(face_depth, 7.0 / 3.0)
    return active * drive / damping


def onehot_sum(ids, values, count):
    targets = lax.iota(jnp.float32, count)
    onehot = (targets[:, None] == ids[None, :]).astype(jnp.float32)
    return jnp.dot(onehot, values, precision=lax.Precision.HIGHEST)


def block_term(target_ids, values, start, count):
    targets = start + lax.iota(jnp.int32, count)
    onehot = (target_ids[:, None] == targets[None, :]).astype(jnp.float32)
    return jnp.einsum("tb,tc->bc", onehot, values, precision=lax.Precision.HIGHEST)


def body(
    water_depth,
    flux_east,
    flux_south,
    bed_level,
    roughness,
    land_mask,
    tile_block,
    storage,
    reach_rate,
    downstream,
):
    cell_rows, cell_cols = water_depth.shape
    block_rows, reach_width = storage.shape
    row_count = lax.axis_size("gy")
    col_count = lax.axis_size("gx")
    row_index = lax.axis_index("gy")
    col_index = lax.axis_index("gx")
    device_count = row_count * col_count
    tile_count = tile_block.shape[0]
    slot_cap = max(2, 2 * tile_count // device_count)
    land_float = land_mask.astype(jnp.float32)
    global_cols = col_index * cell_cols + lax.iota(jnp.int32, cell_cols)
    global_rows = row_index * cell_rows + lax.iota(jnp.int32, cell_rows)
    east_open = land_float * (global_cols < cell_cols * col_count - 1).astype(jnp.float32)[None, :]
    south_open = land_float * (global_rows < cell_rows * row_count - 1).astype(jnp.float32)[:, None]
    device_index = row_index * col_count + col_index
    first_block = device_index * block_rows

    column_slots = row_count * slot_cap
    tile_owner = tile_block // block_rows
    owner_row = tile_owner // col_count
    owner_col = tile_owner % col_count
    owner_hits = (tile_owner[:, None] == lax.iota(jnp.int32, device_count)[None, :]).astype(
        jnp.int32
    )
    earlier = jnp.sum((jnp.cumsum(owner_hits, axis=0) - owner_hits) * owner_hits, axis=1)
    send_pos = owner_col * column_slots + owner_row * slot_cap + earlier
    column_ids = (owner_row * block_rows + tile_block % block_rows).astype(jnp.float32)
    send_ids = jnp.full((col_count * column_slots,), -1.0, jnp.float32).at[send_pos].set(column_ids)
    id_rows = -(-column_slots // reach_width)
    send_ids = jnp.pad(
        send_ids.reshape(col_count, column_slots),
        ((0, 0), (0, id_rows * reach_width - column_slots)),
        constant_values=-1.0,
    ).reshape(col_count, id_rows, reach_width)
    gather_onehot = (
        lax.iota(jnp.int32, col_count * column_slots)[:, None] == send_pos[None, :]
    ).astype(jnp.float32)

    def lateral_of(drained, first):
        tile_sums = drained.reshape(
            cell_rows // STRIP, STRIP, cell_cols // reach_width, reach_width
        ).sum(axis=1)
        tile_sums = tile_sums.reshape(-1, reach_width)
        packed = jnp.dot(gather_onehot, tile_sums, precision=lax.Precision.HIGHEST)
        packed = packed.reshape(col_count, column_slots, reach_width)
        if first:
            packed = jnp.concatenate([packed, send_ids], axis=1)
        got = lax.all_to_all(packed, "gx", 0, 0, tiled=True)
        got_vals = got[:, :column_slots].reshape(-1, reach_width)
        got_ids = got[:, column_slots:].reshape(col_count, -1)[:, :column_slots].reshape(-1)
        return got_vals, got_ids

    def finish_lateral(got_vals, got_ids):
        by_column = onehot_sum(got_ids, got_vals, row_count * block_rows)
        by_column = by_column.reshape(row_count, block_rows, reach_width)
        parts = lax.all_to_all(by_column, "gy", 0, 0, tiled=True)
        return jnp.sum(parts, axis=0)

    recv_ids = None
    depth = water_depth
    for step in range(STEPS):
        level = bed_level + depth
        east_msg = shifted(jnp.stack([level[:, 0], depth[:, 0]]), "gx", -1)
        south_msg = shifted(jnp.stack([level[0, :], depth[0, :]]), "gy", -1)
        west_msg = shifted(
            jnp.stack(
                [flux_east[:, -1], level[:, -1], depth[:, -1], roughness[:, -1], east_open[:, -1]]
            ),
            "gx",
            1,
        )
        north_msg = shifted(
            jnp.stack(
                [flux_south[-1, :], level[-1, :], depth[-1, :], roughness[-1, :], south_open[-1, :]]
            ),
            "gy",
            1,
        )
        drained = drain_rate * land_float * jnp.abs(depth)
        got_vals, got_ids = lateral_of(drained, step == 0)
        if step == 0:
            recv_ids = got_ids
        level_east = jnp.concatenate([level[:, 1:], east_msg[0][:, None]], axis=1)
        depth_east = jnp.concatenate([depth[:, 1:], east_msg[1][:, None]], axis=1)
        level_south = jnp.concatenate([level[1:], south_msg[0][None, :]], axis=0)
        depth_south = jnp.concatenate([depth[1:], south_msg[1][None, :]], axis=0)
        west_edge = face_update(
            west_msg[0], west_msg[1], level[:, 0], west_msg[2], depth[:, 0], west_msg[3], west_msg[4]
        )
        north_edge = face_update(
            north_msg[0], north_msg[1], level[0, :], north_msg[2], depth[0, :], north_msg[3],
            north_msg[4],
        )
        flux_east = face_update(
            flux_east, level, level_east, depth, depth_east, roughness, east_open
        )
        flux_south = face_update(
            flux_south, level, level_south, depth, depth_south, roughness, south_open
        )
        west_flux = jnp.concatenate([west_edge[:, None], flux_east[:, :-1]], axis=1)
        north_flux = jnp.concatenate([north_edge[None, :], flux_south[:-1]], axis=0)
        depth = depth - mass_gain * (flux_east - west_flux + (flux_south - north_flux)) - drained
        lateral = finish_lateral(got_vals, recv_ids)
        ratio = reach_rate * jnp.power(storage, 2.0 / 3.0)
        outflow = storage * ratio / (1.0 + ratio)
        own_part = block_term(downstream, outflow, first_block, block_rows)
        ahead_part = block_term(downstream, outflow, first_block + block_rows, block_rows)
        upstream = own_part + shifted(ahead_part, ("gy", "gx"), 1)
        storage = storage - outflow + upstream + lateral_gain * lateral
    return (depth, flux_east, flux_south, storage)


def solution(mesh):
    placed = (
        P("gy", "gx"),
        P("gy", "gx"),
        P("gy", "gx"),
        P("gy", "gx"),
        P("gy", "gx"),
        P("gy", "gx"),
        P(("gy", "gx")),
        P(("gy", "gx"), None),
        P(("gy", "gx"), None),
        P(("gy", "gx")),
    )
    return jax.shard_map(
        body,
        mesh=mesh,
        in_specs=placed,
        out_specs=(P("gy", "gx"), P("gy", "gx"), P("gy", "gx"), P(("gy", "gx"), None)),
        check_vma=False,
    )
```

time: 124 us -> 126 us (1.016)
  local copies, waits for them, and re-layouts: 19.4 us -> 31.1 us
  starting transfers between devices: 60 us -> 53.1 us
  waiting for transfers between devices: 10.2 us -> 5.31 us
  matrix products: 5.8 us -> 7.28 us
    ppermute x14 -> x10, starting transfers between devices: 35.3 us -> 28 us  [shifted(): lax.ppermute(value, axis, [(source, source + steps) for source in range(f...]
    squeeze x0 -> x8, local copies, waits for them, and re-layouts: none -> 6.93 us  [the longest x2 1.74 us: body(): west_msg[4]]
    reduce_sum x5 -> x4, other arithmetic: 7.7 us -> 1.38 us  [the longest x1 1.18 us: lateral_of(): tile_sums = drained.reshape(cell_rows // STRIP, STRIP, cell_cols // reach...]
    div x2 -> x6, other arithmetic: 11.3 us -> 17.3 us  [face_update(): return active * drive / damping]
    dot_general x0 -> x4, matrix products: none -> 4.36 us  [the longest x2 2.82 us: onehot_sum(): return jnp.dot(onehot, values, precision=lax.Precision.HIGHEST)]
    slice x20 -> x27, local copies, waits for them, and re-layouts: 13.1 us -> 16.7 us  [the longest x2 2.63 us: body(): level_east = jnp.concatenate([level[:, 1:], east_msg[0][:, None]], axis=1)]
    all_to_all x4, waiting for transfers between devices: 7.44 us -> 4.09 us  [the longest x2 2.97 us: finish_lateral(): parts = lax.all_to_all(by_column, 'gy', 0, 0, tiled=True)]
    another operation x0 -> x13, local copies, waits for them, and re-layouts: none -> 2.91 us  [the longest x2 1.76 us: body(): level_east = jnp.concatenate([level[:, 1:], east_msg[0][:, None]], axis=1)]
  transfers between devices with their start and end apart: 18 -> 14, of which waited for: 3 -> 3; matrix products, arithmetic and copies ran while one was open for 30% -> 49% of each run, Pallas kernels for 0% -> 0%
where the time goes in v1:
time: 126 us; the launch traced here: 125 us
  starting transfers between devices  53.1 us (42%)
  local copies, waits for them, and re-layouts  31.1 us (25%)
  other arithmetic  27 us (21%)
  matrix products  7.28 us (6%)
  waiting for transfers between devices  5.31 us (4%)
    ppermute x10, starting transfers between devices, shifted(): lax.ppermute(value, axis, [(source, source + steps) for source in range(f...  28 us
    div x6, other arithmetic, face_update(): return active * drive / damping  17.3 us
    all_to_all x2, starting transfers between devices, lateral_of(): got = lax.all_to_all(packed, 'gx', 0, 0, tiled=True)  16.4 us
    all_to_all x2, starting transfers between devices, finish_lateral(): parts = lax.all_to_all(by_column, 'gy', 0, 0, tiled=True)  8.72 us
    sub x1, other arithmetic, body(): depth - mass_gain * (flux_east - west_flux + (flux_south - north_flux))  4.14 us
    all_to_all x2, waiting for transfers between devices, finish_lateral(): parts = lax.all_to_all(by_column, 'gy', 0, 0, tiled=True)  2.97 us
    dot_general x4, matrix products, block_term(): jnp.einsum('tb,tc->bc', onehot, values, precision=lax.Precision.HIGHEST)  2.92 us
    dot_general x2, matrix products, onehot_sum(): return jnp.dot(onehot, values, precision=lax.Precision.HIGHEST)  2.82 us
  transfers between devices with their start and end apart: 14, of which 3 were waited for; matrix products, arithmetic and copies ran while one was open for 49% of the time, Pallas kernels for 0%

profile of v1, /device:TPU:1, one launch (start us, length us, event | category | flops | bytes accessed | tf_op | source)
XLA Modules:
  0.0 125.0 jit_solution(14471296914263481631)
XLA Ops:
  2.2 4.1 %collective-permute-start.8 = (f32[16,128]{1,0:T(8,128)}, f32[16,128]{1,0:T(8,128)}, u32[]{:S(2)}, u32[]{:S(2)}) collective-permute-start(f32[16,128]{1,0:T(8,128)} %fusion.63), channel_id=1, source_target_pairs={{0,1},{1,2},{2,3},{3,4},{4,5},{5,6},{6,7},{7,8},{8,9},{9,10},{10,1... | collective-permute-start | bytes 24584 | tf_op jit(solution)/shard_map/ppermute | solution.py:21
  6.4 1.8 %add.212 = f32[512,512]{1,0:T(8,128)S(1)} add(f32[512,512]{1,0:T(8,128)} %param.13, f32[512,512]{1,0:T(8,128)} %param.10) | non-fusion elementwise | flops 262144 | bytes 3145728 | tf_op jit(solution)/shard_map/add | solution.py:116
  8.2 3.4 %collective-permute-start.2 = (f32[2,512]{1,0:T(2,128)S(1)}, f32[2,512]{1,0:T(2,128)S(1)}, u32[]{:S(2)}, u32[]{:S(2)}) collective-permute-start(f32[2,512]{1,0:T(2,128)S(1)} %pad_maximum_fusion.2), channel_id=1, source_target_pairs={{16,0},{32,16},{48,32},{64,48},{80,64},{96,80},{112,96},{17,1},{33... | collective-permute-start | bytes 12296 | tf_op jit(solution)/shard_map/ppermute | solution.py:21
  12.3 1.3 %collective-permute-start = (f32[2,512]{1,0:T(2,128)S(1)}, f32[2,512]{1,0:T(2,128)S(1)}, u32[]{:S(2)}, u32[]{:S(2)}) collective-permute-start(f32[2,512]{1,0:T(2,128)S(1)} %pad_maximum_fusion.1), channel_id=1, source_target_pairs={{1,0},{2,1},{3,2},{4,3},{5,4},{6,5},{7,6},{8,7},{9,8},{10,9},{11,1... | collective-permute-start | bytes 12296 | tf_op jit(solution)/shard_map/ppermute | solution.py:21
  13.6 1.2 slice_reduce_fusion.7
  14.8 1.2 slice_reduce_fusion.5
  19.0 1.3 %slice.290 = f32[512,511]{1,0:T(8,128)} slice(f32[512,512]{1,0:T(8,128)S(1)} %add.212), slice={[0:512], [1:512]} | slice | bytes 2093056 | tf_op jit(solution)/shard_map/slice | solution.py:137
  21.4 1.3 %slice.219 = f32[512,511]{1,0:T(8,128)} slice(f32[512,512]{1,0:T(8,128)S(1)} %copy-done), slice={[0:512], [1:512]} | slice | bytes 2093056 | tf_op jit(solution)/shard_map/slice | solution.py:138
  23.4 1.4 %scatter_custom_fusion = f32[512]{0:T(512)S(1)} fusion(s32[256]{0:T(256)S(1)} %get-tuple-element.33, f32[256]{0:T(256)S(1)} %get-tuple-element.30, f32[]{:T(128)} %constant.101.clone.1), kind=kCustom, calls=%fused_computation.177 | custom fusion | bytes 2052 | tf_op jit(solution)/shard_map/scatter | solution.py:82
  26.0 6.3 %fusion.8 = (f32[512,512]{1,0:T(8,128)S(1)}, f32[512,512]{1,0:T(8,128)S(1)}, f32[512,512]{1,0:T(8,128)}, f32[512,512]{1,0:T(8,128)}) fusion(f32[512,512]{1,0:T(8,128)} %param.11, f32[512,512]{1,0:T(8,128)S(1)} %add.212, f32[512,1]{1,0:T(8,128)} %copy.136, f32[512,511]{1,0:T(8,128)} %slice.290, f32[512,512]{1,0:T(8,128)} %param.14, f32[512,1]{1,0:T(8,128)S(1)} %copy.135, ...), kind=kLoop, calls=%fused_computation.13 | loop fusion | flops 9437184 | bytes 14684160 | tf_op jit(solution)/shard_map/div | solution.py:28
  33.5 4.0 %collective-permute-start.1 = (f32[5,512]{1,0:T(8,128)S(1)}, f32[5,512]{1,0:T(8,128)S(1)}, u32[]{:S(2)}, u32[]{:S(2)}) collective-permute-start(f32[5,512]{1,0:T(8,128)S(1)} %stack.25), channel_id=1, source_target_pairs={{0,1},{1,2},{2,3},{3,4},{4,5},{5,6},{6,7},{7,8},{8,9},{9,10},{10,1... | collective-permute-start | bytes 30728 | tf_op jit(solution)/shard_map/ppermute | solution.py:21
  39.2 3.0 %collective-permute-start.3 = (f32[5,512]{1,0:T(8,128)S(1)}, f32[5,512]{1,0:T(8,128)S(1)}, u32[]{:S(2)}, u32[]{:S(2)}) collective-permute-start(f32[5,512]{1,0:T(8,128)S(1)} %stack.27), channel_id=1, source_target_pairs={{0,16},{16,32},{32,48},{48,64},{64,80},{80,96},{96,112},{1,17},{17... | collective-permute-start | bytes 30728 | tf_op jit(solution)/shard_map/ppermute | solution.py:21
  45.9 1.6 %add_divide_fusion.1 = f32[512,1]{1,0:T(8,128)S(1)} fusion(f32[512,1]{1,0:T(8,128)} %copy.142, f32[512,1]{1,0:T(8,128)} %copy.139, f32[512,1]{1,0:T(8,128)} %copy.140, f32[512,1]{1,0:T(8,128)} %copy.138, f32[512,1]{1,0:T(8,128)S(1)} %copy.137, f32[512,512]{1,0:T(8,128)S(1)} %add.212, f32[512,512]{1,0:T(8,128)S(1)} %copy-done), kind=kLoop, calls=%fused_computation.79 | loop fusion | flops 7168 | bytes 16384 | tf_op jit(solution)/shard_map/div | solution.py:28
  47.7 1.2 bitcast_reduce_fusion.1
  49.5 1.1 fusion.40
  51.9 1.3 %collective-permute-start.4 = (f32[2,512]{1,0:T(2,128)}, f32[2,512]{1,0:T(2,128)S(1)}, u32[]{:S(2)}, u32[]{:S(2)}) collective-permute-start(f32[2,512]{1,0:T(2,128)} %pad_maximum_fusion.3), channel_id=1, source_target_pairs={{1,0},{2,1},{3,2},{4,3},{5,4},{6,5},{7,6},{8,7},{9,8},{10,9},{11,1... | collective-permute-start | bytes 12296 | tf_op jit(solution)/shard_map/ppermute | solution.py:21
  55.1 1.3 %slice.316 = f32[512,511]{1,0:T(8,128)} slice(f32[512,512]{1,0:T(8,128)S(1)} %add.228), slice={[0:512], [1:512]} | slice | bytes 2093056 | tf_op jit(solution)/shard_map/slice | solution.py:137
  57.5 1.3 %slice.312 = f32[512,511]{1,0:T(8,128)} slice(f32[512,512]{1,0:T(8,128)S(1)} %get-tuple-element.35), slice={[0:512], [1:512]} | slice | bytes 2093056 | tf_op jit(solution)/shard_map/slice | solution.py:138
  58.8 10.2 %all-to-all-start = ((f32[16,33,128]{2,1,0:T(8,128)}), f32[16,33,128]{2,1,0:T(8,128)S(1)}, u32[]{:S(2)}, u32[]{:S(2)}) async-start(f32[16,33,128]{2,1,0:T(8,128)} %pad_maximum_fusion), calls=%async_computation | async-start | bytes 655360 | tf_op jit(solution)/shard_map/all_to_all | solution.py:102
  69.0 2.5 %collective-permute-start.7 = (f32[5,512]{1,0:T(8,128)S(1)}, f32[5,512]{1,0:T(8,128)S(1)}, u32[]{:S(2)}, u32[]{:S(2)}) collective-permute-start(f32[5,512]{1,0:T(8,128)S(1)} %stack.31), channel_id=1, source_target_pairs={{0,16},{16,32},{32,48},{48,64},{64,80},{80,96},{96,112},{1,17},{17... | collective-permute-start | bytes 30728 | tf_op jit(solution)/shard_map/ppermute | solution.py:21
  71.5 3.5 %collective-permute-start.5 = (f32[5,512]{1,0:T(8,128)S(1)}, f32[5,512]{1,0:T(8,128)S(1)}, u32[]{:S(2)}, u32[]{:S(2)}) collective-permute-start(f32[5,512]{1,0:T(8,128)S(1)} %stack.29), channel_id=1, source_target_pairs={{0,1},{1,2},{2,3},{3,4},{4,5},{5,6},{6,7},{7,8},{8,9},{9,10},{10,1... | collective-permute-start | bytes 30728 | tf_op jit(solution)/shard_map/ppermute | solution.py:21
  76.9 1.9 %collective-permute-start.6 = (f32[2,512]{1,0:T(2,128)S(1)}, f32[2,512]{1,0:T(2,128)S(1)}, u32[]{:S(2)}, u32[]{:S(2)}) collective-permute-start(f32[2,512]{1,0:T(2,128)S(1)} %pad_maximum_fusion.4), channel_id=1, source_target_pairs={{16,0},{32,16},{48,32},{64,48},{80,64},{96,80},{112,96},{17,1},{33... | collective-permute-start | bytes 12296 | tf_op jit(solution)/shard_map/ppermute | solution.py:21
  83.2 2.2 %add_divide_fusion = f32[512,1]{1,0:T(8,128)} fusion(f32[512,1]{1,0:T(8,128)} %copy.150, f32[512,1]{1,0:T(8,128)} %copy.147, f32[512,1]{1,0:T(8,128)} %copy.148, f32[512,1]{1,0:T(8,128)} %copy.146, f32[512,1]{1,0:T(8,128)} %copy.145, f32[512,512]{1,0:T(8,128)S(1)} %get-tuple-element.35, f32[512,512]{1,0:T(8,128)S(1)} %add.228), kind=kLoop, calls=%fused_computation.78 | loop fusion | flops 7168 | bytes 16384 | tf_op jit(solution)/shard_map/div | solution.py:28
  85.5 6.3 %all-to-all-start.2 = ((f32[16,32,128]{2,1,0:T(8,128)}), f32[16,32,128]{2,1,0:T(8,128)}, u32[]{:S(2)}, u32[]{:S(2)}) async-start(f32[16,32,128]{2,1,0:T(8,128)} %fusion.40), calls=%async_computation.2 | async-start | bytes 524288 | tf_op jit(solution)/shard_map/all_to_all | solution.py:102
  91.7 7.1 %fusion.37 = (f32[512,512]{1,0:T(8,128)}, f32[512,512]{1,0:T(8,128)}) fusion(f32[512,512]{1,0:T(8,128)} %get-tuple-element.41, f32[512,512]{1,0:T(8,128)} %get-tuple-element.40, f32[512,512]{1,0:T(8,128)S(1)} %add.228, f32[1,512]{1,0:T(1,128)S(1)} %get-tuple-element.62, f32[511,512]{1,0:T(8,128)} %slice.331, f32[512,512]{1,0:T(8,128)} %param.14, ...), kind=kLoop, calls=%fused_computation.51 | loop fusion | flops 8650752 | bytes 13631488 | tf_op jit(solution)/shard_map/div | solution.py:28
  101.0 4.7 %all-to-all-start.1 = ((f32[8,16,128]{2,1,0:T(8,128)}), f32[8,16,128]{2,1,0:T(8,128)S(1)}, u32[]{:S(2)}, u32[]{:S(2)}) async-start(f32[8,16,128]{2,1,0:T(8,128)} %fusion.46), calls=%async_computation.1 | async-start | bytes 131072 | tf_op jit(solution)/shard_map/all_to_all | solution.py:110
  105.7 1.9 %fusion.44 = f32[8,16,128]{2,1,0:T(8,128)} fusion(f32[512,128,1]{1,0,2:T(8,128)} %bitcast.29, f32[512]{0:T(512)S(1)} %eq.147, f32[8,16]{1,0:T(8,128)S(1)} %multiply_add_fusion.2), kind=kOutput, calls=%fused_computation.64 | convolution fusion | flops 100728832 | bytes 330240 | tf_op jit(solution)/shard_map/dot_general | solution.py:34
  107.6 3.0 %all-to-all-done.1 = f32[8,16,128]{2,1,0:T(8,128)S(1)} async-done(((f32[8,16,128]{2,1,0:T(8,128)}), f32[8,16,128]{2,1,0:T(8,128)S(1)}, u32[]{:S(2)}, u32[]{:S(2)}) %all-to-all-start.1) | async-done | bytes 65568 | tf_op jit(solution)/shard_map/all_to_all | solution.py:110
  110.5 4.0 %all-to-all-start.3 = ((f32[8,16,128]{2,1,0:T(8,128)}), f32[8,16,128]{2,1,0:T(8,128)S(1)}, u32[]{:S(2)}, u32[]{:S(2)}) async-start(f32[8,16,128]{2,1,0:T(8,128)} %fusion.44), calls=%async_computation.3 | async-start | bytes 131072 | tf_op jit(solution)/shard_map/all_to_all | solution.py:110
  115.9 2.9 %collective-permute-start.9 = (f32[16,128]{1,0:T(8,128)S(1)}, f32[16,128]{1,0:T(8,128)S(1)}, u32[]{:S(2)}, u32[]{:S(2)}) collective-permute-start(f32[16,128]{1,0:T(8,128)S(1)} %fusion.61), channel_id=1, source_target_pairs={{0,1},{1,2},{2,3},{3,4},{4,5},{5,6},{6,7},{7,8},{8,9},{9,10},{10,1... | collective-permute-start | bytes 24584 | tf_op jit(solution)/shard_map/ppermute | solution.py:21
  118.8 4.1 %fusion.30 = f32[512,512]{1,0:T(8,128)} fusion(f32[512,512]{1,0:T(8,128)S(1)} %get-tuple-element.35, f32[512,512]{1,0:T(8,128)} %get-tuple-element.43, f32[512,511]{1,0:T(8,128)} %bitcast.85, f32[512,1]{1,0:T(8,128)S(1)} %copy-done.6, f32[512,512]{1,0:T(8,128)} %get-tuple-element.42, f32[511,512]{1,0:T(8,128)} %bitcast.84, ...), kind=kLoop, calls=%fused_computation.42 | loop fusion | flops 3145728 | bytes 7340032 | tf_op jit(solution)/shard_map/sub | solution.py:156
  123.0 1.2 collective-permute-done.9
  (124 shorter events, 30.3 us)
Async XLA Ops:
  0.6 0.7 copy-start.10
  0.6 0.7 copy-start.8
  0.7 0.7 copy-start.12
  1.4 0.9 copy-start.14
  2.2 5.9 %copy-start = (f32[512,512]{1,0:T(8,128)S(1)}, f32[512,512]{1,0:T(8,128)}, u32[]{:S(2)}) copy-start(f32[512,512]{1,0:T(8,128)} %param.10) | copy-start | bytes 3145732
  2.2 112.4 %collective-permute-start.8 = (f32[16,128]{1,0:T(8,128)}, f32[16,128]{1,0:T(8,128)}, u32[]{:S(2)}, u32[]{:S(2)}) collective-permute-start(f32[16,128]{1,0:T(8,128)} %fusion.63), channel_id=1, source_target_pairs={{0,1},{1,2},{2,3},{3,4},{4,5},{5,6},{6,7},{7,8},{8,9},{9,10},{10,1... | collective-permute-start | bytes 24584 | tf_op jit(solution)/shard_map/ppermute | solution.py:21
  8.2 17.8 %collective-permute-start.2 = (f32[2,512]{1,0:T(2,128)S(1)}, f32[2,512]{1,0:T(2,128)S(1)}, u32[]{:S(2)}, u32[]{:S(2)}) collective-permute-start(f32[2,512]{1,0:T(2,128)S(1)} %pad_maximum_fusion.2), channel_id=1, source_target_pairs={{16,0},{32,16},{48,32},{64,48},{80,64},{96,80},{112,96},{17,1},{33... | collective-permute-start | bytes 12296 | tf_op jit(solution)/shard_map/ppermute | solution.py:21
  12.3 12.7 %collective-permute-start = (f32[2,512]{1,0:T(2,128)S(1)}, f32[2,512]{1,0:T(2,128)S(1)}, u32[]{:S(2)}, u32[]{:S(2)}) collective-permute-start(f32[2,512]{1,0:T(2,128)S(1)} %pad_maximum_fusion.1), channel_id=1, source_target_pairs={{1,0},{2,1},{3,2},{4,3},{5,4},{6,5},{7,6},{8,7},{9,8},{10,9},{11,1... | collective-permute-start | bytes 12296 | tf_op jit(solution)/shard_map/ppermute | solution.py:21
  14.8 1.2 copy-start.7
  32.3 1.0 copy-start.4
  33.5 8.7 %collective-permute-start.1 = (f32[5,512]{1,0:T(8,128)S(1)}, f32[5,512]{1,0:T(8,128)S(1)}, u32[]{:S(2)}, u32[]{:S(2)}) collective-permute-start(f32[5,512]{1,0:T(8,128)S(1)} %stack.25), channel_id=1, source_target_pairs={{0,1},{1,2},{2,3},{3,4},{4,5},{5,6},{6,7},{7,8},{8,9},{9,10},{10,1... | collective-permute-start | bytes 30728 | tf_op jit(solution)/shard_map/ppermute | solution.py:21
  39.2 8.3 %collective-permute-start.3 = (f32[5,512]{1,0:T(8,128)S(1)}, f32[5,512]{1,0:T(8,128)S(1)}, u32[]{:S(2)}, u32[]{:S(2)}) collective-permute-start(f32[5,512]{1,0:T(8,128)S(1)} %stack.27), channel_id=1, source_target_pairs={{0,16},{16,32},{32,48},{48,64},{64,80},{80,96},{96,112},{1,17},{17... | collective-permute-start | bytes 30728 | tf_op jit(solution)/shard_map/ppermute | solution.py:21
  45.9 1.7 %copy-start.1 = (f32[512,512]{1,0:T(8,128)S(1)}, f32[512,512]{1,0:T(8,128)}, u32[]{:S(2)}) copy-start(f32[512,512]{1,0:T(8,128)} %get-tuple-element.40) | copy-start | bytes 3145732
  45.9 1.9 %copy-start.2 = (s32[512,512]{1,0:T(8,128)S(1)}, s32[512,512]{1,0:T(8,128)}, u32[]{:S(2)}) copy-start(s32[512,512]{1,0:T(8,128)} %param.15) | copy-start | bytes 3145732
  47.7 1.5 %copy-start.5 = (f32[512,512]{1,0:T(8,128)S(1)}, f32[512,512]{1,0:T(8,128)}, u32[]{:S(2)}) copy-start(f32[512,512]{1,0:T(8,128)} %param.13) | copy-start | bytes 3145732
  51.9 23.1 %collective-permute-start.4 = (f32[2,512]{1,0:T(2,128)}, f32[2,512]{1,0:T(2,128)S(1)}, u32[]{:S(2)}, u32[]{:S(2)}) collective-permute-start(f32[2,512]{1,0:T(2,128)} %pad_maximum_fusion.3), channel_id=1, source_target_pairs={{1,0},{2,1},{3,2},{4,3},{5,4},{6,5},{7,6},{8,7},{9,8},{10,9},{11,1... | collective-permute-start | bytes 12296 | tf_op jit(solution)/shard_map/ppermute | solution.py:21
  58.8 26.6 %all-to-all-start = ((f32[16,33,128]{2,1,0:T(8,128)}), f32[16,33,128]{2,1,0:T(8,128)S(1)}, u32[]{:S(2)}, u32[]{:S(2)}) async-start(f32[16,33,128]{2,1,0:T(8,128)} %pad_maximum_fusion), calls=%async_computation | async-start | bytes 655360 | tf_op jit(solution)/shard_map/all_to_all | solution.py:102
  69.0 7.8 %collective-permute-start.7 = (f32[5,512]{1,0:T(8,128)S(1)}, f32[5,512]{1,0:T(8,128)S(1)}, u32[]{:S(2)}, u32[]{:S(2)}) collective-permute-start(f32[5,512]{1,0:T(8,128)S(1)} %stack.31), channel_id=1, source_target_pairs={{0,16},{16,32},{32,48},{48,64},{64,80},{80,96},{96,112},{1,17},{17... | collective-permute-start | bytes 30728 | tf_op jit(solution)/shard_map/ppermute | solution.py:21
  71.5 7.3 %collective-permute-start.5 = (f32[5,512]{1,0:T(8,128)S(1)}, f32[5,512]{1,0:T(8,128)S(1)}, u32[]{:S(2)}, u32[]{:S(2)}) collective-permute-start(f32[5,512]{1,0:T(8,128)S(1)} %stack.29), channel_id=1, source_target_pairs={{0,1},{1,2},{2,3},{3,4},{4,5},{5,6},{6,7},{7,8},{8,9},{9,10},{10,1... | collective-permute-start | bytes 30728 | tf_op jit(solution)/shard_map/ppermute | solution.py:21
  76.9 8.5 %collective-permute-start.6 = (f32[2,512]{1,0:T(2,128)S(1)}, f32[2,512]{1,0:T(2,128)S(1)}, u32[]{:S(2)}, u32[]{:S(2)}) collective-permute-start(f32[2,512]{1,0:T(2,128)S(1)} %pad_maximum_fusion.4), channel_id=1, source_target_pairs={{16,0},{32,16},{48,32},{64,48},{80,64},{96,80},{112,96},{17,1},{33... | collective-permute-start | bytes 12296 | tf_op jit(solution)/shard_map/ppermute | solution.py:21
  85.5 15.5 %all-to-all-start.2 = ((f32[16,32,128]{2,1,0:T(8,128)}), f32[16,32,128]{2,1,0:T(8,128)}, u32[]{:S(2)}, u32[]{:S(2)}) async-start(f32[16,32,128]{2,1,0:T(8,128)} %fusion.40), calls=%async_computation.2 | async-start | bytes 524288 | tf_op jit(solution)/shard_map/all_to_all | solution.py:102
  98.8 20.0 %copy-start.3 = (s32[512,512]{1,0:T(8,128)S(1)}, s32[512,512]{1,0:T(8,128)}, u32[]{:S(2)}) copy-start(s32[512,512]{1,0:T(8,128)} %param.15) | copy-start | bytes 3145732
  98.9 15.7 %copy-start.9 = (f32[16,128]{1,0:T(8,128)S(1)}, f32[16,128]{1,0:T(8,128)}, u32[]{:S(2)}) copy-start(f32[16,128]{1,0:T(8,128)} %param.17) | copy-start | bytes 24580
  98.9 15.7 %copy-start.11 = (f32[16,128]{1,0:T(8,128)S(1)}, f32[16,128]{1,0:T(8,128)}, u32[]{:S(2)}) copy-start(f32[16,128]{1,0:T(8,128)} %param.18) | copy-start | bytes 24580
  98.9 15.7 %copy-start.13 = (s32[16]{0:T(128)S(1)}, s32[16]{0:T(128)}, u32[]{:S(2)}) copy-start(s32[16]{0:T(128)} %param.19) | copy-start | bytes 196
  98.9 15.7 %copy-start.16 = (s32[16]{0:T(128)S(1)}, s32[16]{0:T(128)}, u32[]{:S(2)}) copy-start(s32[16]{0:T(128)} %iota_add_fusion.1) | copy-start | bytes 196
  101.0 9.5 %all-to-all-start.1 = ((f32[8,16,128]{2,1,0:T(8,128)}), f32[8,16,128]{2,1,0:T(8,128)S(1)}, u32[]{:S(2)}, u32[]{:S(2)}) async-start(f32[8,16,128]{2,1,0:T(8,128)} %fusion.46), calls=%async_computation.1 | async-start | bytes 131072 | tf_op jit(solution)/shard_map/all_to_all | solution.py:110
  107.6 11.2 %copy-start.6 = (f32[512,1]{1,0:T(8,128)S(1)}, f32[512,1]{1,0:T(8,128)}, u32[]{:S(2)}) copy-start(f32[512,1]{1,0:T(8,128)} %add_divide_fusion) | copy-start | bytes 6148
  110.5 12.4 %all-to-all-start.3 = ((f32[8,16,128]{2,1,0:T(8,128)}), f32[8,16,128]{2,1,0:T(8,128)S(1)}, u32[]{:S(2)}, u32[]{:S(2)}) async-start(f32[8,16,128]{2,1,0:T(8,128)} %fusion.44), calls=%async_computation.3 | async-start | bytes 131072 | tf_op jit(solution)/shard_map/all_to_all | solution.py:110
  114.6 1.0 copy-start.15
  115.9 8.3 %collective-permute-start.9 = (f32[16,128]{1,0:T(8,128)S(1)}, f32[16,128]{1,0:T(8,128)S(1)}, u32[]{:S(2)}, u32[]{:S(2)}) collective-permute-start(f32[16,128]{1,0:T(8,128)S(1)} %fusion.61), channel_id=1, source_target_pairs={{0,1},{1,2},{2,3},{3,4},{4,5},{5,6},{6,7},{7,8},{8,9},{9,10},{10,1... | collective-permute-start | bytes 24584 | tf_op jit(solution)/shard_map/ppermute | solution.py:21

commit v2 on v1

--- a/solution.py
+++ b/solution.py
@@ -26,12 +26,6 @@
     drive = flux - slope_gain * face_depth * (level_next - level)
     damping = 1.0 + friction_gain * roughness * jnp.abs(flux) / jnp.power(face_depth, 7.0 / 3.0)
     return active * drive / damping
-
-
-def onehot_sum(ids, values, count):
-    targets = lax.iota(jnp.float32, count)
-    onehot = (targets[:, None] == ids[None, :]).astype(jnp.float32)
-    return jnp.dot(onehot, values, precision=lax.Precision.HIGHEST)
 
 
 def block_term(target_ids, values, start, count):
@@ -69,48 +63,16 @@
     device_index = row_index * col_count + col_index
     first_block = device_index * block_rows
 
-    column_slots = row_count * slot_cap
-    tile_owner = tile_block // block_rows
-    owner_row = tile_owner // col_count
-    owner_col = tile_owner % col_count
-    owner_hits = (tile_owner[:, None] == lax.iota(jnp.int32, device_count)[None, :]).astype(
-        jnp.int32
-    )
-    earlier = jnp.sum((jnp.cumsum(owner_hits, axis=0) - owner_hits) * owner_hits, axis=1)
-    send_pos = owner_col * column_slots + owner_row * slot_cap + earlier
-    column_ids = (owner_row * block_rows + tile_block % block_rows).astype(jnp.float32)
-    send_ids = jnp.full((col_count * column_slots,), -1.0, jnp.float32).at[send_pos].set(column_ids)
-    id_rows = -(-column_slots // reach_width)
-    send_ids = jnp.pad(
-        send_ids.reshape(col_count, column_slots),
-        ((0, 0), (0, id_rows * reach_width - column_slots)),
-        constant_values=-1.0,
-    ).reshape(col_count, id_rows, reach_width)
-    gather_onehot = (
-        lax.iota(jnp.int32, col_count * column_slots)[:, None] == send_pos[None, :]
-    ).astype(jnp.float32)
+    total_blocks = block_rows * device_count
 
-    def lateral_of(drained, first):
+    def lateral_of(drained):
         tile_sums = drained.reshape(
             cell_rows // STRIP, STRIP, cell_cols // reach_width, reach_width
         ).sum(axis=1)
         tile_sums = tile_sums.reshape(-1, reach_width)
-        packed = jnp.dot(gather_onehot, tile_sums, precision=lax.Precision.HIGHEST)
-        packed = packed.reshape(col_count, column_slots, reach_width)
-        if first:
-            packed = jnp.concatenate([packed, send_ids], axis=1)
-        got = lax.all_to_all(packed, "gx", 0, 0, tiled=True)
-        got_vals = got[:, :column_slots].reshape(-1, reach_width)
-        got_ids = got[:, column_slots:].reshape(col_count, -1)[:, :column_slots].reshape(-1)
-        return got_vals, got_ids
+        every_block = block_term(tile_block, tile_sums, 0, total_blocks)
+        return lax.psum_scatter(every_block, ("gy", "gx"), scatter_dimension=0, tiled=True)
 
-    def finish_lateral(got_vals, got_ids):
-        by_column = onehot_sum(got_ids, got_vals, row_count * block_rows)
-        by_column = by_column.reshape(row_count, block_rows, reach_width)
-        parts = lax.all_to_all(by_column, "gy", 0, 0, tiled=True)
-        return jnp.sum(parts, axis=0)
-
-    recv_ids = None
     depth = water_depth
     for step in range(STEPS):
         level = bed_level + depth
@@ -131,9 +93,7 @@
             1,
         )
         drained = drain_rate * land_float * jnp.abs(depth)
-        got_vals, got_ids = lateral_of(drained, step == 0)
-        if step == 0:
-            recv_ids = got_ids
+        lateral = lateral_of(drained)
         level_east = jnp.concatenate([level[:, 1:], east_msg[0][:, None]], axis=1)
         depth_east = jnp.concatenate([depth[:, 1:], east_msg[1][:, None]], axis=1)
         level_south = jnp.concatenate([level[1:], south_msg[0][None, :]], axis=0)
@@ -154,7 +114,6 @@
         west_flux = jnp.concatenate([west_edge[:, None], flux_east[:, :-1]], axis=1)
         north_flux = jnp.concatenate([north_edge[None, :], flux_south[:-1]], axis=0)
         depth = depth - mass_gain * (flux_east - west_flux + (flux_south - north_flux)) - drained
-        lateral = finish_lateral(got_vals, recv_ids)
         ratio = reach_rate * jnp.power(storage, 2.0 / 3.0)
         outflow = storage * ratio / (1.0 + ratio)
         own_part = block_term(downstream, outflow, first_block, block_rows)

time: 126 us -> 1350 us (10.71)
  the two profiles are of different devices: /device:TPU:1 before, /device:TPU:0 now
where the time goes in v2:
time: 1350 us
  waiting for transfers between devices  1250 us (93%)
  local copies, waits for them, and re-layouts  28.9 us (2%)
  starting transfers between devices  24.9 us (2%)
  other arithmetic  24.9 us (2%)
  between operations  14.4 us (1%)
    reduce_scatter x2, waiting for transfers between devices, lateral_of(): lax.psum_scatter(every_block, ('gy', 'gx'), scatter_dimension=0, tiled=True)  1250 us
  transfers between devices with their start and end apart: 12, of which 2 were waited for; matrix products, arithmetic and copies ran while one was open for 3% of the time, Pallas kernels for 0%

profile of v2, /device:TPU:0, one launch (start us, length us, event | category | flops | bytes accessed | tf_op | source)
XLA Modules:
  0.0 1352.3 jit_solution(16816374604274226188)
XLA Ops:
  7.2 1.8 add.177
  9.1 1.3 collective-permute-start.2
  11.0 1.3 collective-permute-start
  12.3 1.2 slice_reduce_fusion.7
  13.5 1.2 slice_reduce_fusion.5
  14.7 1.1 slice.282
  15.8 1.3 slice.270
  17.1 1.1 slice.221
  18.2 1.3 slice.204
  20.6 6.3 fusion.10
  28.1 4.5 collective-permute-start.1
  34.9 2.5 collective-permute-start.3
  41.0 1.6 add_divide_fusion.1
  42.9 1.2 bitcast_reduce_fusion.1
  44.1 2.9 fusion.1
  47.3 3.6 collective-permute-start.8
  51.9 1.4 add.193
  54.0 1.5 collective-permute-start.4
  55.5 2.9 fusion
  59.5 1.4 slice.296
  60.8 1.1 slice.307
  61.9 1.3 slice.292
  63.3 3.3 collective-permute-start.7
  66.6 4.3 collective-permute-start.5
  72.7 1.3 collective-permute-start.6
  78.3 1.7 add_divide_fusion
  80.3 6.5 fusion.39
  86.8 614.1 %reduce-scatter.3.cloned.1.call-done = f32[16,128]{1,0:T(8,128)} async-done(((f32[2048,128]{1,0:T(8,128)}), f32[16,128]{1,0:T(8,128)}) %reduce-scatter.3.cloned.1.call-update) | async-done | bytes 8208 | tf_op jit(solution)/shard_map/reduce_scatter | solution.py:74
  702.1 1.3 collective-permute-start.9
  703.4 4.3 fusion.32
  707.6 636.2 %reduce-scatter.5.cloned.1.call-done = f32[16,128]{1,0:T(8,128)} async-done(((f32[2048,128]{1,0:T(8,128)}), f32[16,128]{1,0:T(8,128)}) %reduce-scatter.5.cloned.1.call-update) | async-done | bytes 8208 | tf_op jit(solution)/shard_map/reduce_scatter | solution.py:74
  1343.9 1.6 multiply_add_fusion
  (84 shorter events, 19.7 us)
Async XLA Ops:
  7.2 1.9 copy-start
  7.2 693.7 %reduce-scatter.3.cloned.1.call-start = ((), (), s32[]{:S(2)}) async-start(), calls=%async_computation.2 | async-start | bytes 1056768 | tf_op jit(solution)/shard_map/reduce_scatter | solution.py:74
  9.1 11.5 collective-permute-start.2
  11.0 8.5 collective-permute-start
  26.9 1.0 copy-start.5
  28.1 9.2 collective-permute-start.1
  34.9 7.7 collective-permute-start.3
  41.0 1.7 copy-start.1
  41.0 1.9 copy-start.3
  42.9 1.2 copy-start.6
  44.0 3.0 copy-start.7
  44.1 3.0 copy-start.8
  44.1 3.0 copy-start.9
  47.0 1296.9 %reduce-scatter.5.cloned.1.call-start = ((), (), s32[]{:S(2)}) async-start(), calls=%async_computation.3 | async-start | bytes 1056768 | tf_op jit(solution)/shard_map/reduce_scatter | solution.py:74
  47.3 39.4 %collective-permute-start.8 = (f32[16,128]{1,0:T(8,128)S(1)}, f32[16,128]{1,0:T(8,128)S(1)}, u32[]{:S(2)}, u32[]{:S(2)}) collective-permute-start(f32[16,128]{1,0:T(8,128)S(1)} %fusion.46), channel_id=1, source_target_pairs={{0,1},{1,2},{2,3},{3,4},{4,5},{5,6},{6,7},{7,8},{8,9},{9,10},{10,1... | collective-permute-start | bytes 24584 | tf_op jit(solution)/shard_map/ppermute | solution.py:21
  54.0 16.9 %collective-permute-start.4 = (f32[2,512]{1,0:T(2,128)S(1)}, f32[2,512]{1,0:T(2,128)S(1)}, u32[]{:S(2)}, u32[]{:S(2)}) collective-permute-start(f32[2,512]{1,0:T(2,128)S(1)} %pad_maximum_fusion.2), channel_id=1, source_target_pairs={{1,0},{2,1},{3,2},{4,3},{5,4},{6,5},{7,6},{8,7},{9,8},{10,9},{11,1... | collective-permute-start | bytes 12296 | tf_op jit(solution)/shard_map/ppermute | solution.py:21
  63.3 9.4 collective-permute-start.7
  66.6 7.4 collective-permute-start.5
  72.7 7.3 collective-permute-start.6
  78.3 1.7 copy-start.2
  78.3 1.9 copy-start.4
  702.1 641.8 %collective-permute-start.9 = (f32[16,128]{1,0:T(8,128)S(1)}, f32[16,128]{1,0:T(8,128)S(1)}, u32[]{:S(2)}, u32[]{:S(2)}) collective-permute-start(f32[16,128]{1,0:T(8,128)S(1)} %fusion.44), channel_id=1, source_target_pairs={{0,1},{1,2},{2,3},{3,4},{4,5},{5,6},{6,7},{7,8},{8,9},{9,10},{10,1... | collective-permute-start | bytes 24584 | tf_op jit(solution)/shard_map/ppermute | solution.py:21
Sparse Core Ops, SparseCore 0:
  47.1 653.7 reduce-scatter.2
  703.2 640.6 reduce-scatter.4

commit v3 on v0

v3 whole, which is shorter than its diff:
```python
import functools

import jax
import jax.numpy as jnp
from jax import lax
from jax.experimental import pallas as pl
from jax.experimental.pallas import tpu as pltpu
from jax.sharding import PartitionSpec as P

STRIP = 8
STEPS = 2


rim_depth = 0.1
slope_gain = 0.1
friction_gain = 1.0
mass_gain = 0.05
drain_rate = 0.05
lateral_gain = 0.125


def shifted(value, axis, steps):
    count = lax.axis_size(axis)
    first, last = (max(0, -steps), min(count, count - steps))
    return lax.ppermute(value, axis, [(source, source + steps) for source in range(first, last)])


def face_update(flux, level, level_next, depth, depth_next, roughness, active):
    face_depth = rim_depth + 0.5 * (jnp.abs(depth) + jnp.abs(depth_next))
    drive = flux - slope_gain * face_depth * (level_next - level)
    damping = 1.0 + friction_gain * roughness * jnp.abs(flux) / jnp.power(face_depth, 7.0 / 3.0)
    return active * drive / damping


def block_term(target_ids, values, start, count):
    targets = start + lax.iota(jnp.int32, count)
    onehot = (target_ids[:, None] == targets[None, :]).astype(jnp.float32)
    return jnp.einsum("tb,tc->bc", onehot, values, precision=lax.Precision.HIGHEST)


def write_edges(level, depth, flux_e, flux_s, rough, eopen, sopen, to_west, to_north, to_east,
                to_south):
    to_west[:, 0:1] = level[:, 0:1]
    to_west[:, 1:2] = depth[:, 0:1]
    to_north[0:1, :] = level[0:1, :]
    to_north[1:2, :] = depth[0:1, :]
    to_east[:, 0:1] = flux_e[:, -1:]
    to_east[:, 1:2] = level[:, -1:]
    to_east[:, 2:3] = depth[:, -1:]
    to_east[:, 3:4] = rough[:, -1:]
    to_east[:, 4:5] = eopen[:, -1:]
    to_south[0:1, :] = flux_s[-1:, :]
    to_south[1:2, :] = level[-1:, :]
    to_south[2:3, :] = depth[-1:, :]
    to_south[3:4, :] = rough[-1:, :]
    to_south[4:5, :] = sopen[-1:, :]


def open_masks(flags_ref, land):
    ny, nx = land.shape
    col = lax.broadcasted_iota(jnp.int32, (ny, nx), 1)
    row = lax.broadcasted_iota(jnp.int32, (ny, nx), 0)
    eopen = jnp.where((col == nx - 1) & (flags_ref[0] == 1), 0.0, land)
    sopen = jnp.where((row == ny - 1) & (flags_ref[1] == 1), 0.0, land)
    return col, row, eopen, sopen


def edge_kernel(flags_ref, d_ref, e_ref, s_ref, bed_ref, r_ref, land_ref,
                to_west, to_north, to_east, to_south):
    depth = d_ref[...]
    level = bed_ref[...] + depth
    _, _, eopen, sopen = open_masks(flags_ref, land_ref[...])
    write_edges(level, depth, e_ref[...], s_ref[...], r_ref[...], eopen, sopen,
                to_west, to_north, to_east, to_south)


def step_kernel(flags_ref, d_ref, e_ref, s_ref, bed_ref, r_ref, land_ref,
                east_ref, south_ref, west_ref, north_ref,
                d_out, e_out, s_out, tile_out, to_west, to_north, to_east, to_south):
    ny, nx = d_ref.shape
    depth = d_ref[...]
    bed = bed_ref[...]
    land = land_ref[...]
    rough = r_ref[...]
    level = bed + depth
    col, row, eopen, sopen = open_masks(flags_ref, land)
    level_e = jnp.where(col == nx - 1, east_ref[:, 0:1], pltpu.roll(level, nx - 1, 1))
    depth_e = jnp.where(col == nx - 1, east_ref[:, 1:2], pltpu.roll(depth, nx - 1, 1))
    level_s = jnp.where(row == ny - 1, south_ref[0:1, :], pltpu.roll(level, ny - 1, 0))
    depth_s = jnp.where(row == ny - 1, south_ref[1:2, :], pltpu.roll(depth, ny - 1, 0))
    flux_e = face_update(e_ref[...], level, level_e, depth, depth_e, rough, eopen)
    flux_s = face_update(s_ref[...], level, level_s, depth, depth_s, rough, sopen)
    west_edge = face_update(
        west_ref[:, 0:1], west_ref[:, 1:2], level[:, 0:1], west_ref[:, 2:3], depth[:, 0:1],
        west_ref[:, 3:4], west_ref[:, 4:5],
    )
    north_edge = face_update(
        north_ref[0:1, :], north_ref[1:2, :], level[0:1, :], north_ref[2:3, :], depth[0:1, :],
        north_ref[3:4, :], north_ref[4:5, :],
    )
    west_flux = jnp.where(col == 0, west_edge, pltpu.roll(flux_e, 1, 1))
    north_flux = jnp.where(row == 0, north_edge, pltpu.roll(flux_s, 1, 0))
    drained = drain_rate * land * jnp.abs(depth)
    new_depth = depth - mass_gain * (flux_e - west_flux + (flux_s - north_flux)) - drained
    d_out[...] = new_depth
    e_out[...] = flux_e
    s_out[...] = flux_s
    tile_out[...] = drained.reshape(ny // STRIP, STRIP, nx).sum(axis=1)
    write_edges(bed + new_depth, new_depth, flux_e, flux_s, rough, eopen, sopen,
                to_west, to_north, to_east, to_south)


def edge_shapes(ny, nx):
    f32 = jnp.float32
    return (
        jax.ShapeDtypeStruct((ny, 2), f32),
        jax.ShapeDtypeStruct((2, nx), f32),
        jax.ShapeDtypeStruct((ny, 5), f32),
        jax.ShapeDtypeStruct((5, nx), f32),
    )


def vmem_specs(count):
    return [pl.BlockSpec(memory_space=pltpu.VMEM) for _ in range(count)]


def body(
    water_depth,
    flux_east,
    flux_south,
    bed_level,
    roughness,
    land_mask,
    tile_block,
    storage,
    reach_rate,
    downstream,
):
    cell_rows, cell_cols = water_depth.shape
    block_rows, reach_width = storage.shape
    row_count = lax.axis_size("gy")
    col_count = lax.axis_size("gx")
    row_index = lax.axis_index("gy")
    col_index = lax.axis_index("gx")
    device_count = row_count * col_count
    tile_count = tile_block.shape[0]
    slot_cap = max(2, 2 * tile_count // device_count)
    land_float = land_mask.astype(jnp.float32)
    flags = jnp.stack(
        [(col_index == col_count - 1).astype(jnp.int32), (row_index == row_count - 1).astype(jnp.int32)]
    )
    device_index = row_index * col_count + col_index
    first_block = device_index * block_rows
    f32 = jnp.float32
    grid_shape = jax.ShapeDtypeStruct((cell_rows, cell_cols), f32)
    smem_spec = pl.BlockSpec(memory_space=pltpu.SMEM)

    edges = pl.pallas_call(
        edge_kernel,
        out_shape=edge_shapes(cell_rows, cell_cols),
        in_specs=[smem_spec] + vmem_specs(6),
        out_specs=vmem_specs(4),
    )(flags, water_depth, flux_east, flux_south, bed_level, roughness, land_float)

    step_call = pl.pallas_call(
        step_kernel,
        out_shape=(grid_shape, grid_shape, grid_shape,
                   jax.ShapeDtypeStruct((cell_rows // STRIP, cell_cols), f32))
        + edge_shapes(cell_rows, cell_cols),
        in_specs=[smem_spec] + vmem_specs(10),
        out_specs=vmem_specs(8),
    )

    depth = water_depth
    tile_parts = []
    for step in range(STEPS):
        to_west, to_north, to_east, to_south = edges
        east_in = shifted(to_west, "gx", -1)
        south_in = shifted(to_north, "gy", -1)
        west_in = shifted(to_east, "gx", 1)
        north_in = shifted(to_south, "gy", 1)
        depth, flux_east, flux_south, tiles, *edges = step_call(
            flags, depth, flux_east, flux_south, bed_level, roughness, land_float,
            east_in, south_in, west_in, north_in,
        )
        tile_parts.append(tiles.reshape(cell_rows // STRIP, cell_cols // reach_width, reach_width)
                          .reshape(-1, reach_width))

    column_slots = row_count * slot_cap
    tile_owner = tile_block // block_rows
    owner_row = tile_owner // col_count
    owner_col = tile_owner % col_count
    owner_hits = (tile_owner[:, None] == lax.iota(jnp.int32, device_count)[None, :]).astype(
        jnp.int32
    )
    earlier = jnp.sum((jnp.cumsum(owner_hits, axis=0) - owner_hits) * owner_hits, axis=1)
    send_pos = owner_col * column_slots + owner_row * slot_cap + earlier
    column_ids = (owner_row * block_rows + tile_block % block_rows).astype(f32)
    send_ids = jnp.full((col_count * column_slots,), -1.0, f32).at[send_pos].set(column_ids)
    id_rows = -(-column_slots // reach_width)
    send_ids = jnp.pad(
        send_ids.reshape(col_count, column_slots),
        ((0, 0), (0, id_rows * reach_width - column_slots)),
        constant_values=-1.0,
    ).reshape(col_count, id_rows, reach_width)
    gather_onehot = (
        lax.iota(jnp.int32, col_count * column_slots)[:, None] == send_pos[None, :]
    ).astype(f32)
    packed = [
        jnp.dot(gather_onehot, part, precision=lax.Precision.HIGHEST).reshape(
            col_count, column_slots, reach_width
        )
        for part in tile_parts
    ]
    got = lax.all_to_all(jnp.concatenate(packed + [send_ids], axis=1), "gx", 0, 0, tiled=True)
    got_ids = got[:, STEPS * column_slots:].reshape(col_count, -1)[:, :column_slots].reshape(-1)
    targets = lax.iota(f32, row_count * block_rows)
    scatter_onehot = (targets[:, None] == got_ids[None, :]).astype(f32)
    by_column = jnp.stack(
        [
            jnp.dot(
                scatter_onehot,
                got[:, step * column_slots:(step + 1) * column_slots].reshape(-1, reach_width),
                precision=lax.Precision.HIGHEST,
            ).reshape(row_count, block_rows, reach_width)
            for step in range(STEPS)
        ],
        axis=1,
    )
    laterals = jnp.sum(lax.all_to_all(by_column, "gy", 0, 0, tiled=True), axis=0)

    for step in range(STEPS):
        ratio = reach_rate * jnp.power(storage, 2.0 / 3.0)
        outflow = storage * ratio / (1.0 + ratio)
        own_part = block_term(downstream, outflow, first_block, block_rows)
        ahead_part = block_term(downstream, outflow, first_block + block_rows, block_rows)
        upstream = own_part + shifted(ahead_part, ("gy", "gx"), 1)
        storage = storage - outflow + upstream + lateral_gain * laterals[step]
    return (depth, flux_east, flux_south, storage)


def solution(mesh):
    placed = (
        P("gy", "gx"),
        P("gy", "gx"),
        P("gy", "gx"),
        P("gy", "gx"),
        P("gy", "gx"),
        P("gy", "gx"),
        P(("gy", "gx")),
        P(("gy", "gx"), None),
        P(("gy", "gx"), None),
        P(("gy", "gx")),
    )
    return jax.shard_map(
        body,
        mesh=mesh,
        in_specs=placed,
        out_specs=(P("gy", "gx"), P("gy", "gx"), P("gy", "gx"), P(("gy", "gx"), None)),
        check_vma=False,
    )
```

time: 124 us -> 108 us (0.87)
  other arithmetic: 26.1 us -> 4.36 us
  Pallas kernels: 0 us -> 21.1 us
  waiting for transfers between devices: 10.2 us -> 26.2 us
  starting transfers between devices: 60 us -> 45 us
  local copies, waits for them, and re-layouts: 19.4 us -> 6.26 us
  matrix products: 5.8 us -> 3.08 us
    pallas_call x0 -> x3, Pallas kernels: none -> 21.1 us  [the longest x2 17.1 us: body(): step_call(flags, depth, flux_east, flux_south, bed_level, roughness, land...]
    slice x20 -> x2, local copies, waits for them, and re-layouts: 13.1 us -> 0.06 us  [the longest x1 0.05 us: body(): got[:, step * column_slots:(step + 1) * column_slots]]
    div x2 -> x0, other arithmetic: 11.3 us -> none  [face_update(): return active * drive / damping]
    ppermute x14 -> x10, waiting for transfers between devices: 2.77 us -> 12 us  [shifted(): lax.ppermute(value, axis, [(source, source + steps) for source in range(f...]
    ppermute x14 -> x10, starting transfers between devices: 35.3 us -> 27.2 us  [shifted(): lax.ppermute(value, axis, [(source, source + steps) for source in range(f...]
    reduce_sum x5 -> x2, other arithmetic: 7.7 us -> 0.19 us  [the longest x1 0.18 us: body(): jnp.sum((jnp.cumsum(owner_hits, axis=0) - owner_hits) * owner_hits, axis=1)]
    all_to_all x4 -> x2, starting transfers between devices: 24.7 us -> 17.7 us  [the longest x1 11.6 us: body(): lax.all_to_all(jnp.concatenate(packed + [send_ids], axis=1), 'gx', 0, 0,...]
    all_to_all x4 -> x2, waiting for transfers between devices: 7.44 us -> 14.2 us  [the longest x1 11.4 us: body(): lax.all_to_all(jnp.concatenate(packed + [send_ids], axis=1), 'gx', 0, 0,...]
  transfers between devices with their start and end apart: 18 -> 12, of which waited for: 3 -> 6; matrix products, arithmetic and copies ran while one was open for 30% -> 3% of each run, Pallas kernels for 0% -> 0%
where the time goes in v3:
time: 108 us; the launch traced here: 107 us
  starting transfers between devices  45 us (42%)
  waiting for transfers between devices  26.2 us (24%)
  Pallas kernels  21.1 us (20%)
  local copies, waits for them, and re-layouts  6.26 us (6%)
  other arithmetic  4.36 us (4%)
  matrix products  3.08 us (3%)
    ppermute x10, starting transfers between devices, shifted(): lax.ppermute(value, axis, [(source, source + steps) for source in range(f...  27.2 us
    pallas_call x2, Pallas kernels, body(): step_call(flags, depth, flux_east, flux_south, bed_level, roughness, land...  17.1 us
    ppermute x10, waiting for transfers between devices, shifted(): lax.ppermute(value, axis, [(source, source + steps) for source in range(f...  12 us
    all_to_all x1, starting transfers between devices, body(): lax.all_to_all(jnp.concatenate(packed + [send_ids], axis=1), 'gx', 0, 0,...  11.6 us
    all_to_all x1, waiting for transfers between devices, body(): lax.all_to_all(jnp.concatenate(packed + [send_ids], axis=1), 'gx', 0, 0,...  11.4 us
    all_to_all x1, starting transfers between devices, body(): lax.all_to_all(by_column, 'gy', 0, 0, tiled=True)  6.09 us
    pallas_call x1, Pallas kernels, body(): pl.pallas_call(edge_kernel, out_shape=edge_shapes(cell_rows, cell_cols),...  4.01 us
    all_to_all x1, waiting for transfers between devices, body(): lax.all_to_all(by_column, 'gy', 0, 0, tiled=True)  2.86 us
  transfers between devices with their start and end apart: 12, of which 6 were waited for; matrix products, arithmetic and copies ran while one was open for 3% of the time, Pallas kernels for 0%

profile of v3, /device:TPU:1, one launch (start us, length us, event | category | flops | bytes accessed | tf_op | source)
XLA Modules:
  0.0 106.9 jit_solution(6914204077790044536)
XLA Ops:
  0.6 2.3 %convert_element_type.10.land_ref = f32[512,512]{1,0:T(8,128)} convert(s32[512,512]{1,0:T(8,128)} %param.15) | non-fusion elementwise | flops 262144 | bytes 2097152 | tf_op jit(solution)/shard_map/convert_element_type | solution.py:148
  2.9 0.7 add_convert_fusion.flags_ref
  3.6 4.0 %shard_map.129 = (f32[512,2]{1,0:T(8,128)}, f32[2,512]{1,0:T(2,128)}, f32[512,5]{1,0:T(8,128)}, f32[5,512]{1,0:T(8,128)}) custom-call(s32[2]{0:T(128)} %add_convert_fusion.flags_ref, f32[512,512]{1,0:T(8,128)} %d_ref.3, f32[512,512]{1,0:T(8,128)} %e_ref.3, f32[512,512]{1,0:T(8,128)} %s_ref.3, f32[512,512]{1,0:T(8,128)} %bed_ref.5, f32[512,512]{1,0:T(8,128)} %r_ref.5, ...), custom_call_target="tpu_custom_call" | custom-call | tf_op jit(solution)/shard_map/pallas_call | solution.py:158
  7.6 1.4 %collective-permute-start = (f32[512,2]{1,0:T(8,128)}, f32[512,2]{1,0:T(8,128)S(1)}, u32[]{:S(2)}, u32[]{:S(2)}) collective-permute-start(f32[512,2]{1,0:T(8,128)} %get-tuple-element.20), channel_id=1, source_target_pairs={{1,0},{2,1},{3,2},{4,3},{5,4},{6,5},{7,6},{8,7},{9,8},{10,9},{11,1... | collective-permute-start | bytes 12296 | tf_op jit(solution)/shard_map/ppermute | solution.py:25
  9.0 4.7 %collective-permute-start.2 = (f32[512,5]{1,0:T(8,128)}, f32[512,5]{1,0:T(8,128)S(1)}, u32[]{:S(2)}, u32[]{:S(2)}) collective-permute-start(f32[512,5]{1,0:T(8,128)} %get-tuple-element.22), channel_id=1, source_target_pairs={{0,1},{1,2},{2,3},{3,4},{4,5},{5,6},{6,7},{7,8},{8,9},{9,10},{10,1... | collective-permute-start | bytes 30728 | tf_op jit(solution)/shard_map/ppermute | solution.py:25
  13.7 4.4 %collective-permute-start.3 = (f32[5,512]{1,0:T(8,128)}, f32[5,512]{1,0:T(8,128)S(1)}, u32[]{:S(2)}, u32[]{:S(2)}) collective-permute-start(f32[5,512]{1,0:T(8,128)} %get-tuple-element.23), channel_id=1, source_target_pairs={{0,16},{16,32},{32,48},{48,64},{64,80},{80,96},{96,112},{1,17},{17... | collective-permute-start | bytes 30728 | tf_op jit(solution)/shard_map/ppermute | solution.py:25
  18.1 1.9 %collective-permute-start.1 = (f32[2,512]{1,0:T(2,128)S(1)}, f32[2,512]{1,0:T(2,128)S(1)}, u32[]{:S(2)}, u32[]{:S(2)}) collective-permute-start(f32[2,512]{1,0:T(2,128)S(1)} %copy-done.11), channel_id=1, source_target_pairs={{16,0},{32,16},{48,32},{64,48},{80,64},{96,80},{112,96},{17,1},{33... | collective-permute-start | bytes 12296 | tf_op jit(solution)/shard_map/ppermute | solution.py:25
  20.7 1.4 %scatter_custom_fusion = f32[512]{0:T(512)S(1)} fusion(s32[256]{0:T(256)S(1)} %get-tuple-element.39, f32[256]{0:T(256)S(1)} %get-tuple-element.36, f32[]{:T(128)} %constant.82.clone.1), kind=kCustom, calls=%fused_computation.72 | custom fusion | bytes 2052 | tf_op jit(solution)/shard_map/scatter | solution.py:199
  22.2 0.8 collective-permute-done.1.south_ref
  23.1 0.6 copy-done.6
  23.8 0.6 copy-done.4
  24.4 8.6 %shard_map.130 = (f32[512,512]{1,0:T(8,128)}, f32[512,512]{1,0:T(8,128)}, f32[512,512]{1,0:T(8,128)}, f32[64,512]{1,0:T(8,128)}, f32[512,2]{1,0:T(8,128)}, /*ind...) custom-call(s32[2]{0:T(128)} %add_convert_fusion.flags_ref, f32[512,512]{1,0:T(8,128)} %d_ref.3, ...), custom_call_target="tpu_custom_call" | custom-call | tf_op jit(solution)/shard_map/pallas_call | solution.py:182
  32.9 1.3 %collective-permute-start.4 = (f32[512,2]{1,0:T(8,128)}, f32[512,2]{1,0:T(8,128)S(1)}, u32[]{:S(2)}, u32[]{:S(2)}) collective-permute-start(f32[512,2]{1,0:T(8,128)} %get-tuple-element.27), channel_id=1, source_target_pairs={{1,0},{2,1},{3,2},{4,3},{5,4},{6,5},{7,6},{8,7},{9,8},{10,9},{11,1... | collective-permute-start | bytes 12296 | tf_op jit(solution)/shard_map/ppermute | solution.py:25
  34.2 4.0 %collective-permute-start.6 = (f32[512,5]{1,0:T(8,128)}, f32[512,5]{1,0:T(8,128)S(1)}, u32[]{:S(2)}, u32[]{:S(2)}) collective-permute-start(f32[512,5]{1,0:T(8,128)} %get-tuple-element.29), channel_id=1, source_target_pairs={{0,1},{1,2},{2,3},{3,4},{4,5},{5,6},{6,7},{7,8},{8,9},{9,10},{10,1... | collective-permute-start | bytes 30728 | tf_op jit(solution)/shard_map/ppermute | solution.py:25
  38.3 3.4 %collective-permute-start.7 = (f32[5,512]{1,0:T(8,128)}, f32[5,512]{1,0:T(8,128)S(1)}, u32[]{:S(2)}, u32[]{:S(2)}) collective-permute-start(f32[5,512]{1,0:T(8,128)} %get-tuple-element.30), channel_id=1, source_target_pairs={{0,16},{16,32},{32,48},{48,64},{64,80},{80,96},{96,112},{1,17},{17... | collective-permute-start | bytes 30728 | tf_op jit(solution)/shard_map/ppermute | solution.py:25
  41.7 2.1 %collective-permute-start.5 = (f32[2,512]{1,0:T(2,128)S(1)}, f32[2,512]{1,0:T(2,128)S(1)}, u32[]{:S(2)}, u32[]{:S(2)}) collective-permute-start(f32[2,512]{1,0:T(2,128)S(1)} %copy-done.12), channel_id=1, source_target_pairs={{16,0},{32,16},{48,32},{64,48},{80,64},{96,80},{112,96},{17,1},{33... | collective-permute-start | bytes 12296 | tf_op jit(solution)/shard_map/ppermute | solution.py:25
  43.8 0.9 reshape.134
  45.2 1.5 %collective-permute-done.5.south_ref = f32[2,512]{1,0:T(2,128)S(1)} collective-permute-done((f32[2,512]{1,0:T(2,128)S(1)}, f32[2,512]{1,0:T(2,128)S(1)}, u32[]{:S(2)}, u32[]{:S(2)}) %collective-permute-start.5) | collective-permute-done | bytes 4128 | tf_op jit(solution)/shard_map/ppermute | solution.py:25
  46.7 0.6 copy-done.7
  47.4 8.5 %shard_map.131 = (f32[512,512]{1,0:T(8,128)}, f32[512,512]{1,0:T(8,128)}, f32[512,512]{1,0:T(8,128)}, f32[64,512]{1,0:T(8,128)}, f32[512,2]{1,0:T(8,128)}, /*ind...) custom-call(s32[2]{0:T(128)} %add_convert_fusion.flags_ref, f32[512,512]{1,0:T(8,128)} %get-tuple-element.24.d_ref, ...), custom_call_target="tpu_custom_call" | custom-call | tf_op jit(solution)/shard_map/pallas_call | solution.py:182
  55.9 0.9 reshape.135
  57.3 0.9 pad_maximum_fusion
  58.1 11.6 %all-to-all-start = ((f32[16,65,128]{2,1,0:T(8,128)}), f32[16,65,128]{2,1,0:T(8,128)S(1)}, u32[]{:S(2)}, u32[]{:S(2)}) async-start(f32[16,65,128]{2,1,0:T(8,128)} %pad_maximum_fusion), calls=%async_computation | async-start | bytes 1179648 | tf_op jit(solution)/shard_map/all_to_all | solution.py:215
  69.8 11.4 %all-to-all-done = f32[16,65,128]{2,1,0:T(8,128)S(1)} async-done(((f32[16,65,128]{2,1,0:T(8,128)}), f32[16,65,128]{2,1,0:T(8,128)S(1)}, u32[]{:S(2)}, u32[]{:S(2)}) %all-to-all-start) | async-done | bytes 532512 | tf_op jit(solution)/shard_map/all_to_all | solution.py:215
  81.9 0.7 copy.18
  82.6 6.1 %all-to-all-start.1 = ((f32[8,2,16,128]{3,2,1,0:T(8,128)}), f32[8,2,16,128]{3,2,1,0:T(8,128)S(1)}, u32[]{:S(2)}, u32[]{:S(2)}) async-start(f32[8,2,16,128]{3,2,1,0:T(8,128)} %copy.18), calls=%async_computation.1 | async-start | bytes 262144 | tf_op jit(solution)/shard_map/all_to_all | solution.py:230
  89.0 2.1 %collective-permute-start.8 = (f32[16,128]{1,0:T(8,128)S(1)}, f32[16,128]{1,0:T(8,128)S(1)}, u32[]{:S(2)}, u32[]{:S(2)}) collective-permute-start(f32[16,128]{1,0:T(8,128)S(1)} %fusion.23), channel_id=1, source_target_pairs={{0,1},{1,2},{2,3},{3,4},{4,5},{5,6},{6,7},{7,8},{8,9},{9,10},{10,1... | collective-permute-start | bytes 24584 | tf_op jit(solution)/shard_map/ppermute | solution.py:25
  91.1 2.9 %all-to-all-done.1 = f32[8,2,16,128]{3,2,1,0:T(8,128)S(1)} async-done(((f32[8,2,16,128]{3,2,1,0:T(8,128)}), f32[8,2,16,128]{3,2,1,0:T(8,128)S(1)}, u32[]{:S(2)}, u32[]{:S(2)}) %all-to-all-start.1) | async-done | bytes 131104 | tf_op jit(solution)/shard_map/all_to_all | solution.py:230
  94.0 3.3 %collective-permute-done.8 = f32[16,128]{1,0:T(8,128)S(1)} collective-permute-done((f32[16,128]{1,0:T(8,128)S(1)}, f32[16,128]{1,0:T(8,128)S(1)}, u32[]{:S(2)}, u32[]{:S(2)}) %collective-permute-start.8) | collective-permute-done | bytes 8224 | tf_op jit(solution)/shard_map/ppermute | solution.py:25
  97.8 1.9 %collective-permute-start.9 = (f32[16,128]{1,0:T(8,128)S(1)}, f32[16,128]{1,0:T(8,128)S(1)}, u32[]{:S(2)}, u32[]{:S(2)}) collective-permute-start(f32[16,128]{1,0:T(8,128)S(1)} %fusion.21), channel_id=1, source_target_pairs={{0,1},{1,2},{2,3},{3,4},{4,5},{5,6},{6,7},{7,8},{8,9},{9,10},{10,1... | collective-permute-start | bytes 24584 | tf_op jit(solution)/shard_map/ppermute | solution.py:25
  99.7 6.4 %collective-permute-done.9 = f32[16,128]{1,0:T(8,128)S(1)} collective-permute-done((f32[16,128]{1,0:T(8,128)S(1)}, f32[16,128]{1,0:T(8,128)S(1)}, u32[]{:S(2)}, u32[]{:S(2)}) %collective-permute-start.9) | collective-permute-done | bytes 8224 | tf_op jit(solution)/shard_map/ppermute | solution.py:25
  106.1 0.9 fusion.28
  (60 shorter events, 3.4 us)
Async XLA Ops:
  7.6 10.5 %copy-start.11 = (f32[2,512]{1,0:T(2,128)S(1)}, f32[2,512]{1,0:T(2,128)}, u32[]{:S(2)}) copy-start(f32[2,512]{1,0:T(2,128)} %get-tuple-element.21) | copy-start | bytes 12292
  7.6 14.6 %collective-permute-start = (f32[512,2]{1,0:T(8,128)}, f32[512,2]{1,0:T(8,128)S(1)}, u32[]{:S(2)}, u32[]{:S(2)}) collective-permute-start(f32[512,2]{1,0:T(8,128)} %get-tuple-element.20), channel_id=1, source_target_pairs={{1,0},{2,1},{3,2},{4,3},{5,4},{6,5},{7,6},{8,7},{9,8},{10,9},{11,1... | collective-permute-start | bytes 12296 | tf_op jit(solution)/shard_map/ppermute | solution.py:25
  9.0 14.0 %collective-permute-start.2 = (f32[512,5]{1,0:T(8,128)}, f32[512,5]{1,0:T(8,128)S(1)}, u32[]{:S(2)}, u32[]{:S(2)}) collective-permute-start(f32[512,5]{1,0:T(8,128)} %get-tuple-element.22), channel_id=1, source_target_pairs={{0,1},{1,2},{2,3},{3,4},{4,5},{5,6},{6,7},{7,8},{8,9},{9,10},{10,1... | collective-permute-start | bytes 30728 | tf_op jit(solution)/shard_map/ppermute | solution.py:25
  13.7 6.4 %copy-start.8 = (s32[256]{0:T(256)S(1)}, s32[256]{0:T(256)}, u32[]{:S(2)}) copy-start(s32[256]{0:T(256)} %param.16) | copy-start | bytes 3076
  13.7 9.4 %collective-permute-start.3 = (f32[5,512]{1,0:T(8,128)}, f32[5,512]{1,0:T(8,128)S(1)}, u32[]{:S(2)}, u32[]{:S(2)}) collective-permute-start(f32[5,512]{1,0:T(8,128)} %get-tuple-element.23), channel_id=1, source_target_pairs={{0,16},{16,32},{32,48},{48,64},{64,80},{80,96},{96,112},{1,17},{17... | collective-permute-start | bytes 30728 | tf_op jit(solution)/shard_map/ppermute | solution.py:25
  18.1 4.9 %collective-permute-start.1 = (f32[2,512]{1,0:T(2,128)S(1)}, f32[2,512]{1,0:T(2,128)S(1)}, u32[]{:S(2)}, u32[]{:S(2)}) collective-permute-start(f32[2,512]{1,0:T(2,128)S(1)} %copy-done.11), channel_id=1, source_target_pairs={{16,0},{32,16},{48,32},{64,48},{80,64},{96,80},{112,96},{17,1},{33... | collective-permute-start | bytes 12296 | tf_op jit(solution)/shard_map/ppermute | solution.py:25
  22.2 0.9 copy-start
  23.1 0.6 copy-start.6
  23.1 0.7 copy-start.1
  23.8 0.6 copy-start.4
  32.9 8.8 %copy-start.12 = (f32[2,512]{1,0:T(2,128)S(1)}, f32[2,512]{1,0:T(2,128)}, u32[]{:S(2)}) copy-start(f32[2,512]{1,0:T(2,128)} %get-tuple-element.28) | copy-start | bytes 12292
  32.9 12.2 %collective-permute-start.4 = (f32[512,2]{1,0:T(8,128)}, f32[512,2]{1,0:T(8,128)S(1)}, u32[]{:S(2)}, u32[]{:S(2)}) collective-permute-start(f32[512,2]{1,0:T(8,128)} %get-tuple-element.27), channel_id=1, source_target_pairs={{1,0},{2,1},{3,2},{4,3},{5,4},{6,5},{7,6},{8,7},{9,8},{10,9},{11,1... | collective-permute-start | bytes 12296 | tf_op jit(solution)/shard_map/ppermute | solution.py:25
  34.2 12.4 %collective-permute-start.6 = (f32[512,5]{1,0:T(8,128)}, f32[512,5]{1,0:T(8,128)S(1)}, u32[]{:S(2)}, u32[]{:S(2)}) collective-permute-start(f32[512,5]{1,0:T(8,128)} %get-tuple-element.29), channel_id=1, source_target_pairs={{0,1},{1,2},{2,3},{3,4},{4,5},{5,6},{6,7},{7,8},{8,9},{9,10},{10,1... | collective-permute-start | bytes 30728 | tf_op jit(solution)/shard_map/ppermute | solution.py:25
  38.3 8.4 %collective-permute-start.7 = (f32[5,512]{1,0:T(8,128)}, f32[5,512]{1,0:T(8,128)S(1)}, u32[]{:S(2)}, u32[]{:S(2)}) collective-permute-start(f32[5,512]{1,0:T(8,128)} %get-tuple-element.30), channel_id=1, source_target_pairs={{0,16},{16,32},{32,48},{48,64},{64,80},{80,96},{96,112},{1,17},{17... | collective-permute-start | bytes 30728 | tf_op jit(solution)/shard_map/ppermute | solution.py:25
  41.7 4.9 %collective-permute-start.5 = (f32[2,512]{1,0:T(2,128)S(1)}, f32[2,512]{1,0:T(2,128)S(1)}, u32[]{:S(2)}, u32[]{:S(2)}) collective-permute-start(f32[2,512]{1,0:T(2,128)S(1)} %copy-done.12), channel_id=1, source_target_pairs={{16,0},{32,16},{48,32},{64,48},{80,64},{96,80},{112,96},{17,1},{33... | collective-permute-start | bytes 12296 | tf_op jit(solution)/shard_map/ppermute | solution.py:25
  45.2 1.5 %copy-start.2 = (f32[512,2]{1,0:T(8,128)}, f32[512,2]{1,0:T(8,128)S(1)}, u32[]{:S(2)}) copy-start(f32[512,2]{1,0:T(8,128)S(1)} %collective-permute-done.4.east_ref) | copy-start | bytes 12292
  46.6 0.6 copy-start.7
  46.7 0.7 copy-start.3
  46.7 0.7 copy-start.5
  58.1 23.0 %all-to-all-start = ((f32[16,65,128]{2,1,0:T(8,128)}), f32[16,65,128]{2,1,0:T(8,128)S(1)}, u32[]{:S(2)}, u32[]{:S(2)}) async-start(f32[16,65,128]{2,1,0:T(8,128)} %pad_maximum_fusion), calls=%async_computation | async-start | bytes 1179648 | tf_op jit(solution)/shard_map/all_to_all | solution.py:215
  82.6 6.1 %copy-start.9 = (f32[16,128]{1,0:T(8,128)S(1)}, f32[16,128]{1,0:T(8,128)}, u32[]{:S(2)}) copy-start(f32[16,128]{1,0:T(8,128)} %param.17) | copy-start | bytes 24580
  82.6 6.1 %copy-start.10 = (f32[16,128]{1,0:T(8,128)S(1)}, f32[16,128]{1,0:T(8,128)}, u32[]{:S(2)}) copy-start(f32[16,128]{1,0:T(8,128)} %param.18) | copy-start | bytes 24580
  82.6 6.1 %copy-start.13 = (s32[16]{0:T(128)S(1)}, s32[16]{0:T(128)}, u32[]{:S(2)}) copy-start(s32[16]{0:T(128)} %param.19) | copy-start | bytes 196
  82.6 11.3 %all-to-all-start.1 = ((f32[8,2,16,128]{3,2,1,0:T(8,128)}), f32[8,2,16,128]{3,2,1,0:T(8,128)S(1)}, u32[]{:S(2)}, u32[]{:S(2)}) async-start(f32[8,2,16,128]{3,2,1,0:T(8,128)} %copy.18), calls=%async_computation.1 | async-start | bytes 262144 | tf_op jit(solution)/shard_map/all_to_all | solution.py:230
  89.0 8.3 %collective-permute-start.8 = (f32[16,128]{1,0:T(8,128)S(1)}, f32[16,128]{1,0:T(8,128)S(1)}, u32[]{:S(2)}, u32[]{:S(2)}) collective-permute-start(f32[16,128]{1,0:T(8,128)S(1)} %fusion.23), channel_id=1, source_target_pairs={{0,1},{1,2},{2,3},{3,4},{4,5},{5,6},{6,7},{7,8},{8,9},{9,10},{10,1... | collective-permute-start | bytes 24584 | tf_op jit(solution)/shard_map/ppermute | solution.py:25
  97.8 8.3 %collective-permute-start.9 = (f32[16,128]{1,0:T(8,128)S(1)}, f32[16,128]{1,0:T(8,128)S(1)}, u32[]{:S(2)}, u32[]{:S(2)}) collective-permute-start(f32[16,128]{1,0:T(8,128)S(1)} %fusion.21), channel_id=1, source_target_pairs={{0,1},{1,2},{2,3},{3,4},{4,5},{5,6},{6,7},{7,8},{8,9},{9,10},{10,1... | collective-permute-start | bytes 24584 | tf_op jit(solution)/shard_map/ppermute | solution.py:25

commit v4 on v3

--- a/solution.py
+++ b/solution.py
@@ -65,22 +65,38 @@
     return col, row, eopen, sopen
 
 
-def edge_kernel(flags_ref, d_ref, e_ref, s_ref, bed_ref, r_ref, land_ref,
-                to_west, to_north, to_east, to_south):
+def edge_kernel(flags_ref, d_ref, land_ref, bed_first_col, bed_last_col, bed_first_row,
+                bed_last_row, e_ref, s_ref, r_col, r_row,
+                tile_out, to_west, to_north, to_east, to_south):
+    ny, nx = d_ref.shape
     depth = d_ref[...]
-    level = bed_ref[...] + depth
-    _, _, eopen, sopen = open_masks(flags_ref, land_ref[...])
-    write_edges(level, depth, e_ref[...], s_ref[...], r_ref[...], eopen, sopen,
-                to_west, to_north, to_east, to_south)
-
-
-def step_kernel(flags_ref, d_ref, e_ref, s_ref, bed_ref, r_ref, land_ref,
+    land = land_ref[...].astype(jnp.float32)
+    drained = drain_rate * land * jnp.abs(depth)
+    tile_out[...] = drained.reshape(ny // STRIP, STRIP, nx).sum(axis=1)
+    _, _, eopen, sopen = open_masks(flags_ref, land)
+    to_west[:, 0:1] = bed_first_col[:, 0:1] + depth[:, 0:1]
+    to_west[:, 1:2] = depth[:, 0:1]
+    to_north[0:1, :] = bed_first_row[0:1, :] + depth[0:1, :]
+    to_north[1:2, :] = depth[0:1, :]
+    to_east[:, 0:1] = e_ref[:, -1:]
+    to_east[:, 1:2] = bed_last_col[:, -1:] + depth[:, -1:]
+    to_east[:, 2:3] = depth[:, -1:]
+    to_east[:, 3:4] = r_col[:, -1:]
+    to_east[:, 4:5] = eopen[:, -1:]
+    to_south[0:1, :] = s_ref[-1:, :]
+    to_south[1:2, :] = bed_last_row[-1:, :] + depth[-1:, :]
+    to_south[2:3, :] = depth[-1:, :]
+    to_south[3:4, :] = r_row[-1:, :]
+    to_south[4:5, :] = sopen[-1:, :]
+
+
+def step_kernel(with_edges, flags_ref, d_ref, e_ref, s_ref, bed_ref, r_ref, land_ref,
                 east_ref, south_ref, west_ref, north_ref,
-                d_out, e_out, s_out, tile_out, to_west, to_north, to_east, to_south):
+                d_out, e_out, s_out, *more):
     ny, nx = d_ref.shape
     depth = d_ref[...]
     bed = bed_ref[...]
-    land = land_ref[...]
+    land = land_ref[...].astype(jnp.float32)
     rough = r_ref[...]
     level = bed + depth
     col, row, eopen, sopen = open_masks(flags_ref, land)
@@ -105,9 +121,12 @@
     d_out[...] = new_depth
     e_out[...] = flux_e
     s_out[...] = flux_s
-    tile_out[...] = drained.reshape(ny // STRIP, STRIP, nx).sum(axis=1)
-    write_edges(bed + new_depth, new_depth, flux_e, flux_s, rough, eopen, sopen,
-                to_west, to_north, to_east, to_south)
+    if with_edges:
+        tile_out, to_west, to_north, to_east, to_south = more
+        next_drained = drain_rate * land * jnp.abs(new_depth)
+        tile_out[...] = next_drained.reshape(ny // STRIP, STRIP, nx).sum(axis=1)
+        write_edges(bed + new_depth, new_depth, flux_e, flux_s, rough, eopen, sopen,
+                    to_west, to_north, to_east, to_south)
 
 
 def edge_shapes(ny, nx):
@@ -145,7 +164,6 @@
     device_count = row_count * col_count
     tile_count = tile_block.shape[0]
     slot_cap = max(2, 2 * tile_count // device_count)
-    land_float = land_mask.astype(jnp.float32)
     flags = jnp.stack(
         [(col_index == col_count - 1).astype(jnp.int32), (row_index == row_count - 1).astype(jnp.int32)]
     )
@@ -155,36 +173,34 @@
     grid_shape = jax.ShapeDtypeStruct((cell_rows, cell_cols), f32)
     smem_spec = pl.BlockSpec(memory_space=pltpu.SMEM)
 
-    edges = pl.pallas_call(
+    col_blocks = cell_cols // 128
+    row_blocks = cell_rows // 8
+    col_spec = lambda k: pl.BlockSpec((cell_rows, 128), lambda i: (0, k))
+    row_spec = lambda k: pl.BlockSpec((8, cell_cols), lambda i: (k, 0))
+    tile_shape = jax.ShapeDtypeStruct((cell_rows // STRIP, cell_cols), f32)
+    tiles, *edges = pl.pallas_call(
         edge_kernel,
-        out_shape=edge_shapes(cell_rows, cell_cols),
-        in_specs=[smem_spec] + vmem_specs(6),
-        out_specs=vmem_specs(4),
-    )(flags, water_depth, flux_east, flux_south, bed_level, roughness, land_float)
-
-    step_call = pl.pallas_call(
-        step_kernel,
-        out_shape=(grid_shape, grid_shape, grid_shape,
-                   jax.ShapeDtypeStruct((cell_rows // STRIP, cell_cols), f32))
-        + edge_shapes(cell_rows, cell_cols),
-        in_specs=[smem_spec] + vmem_specs(10),
-        out_specs=vmem_specs(8),
-    )
-
-    depth = water_depth
-    tile_parts = []
-    for step in range(STEPS):
-        to_west, to_north, to_east, to_south = edges
-        east_in = shifted(to_west, "gx", -1)
-        south_in = shifted(to_north, "gy", -1)
-        west_in = shifted(to_east, "gx", 1)
-        north_in = shifted(to_south, "gy", 1)
-        depth, flux_east, flux_south, tiles, *edges = step_call(
-            flags, depth, flux_east, flux_south, bed_level, roughness, land_float,
-            east_in, south_in, west_in, north_in,
+        grid=(1,),
+        out_shape=(tile_shape,) + edge_shapes(cell_rows, cell_cols),
+        in_specs=[smem_spec] + vmem_specs(2)
+        + [col_spec(0), col_spec(col_blocks - 1), row_spec(0), row_spec(row_blocks - 1),
+           col_spec(col_blocks - 1), row_spec(row_blocks - 1),
+           col_spec(col_blocks - 1), row_spec(row_blocks - 1)],
+        out_specs=vmem_specs(5),
+    )(flags, water_depth, land_mask, bed_level, bed_level, bed_level, bed_level,
+      flux_east, flux_south, roughness, roughness)
+    tile_parts = [tiles]
+
+    def step_call(with_edges):
+        outs = (grid_shape, grid_shape, grid_shape)
+        if with_edges:
+            outs = outs + (tile_shape,) + edge_shapes(cell_rows, cell_cols)
+        return pl.pallas_call(
+            functools.partial(step_kernel, with_edges),
+            out_shape=outs,
+            in_specs=[smem_spec] + vmem_specs(10),
+            out_specs=vmem_specs(len(outs)),
         )
-        tile_parts.append(tiles.reshape(cell_rows // STRIP, cell_cols // reach_width, reach_width)
-                          .reshape(-1, reach_width))
 
     column_slots = row_count * slot_cap
     tile_owner = tile_block // block_rows
@@ -206,13 +222,44 @@
     gather_onehot = (
         lax.iota(jnp.int32, col_count * column_slots)[:, None] == send_pos[None, :]
     ).astype(f32)
-    packed = [
-        jnp.dot(gather_onehot, part, precision=lax.Precision.HIGHEST).reshape(
-            col_count, column_slots, reach_width
+    def start_lateral(parts):
+        parts = [
+            part.reshape(cell_rows // STRIP, cell_cols // reach_width, reach_width).reshape(
+                -1, reach_width
+            )
+            for part in parts
+        ]
+        packed = [
+            jnp.dot(gather_onehot, part, precision=lax.Precision.HIGHEST).reshape(
+                col_count, column_slots, reach_width
+            )
+            for part in parts
+        ]
+        return jnp.concatenate(packed + [send_ids], axis=1)
+
+    depth = water_depth
+    for step in range(STEPS):
+        to_west, to_north, to_east, to_south = edges
+        east_in = shifted(to_west, "gx", -1)
+        south_in = shifted(to_north, "gy", -1)
+        west_in = shifted(to_east, "gx", 1)
+        north_in = shifted(to_south, "gy", 1)
+        last = step == STEPS - 1
+        if last:
+            lateral_started = start_lateral(tile_parts)
+            east_in, south_in, west_in, north_in, lateral_started = lax.optimization_barrier(
+                (east_in, south_in, west_in, north_in, lateral_started)
+            )
+        outs = step_call(not last)(
+            flags, depth, flux_east, flux_south, bed_level, roughness, land_mask,
+            east_in, south_in, west_in, north_in,
         )
-        for part in tile_parts
-    ]
-    got = lax.all_to_all(jnp.concatenate(packed + [send_ids], axis=1), "gx", 0, 0, tiled=True)
+        depth, flux_east, flux_south = outs[:3]
+        if not last:
+            tile_parts.append(outs[3])
+            edges = outs[4:]
+
+    got = lax.all_to_all(lateral_started, "gx", 0, 0, tiled=True)
     got_ids = got[:, STEPS * column_slots:].reshape(col_count, -1)[:, :column_slots].reshape(-1)
     targets = lax.iota(f32, row_count * block_rows)
     scatter_onehot = (targets[:, None] == got_ids[None, :]).astype(f32)

time: 108 us -> 98.5 us (0.912)
  waiting for transfers between devices: 26.2 us -> 19.8 us
  other arithmetic: 4.36 us -> 1.93 us
  Pallas kernels: 21.1 us -> 19.9 us
    ppermute x10, waiting for transfers between devices: 12 us -> 5.46 us  [shifted(): lax.ppermute(value, axis, [(source, source + steps) for source in range(f...]
    convert_element_type x1 -> x0, other arithmetic: 2.31 us -> none  [body(): land_float = land_mask.astype(jnp.float32)]
    pallas_call x3, Pallas kernels: 21.1 us -> 19.9 us  [the longest x2 16.7 us: body(): step_call(not last)]
    unnamed x29 -> x37, local copies, waits for them, and re-layouts: 2.02 us -> 2.77 us
  transfers between devices with their start and end apart: 12 -> 12, of which waited for: 6 -> 4; matrix products, arithmetic and copies ran while one was open for 3% -> 4% of each run, Pallas kernels for 0% -> 8%
where the time goes in v4:
time: 98.5 us; the launch traced here: 97.8 us
  starting transfers between devices  45.9 us (47%)
  Pallas kernels  19.9 us (20%)
  waiting for transfers between devices  19.8 us (20%)
  local copies, waits for them, and re-layouts  6.15 us (6%)
  matrix products  3.09 us (3%)
  other arithmetic  1.93 us (2%)
  between operations  1.04 us (1%)
    ppermute x10, starting transfers between devices, shifted(): lax.ppermute(value, axis, [(source, source + steps) for source in range(f...  27.8 us
    pallas_call x2, Pallas kernels, body(): step_call(not last)  16.7 us
    all_to_all x1, starting transfers between devices, body(): got = lax.all_to_all(lateral_started, 'gx', 0, 0, tiled=True)  11.6 us
    all_to_all x1, waiting for transfers between devices, body(): got = lax.all_to_all(lateral_started, 'gx', 0, 0, tiled=True)  11.4 us
    all_to_all x1, starting transfers between devices, body(): lax.all_to_all(by_column, 'gy', 0, 0, tiled=True)  6.48 us
    ppermute x10, waiting for transfers between devices, shifted(): lax.ppermute(value, axis, [(source, source + steps) for source in range(f...  5.46 us
    pallas_call x1, Pallas kernels, body(): pl.pallas_call(edge_kernel, grid=(1,), out_shape=(tile_shape,) + edge_sha...  3.2 us
    all_to_all x1, waiting for transfers between devices, body(): lax.all_to_all(by_column, 'gy', 0, 0, tiled=True)  2.95 us
  transfers between devices with their start and end apart: 12, of which 4 were waited for; matrix products, arithmetic and copies ran while one was open for 4% of the time, Pallas kernels for 8%

profile of v4, /device:TPU:1, one launch (start us, length us, event | category | flops | bytes accessed | tf_op | source)
XLA Modules:
  0.0 97.8 jit_solution(3911456545307184574)
XLA Ops:
  0.6 0.6 add_convert_fusion.flags_ref
  1.2 3.2 %shard_map.129 = (f32[64,512]{1,0:T(8,128)}, f32[512,2]{1,0:T(8,128)}, f32[2,512]{1,0:T(2,128)}, f32[512,5]{1,0:T(8,128)}, f32[5,512]{1,0:T(8,128)}) custom-call(s32[2]{0:T(128)} %add_convert_fusion.flags_ref, f32[512,512]{1,0:T(8,128)} %d_ref.3, s32[512,512]{1,0:T(8,128)} %land_ref.5, f32[512,512]{1,0:T(8,128)} %bed_ref.3, f32[512,512]{1,0:T(8,128)} %bed_ref.3, ...), custom_call_target="tpu_custom_call" | custom-call | tf_op jit(solution)/shard_map/pallas_call | solution.py:181
  4.4 1.3 %collective-permute-start = (f32[512,2]{1,0:T(8,128)}, f32[512,2]{1,0:T(8,128)S(1)}, u32[]{:S(2)}, u32[]{:S(2)}) collective-permute-start(f32[512,2]{1,0:T(8,128)} %get-tuple-element.25), channel_id=1, source_target_pairs={{1,0},{2,1},{3,2},{4,3},{5,4},{6,5},{7,6},{8,7},{9,8},{10,9},{11,1... | collective-permute-start | bytes 12296 | tf_op jit(solution)/shard_map/ppermute | solution.py:25
  5.7 4.7 %collective-permute-start.2 = (f32[512,5]{1,0:T(8,128)}, f32[512,5]{1,0:T(8,128)S(1)}, u32[]{:S(2)}, u32[]{:S(2)}) collective-permute-start(f32[512,5]{1,0:T(8,128)} %get-tuple-element.27), channel_id=1, source_target_pairs={{0,1},{1,2},{2,3},{3,4},{4,5},{5,6},{6,7},{7,8},{8,9},{9,10},{10,1... | collective-permute-start | bytes 30728 | tf_op jit(solution)/shard_map/ppermute | solution.py:25
  10.4 4.4 %collective-permute-start.3 = (f32[5,512]{1,0:T(8,128)}, f32[5,512]{1,0:T(8,128)S(1)}, u32[]{:S(2)}, u32[]{:S(2)}) collective-permute-start(f32[5,512]{1,0:T(8,128)} %get-tuple-element.28), channel_id=1, source_target_pairs={{0,16},{16,32},{32,48},{48,64},{64,80},{80,96},{96,112},{1,17},{17... | collective-permute-start | bytes 30728 | tf_op jit(solution)/shard_map/ppermute | solution.py:25
  14.8 1.9 %collective-permute-start.1 = (f32[2,512]{1,0:T(2,128)S(1)}, f32[2,512]{1,0:T(2,128)S(1)}, u32[]{:S(2)}, u32[]{:S(2)}) collective-permute-start(f32[2,512]{1,0:T(2,128)S(1)} %copy-done.15), channel_id=1, source_target_pairs={{16,0},{32,16},{48,32},{64,48},{80,64},{96,80},{112,96},{17,1},{33... | collective-permute-start | bytes 12296 | tf_op jit(solution)/shard_map/ppermute | solution.py:25
  17.4 0.7 copy-done.4
  18.1 0.4 fusion.4
  18.6 1.4 %scatter_custom_fusion = f32[512]{0:T(512)S(1)} fusion(s32[256]{0:T(256)S(1)} %get-tuple-element.49, f32[256]{0:T(256)S(1)} %get-tuple-element.46, f32[]{:T(128)} %constant.79.clone.1), kind=kCustom, calls=%fused_computation.72 | custom fusion | bytes 2052 | tf_op jit(solution)/shard_map/scatter | solution.py:215
  20.1 0.6 copy-done.2
  20.8 0.6 copy-done.6
  21.4 8.7 %shard_map.130 = (f32[512,512]{1,0:T(8,128)}, f32[512,512]{1,0:T(8,128)}, f32[512,512]{1,0:T(8,128)}, f32[64,512]{1,0:T(8,128)}, f32[512,2]{1,0:T(8,128)}, /*ind...) custom-call(s32[2]{0:T(128)} %add_convert_fusion.flags_ref, f32[512,512]{1,0:T(8,128)} %d_ref.3, ...), custom_call_target="tpu_custom_call" | custom-call | tf_op jit(solution)/shard_map/pallas_call | solution.py:253
  30.1 1.0 reshape.135
  31.1 0.4 fusion.2
  31.6 1.3 %collective-permute-start.4 = (f32[512,2]{1,0:T(8,128)S(1)}, f32[512,2]{1,0:T(8,128)S(1)}, u32[]{:S(2)}, u32[]{:S(2)}) collective-permute-start(f32[512,2]{1,0:T(8,128)S(1)} %copy-done.11), channel_id=1, source_target_pairs={{1,0},{2,1},{3,2},{4,3},{5,4},{6,5},{7,6},{8,7},{9,8},{10,9},{11,1... | collective-permute-start | bytes 12296 | tf_op jit(solution)/shard_map/ppermute | solution.py:25
  32.9 4.0 %collective-permute-start.6 = (f32[512,5]{1,0:T(8,128)S(1)}, f32[512,5]{1,0:T(8,128)S(1)}, u32[]{:S(2)}, u32[]{:S(2)}) collective-permute-start(f32[512,5]{1,0:T(8,128)S(1)} %copy-done.10), channel_id=1, source_target_pairs={{0,1},{1,2},{2,3},{3,4},{4,5},{5,6},{6,7},{7,8},{8,9},{9,10},{10,1... | collective-permute-start | bytes 30728 | tf_op jit(solution)/shard_map/ppermute | solution.py:25
  36.9 4.2 %collective-permute-start.7 = (f32[5,512]{1,0:T(8,128)S(1)}, f32[5,512]{1,0:T(8,128)S(1)}, u32[]{:S(2)}, u32[]{:S(2)}) collective-permute-start(f32[5,512]{1,0:T(8,128)S(1)} %copy-done.12), channel_id=1, source_target_pairs={{0,16},{16,32},{32,48},{48,64},{64,80},{80,96},{96,112},{1,17},{17... | collective-permute-start | bytes 30728 | tf_op jit(solution)/shard_map/ppermute | solution.py:25
  41.1 1.9 %collective-permute-start.5 = (f32[2,512]{1,0:T(2,128)S(1)}, f32[2,512]{1,0:T(2,128)S(1)}, u32[]{:S(2)}, u32[]{:S(2)}) collective-permute-start(f32[2,512]{1,0:T(2,128)S(1)} %copy-done.16), channel_id=1, source_target_pairs={{16,0},{32,16},{48,32},{64,48},{80,64},{96,80},{112,96},{17,1},{33... | collective-permute-start | bytes 12296 | tf_op jit(solution)/shard_map/ppermute | solution.py:25
  43.0 0.9 pad_maximum_fusion
  43.9 2.1 %collective-permute-done.5.south_ref = f32[2,512]{1,0:T(2,128)S(1)} collective-permute-done((f32[2,512]{1,0:T(2,128)S(1)}, f32[2,512]{1,0:T(2,128)S(1)}, u32[]{:S(2)}, u32[]{:S(2)}) %collective-permute-start.5) | collective-permute-done | bytes 4128 | tf_op jit(solution)/shard_map/ppermute | solution.py:25
  46.1 0.6 copy-done.7
  46.7 11.6 %all-to-all-start = ((f32[16,65,128]{2,1,0:T(8,128)}), f32[16,65,128]{2,1,0:T(8,128)S(1)}, u32[]{:S(2)}, u32[]{:S(2)}) async-start(f32[16,65,128]{2,1,0:T(8,128)} %pad_maximum_fusion), calls=%async_computation | async-start | bytes 1179648 | tf_op jit(solution)/shard_map/all_to_all | solution.py:262
  58.4 11.4 %all-to-all-done = f32[16,65,128]{2,1,0:T(8,128)S(1)} async-done(((f32[16,65,128]{2,1,0:T(8,128)}), f32[16,65,128]{2,1,0:T(8,128)S(1)}, u32[]{:S(2)}, u32[]{:S(2)}) %all-to-all-start) | async-done | bytes 532512 | tf_op jit(solution)/shard_map/all_to_all | solution.py:262
  69.9 0.3 convolution_bitcast_fusion.1
  70.5 0.7 copy.18
  71.2 6.5 %all-to-all-start.1 = ((f32[8,2,16,128]{3,2,1,0:T(8,128)}), f32[8,2,16,128]{3,2,1,0:T(8,128)S(1)}, u32[]{:S(2)}, u32[]{:S(2)}) async-start(f32[8,2,16,128]{3,2,1,0:T(8,128)} %copy.18), calls=%async_computation.1 | async-start | bytes 262144 | tf_op jit(solution)/shard_map/all_to_all | solution.py:277
  78.0 2.0 %collective-permute-start.8 = (f32[16,128]{1,0:T(8,128)S(1)}, f32[16,128]{1,0:T(8,128)S(1)}, u32[]{:S(2)}, u32[]{:S(2)}) collective-permute-start(f32[16,128]{1,0:T(8,128)S(1)} %fusion.23), channel_id=1, source_target_pairs={{0,1},{1,2},{2,3},{3,4},{4,5},{5,6},{6,7},{7,8},{8,9},{9,10},{10,1... | collective-permute-start | bytes 24584 | tf_op jit(solution)/shard_map/ppermute | solution.py:25
  80.0 2.9 %all-to-all-done.1 = f32[8,2,16,128]{3,2,1,0:T(8,128)S(1)} async-done(((f32[8,2,16,128]{3,2,1,0:T(8,128)}), f32[8,2,16,128]{3,2,1,0:T(8,128)S(1)}, u32[]{:S(2)}, u32[]{:S(2)}) %all-to-all-start.1) | async-done | bytes 131104 | tf_op jit(solution)/shard_map/all_to_all | solution.py:277
  82.9 3.3 %collective-permute-done.8 = f32[16,128]{1,0:T(8,128)S(1)} collective-permute-done((f32[16,128]{1,0:T(8,128)S(1)}, f32[16,128]{1,0:T(8,128)S(1)}, u32[]{:S(2)}, u32[]{:S(2)}) %collective-permute-start.8) | collective-permute-done | bytes 8224 | tf_op jit(solution)/shard_map/ppermute | solution.py:25
  86.8 2.1 %collective-permute-start.9 = (f32[16,128]{1,0:T(8,128)S(1)}, f32[16,128]{1,0:T(8,128)S(1)}, u32[]{:S(2)}, u32[]{:S(2)}) collective-permute-start(f32[16,128]{1,0:T(8,128)S(1)} %fusion.21), channel_id=1, source_target_pairs={{0,1},{1,2},{2,3},{3,4},{4,5},{5,6},{6,7},{7,8},{8,9},{9,10},{10,1... | collective-permute-start | bytes 24584 | tf_op jit(solution)/shard_map/ppermute | solution.py:25
  88.9 8.1 %shard_map.131 = (f32[512,512]{1,0:T(8,128)}, f32[512,512]{1,0:T(8,128)}, f32[512,512]{1,0:T(8,128)}) custom-call(s32[2]{0:T(128)} %add_convert_fusion.flags_ref, f32[512,512]{1,0:T(8,128)} %get-tuple-element.29.d_ref, f32[512,512]{1,0:T(8,128)} %get-tuple-element.30.e_ref, f32[512,512]{1,0:T(8,128)} %get-tuple-element.31.s_ref, f32[512,512]{1,0:T(8,128)} %bed_ref.3, ...), custom_call_target="tpu_custom_call" | custom-call | tf_op jit(solution)/shard_map/pallas_call | solution.py:253
  96.9 0.9 fusion.28
  (67 shorter events, 2.2 us)
Async XLA Ops:
  4.4 10.4 %copy-start.15 = (f32[2,512]{1,0:T(2,128)S(1)}, f32[2,512]{1,0:T(2,128)}, u32[]{:S(2)}) copy-start(f32[2,512]{1,0:T(2,128)} %get-tuple-element.26) | copy-start | bytes 12292
  4.4 15.6 %collective-permute-start = (f32[512,2]{1,0:T(8,128)}, f32[512,2]{1,0:T(8,128)S(1)}, u32[]{:S(2)}, u32[]{:S(2)}) collective-permute-start(f32[512,2]{1,0:T(8,128)} %get-tuple-element.25), channel_id=1, source_target_pairs={{1,0},{2,1},{3,2},{4,3},{5,4},{6,5},{7,6},{8,7},{9,8},{10,9},{11,1... | collective-permute-start | bytes 12296 | tf_op jit(solution)/shard_map/ppermute | solution.py:25
  5.7 14.4 %collective-permute-start.2 = (f32[512,5]{1,0:T(8,128)}, f32[512,5]{1,0:T(8,128)S(1)}, u32[]{:S(2)}, u32[]{:S(2)}) collective-permute-start(f32[512,5]{1,0:T(8,128)} %get-tuple-element.27), channel_id=1, source_target_pairs={{0,1},{1,2},{2,3},{3,4},{4,5},{5,6},{6,7},{7,8},{8,9},{9,10},{10,1... | collective-permute-start | bytes 30728 | tf_op jit(solution)/shard_map/ppermute | solution.py:25
  10.4 9.7 %collective-permute-start.3 = (f32[5,512]{1,0:T(8,128)}, f32[5,512]{1,0:T(8,128)S(1)}, u32[]{:S(2)}, u32[]{:S(2)}) collective-permute-start(f32[5,512]{1,0:T(8,128)} %get-tuple-element.28), channel_id=1, source_target_pairs={{0,16},{16,32},{32,48},{48,64},{64,80},{80,96},{96,112},{1,17},{17... | collective-permute-start | bytes 30728 | tf_op jit(solution)/shard_map/ppermute | solution.py:25
  14.8 2.0 %copy-start.9 = (s32[256]{0:T(256)S(1)}, s32[256]{0:T(256)}, u32[]{:S(2)}) copy-start(s32[256]{0:T(256)} %param.16) | copy-start | bytes 3076
  14.8 5.3 %collective-permute-start.1 = (f32[2,512]{1,0:T(2,128)S(1)}, f32[2,512]{1,0:T(2,128)S(1)}, u32[]{:S(2)}, u32[]{:S(2)}) collective-permute-start(f32[2,512]{1,0:T(2,128)S(1)} %copy-done.15), channel_id=1, source_target_pairs={{16,0},{32,16},{48,32},{64,48},{80,64},{96,80},{112,96},{17,1},{33... | collective-permute-start | bytes 12296 | tf_op jit(solution)/shard_map/ppermute | solution.py:25
  17.2 0.9 copy-start.4
  20.1 0.7 copy-start.2
  20.1 0.7 copy-start.8
  20.1 0.8 copy-start.3
  20.8 0.6 copy-start.6
  30.1 1.4 %copy-start.11 = (f32[512,2]{1,0:T(8,128)S(1)}, f32[512,2]{1,0:T(8,128)}, u32[]{:S(2)}) copy-start(f32[512,2]{1,0:T(8,128)} %get-tuple-element.32) | copy-start | bytes 12292
  31.1 1.8 %copy-start.10 = (f32[512,5]{1,0:T(8,128)S(1)}, f32[512,5]{1,0:T(8,128)}, u32[]{:S(2)}) copy-start(f32[512,5]{1,0:T(8,128)} %get-tuple-element.34) | copy-start | bytes 30724
  31.1 5.8 %copy-start.12 = (f32[5,512]{1,0:T(8,128)S(1)}, f32[5,512]{1,0:T(8,128)}, u32[]{:S(2)}) copy-start(f32[5,512]{1,0:T(8,128)} %get-tuple-element.35) | copy-start | bytes 30724
  31.5 9.6 %copy-start.16 = (f32[2,512]{1,0:T(2,128)S(1)}, f32[2,512]{1,0:T(2,128)}, u32[]{:S(2)}) copy-start(f32[2,512]{1,0:T(2,128)} %get-tuple-element.33) | copy-start | bytes 12292
  31.6 12.3 %collective-permute-start.4 = (f32[512,2]{1,0:T(8,128)S(1)}, f32[512,2]{1,0:T(8,128)S(1)}, u32[]{:S(2)}, u32[]{:S(2)}) collective-permute-start(f32[512,2]{1,0:T(8,128)S(1)} %copy-done.11), channel_id=1, source_target_pairs={{1,0},{2,1},{3,2},{4,3},{5,4},{6,5},{7,6},{8,7},{9,8},{10,9},{11,1... | collective-permute-start | bytes 12296 | tf_op jit(solution)/shard_map/ppermute | solution.py:25
  32.9 13.2 %collective-permute-start.6 = (f32[512,5]{1,0:T(8,128)S(1)}, f32[512,5]{1,0:T(8,128)S(1)}, u32[]{:S(2)}, u32[]{:S(2)}) collective-permute-start(f32[512,5]{1,0:T(8,128)S(1)} %copy-done.10), channel_id=1, source_target_pairs={{0,1},{1,2},{2,3},{3,4},{4,5},{5,6},{6,7},{7,8},{8,9},{9,10},{10,1... | collective-permute-start | bytes 30728 | tf_op jit(solution)/shard_map/ppermute | solution.py:25
  36.9 9.1 %collective-permute-start.7 = (f32[5,512]{1,0:T(8,128)S(1)}, f32[5,512]{1,0:T(8,128)S(1)}, u32[]{:S(2)}, u32[]{:S(2)}) collective-permute-start(f32[5,512]{1,0:T(8,128)S(1)} %copy-done.12), channel_id=1, source_target_pairs={{0,16},{16,32},{32,48},{48,64},{64,80},{80,96},{96,112},{1,17},{17... | collective-permute-start | bytes 30728 | tf_op jit(solution)/shard_map/ppermute | solution.py:25
  41.1 4.9 %collective-permute-start.5 = (f32[2,512]{1,0:T(2,128)S(1)}, f32[2,512]{1,0:T(2,128)S(1)}, u32[]{:S(2)}, u32[]{:S(2)}) collective-permute-start(f32[2,512]{1,0:T(2,128)S(1)} %copy-done.16), channel_id=1, source_target_pairs={{16,0},{32,16},{48,32},{64,48},{80,64},{96,80},{112,96},{17,1},{33... | collective-permute-start | bytes 12296 | tf_op jit(solution)/shard_map/ppermute | solution.py:25
  43.9 2.2 %copy-start = (f32[512,2]{1,0:T(8,128)}, f32[512,2]{1,0:T(8,128)S(1)}, u32[]{:S(2)}) copy-start(f32[512,2]{1,0:T(8,128)S(1)} %collective-permute-done.4.east_ref) | copy-start | bytes 12292
  46.0 0.6 copy-start.7
  46.0 0.7 copy-start.1
  46.0 0.7 copy-start.5
  46.7 23.0 %all-to-all-start = ((f32[16,65,128]{2,1,0:T(8,128)}), f32[16,65,128]{2,1,0:T(8,128)S(1)}, u32[]{:S(2)}, u32[]{:S(2)}) async-start(f32[16,65,128]{2,1,0:T(8,128)} %pad_maximum_fusion), calls=%async_computation | async-start | bytes 1179648 | tf_op jit(solution)/shard_map/all_to_all | solution.py:262
  71.2 6.5 %copy-start.13 = (f32[16,128]{1,0:T(8,128)S(1)}, f32[16,128]{1,0:T(8,128)}, u32[]{:S(2)}) copy-start(f32[16,128]{1,0:T(8,128)} %param.17) | copy-start | bytes 24580
  71.2 6.5 %copy-start.14 = (f32[16,128]{1,0:T(8,128)S(1)}, f32[16,128]{1,0:T(8,128)}, u32[]{:S(2)}) copy-start(f32[16,128]{1,0:T(8,128)} %param.18) | copy-start | bytes 24580
  71.2 6.5 %copy-start.17 = (s32[16]{0:T(128)S(1)}, s32[16]{0:T(128)}, u32[]{:S(2)}) copy-start(s32[16]{0:T(128)} %param.19) | copy-start | bytes 196
  71.2 11.7 %all-to-all-start.1 = ((f32[8,2,16,128]{3,2,1,0:T(8,128)}), f32[8,2,16,128]{3,2,1,0:T(8,128)S(1)}, u32[]{:S(2)}, u32[]{:S(2)}) async-start(f32[8,2,16,128]{3,2,1,0:T(8,128)} %copy.18), calls=%async_computation.1 | async-start | bytes 262144 | tf_op jit(solution)/shard_map/all_to_all | solution.py:277
  78.0 8.3 %collective-permute-start.8 = (f32[16,128]{1,0:T(8,128)S(1)}, f32[16,128]{1,0:T(8,128)S(1)}, u32[]{:S(2)}, u32[]{:S(2)}) collective-permute-start(f32[16,128]{1,0:T(8,128)S(1)} %fusion.23), channel_id=1, source_target_pairs={{0,1},{1,2},{2,3},{3,4},{4,5},{5,6},{6,7},{7,8},{8,9},{9,10},{10,1... | collective-permute-start | bytes 24584 | tf_op jit(solution)/shard_map/ppermute | solution.py:25
  86.8 10.2 %collective-permute-start.9 = (f32[16,128]{1,0:T(8,128)S(1)}, f32[16,128]{1,0:T(8,128)S(1)}, u32[]{:S(2)}, u32[]{:S(2)}) collective-permute-start(f32[16,128]{1,0:T(8,128)S(1)} %fusion.21), channel_id=1, source_target_pairs={{0,1},{1,2},{2,3},{3,4},{4,5},{5,6},{6,7},{7,8},{8,9},{9,10},{10,1... | collective-permute-start | bytes 24584 | tf_op jit(solution)/shard_map/ppermute | solution.py:25

commit v5 on v4

--- a/solution.py
+++ b/solution.py
@@ -202,25 +202,22 @@
             out_specs=vmem_specs(len(outs)),
         )
 
-    column_slots = row_count * slot_cap
     tile_owner = tile_block // block_rows
-    owner_row = tile_owner // col_count
-    owner_col = tile_owner % col_count
     owner_hits = (tile_owner[:, None] == lax.iota(jnp.int32, device_count)[None, :]).astype(
         jnp.int32
     )
     earlier = jnp.sum((jnp.cumsum(owner_hits, axis=0) - owner_hits) * owner_hits, axis=1)
-    send_pos = owner_col * column_slots + owner_row * slot_cap + earlier
-    column_ids = (owner_row * block_rows + tile_block % block_rows).astype(f32)
-    send_ids = jnp.full((col_count * column_slots,), -1.0, f32).at[send_pos].set(column_ids)
-    id_rows = -(-column_slots // reach_width)
+    send_pos = tile_owner * slot_cap + earlier
+    local_ids = (tile_block % block_rows).astype(f32)
+    send_ids = jnp.full((device_count * slot_cap,), -1.0, f32).at[send_pos].set(local_ids)
+    id_rows = -(-slot_cap // reach_width)
     send_ids = jnp.pad(
-        send_ids.reshape(col_count, column_slots),
-        ((0, 0), (0, id_rows * reach_width - column_slots)),
+        send_ids.reshape(device_count, slot_cap),
+        ((0, 0), (0, id_rows * reach_width - slot_cap)),
         constant_values=-1.0,
-    ).reshape(col_count, id_rows, reach_width)
+    ).reshape(device_count, id_rows, reach_width)
     gather_onehot = (
-        lax.iota(jnp.int32, col_count * column_slots)[:, None] == send_pos[None, :]
+        lax.iota(jnp.int32, device_count * slot_cap)[:, None] == send_pos[None, :]
     ).astype(f32)
     def start_lateral(parts):
         parts = [
@@ -231,7 +228,7 @@
         ]
         packed = [
             jnp.dot(gather_onehot, part, precision=lax.Precision.HIGHEST).reshape(
-                col_count, column_slots, reach_width
+                device_count, slot_cap, reach_width
             )
             for part in parts
         ]
@@ -259,22 +256,18 @@
             tile_parts.append(outs[3])
             edges = outs[4:]
 
-    got = lax.all_to_all(lateral_started, "gx", 0, 0, tiled=True)
-    got_ids = got[:, STEPS * column_slots:].reshape(col_count, -1)[:, :column_slots].reshape(-1)
-    targets = lax.iota(f32, row_count * block_rows)
+    got = lax.all_to_all(lateral_started, ("gy", "gx"), 0, 0, tiled=True)
+    got_ids = got[:, STEPS * slot_cap:].reshape(device_count, -1)[:, :slot_cap].reshape(-1)
+    targets = lax.iota(f32, block_rows)
     scatter_onehot = (targets[:, None] == got_ids[None, :]).astype(f32)
-    by_column = jnp.stack(
-        [
-            jnp.dot(
-                scatter_onehot,
-                got[:, step * column_slots:(step + 1) * column_slots].reshape(-1, reach_width),
-                precision=lax.Precision.HIGHEST,
-            ).reshape(row_count, block_rows, reach_width)
-            for step in range(STEPS)
-        ],
-        axis=1,
-    )
-    laterals = jnp.sum(lax.all_to_all(by_column, "gy", 0, 0, tiled=True), axis=0)
+    laterals = [
+        jnp.dot(
+            scatter_onehot,
+            got[:, step * slot_cap:(step + 1) * slot_cap].reshape(-1, reach_width),
+            precision=lax.Precision.HIGHEST,
+        )
+        for step in range(STEPS)
+    ]
 
     for step in range(STEPS):
         ratio = reach_rate * jnp.power(storage, 2.0 / 3.0)

time: 98.5 us -> 90.7 us (0.921)
  waiting for transfers between devices: 19.8 us -> 15 us
  starting transfers between devices: 45.9 us -> 43.3 us
    all_to_all x2 -> x1, waiting for transfers between devices: 14.3 us -> 6.42 us  [body(): got = lax.all_to_all(lateral_started, ('gy', 'gx'), 0, 0, tiled=True)]
    all_to_all x2 -> x1, starting transfers between devices: 18.1 us -> 13.7 us  [body(): got = lax.all_to_all(lateral_started, ('gy', 'gx'), 0, 0, tiled=True)]
    ppermute x10, waiting for transfers between devices: 5.46 us -> 8.57 us  [shifted(): lax.ppermute(value, axis, [(source, source + steps) for source in range(f...]
    ppermute x10, starting transfers between devices: 27.8 us -> 29.6 us  [shifted(): lax.ppermute(value, axis, [(source, source + steps) for source in range(f...]
    optimization_barrier x0 -> x1, local copies, waits for them, and re-layouts: none -> 1.33 us  [body(): lax.optimization_barrier((east_in, south_in, west_in, north_in, lateral_s...]
  transfers between devices with their start and end apart: 12 -> 11, of which waited for: 4 -> 3; matrix products, arithmetic and copies ran while one was open for 4% -> 4% of each run, Pallas kernels for 8% -> 9%
where the time goes in v5:
time: 90.7 us; the launch traced here: 90.2 us
  starting transfers between devices  43.3 us (48%)
  Pallas kernels  19.9 us (22%)
  waiting for transfers between devices  15 us (17%)
  local copies, waits for them, and re-layouts  6.91 us (8%)
  matrix products  2.87 us (3%)
  other arithmetic  1.13 us (1%)
  between operations  1.09 us (1%)
    ppermute x10, starting transfers between devices, shifted(): lax.ppermute(value, axis, [(source, source + steps) for source in range(f...  29.6 us
    pallas_call x2, Pallas kernels, body(): step_call(not last)  16.7 us
    all_to_all x1, starting transfers between devices, body(): got = lax.all_to_all(lateral_started, ('gy', 'gx'), 0, 0, tiled=True)  13.7 us
    ppermute x10, waiting for transfers between devices, shifted(): lax.ppermute(value, axis, [(source, source + steps) for source in range(f...  8.57 us
    all_to_all x1, waiting for transfers between devices, body(): got = lax.all_to_all(lateral_started, ('gy', 'gx'), 0, 0, tiled=True)  6.42 us
    pallas_call x1, Pallas kernels, body(): pl.pallas_call(edge_kernel, grid=(1,), out_shape=(tile_shape,) + edge_sha...  3.19 us
    unnamed x37, local copies, waits for them, and re-layouts  2.75 us
  transfers between devices with their start and end apart: 11, of which 3 were waited for; matrix products, arithmetic and copies ran while one was open for 4% of the time, Pallas kernels for 9%

profile of v5, /device:TPU:1, one launch (start us, length us, event | category | flops | bytes accessed | tf_op | source)
XLA Modules:
  0.0 90.2 jit_solution(8844360928997916982)
XLA Ops:
  0.6 0.6 add_convert_fusion.flags_ref
  1.3 3.2 %shard_map.129 = (f32[64,512]{1,0:T(8,128)}, f32[512,2]{1,0:T(8,128)}, f32[2,512]{1,0:T(2,128)}, f32[512,5]{1,0:T(8,128)}, f32[5,512]{1,0:T(8,128)}) custom-call(s32[2]{0:T(128)} %add_convert_fusion.flags_ref, f32[512,512]{1,0:T(8,128)} %d_ref.3, s32[512,512]{1,0:T(8,128)} %land_ref.5, f32[512,512]{1,0:T(8,128)} %bed_ref.3, f32[512,512]{1,0:T(8,128)} %bed_ref.3, ...), custom_call_target="tpu_custom_call" | custom-call | tf_op jit(solution)/shard_map/pallas_call | solution.py:181
  4.5 1.3 %collective-permute-start = (f32[512,2]{1,0:T(8,128)}, f32[512,2]{1,0:T(8,128)S(1)}, u32[]{:S(2)}, u32[]{:S(2)}) collective-permute-start(f32[512,2]{1,0:T(8,128)} %get-tuple-element.25), channel_id=1, source_target_pairs={{1,0},{2,1},{3,2},{4,3},{5,4},{6,5},{7,6},{8,7},{9,8},{10,9},{11,1... | collective-permute-start | bytes 12296 | tf_op jit(solution)/shard_map/ppermute | solution.py:25
  5.8 4.7 %collective-permute-start.2 = (f32[512,5]{1,0:T(8,128)}, f32[512,5]{1,0:T(8,128)S(1)}, u32[]{:S(2)}, u32[]{:S(2)}) collective-permute-start(f32[512,5]{1,0:T(8,128)} %get-tuple-element.27), channel_id=1, source_target_pairs={{0,1},{1,2},{2,3},{3,4},{4,5},{5,6},{6,7},{7,8},{8,9},{9,10},{10,1... | collective-permute-start | bytes 30728 | tf_op jit(solution)/shard_map/ppermute | solution.py:25
  10.4 4.4 %collective-permute-start.3 = (f32[5,512]{1,0:T(8,128)}, f32[5,512]{1,0:T(8,128)S(1)}, u32[]{:S(2)}, u32[]{:S(2)}) collective-permute-start(f32[5,512]{1,0:T(8,128)} %get-tuple-element.28), channel_id=1, source_target_pairs={{0,16},{16,32},{32,48},{48,64},{64,80},{80,96},{96,112},{1,17},{17... | collective-permute-start | bytes 30728 | tf_op jit(solution)/shard_map/ppermute | solution.py:25
  14.9 1.9 %collective-permute-start.1 = (f32[2,512]{1,0:T(2,128)S(1)}, f32[2,512]{1,0:T(2,128)S(1)}, u32[]{:S(2)}, u32[]{:S(2)}) collective-permute-start(f32[2,512]{1,0:T(2,128)S(1)} %copy-done.15), channel_id=1, source_target_pairs={{16,0},{32,16},{48,32},{64,48},{80,64},{96,80},{112,96},{17,1},{33... | collective-permute-start | bytes 12296 | tf_op jit(solution)/shard_map/ppermute | solution.py:25
  17.4 0.7 copy-done.4
  18.2 1.4 %scatter_custom_fusion = f32[512]{0:T(512)S(1)} fusion(s32[256]{0:T(256)S(1)} %get-tuple-element.46, f32[256]{0:T(256)S(1)} %get-tuple-element.50, f32[]{:T(128)} %constant.54.clone.1), kind=kCustom, calls=%fused_computation.56 | custom fusion | bytes 2052 | tf_op jit(solution)/shard_map/scatter | solution.py:212
  19.7 0.4 fusion.4
  20.2 0.6 copy-done
  20.9 0.6 copy-done.5
  21.5 8.7 %shard_map.130 = (f32[512,512]{1,0:T(8,128)}, f32[512,512]{1,0:T(8,128)}, f32[512,512]{1,0:T(8,128)}, f32[64,512]{1,0:T(8,128)}, f32[512,2]{1,0:T(8,128)}, /*ind...) custom-call(s32[2]{0:T(128)} %add_convert_fusion.flags_ref, f32[512,512]{1,0:T(8,128)} %d_ref.3, ...), custom_call_target="tpu_custom_call" | custom-call | tf_op jit(solution)/shard_map/pallas_call | solution.py:250
  30.2 1.0 %reshape.96 = f32[256,128,1]{1,0,2:T(8,128)S(1)} reshape(f32[64,512]{1,0:T(8,128)} %get-tuple-element.37) | data formatting | bytes 262144 | tf_op jit(solution)/shard_map/reshape;reshape | solution.py:224
  31.2 0.4 fusion.2
  31.6 1.3 %collective-permute-start.4 = (f32[512,2]{1,0:T(8,128)S(1)}, f32[512,2]{1,0:T(8,128)S(1)}, u32[]{:S(2)}, u32[]{:S(2)}) collective-permute-start(f32[512,2]{1,0:T(8,128)S(1)} %copy-done.11), channel_id=1, source_target_pairs={{1,0},{2,1},{3,2},{4,3},{5,4},{6,5},{7,6},{8,7},{9,8},{10,9},{11,1... | collective-permute-start | bytes 12296 | tf_op jit(solution)/shard_map/ppermute | solution.py:25
  32.9 4.0 %collective-permute-start.6 = (f32[512,5]{1,0:T(8,128)S(1)}, f32[512,5]{1,0:T(8,128)S(1)}, u32[]{:S(2)}, u32[]{:S(2)}) collective-permute-start(f32[512,5]{1,0:T(8,128)S(1)} %copy-done.10), channel_id=1, source_target_pairs={{0,1},{1,2},{2,3},{3,4},{4,5},{5,6},{6,7},{7,8},{8,9},{9,10},{10,1... | collective-permute-start | bytes 30728 | tf_op jit(solution)/shard_map/ppermute | solution.py:25
  36.9 4.2 %collective-permute-start.7 = (f32[5,512]{1,0:T(8,128)S(1)}, f32[5,512]{1,0:T(8,128)S(1)}, u32[]{:S(2)}, u32[]{:S(2)}) collective-permute-start(f32[5,512]{1,0:T(8,128)S(1)} %copy-done.12), channel_id=1, source_target_pairs={{0,16},{16,32},{32,48},{48,64},{64,80},{80,96},{96,112},{1,17},{17... | collective-permute-start | bytes 30728 | tf_op jit(solution)/shard_map/ppermute | solution.py:25
  41.2 1.9 %collective-permute-start.5 = (f32[2,512]{1,0:T(2,128)S(1)}, f32[2,512]{1,0:T(2,128)S(1)}, u32[]{:S(2)}, u32[]{:S(2)}) collective-permute-start(f32[2,512]{1,0:T(2,128)S(1)} %copy-done.16), channel_id=1, source_target_pairs={{16,0},{32,16},{48,32},{64,48},{80,64},{96,80},{112,96},{17,1},{33... | collective-permute-start | bytes 12296 | tf_op jit(solution)/shard_map/ppermute | solution.py:25
  43.1 2.9 %collective-permute-done.5.south_ref = f32[2,512]{1,0:T(2,128)S(1)} collective-permute-done((f32[2,512]{1,0:T(2,128)S(1)}, f32[2,512]{1,0:T(2,128)S(1)}, u32[]{:S(2)}, u32[]{:S(2)}) %collective-permute-start.5) | collective-permute-done | bytes 4128 | tf_op jit(solution)/shard_map/ppermute | solution.py:25
  46.1 1.3 %copy.20 = f32[128,9,128]{2,1,0:T(8,128)} copy(f32[128,9,128]{2,0,1:T(8,128)S(1)} %pad_maximum_fusion) | data formatting | bytes 1179648 | tf_op jit(solution)/shard_map/optimization_barrier | solution.py:247
  47.5 13.7 %all-to-all-start = ((f32[128,9,128]{2,1,0:T(8,128)}), f32[128,9,128]{2,1,0:T(8,128)S(1)}, u32[]{:S(2)}, u32[]{:S(2)}) async-start(f32[128,9,128]{2,1,0:T(8,128)} %copy.20), calls=%async_computation | async-start | bytes 2097152 | tf_op jit(solution)/shard_map/all_to_all | solution.py:259
  61.2 0.6 copy-done.13
  61.8 0.2 fusion.19
  62.1 3.4 %collective-permute-start.8 = (f32[16,128]{1,0:T(8,128)S(1)}, f32[16,128]{1,0:T(8,128)S(1)}, u32[]{:S(2)}, u32[]{:S(2)}) collective-permute-start(f32[16,128]{1,0:T(8,128)S(1)} %fusion.19), channel_id=1, source_target_pairs={{0,1},{1,2},{2,3},{3,4},{4,5},{5,6},{6,7},{7,8},{8,9},{9,10},{10,1... | collective-permute-start | bytes 24584 | tf_op jit(solution)/shard_map/ppermute | solution.py:25
  65.6 8.1 %shard_map.131 = (f32[512,512]{1,0:T(8,128)}, f32[512,512]{1,0:T(8,128)}, f32[512,512]{1,0:T(8,128)}) custom-call(s32[2]{0:T(128)} %add_convert_fusion.flags_ref, f32[512,512]{1,0:T(8,128)} %get-tuple-element.29.d_ref, f32[512,512]{1,0:T(8,128)} %get-tuple-element.30.e_ref, f32[512,512]{1,0:T(8,128)} %get-tuple-element.31.s_ref, f32[512,512]{1,0:T(8,128)} %bed_ref.3, ...), custom_call_target="tpu_custom_call" | custom-call | tf_op jit(solution)/shard_map/pallas_call | solution.py:250
  73.6 6.4 %all-to-all-done = f32[128,9,128]{2,1,0:T(8,128)S(1)} async-done(((f32[128,9,128]{2,1,0:T(8,128)}), f32[128,9,128]{2,1,0:T(8,128)S(1)}, u32[]{:S(2)}, u32[]{:S(2)}) %all-to-all-start) | async-done | bytes 589856 | tf_op jit(solution)/shard_map/all_to_all | solution.py:259
  80.3 0.2 convolution_multiply_fusion.1
  80.5 0.3 fusion.1
  80.7 0.3 fusion.17
  81.0 2.5 %collective-permute-start.9 = (f32[16,128]{1,0:T(8,128)S(1)}, f32[16,128]{1,0:T(8,128)S(1)}, u32[]{:S(2)}, u32[]{:S(2)}) collective-permute-start(f32[16,128]{1,0:T(8,128)S(1)} %fusion.17), channel_id=1, source_target_pairs={{0,1},{1,2},{2,3},{3,4},{4,5},{5,6},{6,7},{7,8},{8,9},{9,10},{10,1... | collective-permute-start | bytes 24584 | tf_op jit(solution)/shard_map/ppermute | solution.py:25
  83.7 5.6 %collective-permute-done.9 = f32[16,128]{1,0:T(8,128)S(1)} collective-permute-done((f32[16,128]{1,0:T(8,128)S(1)}, f32[16,128]{1,0:T(8,128)S(1)}, u32[]{:S(2)}, u32[]{:S(2)}) %collective-permute-start.9) | collective-permute-done | bytes 8224 | tf_op jit(solution)/shard_map/ppermute | solution.py:25
  89.3 0.9 add_add_fusion
  (62 shorter events, 1.4 us)
Async XLA Ops:
  4.4 10.4 %copy-start.15 = (f32[2,512]{1,0:T(2,128)S(1)}, f32[2,512]{1,0:T(2,128)}, u32[]{:S(2)}) copy-start(f32[2,512]{1,0:T(2,128)} %get-tuple-element.26) | copy-start | bytes 12292
  4.5 15.7 %collective-permute-start = (f32[512,2]{1,0:T(8,128)}, f32[512,2]{1,0:T(8,128)S(1)}, u32[]{:S(2)}, u32[]{:S(2)}) collective-permute-start(f32[512,2]{1,0:T(8,128)} %get-tuple-element.25), channel_id=1, source_target_pairs={{1,0},{2,1},{3,2},{4,3},{5,4},{6,5},{7,6},{8,7},{9,8},{10,9},{11,1... | collective-permute-start | bytes 12296 | tf_op jit(solution)/shard_map/ppermute | solution.py:25
  5.8 14.4 %collective-permute-start.2 = (f32[512,5]{1,0:T(8,128)}, f32[512,5]{1,0:T(8,128)S(1)}, u32[]{:S(2)}, u32[]{:S(2)}) collective-permute-start(f32[512,5]{1,0:T(8,128)} %get-tuple-element.27), channel_id=1, source_target_pairs={{0,1},{1,2},{2,3},{3,4},{4,5},{5,6},{6,7},{7,8},{8,9},{9,10},{10,1... | collective-permute-start | bytes 30728 | tf_op jit(solution)/shard_map/ppermute | solution.py:25
  10.4 9.8 %collective-permute-start.3 = (f32[5,512]{1,0:T(8,128)}, f32[5,512]{1,0:T(8,128)S(1)}, u32[]{:S(2)}, u32[]{:S(2)}) collective-permute-start(f32[5,512]{1,0:T(8,128)} %get-tuple-element.28), channel_id=1, source_target_pairs={{0,16},{16,32},{32,48},{48,64},{64,80},{80,96},{96,112},{1,17},{17... | collective-permute-start | bytes 30728 | tf_op jit(solution)/shard_map/ppermute | solution.py:25
  14.8 2.0 %copy-start.9 = (s32[256]{0:T(256)S(1)}, s32[256]{0:T(256)}, u32[]{:S(2)}) copy-start(s32[256]{0:T(256)} %param.16) | copy-start | bytes 3076
  14.9 5.3 %collective-permute-start.1 = (f32[2,512]{1,0:T(2,128)S(1)}, f32[2,512]{1,0:T(2,128)S(1)}, u32[]{:S(2)}, u32[]{:S(2)}) collective-permute-start(f32[2,512]{1,0:T(2,128)S(1)} %copy-done.15), channel_id=1, source_target_pairs={{16,0},{32,16},{48,32},{64,48},{80,64},{96,80},{112,96},{17,1},{33... | collective-permute-start | bytes 12296 | tf_op jit(solution)/shard_map/ppermute | solution.py:25
  17.2 0.9 %copy-start.4 = (f32[64,512]{1,0:T(8,128)S(1)}, f32[64,512]{1,0:T(8,128)}, u32[]{:S(2)}) copy-start(f32[64,512]{1,0:T(8,128)} %get-tuple-element.36) | copy-start | bytes 393220
  20.1 0.7 copy-start
  20.1 0.7 copy-start.7
  20.2 0.7 copy-start.1
  20.9 0.6 copy-start.5
  30.2 1.4 %copy-start.11 = (f32[512,2]{1,0:T(8,128)S(1)}, f32[512,2]{1,0:T(8,128)}, u32[]{:S(2)}) copy-start(f32[512,2]{1,0:T(8,128)} %get-tuple-element.32) | copy-start | bytes 12292
  31.1 1.8 %copy-start.10 = (f32[512,5]{1,0:T(8,128)S(1)}, f32[512,5]{1,0:T(8,128)}, u32[]{:S(2)}) copy-start(f32[512,5]{1,0:T(8,128)} %get-tuple-element.34) | copy-start | bytes 30724
  31.2 5.8 %copy-start.12 = (f32[5,512]{1,0:T(8,128)S(1)}, f32[5,512]{1,0:T(8,128)}, u32[]{:S(2)}) copy-start(f32[5,512]{1,0:T(8,128)} %get-tuple-element.35) | copy-start | bytes 30724
  31.6 9.6 %copy-start.16 = (f32[2,512]{1,0:T(2,128)S(1)}, f32[2,512]{1,0:T(2,128)}, u32[]{:S(2)}) copy-start(f32[2,512]{1,0:T(2,128)} %get-tuple-element.33) | copy-start | bytes 12292
  31.6 11.5 %collective-permute-start.4 = (f32[512,2]{1,0:T(8,128)S(1)}, f32[512,2]{1,0:T(8,128)S(1)}, u32[]{:S(2)}, u32[]{:S(2)}) collective-permute-start(f32[512,2]{1,0:T(8,128)S(1)} %copy-done.11), channel_id=1, source_target_pairs={{1,0},{2,1},{3,2},{4,3},{5,4},{6,5},{7,6},{8,7},{9,8},{10,9},{11,1... | collective-permute-start | bytes 12296 | tf_op jit(solution)/shard_map/ppermute | solution.py:25
  32.9 13.2 %collective-permute-start.6 = (f32[512,5]{1,0:T(8,128)S(1)}, f32[512,5]{1,0:T(8,128)S(1)}, u32[]{:S(2)}, u32[]{:S(2)}) collective-permute-start(f32[512,5]{1,0:T(8,128)S(1)} %copy-done.10), channel_id=1, source_target_pairs={{0,1},{1,2},{2,3},{3,4},{4,5},{5,6},{6,7},{7,8},{8,9},{9,10},{10,1... | collective-permute-start | bytes 30728 | tf_op jit(solution)/shard_map/ppermute | solution.py:25
  36.9 9.2 %collective-permute-start.7 = (f32[5,512]{1,0:T(8,128)S(1)}, f32[5,512]{1,0:T(8,128)S(1)}, u32[]{:S(2)}, u32[]{:S(2)}) collective-permute-start(f32[5,512]{1,0:T(8,128)S(1)} %copy-done.12), channel_id=1, source_target_pairs={{0,16},{16,32},{32,48},{48,64},{64,80},{80,96},{96,112},{1,17},{17... | collective-permute-start | bytes 30728 | tf_op jit(solution)/shard_map/ppermute | solution.py:25
  41.2 4.9 %collective-permute-start.5 = (f32[2,512]{1,0:T(2,128)S(1)}, f32[2,512]{1,0:T(2,128)S(1)}, u32[]{:S(2)}, u32[]{:S(2)}) collective-permute-start(f32[2,512]{1,0:T(2,128)S(1)} %copy-done.16), channel_id=1, source_target_pairs={{16,0},{32,16},{48,32},{64,48},{80,64},{96,80},{112,96},{17,1},{33... | collective-permute-start | bytes 12296 | tf_op jit(solution)/shard_map/ppermute | solution.py:25
  43.1 4.3 %copy-start.2 = (f32[512,2]{1,0:T(8,128)}, f32[512,2]{1,0:T(8,128)S(1)}, u32[]{:S(2)}) copy-start(f32[512,2]{1,0:T(8,128)S(1)} %collective-permute-done.4.east_ref) | copy-start | bytes 12292
  46.1 1.4 %copy-start.8 = (f32[2,512]{1,0:T(2,128)}, f32[2,512]{1,0:T(2,128)S(1)}, u32[]{:S(2)}) copy-start(f32[2,512]{1,0:T(2,128)S(1)} %collective-permute-done.5.south_ref) | copy-start | bytes 12292
  46.1 1.4 %copy-start.3 = (f32[512,5]{1,0:T(8,128)}, f32[512,5]{1,0:T(8,128)S(1)}, u32[]{:S(2)}) copy-start(f32[512,5]{1,0:T(8,128)S(1)} %collective-permute-done.6.west_ref) | copy-start | bytes 30724
  46.1 1.4 %copy-start.6 = (f32[5,512]{1,0:T(8,128)}, f32[5,512]{1,0:T(8,128)S(1)}, u32[]{:S(2)}) copy-start(f32[5,512]{1,0:T(8,128)S(1)} %collective-permute-done.7.north_ref) | copy-start | bytes 30724
  47.4 13.7 %copy-start.14 = (f32[16,128]{1,0:T(8,128)S(1)}, f32[16,128]{1,0:T(8,128)}, u32[]{:S(2)}) copy-start(f32[16,128]{1,0:T(8,128)} %param.18) | copy-start | bytes 24580
  47.5 32.6 %all-to-all-start = ((f32[128,9,128]{2,1,0:T(8,128)}), f32[128,9,128]{2,1,0:T(8,128)S(1)}, u32[]{:S(2)}, u32[]{:S(2)}) async-start(f32[128,9,128]{2,1,0:T(8,128)} %copy.20), calls=%async_computation | async-start | bytes 2097152 | tf_op jit(solution)/shard_map/all_to_all | solution.py:259
  61.1 0.7 copy-start.13
  61.2 0.7 copy-start.17
  62.1 18.4 %collective-permute-start.8 = (f32[16,128]{1,0:T(8,128)S(1)}, f32[16,128]{1,0:T(8,128)S(1)}, u32[]{:S(2)}, u32[]{:S(2)}) collective-permute-start(f32[16,128]{1,0:T(8,128)S(1)} %fusion.19), channel_id=1, source_target_pairs={{0,1},{1,2},{2,3},{3,4},{4,5},{5,6},{6,7},{7,8},{8,9},{9,10},{10,1... | collective-permute-start | bytes 24584 | tf_op jit(solution)/shard_map/ppermute | solution.py:25
  81.0 8.3 %collective-permute-start.9 = (f32[16,128]{1,0:T(8,128)S(1)}, f32[16,128]{1,0:T(8,128)S(1)}, u32[]{:S(2)}, u32[]{:S(2)}) collective-permute-start(f32[16,128]{1,0:T(8,128)S(1)} %fusion.17), channel_id=1, source_target_pairs={{0,1},{1,2},{2,3},{3,4},{4,5},{5,6},{6,7},{7,8},{8,9},{9,10},{10,1... | collective-permute-start | bytes 24584 | tf_op jit(solution)/shard_map/ppermute | solution.py:25

commit v6 on v5

--- a/solution.py
+++ b/solution.py
@@ -38,17 +38,31 @@
     return jnp.einsum("tb,tc->bc", onehot, values, precision=lax.Precision.HIGHEST)
 
 
+def first_col_row(x):
+    return jnp.transpose(x[:, :128])[0:1, :]
+
+
+def last_col_row(x):
+    return jnp.transpose(x[:, -128:])[127:128, :]
+
+
+def rows_as_cols(msg):
+    count, length = msg.shape
+    pad = jnp.zeros((128 - count, length), jnp.float32)
+    return jnp.transpose(jnp.concatenate([msg, pad], axis=0))
+
+
 def write_edges(level, depth, flux_e, flux_s, rough, eopen, sopen, to_west, to_north, to_east,
                 to_south):
-    to_west[:, 0:1] = level[:, 0:1]
-    to_west[:, 1:2] = depth[:, 0:1]
+    to_west[0:1, :] = first_col_row(level)
+    to_west[1:2, :] = first_col_row(depth)
     to_north[0:1, :] = level[0:1, :]
     to_north[1:2, :] = depth[0:1, :]
-    to_east[:, 0:1] = flux_e[:, -1:]
-    to_east[:, 1:2] = level[:, -1:]
-    to_east[:, 2:3] = depth[:, -1:]
-    to_east[:, 3:4] = rough[:, -1:]
-    to_east[:, 4:5] = eopen[:, -1:]
+    to_east[0:1, :] = last_col_row(flux_e)
+    to_east[1:2, :] = last_col_row(level)
+    to_east[2:3, :] = last_col_row(depth)
+    to_east[3:4, :] = last_col_row(rough)
+    to_east[4:5, :] = last_col_row(eopen)
     to_south[0:1, :] = flux_s[-1:, :]
     to_south[1:2, :] = level[-1:, :]
     to_south[2:3, :] = depth[-1:, :]
@@ -74,15 +88,15 @@
     drained = drain_rate * land * jnp.abs(depth)
     tile_out[...] = drained.reshape(ny // STRIP, STRIP, nx).sum(axis=1)
     _, _, eopen, sopen = open_masks(flags_ref, land)
-    to_west[:, 0:1] = bed_first_col[:, 0:1] + depth[:, 0:1]
-    to_west[:, 1:2] = depth[:, 0:1]
+    to_west[0:1, :] = first_col_row(bed_first_col[...] + depth[:, :128])
+    to_west[1:2, :] = first_col_row(depth)
     to_north[0:1, :] = bed_first_row[0:1, :] + depth[0:1, :]
     to_north[1:2, :] = depth[0:1, :]
-    to_east[:, 0:1] = e_ref[:, -1:]
-    to_east[:, 1:2] = bed_last_col[:, -1:] + depth[:, -1:]
-    to_east[:, 2:3] = depth[:, -1:]
-    to_east[:, 3:4] = r_col[:, -1:]
-    to_east[:, 4:5] = eopen[:, -1:]
+    to_east[0:1, :] = last_col_row(e_ref[...])
+    to_east[1:2, :] = last_col_row(bed_last_col[...] + depth[:, -128:])
+    to_east[2:3, :] = last_col_row(depth)
+    to_east[3:4, :] = last_col_row(r_col[...])
+    to_east[4:5, :] = last_col_row(eopen)
     to_south[0:1, :] = s_ref[-1:, :]
     to_south[1:2, :] = bed_last_row[-1:, :] + depth[-1:, :]
     to_south[2:3, :] = depth[-1:, :]
@@ -100,15 +114,17 @@
     rough = r_ref[...]
     level = bed + depth
     col, row, eopen, sopen = open_masks(flags_ref, land)
-    level_e = jnp.where(col == nx - 1, east_ref[:, 0:1], pltpu.roll(level, nx - 1, 1))
-    depth_e = jnp.where(col == nx - 1, east_ref[:, 1:2], pltpu.roll(depth, nx - 1, 1))
+    east = rows_as_cols(east_ref[...])
+    west = rows_as_cols(west_ref[...])
+    level_e = jnp.where(col == nx - 1, east[:, 0:1], pltpu.roll(level, nx - 1, 1))
+    depth_e = jnp.where(col == nx - 1, east[:, 1:2], pltpu.roll(depth, nx - 1, 1))
     level_s = jnp.where(row == ny - 1, south_ref[0:1, :], pltpu.roll(level, ny - 1, 0))
     depth_s = jnp.where(row == ny - 1, south_ref[1:2, :], pltpu.roll(depth, ny - 1, 0))
     flux_e = face_update(e_ref[...], level, level_e, depth, depth_e, rough, eopen)
     flux_s = face_update(s_ref[...], level, level_s, depth, depth_s, rough, sopen)
     west_edge = face_update(
-        west_ref[:, 0:1], west_ref[:, 1:2], level[:, 0:1], west_ref[:, 2:3], depth[:, 0:1],
-        west_ref[:, 3:4], west_ref[:, 4:5],
+        west[:, 0:1], west[:, 1:2], level[:, 0:1], west[:, 2:3], depth[:, 0:1],
+        west[:, 3:4], west[:, 4:5],
     )
     north_edge = face_update(
         north_ref[0:1, :], north_ref[1:2, :], level[0:1, :], north_ref[2:3, :], depth[0:1, :],
@@ -132,9 +148,9 @@
 def edge_shapes(ny, nx):
     f32 = jnp.float32
     return (
-        jax.ShapeDtypeStruct((ny, 2), f32),
+        jax.ShapeDtypeStruct((2, ny), f32),
         jax.ShapeDtypeStruct((2, nx), f32),
-        jax.ShapeDtypeStruct((ny, 5), f32),
+        jax.ShapeDtypeStruct((5, ny), f32),
         jax.ShapeDtypeStruct((5, nx), f32),
     )
 

time: 90.7 us -> 87.9 us (0.969)
  starting transfers between devices: 43.3 us -> 40.4 us
    all_to_all x1, starting transfers between devices: 13.7 us -> 12.2 us  [body(): got = lax.all_to_all(lateral_started, ('gy', 'gx'), 0, 0, tiled=True)]
    ppermute x10, starting transfers between devices: 29.6 us -> 28.2 us  [shifted(): lax.ppermute(value, axis, [(source, source + steps) for source in range(f...]
  transfers between devices with their start and end apart: 11 -> 11, of which waited for: 3 -> 4; matrix products, arithmetic and copies ran while one was open for 4% -> 4% of each run, Pallas kernels for 9% -> 9%
where the time goes in v6:
time: 87.9 us; the launch traced here: 87.3 us
  starting transfers between devices  40.4 us (46%)
  Pallas kernels  19.9 us (23%)
  waiting for transfers between devices  14.9 us (17%)
  local copies, waits for them, and re-layouts  6.99 us (8%)
  matrix products  2.87 us (3%)
  other arithmetic  1.12 us (1%)
  between operations  1.08 us (1%)
    ppermute x10, starting transfers between devices, shifted(): lax.ppermute(value, axis, [(source, source + steps) for source in range(f...  28.2 us
    pallas_call x2, Pallas kernels, body(): step_call(not last)  16.6 us
    all_to_all x1, starting transfers between devices, body(): got = lax.all_to_all(lateral_started, ('gy', 'gx'), 0, 0, tiled=True)  12.2 us
    ppermute x10, waiting for transfers between devices, shifted(): lax.ppermute(value, axis, [(source, source + steps) for source in range(f...  8.58 us
    all_to_all x1, waiting for transfers between devices, body(): got = lax.all_to_all(lateral_started, ('gy', 'gx'), 0, 0, tiled=True)  6.33 us
    pallas_call x1, Pallas kernels, body(): pl.pallas_call(edge_kernel, grid=(1,), out_shape=(tile_shape,) + edge_sha...  3.27 us
    unnamed x37, local copies, waits for them, and re-layouts  2.87 us
  transfers between devices with their start and end apart: 11, of which 4 were waited for; matrix products, arithmetic and copies ran while one was open for 4% of the time, Pallas kernels for 9%

profile of v6, /device:TPU:1, one launch (start us, length us, event | category | flops | bytes accessed | tf_op | source)
XLA Modules:
  0.0 87.3 jit_solution(7164975959840821321)
XLA Ops:
  0.6 0.6 add_convert_fusion.flags_ref
  1.2 3.3 %shard_map.129 = (f32[64,512]{1,0:T(8,128)}, f32[2,512]{1,0:T(2,128)}, f32[2,512]{1,0:T(2,128)}, f32[5,512]{1,0:T(8,128)}, f32[5,512]{1,0:T(8,128)}) custom-call(s32[2]{0:T(128)} %add_convert_fusion.flags_ref, f32[512,512]{1,0:T(8,128)} %d_ref.3, s32[512,512]{1,0:T(8,128)} %land_ref.5, f32[512,512]{1,0:T(8,128)} %bed_ref.3, f32[512,512]{1,0:T(8,128)} %bed_ref.3, ...), custom_call_target="tpu_custom_call" | custom-call | tf_op jit(solution)/shard_map/pallas_call | solution.py:197
  4.5 4.0 %collective-permute-start.2 = (f32[5,512]{1,0:T(8,128)}, f32[5,512]{1,0:T(8,128)S(1)}, u32[]{:S(2)}, u32[]{:S(2)}) collective-permute-start(f32[5,512]{1,0:T(8,128)} %get-tuple-element.27), channel_id=1, source_target_pairs={{0,1},{1,2},{2,3},{3,4},{4,5},{5,6},{6,7},{7,8},{8,9},{9,10},{10,1... | collective-permute-start | bytes 30728 | tf_op jit(solution)/shard_map/ppermute | solution.py:25
  8.6 4.0 %collective-permute-start.3 = (f32[5,512]{1,0:T(8,128)}, f32[5,512]{1,0:T(8,128)S(1)}, u32[]{:S(2)}, u32[]{:S(2)}) collective-permute-start(f32[5,512]{1,0:T(8,128)} %get-tuple-element.28), channel_id=1, source_target_pairs={{0,16},{16,32},{32,48},{48,64},{64,80},{80,96},{96,112},{1,17},{17... | collective-permute-start | bytes 30728 | tf_op jit(solution)/shard_map/ppermute | solution.py:25
  12.5 1.3 %collective-permute-start = (f32[2,512]{1,0:T(2,128)}, f32[2,512]{1,0:T(2,128)S(1)}, u32[]{:S(2)}, u32[]{:S(2)}) collective-permute-start(f32[2,512]{1,0:T(2,128)} %get-tuple-element.25), channel_id=1, source_target_pairs={{1,0},{2,1},{3,2},{4,3},{5,4},{6,5},{7,6},{8,7},{9,8},{10,9},{11,1... | collective-permute-start | bytes 12296 | tf_op jit(solution)/shard_map/ppermute | solution.py:25
  13.8 1.9 %collective-permute-start.1 = (f32[2,512]{1,0:T(2,128)S(1)}, f32[2,512]{1,0:T(2,128)S(1)}, u32[]{:S(2)}, u32[]{:S(2)}) collective-permute-start(f32[2,512]{1,0:T(2,128)S(1)} %copy-done.14), channel_id=1, source_target_pairs={{16,0},{32,16},{48,32},{64,48},{80,64},{96,80},{112,96},{17,1},{33... | collective-permute-start | bytes 12296 | tf_op jit(solution)/shard_map/ppermute | solution.py:25
  16.4 0.7 copy-done
  17.1 1.4 %scatter_custom_fusion = f32[512]{0:T(512)S(1)} fusion(s32[256]{0:T(256)S(1)} %get-tuple-element.46, f32[256]{0:T(256)S(1)} %get-tuple-element.50, f32[]{:T(128)} %constant.54.clone.1), kind=kCustom, calls=%fused_computation.56 | custom fusion | bytes 2052 | tf_op jit(solution)/shard_map/scatter | solution.py:228
  18.7 0.4 fusion.4
  19.2 0.5 copy-done.5
  19.8 0.6 copy-done.2
  20.4 8.5 %shard_map.130 = (f32[512,512]{1,0:T(8,128)}, f32[512,512]{1,0:T(8,128)}, f32[512,512]{1,0:T(8,128)}, f32[64,512]{1,0:T(8,128)}, f32[2,512]{1,0:T(2,128)}, /*ind...) custom-call(s32[2]{0:T(128)} %add_convert_fusion.flags_ref, f32[512,512]{1,0:T(8,128)} %d_ref.3, ...), custom_call_target="tpu_custom_call" | custom-call | tf_op jit(solution)/shard_map/pallas_call | solution.py:266
  28.8 0.9 %reshape.96 = f32[256,128,1]{1,0,2:T(8,128)S(1)} reshape(f32[64,512]{1,0:T(8,128)} %get-tuple-element.37) | data formatting | bytes 262144 | tf_op jit(solution)/shard_map/reshape;reshape | solution.py:240
  29.8 0.4 fusion.2
  30.2 0.3 copy-done.11
  30.5 4.0 %collective-permute-start.6 = (f32[5,512]{1,0:T(8,128)S(1)}, f32[5,512]{1,0:T(8,128)S(1)}, u32[]{:S(2)}, u32[]{:S(2)}) collective-permute-start(f32[5,512]{1,0:T(8,128)S(1)} %copy-done.11), channel_id=1, source_target_pairs={{0,1},{1,2},{2,3},{3,4},{4,5},{5,6},{6,7},{7,8},{8,9},{9,10},{10,1... | collective-permute-start | bytes 30728 | tf_op jit(solution)/shard_map/ppermute | solution.py:25
  34.5 3.9 %collective-permute-start.7 = (f32[5,512]{1,0:T(8,128)S(1)}, f32[5,512]{1,0:T(8,128)S(1)}, u32[]{:S(2)}, u32[]{:S(2)}) collective-permute-start(f32[5,512]{1,0:T(8,128)S(1)} %copy-done.10), channel_id=1, source_target_pairs={{0,16},{16,32},{32,48},{48,64},{64,80},{80,96},{96,112},{1,17},{17... | collective-permute-start | bytes 30728 | tf_op jit(solution)/shard_map/ppermute | solution.py:25
  38.4 1.3 %collective-permute-start.4 = (f32[2,512]{1,0:T(2,128)S(1)}, f32[2,512]{1,0:T(2,128)S(1)}, u32[]{:S(2)}, u32[]{:S(2)}) collective-permute-start(f32[2,512]{1,0:T(2,128)S(1)} %copy-done.16), channel_id=1, source_target_pairs={{1,0},{2,1},{3,2},{4,3},{5,4},{6,5},{7,6},{8,7},{9,8},{10,9},{11,1... | collective-permute-start | bytes 12296 | tf_op jit(solution)/shard_map/ppermute | solution.py:25
  39.7 1.9 %collective-permute-start.5 = (f32[2,512]{1,0:T(2,128)S(1)}, f32[2,512]{1,0:T(2,128)S(1)}, u32[]{:S(2)}, u32[]{:S(2)}) collective-permute-start(f32[2,512]{1,0:T(2,128)S(1)} %copy-done.15), channel_id=1, source_target_pairs={{16,0},{32,16},{48,32},{64,48},{80,64},{96,80},{112,96},{17,1},{33... | collective-permute-start | bytes 12296 | tf_op jit(solution)/shard_map/ppermute | solution.py:25
  41.7 1.1 %collective-permute-done.4.east_ref = f32[2,512]{1,0:T(2,128)S(1)} collective-permute-done((f32[2,512]{1,0:T(2,128)S(1)}, f32[2,512]{1,0:T(2,128)S(1)}, u32[]{:S(2)}, u32[]{:S(2)}) %collective-permute-start.4) | collective-permute-done | bytes 4128 | tf_op jit(solution)/shard_map/ppermute | solution.py:25
  42.8 1.9 %collective-permute-done.5.south_ref = f32[2,512]{1,0:T(2,128)S(1)} collective-permute-done((f32[2,512]{1,0:T(2,128)S(1)}, f32[2,512]{1,0:T(2,128)S(1)}, u32[]{:S(2)}, u32[]{:S(2)}) %collective-permute-start.5) | collective-permute-done | bytes 4128 | tf_op jit(solution)/shard_map/ppermute | solution.py:25
  44.7 1.3 %copy.20 = f32[128,9,128]{2,1,0:T(8,128)} copy(f32[128,9,128]{2,0,1:T(8,128)S(1)} %pad_maximum_fusion) | data formatting | bytes 1179648 | tf_op jit(solution)/shard_map/optimization_barrier | solution.py:263
  46.0 12.2 %all-to-all-start = ((f32[128,9,128]{2,1,0:T(8,128)}), f32[128,9,128]{2,1,0:T(8,128)S(1)}, u32[]{:S(2)}, u32[]{:S(2)}) async-start(f32[128,9,128]{2,1,0:T(8,128)} %copy.20), calls=%async_computation | async-start | bytes 2097152 | tf_op jit(solution)/shard_map/all_to_all | solution.py:275
  58.3 0.6 copy-done.12
  59.2 3.4 %collective-permute-start.8 = (f32[16,128]{1,0:T(8,128)S(1)}, f32[16,128]{1,0:T(8,128)S(1)}, u32[]{:S(2)}, u32[]{:S(2)}) collective-permute-start(f32[16,128]{1,0:T(8,128)S(1)} %fusion.19), channel_id=1, source_target_pairs={{0,1},{1,2},{2,3},{3,4},{4,5},{5,6},{6,7},{7,8},{8,9},{9,10},{10,1... | collective-permute-start | bytes 24584 | tf_op jit(solution)/shard_map/ppermute | solution.py:25
  62.7 8.1 %shard_map.131 = (f32[512,512]{1,0:T(8,128)}, f32[512,512]{1,0:T(8,128)}, f32[512,512]{1,0:T(8,128)}) custom-call(s32[2]{0:T(128)} %add_convert_fusion.flags_ref, f32[512,512]{1,0:T(8,128)} %get-tuple-element.29.d_ref, f32[512,512]{1,0:T(8,128)} %get-tuple-element.30.e_ref, f32[512,512]{1,0:T(8,128)} %get-tuple-element.31.s_ref, f32[512,512]{1,0:T(8,128)} %bed_ref.3, ...), custom_call_target="tpu_custom_call" | custom-call | tf_op jit(solution)/shard_map/pallas_call | solution.py:266
  70.8 6.3 %all-to-all-done = f32[128,9,128]{2,1,0:T(8,128)S(1)} async-done(((f32[128,9,128]{2,1,0:T(8,128)}), f32[128,9,128]{2,1,0:T(8,128)S(1)}, u32[]{:S(2)}, u32[]{:S(2)}) %all-to-all-start) | async-done | bytes 589856 | tf_op jit(solution)/shard_map/all_to_all | solution.py:275
  77.6 0.3 fusion.1
  77.8 0.3 fusion.17
  78.1 2.5 %collective-permute-start.9 = (f32[16,128]{1,0:T(8,128)S(1)}, f32[16,128]{1,0:T(8,128)S(1)}, u32[]{:S(2)}, u32[]{:S(2)}) collective-permute-start(f32[16,128]{1,0:T(8,128)S(1)} %fusion.17), channel_id=1, source_target_pairs={{0,1},{1,2},{2,3},{3,4},{4,5},{5,6},{6,7},{7,8},{8,9},{9,10},{10,1... | collective-permute-start | bytes 24584 | tf_op jit(solution)/shard_map/ppermute | solution.py:25
  80.8 5.6 %collective-permute-done.9 = f32[16,128]{1,0:T(8,128)S(1)} collective-permute-done((f32[16,128]{1,0:T(8,128)S(1)}, f32[16,128]{1,0:T(8,128)S(1)}, u32[]{:S(2)}, u32[]{:S(2)}) %collective-permute-start.9) | collective-permute-done | bytes 8224 | tf_op jit(solution)/shard_map/ppermute | solution.py:25
  86.4 0.9 add_add_fusion
  (62 shorter events, 1.8 us)
Async XLA Ops:
  4.5 9.3 %copy-start.14 = (f32[2,512]{1,0:T(2,128)S(1)}, f32[2,512]{1,0:T(2,128)}, u32[]{:S(2)}) copy-start(f32[2,512]{1,0:T(2,128)} %get-tuple-element.26) | copy-start | bytes 12292
  4.5 14.6 %collective-permute-start.2 = (f32[5,512]{1,0:T(8,128)}, f32[5,512]{1,0:T(8,128)S(1)}, u32[]{:S(2)}, u32[]{:S(2)}) collective-permute-start(f32[5,512]{1,0:T(8,128)} %get-tuple-element.27), channel_id=1, source_target_pairs={{0,1},{1,2},{2,3},{3,4},{4,5},{5,6},{6,7},{7,8},{8,9},{9,10},{10,1... | collective-permute-start | bytes 30728 | tf_op jit(solution)/shard_map/ppermute | solution.py:25
  8.6 10.6 %collective-permute-start.3 = (f32[5,512]{1,0:T(8,128)}, f32[5,512]{1,0:T(8,128)S(1)}, u32[]{:S(2)}, u32[]{:S(2)}) collective-permute-start(f32[5,512]{1,0:T(8,128)} %get-tuple-element.28), channel_id=1, source_target_pairs={{0,16},{16,32},{32,48},{48,64},{64,80},{80,96},{96,112},{1,17},{17... | collective-permute-start | bytes 30728 | tf_op jit(solution)/shard_map/ppermute | solution.py:25
  12.5 6.6 %collective-permute-start = (f32[2,512]{1,0:T(2,128)}, f32[2,512]{1,0:T(2,128)S(1)}, u32[]{:S(2)}, u32[]{:S(2)}) collective-permute-start(f32[2,512]{1,0:T(2,128)} %get-tuple-element.25), channel_id=1, source_target_pairs={{1,0},{2,1},{3,2},{4,3},{5,4},{6,5},{7,6},{8,7},{9,8},{10,9},{11,1... | collective-permute-start | bytes 12296 | tf_op jit(solution)/shard_map/ppermute | solution.py:25
  13.8 2.0 %copy-start.9 = (s32[256]{0:T(256)S(1)}, s32[256]{0:T(256)}, u32[]{:S(2)}) copy-start(s32[256]{0:T(256)} %param.16) | copy-start | bytes 3076
  13.8 5.3 %collective-permute-start.1 = (f32[2,512]{1,0:T(2,128)S(1)}, f32[2,512]{1,0:T(2,128)S(1)}, u32[]{:S(2)}, u32[]{:S(2)}) collective-permute-start(f32[2,512]{1,0:T(2,128)S(1)} %copy-done.14), channel_id=1, source_target_pairs={{16,0},{32,16},{48,32},{64,48},{80,64},{96,80},{112,96},{17,1},{33... | collective-permute-start | bytes 12296 | tf_op jit(solution)/shard_map/ppermute | solution.py:25
  16.2 0.9 %copy-start = (f32[64,512]{1,0:T(8,128)S(1)}, f32[64,512]{1,0:T(8,128)}, u32[]{:S(2)}) copy-start(f32[64,512]{1,0:T(8,128)} %get-tuple-element.36) | copy-start | bytes 393220
  19.1 0.6 copy-start.5
  19.1 0.6 copy-start.6
  19.2 0.6 copy-start.1
  19.8 0.6 copy-start.2
  29.8 0.7 copy-start.11
  29.8 4.7 %copy-start.10 = (f32[5,512]{1,0:T(8,128)S(1)}, f32[5,512]{1,0:T(8,128)}, u32[]{:S(2)}) copy-start(f32[5,512]{1,0:T(8,128)} %get-tuple-element.35) | copy-start | bytes 30724
  29.8 8.6 %copy-start.16 = (f32[2,512]{1,0:T(2,128)S(1)}, f32[2,512]{1,0:T(2,128)}, u32[]{:S(2)}) copy-start(f32[2,512]{1,0:T(2,128)} %get-tuple-element.32) | copy-start | bytes 12292
  30.2 9.5 %copy-start.15 = (f32[2,512]{1,0:T(2,128)S(1)}, f32[2,512]{1,0:T(2,128)}, u32[]{:S(2)}) copy-start(f32[2,512]{1,0:T(2,128)} %get-tuple-element.33) | copy-start | bytes 12292
  30.5 14.2 %collective-permute-start.6 = (f32[5,512]{1,0:T(8,128)S(1)}, f32[5,512]{1,0:T(8,128)S(1)}, u32[]{:S(2)}, u32[]{:S(2)}) collective-permute-start(f32[5,512]{1,0:T(8,128)S(1)} %copy-done.11), channel_id=1, source_target_pairs={{0,1},{1,2},{2,3},{3,4},{4,5},{5,6},{6,7},{7,8},{8,9},{9,10},{10,1... | collective-permute-start | bytes 30728 | tf_op jit(solution)/shard_map/ppermute | solution.py:25
  34.5 10.2 %collective-permute-start.7 = (f32[5,512]{1,0:T(8,128)S(1)}, f32[5,512]{1,0:T(8,128)S(1)}, u32[]{:S(2)}, u32[]{:S(2)}) collective-permute-start(f32[5,512]{1,0:T(8,128)S(1)} %copy-done.10), channel_id=1, source_target_pairs={{0,16},{16,32},{32,48},{48,64},{64,80},{80,96},{96,112},{1,17},{17... | collective-permute-start | bytes 30728 | tf_op jit(solution)/shard_map/ppermute | solution.py:25
  38.4 4.4 %collective-permute-start.4 = (f32[2,512]{1,0:T(2,128)S(1)}, f32[2,512]{1,0:T(2,128)S(1)}, u32[]{:S(2)}, u32[]{:S(2)}) collective-permute-start(f32[2,512]{1,0:T(2,128)S(1)} %copy-done.16), channel_id=1, source_target_pairs={{1,0},{2,1},{3,2},{4,3},{5,4},{6,5},{7,6},{8,7},{9,8},{10,9},{11,1... | collective-permute-start | bytes 12296 | tf_op jit(solution)/shard_map/ppermute | solution.py:25
  39.7 4.9 %collective-permute-start.5 = (f32[2,512]{1,0:T(2,128)S(1)}, f32[2,512]{1,0:T(2,128)S(1)}, u32[]{:S(2)}, u32[]{:S(2)}) collective-permute-start(f32[2,512]{1,0:T(2,128)S(1)} %copy-done.15), channel_id=1, source_target_pairs={{16,0},{32,16},{48,32},{64,48},{80,64},{96,80},{112,96},{17,1},{33... | collective-permute-start | bytes 12296 | tf_op jit(solution)/shard_map/ppermute | solution.py:25
  42.8 3.2 %copy-start.7 = (f32[2,512]{1,0:T(2,128)}, f32[2,512]{1,0:T(2,128)S(1)}, u32[]{:S(2)}) copy-start(f32[2,512]{1,0:T(2,128)S(1)} %collective-permute-done.4.east_ref) | copy-start | bytes 12292
  44.7 1.4 %copy-start.8 = (f32[2,512]{1,0:T(2,128)}, f32[2,512]{1,0:T(2,128)S(1)}, u32[]{:S(2)}) copy-start(f32[2,512]{1,0:T(2,128)S(1)} %collective-permute-done.5.south_ref) | copy-start | bytes 12292
  44.7 1.4 %copy-start.3 = (f32[5,512]{1,0:T(8,128)}, f32[5,512]{1,0:T(8,128)S(1)}, u32[]{:S(2)}) copy-start(f32[5,512]{1,0:T(8,128)S(1)} %collective-permute-done.6.west_ref) | copy-start | bytes 30724
  44.7 1.4 %copy-start.4 = (f32[5,512]{1,0:T(8,128)}, f32[5,512]{1,0:T(8,128)S(1)}, u32[]{:S(2)}) copy-start(f32[5,512]{1,0:T(8,128)S(1)} %collective-permute-done.7.north_ref) | copy-start | bytes 30724
  46.0 12.3 %copy-start.13 = (f32[16,128]{1,0:T(8,128)S(1)}, f32[16,128]{1,0:T(8,128)}, u32[]{:S(2)}) copy-start(f32[16,128]{1,0:T(8,128)} %param.18) | copy-start | bytes 24580
  46.0 31.1 %all-to-all-start = ((f32[128,9,128]{2,1,0:T(8,128)}), f32[128,9,128]{2,1,0:T(8,128)S(1)}, u32[]{:S(2)}, u32[]{:S(2)}) async-start(f32[128,9,128]{2,1,0:T(8,128)} %copy.20), calls=%async_computation | async-start | bytes 2097152 | tf_op jit(solution)/shard_map/all_to_all | solution.py:275
  58.2 0.7 copy-start.12
  58.3 0.7 copy-start.17
  59.2 18.4 %collective-permute-start.8 = (f32[16,128]{1,0:T(8,128)S(1)}, f32[16,128]{1,0:T(8,128)S(1)}, u32[]{:S(2)}, u32[]{:S(2)}) collective-permute-start(f32[16,128]{1,0:T(8,128)S(1)} %fusion.19), channel_id=1, source_target_pairs={{0,1},{1,2},{2,3},{3,4},{4,5},{5,6},{6,7},{7,8},{8,9},{9,10},{10,1... | collective-permute-start | bytes 24584 | tf_op jit(solution)/shard_map/ppermute | solution.py:25
  78.1 8.3 %collective-permute-start.9 = (f32[16,128]{1,0:T(8,128)S(1)}, f32[16,128]{1,0:T(8,128)S(1)}, u32[]{:S(2)}, u32[]{:S(2)}) collective-permute-start(f32[16,128]{1,0:T(8,128)S(1)} %fusion.17), channel_id=1, source_target_pairs={{0,1},{1,2},{2,3},{3,4},{4,5},{5,6},{6,7},{7,8},{8,9},{9,10},{10,1... | collective-permute-start | bytes 24584 | tf_op jit(solution)/shard_map/ppermute | solution.py:25

commit v7 on v6

--- a/solution.py
+++ b/solution.py
@@ -235,7 +235,7 @@
     gather_onehot = (
         lax.iota(jnp.int32, device_count * slot_cap)[:, None] == send_pos[None, :]
     ).astype(f32)
-    def start_lateral(parts):
+    def start_lateral(parts, with_ids=True):
         parts = [
             part.reshape(cell_rows // STRIP, cell_cols // reach_width, reach_width).reshape(
                 -1, reach_width
@@ -248,8 +248,9 @@
             )
             for part in parts
         ]
-        return jnp.concatenate(packed + [send_ids], axis=1)
-
+        return jnp.concatenate(packed + ([send_ids] if with_ids else []), axis=1)
+
+    got_first = lax.all_to_all(start_lateral(tile_parts), ("gy", "gx"), 0, 0, tiled=True)
     depth = water_depth
     for step in range(STEPS):
         to_west, to_north, to_east, to_south = edges
@@ -259,9 +260,11 @@
         north_in = shifted(to_south, "gy", 1)
         last = step == STEPS - 1
         if last:
-            lateral_started = start_lateral(tile_parts)
-            east_in, south_in, west_in, north_in, lateral_started = lax.optimization_barrier(
-                (east_in, south_in, west_in, north_in, lateral_started)
+            lateral_started = start_lateral(tile_parts[1:], False)
+            east_in, south_in, west_in, north_in, lateral_started, got_first = (
+                lax.optimization_barrier(
+                    (east_in, south_in, west_in, north_in, lateral_started, got_first)
+                )
             )
         outs = step_call(not last)(
             flags, depth, flux_east, flux_south, bed_level, roughness, land_mask,
@@ -272,17 +275,17 @@
             tile_parts.append(outs[3])
             edges = outs[4:]
 
-    got = lax.all_to_all(lateral_started, ("gy", "gx"), 0, 0, tiled=True)
-    got_ids = got[:, STEPS * slot_cap:].reshape(device_count, -1)[:, :slot_cap].reshape(-1)
+    got_second = lax.all_to_all(lateral_started, ("gy", "gx"), 0, 0, tiled=True)
+    got_ids = got_first[:, slot_cap:].reshape(device_count, -1)[:, :slot_cap].reshape(-1)
     targets = lax.iota(f32, block_rows)
     scatter_onehot = (targets[:, None] == got_ids[None, :]).astype(f32)
     laterals = [
         jnp.dot(
             scatter_onehot,
-            got[:, step * slot_cap:(step + 1) * slot_cap].reshape(-1, reach_width),
+            got[:, :slot_cap].reshape(-1, reach_width),
             precision=lax.Precision.HIGHEST,
         )
-        for step in range(STEPS)
+        for got in (got_first, got_second)
     ]
 
     for step in range(STEPS):

time: 87.9 us -> 85.5 us (0.973)
  waiting for transfers between devices: 14.9 us -> 2.6 us
  starting transfers between devices: 40.4 us -> 49.3 us
  local copies, waits for them, and re-layouts: 6.99 us -> 8 us
    all_to_all x1 -> x2, starting transfers between devices: 12.2 us -> 21.1 us  [the longest x1 11.4 us: body(): lax.all_to_all(start_lateral(tile_parts), ('gy', 'gx'), 0, 0, tiled=True)]
    all_to_all x1 -> x2, waiting for transfers between devices: 6.33 us -> 0.01 us  [the longest x1 0.01 us: body(): lax.all_to_all(start_lateral(tile_parts), ('gy', 'gx'), 0, 0, tiled=True)]
    ppermute x10, waiting for transfers between devices: 8.58 us -> 2.6 us  [shifted(): lax.ppermute(value, axis, [(source, source + steps) for source in range(f...]
    concatenate x0 -> x1, local copies, waits for them, and re-layouts: none -> 1 us  [start_lateral(): return jnp.concatenate(packed + ([send_ids] if with_ids else []), axis=1)]
    unnamed x37 -> x39, local copies, waits for them, and re-layouts: 2.87 us -> 3.37 us
  transfers between devices with their start and end apart: 11 -> 12, of which waited for: 4 -> 2; matrix products, arithmetic and copies ran while one was open for 4% -> 8% of each run, Pallas kernels for 9% -> 20%
where the time goes in v7:
time: 85.5 us; the launch traced here: 84.9 us
  starting transfers between devices  49.3 us (58%)
  Pallas kernels  19.9 us (23%)
  local copies, waits for them, and re-layouts  8 us (9%)
  matrix products  2.88 us (3%)
  waiting for transfers between devices  2.6 us (3%)
  between operations  1.12 us (1%)
  other arithmetic  1.11 us (1%)
    ppermute x10, starting transfers between devices, shifted(): lax.ppermute(value, axis, [(source, source + steps) for source in range(f...  28.1 us
    pallas_call x2, Pallas kernels, body(): step_call(not last)  16.6 us
    all_to_all x1, starting transfers between devices, body(): lax.all_to_all(start_lateral(tile_parts), ('gy', 'gx'), 0, 0, tiled=True)  11.4 us
    all_to_all x1, starting transfers between devices, body(): got_second = lax.all_to_all(lateral_started, ('gy', 'gx'), 0, 0, tiled=True)  9.7 us
    unnamed x39, local copies, waits for them, and re-layouts  3.37 us
    pallas_call x1, Pallas kernels, body(): pl.pallas_call(edge_kernel, grid=(1,), out_shape=(tile_shape,) + edge_sha...  3.29 us
    ppermute x10, waiting for transfers between devices, shifted(): lax.ppermute(value, axis, [(source, source + steps) for source in range(f...  2.6 us
  transfers between devices with their start and end apart: 12, of which 2 were waited for; matrix products, arithmetic and copies ran while one was open for 8% of the time, Pallas kernels for 20%

profile of v7, /device:TPU:1, one launch (start us, length us, event | category | flops | bytes accessed | tf_op | source)
XLA Modules:
  0.0 84.9 jit_solution(15687316536170713100)
XLA Ops:
  0.6 0.6 add_convert_fusion.flags_ref
  1.3 3.3 %shard_map.129 = (f32[64,512]{1,0:T(8,128)}, f32[2,512]{1,0:T(2,128)}, f32[2,512]{1,0:T(2,128)}, f32[5,512]{1,0:T(8,128)}, f32[5,512]{1,0:T(8,128)}) custom-call(s32[2]{0:T(128)} %add_convert_fusion.flags_ref, f32[512,512]{1,0:T(8,128)} %d_ref.3, s32[512,512]{1,0:T(8,128)} %land_ref.5, f32[512,512]{1,0:T(8,128)} %bed_ref.3, f32[512,512]{1,0:T(8,128)} %bed_ref.3, ...), custom_call_target="tpu_custom_call" | custom-call | tf_op jit(solution)/shard_map/pallas_call | solution.py:197
  4.6 4.0 %collective-permute-start.2 = (f32[5,512]{1,0:T(8,128)}, f32[5,512]{1,0:T(8,128)S(1)}, u32[]{:S(2)}, u32[]{:S(2)}) collective-permute-start(f32[5,512]{1,0:T(8,128)} %get-tuple-element.28), channel_id=1, source_target_pairs={{0,1},{1,2},{2,3},{3,4},{4,5},{5,6},{6,7},{7,8},{8,9},{9,10},{10,1... | collective-permute-start | bytes 30728 | tf_op jit(solution)/shard_map/ppermute | solution.py:25
  8.6 4.0 %collective-permute-start.3 = (f32[5,512]{1,0:T(8,128)}, f32[5,512]{1,0:T(8,128)S(1)}, u32[]{:S(2)}, u32[]{:S(2)}) collective-permute-start(f32[5,512]{1,0:T(8,128)} %get-tuple-element.29), channel_id=1, source_target_pairs={{0,16},{16,32},{32,48},{48,64},{64,80},{80,96},{96,112},{1,17},{17... | collective-permute-start | bytes 30728 | tf_op jit(solution)/shard_map/ppermute | solution.py:25
  12.5 1.3 %collective-permute-start = (f32[2,512]{1,0:T(2,128)}, f32[2,512]{1,0:T(2,128)S(1)}, u32[]{:S(2)}, u32[]{:S(2)}) collective-permute-start(f32[2,512]{1,0:T(2,128)} %get-tuple-element.26), channel_id=1, source_target_pairs={{1,0},{2,1},{3,2},{4,3},{5,4},{6,5},{7,6},{8,7},{9,8},{10,9},{11,1... | collective-permute-start | bytes 12296 | tf_op jit(solution)/shard_map/ppermute | solution.py:25
  13.9 1.9 %collective-permute-start.1 = (f32[2,512]{1,0:T(2,128)S(1)}, f32[2,512]{1,0:T(2,128)S(1)}, u32[]{:S(2)}, u32[]{:S(2)}) collective-permute-start(f32[2,512]{1,0:T(2,128)S(1)} %copy-done.15), channel_id=1, source_target_pairs={{16,0},{32,16},{48,32},{64,48},{80,64},{96,80},{112,96},{17,1},{33... | collective-permute-start | bytes 12296 | tf_op jit(solution)/shard_map/ppermute | solution.py:25
  16.5 0.7 copy-done.1
  17.2 1.4 %scatter_custom_fusion = f32[512]{0:T(512)S(1)} fusion(s32[256]{0:T(256)S(1)} %get-tuple-element.48, f32[256]{0:T(256)S(1)} %get-tuple-element.50, f32[]{:T(128)} %constant.54.clone.1), kind=kCustom, calls=%fused_computation.56 | custom fusion | bytes 2052 | tf_op jit(solution)/shard_map/scatter | solution.py:228
  18.7 0.4 fusion.2
  19.2 1.0 %copy.20 = f32[128,5,128]{2,1,0:T(8,128)} copy(f32[128,5,128]{2,0,1:T(8,128)S(1)} %pad_maximum_fusion) | data formatting | bytes 655360 | tf_op jit(solution)/shard_map/concatenate | solution.py:251
  20.2 11.4 %all-to-all-start = ((f32[128,5,128]{2,1,0:T(8,128)}), f32[128,5,128]{2,1,0:T(8,128)S(1)}, u32[]{:S(2)}, u32[]{:S(2)}) async-start(f32[128,5,128]{2,1,0:T(8,128)} %copy.20), calls=%async_computation | async-start | bytes 1048576 | tf_op jit(solution)/shard_map/all_to_all | solution.py:253
  31.6 0.6 copy-done.13
  32.5 3.3 %collective-permute-start.8 = (f32[16,128]{1,0:T(8,128)S(1)}, f32[16,128]{1,0:T(8,128)S(1)}, u32[]{:S(2)}, u32[]{:S(2)}) collective-permute-start(f32[16,128]{1,0:T(8,128)S(1)} %fusion.19), channel_id=1, source_target_pairs={{0,1},{1,2},{2,3},{3,4},{4,5},{5,6},{6,7},{7,8},{8,9},{9,10},{10,1... | collective-permute-start | bytes 24584 | tf_op jit(solution)/shard_map/ppermute | solution.py:25
  35.9 0.5 copy-done.6
  36.5 0.6 copy-done.3
  37.1 8.5 %shard_map.130 = (f32[512,512]{1,0:T(8,128)}, f32[512,512]{1,0:T(8,128)}, f32[512,512]{1,0:T(8,128)}, f32[64,512]{1,0:T(8,128)}, f32[2,512]{1,0:T(2,128)}, /*ind...) custom-call(s32[2]{0:T(128)} %add_convert_fusion.flags_ref, f32[512,512]{1,0:T(8,128)} %d_ref.3, ...), custom_call_target="tpu_custom_call" | custom-call | tf_op jit(solution)/shard_map/pallas_call | solution.py:269
  45.6 0.9 %reshape.95 = f32[256,128,1]{1,0,2:T(8,128)S(1)} reshape(f32[64,512]{1,0:T(8,128)} %get-tuple-element.37) | data formatting | bytes 262144 | tf_op jit(solution)/shard_map/reshape;reshape | solution.py:240
  46.5 3.1 %collective-permute-start.6 = (f32[5,512]{1,0:T(8,128)S(1)}, f32[5,512]{1,0:T(8,128)S(1)}, u32[]{:S(2)}, u32[]{:S(2)}) collective-permute-start(f32[5,512]{1,0:T(8,128)S(1)} %copy-done.12), channel_id=1, source_target_pairs={{0,1},{1,2},{2,3},{3,4},{4,5},{5,6},{6,7},{7,8},{8,9},{9,10},{10,1... | collective-permute-start | bytes 30728 | tf_op jit(solution)/shard_map/ppermute | solution.py:25
  49.6 3.9 %collective-permute-start.7 = (f32[5,512]{1,0:T(8,128)S(1)}, f32[5,512]{1,0:T(8,128)S(1)}, u32[]{:S(2)}, u32[]{:S(2)}) collective-permute-start(f32[5,512]{1,0:T(8,128)S(1)} %copy-done.11), channel_id=1, source_target_pairs={{0,16},{16,32},{32,48},{48,64},{64,80},{80,96},{96,112},{1,17},{17... | collective-permute-start | bytes 30728 | tf_op jit(solution)/shard_map/ppermute | solution.py:25
  53.6 1.3 %collective-permute-start.4 = (f32[2,512]{1,0:T(2,128)S(1)}, f32[2,512]{1,0:T(2,128)S(1)}, u32[]{:S(2)}, u32[]{:S(2)}) collective-permute-start(f32[2,512]{1,0:T(2,128)S(1)} %copy-done.17), channel_id=1, source_target_pairs={{1,0},{2,1},{3,2},{4,3},{5,4},{6,5},{7,6},{8,7},{9,8},{10,9},{11,1... | collective-permute-start | bytes 12296 | tf_op jit(solution)/shard_map/ppermute | solution.py:25
  54.9 1.9 %collective-permute-start.5 = (f32[2,512]{1,0:T(2,128)S(1)}, f32[2,512]{1,0:T(2,128)S(1)}, u32[]{:S(2)}, u32[]{:S(2)}) collective-permute-start(f32[2,512]{1,0:T(2,128)S(1)} %copy-done.16), channel_id=1, source_target_pairs={{16,0},{32,16},{48,32},{64,48},{80,64},{96,80},{112,96},{17,1},{33... | collective-permute-start | bytes 12296 | tf_op jit(solution)/shard_map/ppermute | solution.py:25
  56.8 0.4 fusion.4
  57.2 0.7 collective-permute-done.4.east_ref
  57.9 1.9 %collective-permute-done.5.south_ref = f32[2,512]{1,0:T(2,128)S(1)} collective-permute-done((f32[2,512]{1,0:T(2,128)S(1)}, f32[2,512]{1,0:T(2,128)S(1)}, u32[]{:S(2)}, u32[]{:S(2)}) %collective-permute-start.5) | collective-permute-done | bytes 4128 | tf_op jit(solution)/shard_map/ppermute | solution.py:25
  59.9 0.5 copy-done.9
  60.8 0.9 %copy.21 = f32[128,4,128]{2,1,0:T(4,128)} copy(f32[128,4,128]{2,0,1:T(8,128)S(1)} %fusion.4) | data formatting | bytes 524288 | tf_op jit(solution)/shard_map/optimization_barrier | solution.py:265
  61.7 9.7 %all-to-all-start.1 = ((f32[128,4,128]{2,1,0:T(4,128)}), f32[128,4,128]{2,1,0:T(4,128)S(1)}, u32[]{:S(2)}, u32[]{:S(2)}) async-start(f32[128,4,128]{2,1,0:T(4,128)} %copy.21), calls=%async_computation.1 | async-start | bytes 524288 | tf_op jit(solution)/shard_map/all_to_all | solution.py:278
  71.7 0.3 fusion.1
  71.9 0.3 fusion.17
  72.2 3.4 %collective-permute-start.9 = (f32[16,128]{1,0:T(8,128)S(1)}, f32[16,128]{1,0:T(8,128)S(1)}, u32[]{:S(2)}, u32[]{:S(2)}) collective-permute-start(f32[16,128]{1,0:T(8,128)S(1)} %fusion.17), channel_id=1, source_target_pairs={{0,1},{1,2},{2,3},{3,4},{4,5},{5,6},{6,7},{7,8},{8,9},{9,10},{10,1... | collective-permute-start | bytes 24584 | tf_op jit(solution)/shard_map/ppermute | solution.py:25
  75.6 8.1 %shard_map.131 = (f32[512,512]{1,0:T(8,128)}, f32[512,512]{1,0:T(8,128)}, f32[512,512]{1,0:T(8,128)}) custom-call(s32[2]{0:T(128)} %add_convert_fusion.flags_ref, f32[512,512]{1,0:T(8,128)} %get-tuple-element.30.d_ref, f32[512,512]{1,0:T(8,128)} %get-tuple-element.31.e_ref, f32[512,512]{1,0:T(8,128)} %get-tuple-element.32.s_ref, f32[512,512]{1,0:T(8,128)} %bed_ref.3, ...), custom_call_target="tpu_custom_call" | custom-call | tf_op jit(solution)/shard_map/pallas_call | solution.py:269
  84.0 0.9 %add_add_fusion = f32[16,128]{1,0:T(8,128)} fusion(f32[16,128]{1,0:T(8,128)S(1)} %convolution_multiply_fusion, f32[16,128]{1,0:T(8,128)S(1)} %fusion.1, f32[16,128]{1,0:T(8,128)S(1)} %collective-permute-done.9, s32[16]{0:T(128)S(1)} %iota_add_fusion.1, s32[16]{0:T(128)S(1)} %copy-done.18, f32[16,128]{1,0:T(8,128)S(1)} %copy-done.14), kind=kOutput, calls=%fused_computation.35 | convolution fusion | flops 418048 | bytes 41088 | tf_op jit(solution)/shard_map/tb,tc->bc/dot_general | solution.py:38
  (68 shorter events, 2.0 us)
Async XLA Ops:
  4.5 9.3 %copy-start.15 = (f32[2,512]{1,0:T(2,128)S(1)}, f32[2,512]{1,0:T(2,128)}, u32[]{:S(2)}) copy-start(f32[2,512]{1,0:T(2,128)} %get-tuple-element.27) | copy-start | bytes 12292
  4.6 31.3 %collective-permute-start.2 = (f32[5,512]{1,0:T(8,128)}, f32[5,512]{1,0:T(8,128)S(1)}, u32[]{:S(2)}, u32[]{:S(2)}) collective-permute-start(f32[5,512]{1,0:T(8,128)} %get-tuple-element.28), channel_id=1, source_target_pairs={{0,1},{1,2},{2,3},{3,4},{4,5},{5,6},{6,7},{7,8},{8,9},{9,10},{10,1... | collective-permute-start | bytes 30728 | tf_op jit(solution)/shard_map/ppermute | solution.py:25
  8.6 27.3 %collective-permute-start.3 = (f32[5,512]{1,0:T(8,128)}, f32[5,512]{1,0:T(8,128)S(1)}, u32[]{:S(2)}, u32[]{:S(2)}) collective-permute-start(f32[5,512]{1,0:T(8,128)} %get-tuple-element.29), channel_id=1, source_target_pairs={{0,16},{16,32},{32,48},{48,64},{64,80},{80,96},{96,112},{1,17},{17... | collective-permute-start | bytes 30728 | tf_op jit(solution)/shard_map/ppermute | solution.py:25
  12.5 23.3 %collective-permute-start = (f32[2,512]{1,0:T(2,128)}, f32[2,512]{1,0:T(2,128)S(1)}, u32[]{:S(2)}, u32[]{:S(2)}) collective-permute-start(f32[2,512]{1,0:T(2,128)} %get-tuple-element.26), channel_id=1, source_target_pairs={{1,0},{2,1},{3,2},{4,3},{5,4},{6,5},{7,6},{8,7},{9,8},{10,9},{11,1... | collective-permute-start | bytes 12296 | tf_op jit(solution)/shard_map/ppermute | solution.py:25
  13.9 2.0 %copy-start.10 = (s32[256]{0:T(256)S(1)}, s32[256]{0:T(256)}, u32[]{:S(2)}) copy-start(s32[256]{0:T(256)} %param.16) | copy-start | bytes 3076
  13.9 22.0 %collective-permute-start.1 = (f32[2,512]{1,0:T(2,128)S(1)}, f32[2,512]{1,0:T(2,128)S(1)}, u32[]{:S(2)}, u32[]{:S(2)}) collective-permute-start(f32[2,512]{1,0:T(2,128)S(1)} %copy-done.15), channel_id=1, source_target_pairs={{16,0},{32,16},{48,32},{64,48},{80,64},{96,80},{112,96},{17,1},{33... | collective-permute-start | bytes 12296 | tf_op jit(solution)/shard_map/ppermute | solution.py:25
  16.3 0.9 %copy-start.1 = (f32[64,512]{1,0:T(8,128)S(1)}, f32[64,512]{1,0:T(8,128)}, u32[]{:S(2)}) copy-start(f32[64,512]{1,0:T(8,128)} %get-tuple-element.38) | copy-start | bytes 393220
  20.2 11.5 %copy-start.14 = (f32[16,128]{1,0:T(8,128)S(1)}, f32[16,128]{1,0:T(8,128)}, u32[]{:S(2)}) copy-start(f32[16,128]{1,0:T(8,128)} %param.18) | copy-start | bytes 24580
  20.2 39.7 %all-to-all-start = ((f32[128,5,128]{2,1,0:T(8,128)}), f32[128,5,128]{2,1,0:T(8,128)S(1)}, u32[]{:S(2)}, u32[]{:S(2)}) async-start(f32[128,5,128]{2,1,0:T(8,128)} %copy.20), calls=%async_computation | async-start | bytes 1048576 | tf_op jit(solution)/shard_map/all_to_all | solution.py:253
  31.6 0.7 copy-start.13
  31.6 0.7 copy-start.18
  32.5 39.1 %collective-permute-start.8 = (f32[16,128]{1,0:T(8,128)S(1)}, f32[16,128]{1,0:T(8,128)S(1)}, u32[]{:S(2)}, u32[]{:S(2)}) collective-permute-start(f32[16,128]{1,0:T(8,128)S(1)} %fusion.19), channel_id=1, source_target_pairs={{0,1},{1,2},{2,3},{3,4},{4,5},{5,6},{6,7},{7,8},{8,9},{9,10},{10,1... | collective-permute-start | bytes 24584 | tf_op jit(solution)/shard_map/ppermute | solution.py:25
  35.8 0.6 copy-start.6
  35.9 0.6 copy-start.7
  35.9 0.6 copy-start.2
  36.5 0.6 copy-start.3
  45.6 1.0 %copy-start.12 = (f32[5,512]{1,0:T(8,128)S(1)}, f32[5,512]{1,0:T(8,128)}, u32[]{:S(2)}) copy-start(f32[5,512]{1,0:T(8,128)} %get-tuple-element.35) | copy-start | bytes 30724
  45.6 4.1 %copy-start.11 = (f32[5,512]{1,0:T(8,128)S(1)}, f32[5,512]{1,0:T(8,128)}, u32[]{:S(2)}) copy-start(f32[5,512]{1,0:T(8,128)} %get-tuple-element.36) | copy-start | bytes 30724
  45.6 8.0 %copy-start.17 = (f32[2,512]{1,0:T(2,128)S(1)}, f32[2,512]{1,0:T(2,128)}, u32[]{:S(2)}) copy-start(f32[2,512]{1,0:T(2,128)} %get-tuple-element.33) | copy-start | bytes 12292
  46.5 8.4 %copy-start.16 = (f32[2,512]{1,0:T(2,128)S(1)}, f32[2,512]{1,0:T(2,128)}, u32[]{:S(2)}) copy-start(f32[2,512]{1,0:T(2,128)} %get-tuple-element.34) | copy-start | bytes 12292
  46.5 13.3 %collective-permute-start.6 = (f32[5,512]{1,0:T(8,128)S(1)}, f32[5,512]{1,0:T(8,128)S(1)}, u32[]{:S(2)}, u32[]{:S(2)}) collective-permute-start(f32[5,512]{1,0:T(8,128)S(1)} %copy-done.12), channel_id=1, source_target_pairs={{0,1},{1,2},{2,3},{3,4},{4,5},{5,6},{6,7},{7,8},{8,9},{9,10},{10,1... | collective-permute-start | bytes 30728 | tf_op jit(solution)/shard_map/ppermute | solution.py:25
  49.6 10.2 %collective-permute-start.7 = (f32[5,512]{1,0:T(8,128)S(1)}, f32[5,512]{1,0:T(8,128)S(1)}, u32[]{:S(2)}, u32[]{:S(2)}) collective-permute-start(f32[5,512]{1,0:T(8,128)S(1)} %copy-done.11), channel_id=1, source_target_pairs={{0,16},{16,32},{32,48},{48,64},{64,80},{80,96},{96,112},{1,17},{17... | collective-permute-start | bytes 30728 | tf_op jit(solution)/shard_map/ppermute | solution.py:25
  53.6 4.4 %collective-permute-start.4 = (f32[2,512]{1,0:T(2,128)S(1)}, f32[2,512]{1,0:T(2,128)S(1)}, u32[]{:S(2)}, u32[]{:S(2)}) collective-permute-start(f32[2,512]{1,0:T(2,128)S(1)} %copy-done.17), channel_id=1, source_target_pairs={{1,0},{2,1},{3,2},{4,3},{5,4},{6,5},{7,6},{8,7},{9,8},{10,9},{11,1... | collective-permute-start | bytes 12296 | tf_op jit(solution)/shard_map/ppermute | solution.py:25
  54.9 4.9 %collective-permute-start.5 = (f32[2,512]{1,0:T(2,128)S(1)}, f32[2,512]{1,0:T(2,128)S(1)}, u32[]{:S(2)}, u32[]{:S(2)}) collective-permute-start(f32[2,512]{1,0:T(2,128)S(1)} %copy-done.16), channel_id=1, source_target_pairs={{16,0},{32,16},{48,32},{64,48},{80,64},{96,80},{112,96},{17,1},{33... | collective-permute-start | bytes 12296 | tf_op jit(solution)/shard_map/ppermute | solution.py:25
  57.9 1.9 %copy-start.8 = (f32[2,512]{1,0:T(2,128)}, f32[2,512]{1,0:T(2,128)S(1)}, u32[]{:S(2)}) copy-start(f32[2,512]{1,0:T(2,128)S(1)} %collective-permute-done.4.east_ref) | copy-start | bytes 12292
  59.8 0.6 copy-start.9
  59.8 0.6 copy-start.4
  59.8 0.6 copy-start.5
  59.9 0.8 copy-start
  61.7 9.7 %slice-start = ((f32[128,5,128]{2,1,0:T(8,128)}), f32[128,4,128]{2,1,0:T(4,128)S(1)}, s32[]{:S(2)}) async-start(f32[128,5,128]{2,1,0:T(8,128)} %copy-done), calls=%async_computation.2 | async-start | bytes 524288 | tf_op jit(solution)/shard_map/slice | solution.py:285
  61.7 22.1 %all-to-all-start.1 = ((f32[128,4,128]{2,1,0:T(4,128)}), f32[128,4,128]{2,1,0:T(4,128)S(1)}, u32[]{:S(2)}, u32[]{:S(2)}) async-start(f32[128,4,128]{2,1,0:T(4,128)} %copy.21), calls=%async_computation.1 | async-start | bytes 524288 | tf_op jit(solution)/shard_map/all_to_all | solution.py:278
  72.2 11.8 %collective-permute-start.9 = (f32[16,128]{1,0:T(8,128)S(1)}, f32[16,128]{1,0:T(8,128)S(1)}, u32[]{:S(2)}, u32[]{:S(2)}) collective-permute-start(f32[16,128]{1,0:T(8,128)S(1)} %fusion.17), channel_id=1, source_target_pairs={{0,1},{1,2},{2,3},{3,4},{4,5},{5,6},{6,7},{7,8},{8,9},{9,10},{10,1... | collective-permute-start | bytes 24584 | tf_op jit(solution)/shard_map/ppermute | solution.py:25

commit v8 on v7

--- a/solution.py
+++ b/solution.py
@@ -28,7 +28,8 @@
 def face_update(flux, level, level_next, depth, depth_next, roughness, active):
     face_depth = rim_depth + 0.5 * (jnp.abs(depth) + jnp.abs(depth_next))
     drive = flux - slope_gain * face_depth * (level_next - level)
-    damping = 1.0 + friction_gain * roughness * jnp.abs(flux) / jnp.power(face_depth, 7.0 / 3.0)
+    inverse_power = jnp.exp((-7.0 / 3.0) * jnp.log(face_depth))
+    damping = 1.0 + friction_gain * roughness * jnp.abs(flux) * inverse_power
     return active * drive / damping
 
 
@@ -225,16 +226,16 @@
     earlier = jnp.sum((jnp.cumsum(owner_hits, axis=0) - owner_hits) * owner_hits, axis=1)
     send_pos = tile_owner * slot_cap + earlier
     local_ids = (tile_block % block_rows).astype(f32)
-    send_ids = jnp.full((device_count * slot_cap,), -1.0, f32).at[send_pos].set(local_ids)
+    gather_onehot = (
+        lax.iota(jnp.int32, device_count * slot_cap)[:, None] == send_pos[None, :]
+    ).astype(f32)
+    send_ids = jnp.dot(gather_onehot, local_ids + 1.0, precision=lax.Precision.HIGHEST) - 1.0
     id_rows = -(-slot_cap // reach_width)
     send_ids = jnp.pad(
         send_ids.reshape(device_count, slot_cap),
         ((0, 0), (0, id_rows * reach_width - slot_cap)),
         constant_values=-1.0,
     ).reshape(device_count, id_rows, reach_width)
-    gather_onehot = (
-        lax.iota(jnp.int32, device_count * slot_cap)[:, None] == send_pos[None, :]
-    ).astype(f32)
     def start_lateral(parts, with_ids=True):
         parts = [
             part.reshape(cell_rows // STRIP, cell_cols // reach_width, reach_width).reshape(

time: 85.5 us -> 83 us (0.971)
  Pallas kernels: 19.9 us -> 18.4 us
  local copies, waits for them, and re-layouts: 8 us -> 6.61 us
    pallas_call x2, Pallas kernels: 16.6 us -> 15.2 us  [body(): step_call(not last)]
    scatter x1 -> x0, local copies, waits for them, and re-layouts: 1.4 us -> none  [body(): jnp.full((device_count * slot_cap,), -1.0, f32).at[send_pos].set(local_ids)]
  transfers between devices with their start and end apart: 12 -> 12, of which waited for: 2 -> 2; matrix products, arithmetic and copies ran while one was open for 8% -> 7% of each run, Pallas kernels for 20% -> 18%
where the time goes in v8:
time: 83 us; the launch traced here: 82.4 us
  starting transfers between devices  49.3 us (59%)
  Pallas kernels  18.4 us (22%)
  local copies, waits for them, and re-layouts  6.61 us (8%)
  matrix products  3.2 us (4%)
  waiting for transfers between devices  2.6 us (3%)
  other arithmetic  1.14 us (1%)
  between operations  1.13 us (1%)
    ppermute x10, starting transfers between devices, shifted(): lax.ppermute(value, axis, [(source, source + steps) for source in range(f...  28.1 us
    pallas_call x2, Pallas kernels, body(): step_call(not last)  15.2 us
    all_to_all x1, starting transfers between devices, body(): lax.all_to_all(start_lateral(tile_parts), ('gy', 'gx'), 0, 0, tiled=True)  11.4 us
    all_to_all x1, starting transfers between devices, body(): got_second = lax.all_to_all(lateral_started, ('gy', 'gx'), 0, 0, tiled=True)  9.7 us
    unnamed x39, local copies, waits for them, and re-layouts  3.36 us
    pallas_call x1, Pallas kernels, body(): pl.pallas_call(edge_kernel, grid=(1,), out_shape=(tile_shape,) + edge_sha...  3.29 us
    ppermute x10, waiting for transfers between devices, shifted(): lax.ppermute(value, axis, [(source, source + steps) for source in range(f...  2.6 us
  transfers between devices with their start and end apart: 12, of which 2 were waited for; matrix products, arithmetic and copies ran while one was open for 7% of the time, Pallas kernels for 18%

profile of v8, /device:TPU:1, one launch (start us, length us, event | category | flops | bytes accessed | tf_op | source)
XLA Modules:
  0.0 82.4 jit_solution(16201393393658881052)
XLA Ops:
  0.6 0.6 add_convert_fusion.flags_ref
  1.3 3.3 %shard_map.129 = (f32[64,512]{1,0:T(8,128)}, f32[2,512]{1,0:T(2,128)}, f32[2,512]{1,0:T(2,128)}, f32[5,512]{1,0:T(8,128)}, f32[5,512]{1,0:T(8,128)}) custom-call(s32[2]{0:T(128)} %add_convert_fusion.flags_ref, f32[512,512]{1,0:T(8,128)} %d_ref.3, s32[512,512]{1,0:T(8,128)} %land_ref.5, f32[512,512]{1,0:T(8,128)} %bed_ref.3, f32[512,512]{1,0:T(8,128)} %bed_ref.3, ...), custom_call_target="tpu_custom_call" | custom-call | tf_op jit(solution)/shard_map/pallas_call | solution.py:198
  4.6 4.0 %collective-permute-start.2 = (f32[5,512]{1,0:T(8,128)}, f32[5,512]{1,0:T(8,128)S(1)}, u32[]{:S(2)}, u32[]{:S(2)}) collective-permute-start(f32[5,512]{1,0:T(8,128)} %get-tuple-element.28), channel_id=1, source_target_pairs={{0,1},{1,2},{2,3},{3,4},{4,5},{5,6},{6,7},{7,8},{8,9},{9,10},{10,1... | collective-permute-start | bytes 30728 | tf_op jit(solution)/shard_map/ppermute | solution.py:25
  8.6 4.0 %collective-permute-start.3 = (f32[5,512]{1,0:T(8,128)}, f32[5,512]{1,0:T(8,128)S(1)}, u32[]{:S(2)}, u32[]{:S(2)}) collective-permute-start(f32[5,512]{1,0:T(8,128)} %get-tuple-element.29), channel_id=1, source_target_pairs={{0,16},{16,32},{32,48},{48,64},{64,80},{80,96},{96,112},{1,17},{17... | collective-permute-start | bytes 30728 | tf_op jit(solution)/shard_map/ppermute | solution.py:25
  12.6 1.3 %collective-permute-start = (f32[2,512]{1,0:T(2,128)}, f32[2,512]{1,0:T(2,128)S(1)}, u32[]{:S(2)}, u32[]{:S(2)}) collective-permute-start(f32[2,512]{1,0:T(2,128)} %get-tuple-element.26), channel_id=1, source_target_pairs={{1,0},{2,1},{3,2},{4,3},{5,4},{6,5},{7,6},{8,7},{9,8},{10,9},{11,1... | collective-permute-start | bytes 12296 | tf_op jit(solution)/shard_map/ppermute | solution.py:25
  13.9 1.9 %collective-permute-start.1 = (f32[2,512]{1,0:T(2,128)S(1)}, f32[2,512]{1,0:T(2,128)S(1)}, u32[]{:S(2)}, u32[]{:S(2)}) collective-permute-start(f32[2,512]{1,0:T(2,128)S(1)} %copy-done.15), channel_id=1, source_target_pairs={{16,0},{32,16},{48,32},{64,48},{80,64},{96,80},{112,96},{17,1},{33... | collective-permute-start | bytes 12296 | tf_op jit(solution)/shard_map/ppermute | solution.py:25
  16.5 0.7 copy-done.1
  17.2 0.3 fusion.6
  17.7 0.4 fusion.2
  18.1 1.0 %copy.20 = f32[128,5,128]{2,1,0:T(8,128)} copy(f32[128,5,128]{2,0,1:T(8,128)S(1)} %pad_maximum_fusion) | data formatting | bytes 655360 | tf_op jit(solution)/shard_map/concatenate | solution.py:252
  19.1 11.4 %all-to-all-start = ((f32[128,5,128]{2,1,0:T(8,128)}), f32[128,5,128]{2,1,0:T(8,128)S(1)}, u32[]{:S(2)}, u32[]{:S(2)}) async-start(f32[128,5,128]{2,1,0:T(8,128)} %copy.20), calls=%async_computation | async-start | bytes 1048576 | tf_op jit(solution)/shard_map/all_to_all | solution.py:254
  30.6 0.6 copy-done.13
  31.5 3.3 %collective-permute-start.8 = (f32[16,128]{1,0:T(8,128)S(1)}, f32[16,128]{1,0:T(8,128)S(1)}, u32[]{:S(2)}, u32[]{:S(2)}) collective-permute-start(f32[16,128]{1,0:T(8,128)S(1)} %fusion.21), channel_id=1, source_target_pairs={{0,1},{1,2},{2,3},{3,4},{4,5},{5,6},{6,7},{7,8},{8,9},{9,10},{10,1... | collective-permute-start | bytes 24584 | tf_op jit(solution)/shard_map/ppermute | solution.py:25
  34.9 0.5 copy-done.7
  35.4 0.6 copy-done.3
  36.1 7.7 %shard_map.130 = (f32[512,512]{1,0:T(8,128)}, f32[512,512]{1,0:T(8,128)}, f32[512,512]{1,0:T(8,128)}, f32[64,512]{1,0:T(8,128)}, f32[2,512]{1,0:T(2,128)}, /*ind...) custom-call(s32[2]{0:T(128)} %add_convert_fusion.flags_ref, f32[512,512]{1,0:T(8,128)} %d_ref.3, ...), custom_call_target="tpu_custom_call" | custom-call | tf_op jit(solution)/shard_map/pallas_call | solution.py:270
  43.8 0.9 %reshape.86 = f32[256,128,1]{1,0,2:T(8,128)S(1)} reshape(f32[64,512]{1,0:T(8,128)} %get-tuple-element.37) | data formatting | bytes 262144 | tf_op jit(solution)/shard_map/reshape;reshape | solution.py:241
  44.8 3.1 %collective-permute-start.6 = (f32[5,512]{1,0:T(8,128)S(1)}, f32[5,512]{1,0:T(8,128)S(1)}, u32[]{:S(2)}, u32[]{:S(2)}) collective-permute-start(f32[5,512]{1,0:T(8,128)S(1)} %copy-done.12), channel_id=1, source_target_pairs={{0,1},{1,2},{2,3},{3,4},{4,5},{5,6},{6,7},{7,8},{8,9},{9,10},{10,1... | collective-permute-start | bytes 30728 | tf_op jit(solution)/shard_map/ppermute | solution.py:25
  47.9 3.9 %collective-permute-start.7 = (f32[5,512]{1,0:T(8,128)S(1)}, f32[5,512]{1,0:T(8,128)S(1)}, u32[]{:S(2)}, u32[]{:S(2)}) collective-permute-start(f32[5,512]{1,0:T(8,128)S(1)} %copy-done.11), channel_id=1, source_target_pairs={{0,16},{16,32},{32,48},{48,64},{64,80},{80,96},{96,112},{1,17},{17... | collective-permute-start | bytes 30728 | tf_op jit(solution)/shard_map/ppermute | solution.py:25
  51.8 1.3 %collective-permute-start.4 = (f32[2,512]{1,0:T(2,128)S(1)}, f32[2,512]{1,0:T(2,128)S(1)}, u32[]{:S(2)}, u32[]{:S(2)}) collective-permute-start(f32[2,512]{1,0:T(2,128)S(1)} %copy-done.17), channel_id=1, source_target_pairs={{1,0},{2,1},{3,2},{4,3},{5,4},{6,5},{7,6},{8,7},{9,8},{10,9},{11,1... | collective-permute-start | bytes 12296 | tf_op jit(solution)/shard_map/ppermute | solution.py:25
  53.1 1.9 %collective-permute-start.5 = (f32[2,512]{1,0:T(2,128)S(1)}, f32[2,512]{1,0:T(2,128)S(1)}, u32[]{:S(2)}, u32[]{:S(2)}) collective-permute-start(f32[2,512]{1,0:T(2,128)S(1)} %copy-done.16), channel_id=1, source_target_pairs={{16,0},{32,16},{48,32},{64,48},{80,64},{96,80},{112,96},{17,1},{33... | collective-permute-start | bytes 12296 | tf_op jit(solution)/shard_map/ppermute | solution.py:25
  55.1 0.4 fusion.4
  55.5 0.7 collective-permute-done.4.east_ref
  56.2 1.9 %collective-permute-done.5.south_ref = f32[2,512]{1,0:T(2,128)S(1)} collective-permute-done((f32[2,512]{1,0:T(2,128)S(1)}, f32[2,512]{1,0:T(2,128)S(1)}, u32[]{:S(2)}, u32[]{:S(2)}) %collective-permute-start.5) | collective-permute-done | bytes 4128 | tf_op jit(solution)/shard_map/ppermute | solution.py:25
  58.1 0.5 copy-done.10
  59.1 0.9 %copy.21 = f32[128,4,128]{2,1,0:T(4,128)} copy(f32[128,4,128]{2,0,1:T(8,128)S(1)} %fusion.4) | data formatting | bytes 524288 | tf_op jit(solution)/shard_map/optimization_barrier | solution.py:266
  60.0 9.7 %all-to-all-start.1 = ((f32[128,4,128]{2,1,0:T(4,128)}), f32[128,4,128]{2,1,0:T(4,128)S(1)}, u32[]{:S(2)}, u32[]{:S(2)}) async-start(f32[128,4,128]{2,1,0:T(4,128)} %copy.21), calls=%async_computation.1 | async-start | bytes 524288 | tf_op jit(solution)/shard_map/all_to_all | solution.py:279
  69.9 0.3 fusion.1
  70.2 0.3 fusion.19
  70.4 3.4 %collective-permute-start.9 = (f32[16,128]{1,0:T(8,128)S(1)}, f32[16,128]{1,0:T(8,128)S(1)}, u32[]{:S(2)}, u32[]{:S(2)}) collective-permute-start(f32[16,128]{1,0:T(8,128)S(1)} %fusion.19), channel_id=1, source_target_pairs={{0,1},{1,2},{2,3},{3,4},{4,5},{5,6},{6,7},{7,8},{8,9},{9,10},{10,1... | collective-permute-start | bytes 24584 | tf_op jit(solution)/shard_map/ppermute | solution.py:25
  73.9 7.4 %shard_map.131 = (f32[512,512]{1,0:T(8,128)}, f32[512,512]{1,0:T(8,128)}, f32[512,512]{1,0:T(8,128)}) custom-call(s32[2]{0:T(128)} %add_convert_fusion.flags_ref, f32[512,512]{1,0:T(8,128)} %get-tuple-element.30.d_ref, f32[512,512]{1,0:T(8,128)} %get-tuple-element.31.e_ref, f32[512,512]{1,0:T(8,128)} %get-tuple-element.32.s_ref, f32[512,512]{1,0:T(8,128)} %bed_ref.3, ...), custom_call_target="tpu_custom_call" | custom-call | tf_op jit(solution)/shard_map/pallas_call | solution.py:270
  81.5 0.9 %add_add_fusion = f32[16,128]{1,0:T(8,128)} fusion(f32[16,128]{1,0:T(8,128)S(1)} %convolution_multiply_fusion, f32[16,128]{1,0:T(8,128)S(1)} %fusion.1, f32[16,128]{1,0:T(8,128)S(1)} %collective-permute-done.9, s32[16]{0:T(128)S(1)} %iota_add_fusion.1, s32[16]{0:T(128)S(1)} %copy-done.18, f32[16,128]{1,0:T(8,128)S(1)} %copy-done.14), kind=kOutput, calls=%fused_computation.37 | convolution fusion | flops 418048 | bytes 41088 | tf_op jit(solution)/shard_map/tb,tc->bc/dot_general | solution.py:39
  (71 shorter events, 2.0 us)
Async XLA Ops:
  4.5 9.3 %copy-start.15 = (f32[2,512]{1,0:T(2,128)S(1)}, f32[2,512]{1,0:T(2,128)}, u32[]{:S(2)}) copy-start(f32[2,512]{1,0:T(2,128)} %get-tuple-element.27) | copy-start | bytes 12292
  4.6 30.3 %collective-permute-start.2 = (f32[5,512]{1,0:T(8,128)}, f32[5,512]{1,0:T(8,128)S(1)}, u32[]{:S(2)}, u32[]{:S(2)}) collective-permute-start(f32[5,512]{1,0:T(8,128)} %get-tuple-element.28), channel_id=1, source_target_pairs={{0,1},{1,2},{2,3},{3,4},{4,5},{5,6},{6,7},{7,8},{8,9},{9,10},{10,1... | collective-permute-start | bytes 30728 | tf_op jit(solution)/shard_map/ppermute | solution.py:25
  8.6 26.3 %collective-permute-start.3 = (f32[5,512]{1,0:T(8,128)}, f32[5,512]{1,0:T(8,128)S(1)}, u32[]{:S(2)}, u32[]{:S(2)}) collective-permute-start(f32[5,512]{1,0:T(8,128)} %get-tuple-element.29), channel_id=1, source_target_pairs={{0,16},{16,32},{32,48},{48,64},{64,80},{80,96},{96,112},{1,17},{17... | collective-permute-start | bytes 30728 | tf_op jit(solution)/shard_map/ppermute | solution.py:25
  12.5 3.3 %copy-start.6 = (s32[256]{0:T(256)S(1)}, s32[256]{0:T(256)}, u32[]{:S(2)}) copy-start(s32[256]{0:T(256)} %param.16) | copy-start | bytes 3076
  12.6 22.2 %collective-permute-start = (f32[2,512]{1,0:T(2,128)}, f32[2,512]{1,0:T(2,128)S(1)}, u32[]{:S(2)}, u32[]{:S(2)}) collective-permute-start(f32[2,512]{1,0:T(2,128)} %get-tuple-element.26), channel_id=1, source_target_pairs={{1,0},{2,1},{3,2},{4,3},{5,4},{6,5},{7,6},{8,7},{9,8},{10,9},{11,1... | collective-permute-start | bytes 12296 | tf_op jit(solution)/shard_map/ppermute | solution.py:25
  13.9 21.0 %collective-permute-start.1 = (f32[2,512]{1,0:T(2,128)S(1)}, f32[2,512]{1,0:T(2,128)S(1)}, u32[]{:S(2)}, u32[]{:S(2)}) collective-permute-start(f32[2,512]{1,0:T(2,128)S(1)} %copy-done.15), channel_id=1, source_target_pairs={{16,0},{32,16},{48,32},{64,48},{80,64},{96,80},{112,96},{17,1},{33... | collective-permute-start | bytes 12296 | tf_op jit(solution)/shard_map/ppermute | solution.py:25
  16.3 0.9 %copy-start.1 = (f32[64,512]{1,0:T(8,128)S(1)}, f32[64,512]{1,0:T(8,128)}, u32[]{:S(2)}) copy-start(f32[64,512]{1,0:T(8,128)} %get-tuple-element.38) | copy-start | bytes 393220
  19.1 11.5 %copy-start.14 = (f32[16,128]{1,0:T(8,128)S(1)}, f32[16,128]{1,0:T(8,128)}, u32[]{:S(2)}) copy-start(f32[16,128]{1,0:T(8,128)} %param.18) | copy-start | bytes 24580
  19.1 39.0 %all-to-all-start = ((f32[128,5,128]{2,1,0:T(8,128)}), f32[128,5,128]{2,1,0:T(8,128)S(1)}, u32[]{:S(2)}, u32[]{:S(2)}) async-start(f32[128,5,128]{2,1,0:T(8,128)} %copy.20), calls=%async_computation | async-start | bytes 1048576 | tf_op jit(solution)/shard_map/all_to_all | solution.py:254
  30.6 0.7 copy-start.13
  30.6 0.7 copy-start.18
  31.5 38.4 %collective-permute-start.8 = (f32[16,128]{1,0:T(8,128)S(1)}, f32[16,128]{1,0:T(8,128)S(1)}, u32[]{:S(2)}, u32[]{:S(2)}) collective-permute-start(f32[16,128]{1,0:T(8,128)S(1)} %fusion.21), channel_id=1, source_target_pairs={{0,1},{1,2},{2,3},{3,4},{4,5},{5,6},{6,7},{7,8},{8,9},{9,10},{10,1... | collective-permute-start | bytes 24584 | tf_op jit(solution)/shard_map/ppermute | solution.py:25
  34.8 0.6 copy-start.7
  34.8 0.6 copy-start.8
  34.8 0.6 copy-start.2
  35.4 0.6 copy-start.3
  43.8 1.0 %copy-start.12 = (f32[5,512]{1,0:T(8,128)S(1)}, f32[5,512]{1,0:T(8,128)}, u32[]{:S(2)}) copy-start(f32[5,512]{1,0:T(8,128)} %get-tuple-element.35) | copy-start | bytes 30724
  43.8 4.1 %copy-start.11 = (f32[5,512]{1,0:T(8,128)S(1)}, f32[5,512]{1,0:T(8,128)}, u32[]{:S(2)}) copy-start(f32[5,512]{1,0:T(8,128)} %get-tuple-element.36) | copy-start | bytes 30724
  43.8 8.0 %copy-start.17 = (f32[2,512]{1,0:T(2,128)S(1)}, f32[2,512]{1,0:T(2,128)}, u32[]{:S(2)}) copy-start(f32[2,512]{1,0:T(2,128)} %get-tuple-element.33) | copy-start | bytes 12292
  44.8 8.4 %copy-start.16 = (f32[2,512]{1,0:T(2,128)S(1)}, f32[2,512]{1,0:T(2,128)}, u32[]{:S(2)}) copy-start(f32[2,512]{1,0:T(2,128)} %get-tuple-element.34) | copy-start | bytes 12292
  44.8 13.3 %collective-permute-start.6 = (f32[5,512]{1,0:T(8,128)S(1)}, f32[5,512]{1,0:T(8,128)S(1)}, u32[]{:S(2)}, u32[]{:S(2)}) collective-permute-start(f32[5,512]{1,0:T(8,128)S(1)} %copy-done.12), channel_id=1, source_target_pairs={{0,1},{1,2},{2,3},{3,4},{4,5},{5,6},{6,7},{7,8},{8,9},{9,10},{10,1... | collective-permute-start | bytes 30728 | tf_op jit(solution)/shard_map/ppermute | solution.py:25
  47.9 10.2 %collective-permute-start.7 = (f32[5,512]{1,0:T(8,128)S(1)}, f32[5,512]{1,0:T(8,128)S(1)}, u32[]{:S(2)}, u32[]{:S(2)}) collective-permute-start(f32[5,512]{1,0:T(8,128)S(1)} %copy-done.11), channel_id=1, source_target_pairs={{0,16},{16,32},{32,48},{48,64},{64,80},{80,96},{96,112},{1,17},{17... | collective-permute-start | bytes 30728 | tf_op jit(solution)/shard_map/ppermute | solution.py:25
  51.8 4.4 %collective-permute-start.4 = (f32[2,512]{1,0:T(2,128)S(1)}, f32[2,512]{1,0:T(2,128)S(1)}, u32[]{:S(2)}, u32[]{:S(2)}) collective-permute-start(f32[2,512]{1,0:T(2,128)S(1)} %copy-done.17), channel_id=1, source_target_pairs={{1,0},{2,1},{3,2},{4,3},{5,4},{6,5},{7,6},{8,7},{9,8},{10,9},{11,1... | collective-permute-start | bytes 12296 | tf_op jit(solution)/shard_map/ppermute | solution.py:25
  53.1 4.9 %collective-permute-start.5 = (f32[2,512]{1,0:T(2,128)S(1)}, f32[2,512]{1,0:T(2,128)S(1)}, u32[]{:S(2)}, u32[]{:S(2)}) collective-permute-start(f32[2,512]{1,0:T(2,128)S(1)} %copy-done.16), channel_id=1, source_target_pairs={{16,0},{32,16},{48,32},{64,48},{80,64},{96,80},{112,96},{17,1},{33... | collective-permute-start | bytes 12296 | tf_op jit(solution)/shard_map/ppermute | solution.py:25
  56.2 1.9 %copy-start.9 = (f32[2,512]{1,0:T(2,128)}, f32[2,512]{1,0:T(2,128)S(1)}, u32[]{:S(2)}) copy-start(f32[2,512]{1,0:T(2,128)S(1)} %collective-permute-done.4.east_ref) | copy-start | bytes 12292
  58.1 0.6 copy-start.10
  58.1 0.6 copy-start.4
  58.1 0.6 copy-start.5
  58.1 0.8 copy-start
  60.0 9.7 %slice-start = ((f32[128,5,128]{2,1,0:T(8,128)}), f32[128,4,128]{2,1,0:T(4,128)S(1)}, s32[]{:S(2)}) async-start(f32[128,5,128]{2,1,0:T(8,128)} %copy-done), calls=%async_computation.2 | async-start | bytes 524288 | tf_op jit(solution)/shard_map/slice | solution.py:286
  60.0 21.3 %all-to-all-start.1 = ((f32[128,4,128]{2,1,0:T(4,128)}), f32[128,4,128]{2,1,0:T(4,128)S(1)}, u32[]{:S(2)}, u32[]{:S(2)}) async-start(f32[128,4,128]{2,1,0:T(4,128)} %copy.21), calls=%async_computation.1 | async-start | bytes 524288 | tf_op jit(solution)/shard_map/all_to_all | solution.py:279
  70.4 11.1 %collective-permute-start.9 = (f32[16,128]{1,0:T(8,128)S(1)}, f32[16,128]{1,0:T(8,128)S(1)}, u32[]{:S(2)}, u32[]{:S(2)}) collective-permute-start(f32[16,128]{1,0:T(8,128)S(1)} %fusion.19), channel_id=1, source_target_pairs={{0,1},{1,2},{2,3},{3,4},{4,5},{5,6},{6,7},{7,8},{8,9},{9,10},{10,1... | collective-permute-start | bytes 24584 | tf_op jit(solution)/shard_map/ppermute | solution.py:25

commit v9 on v8

--- a/solution.py
+++ b/solution.py
@@ -9,6 +9,7 @@
 
 STRIP = 8
 STEPS = 2
+SPAN = 8
 
 
 rim_depth = 0.1
@@ -131,6 +132,7 @@
         north_ref[0:1, :], north_ref[1:2, :], level[0:1, :], north_ref[2:3, :], depth[0:1, :],
         north_ref[3:4, :], north_ref[4:5, :],
     )
+    west_edge = jnp.where(flags_ref[2] == 1, 0.0, west_edge)
     west_flux = jnp.where(col == 0, west_edge, pltpu.roll(flux_e, 1, 1))
     north_flux = jnp.where(row == 0, north_edge, pltpu.roll(flux_s, 1, 0))
     drained = drain_rate * land * jnp.abs(depth)
@@ -182,7 +184,11 @@
     tile_count = tile_block.shape[0]
     slot_cap = max(2, 2 * tile_count // device_count)
     flags = jnp.stack(
-        [(col_index == col_count - 1).astype(jnp.int32), (row_index == row_count - 1).astype(jnp.int32)]
+        [
+            (col_index == col_count - 1).astype(jnp.int32),
+            (row_index == row_count - 1).astype(jnp.int32),
+            (col_index == 0).astype(jnp.int32),
+        ]
     )
     device_index = row_index * col_count + col_index
     first_block = device_index * block_rows
@@ -251,13 +257,38 @@
         ]
         return jnp.concatenate(packed + ([send_ids] if with_ids else []), axis=1)
 
-    got_first = lax.all_to_all(start_lateral(tile_parts), ("gy", "gx"), 0, 0, tiled=True)
+    first_rows = slot_cap + id_rows
+    got_first = lax.all_to_all(
+        start_lateral(tile_parts).reshape(device_count, first_rows * reach_width),
+        ("gy", "gx"), 0, 0, tiled=True,
+    ).reshape(device_count, first_rows, reach_width)
+
+    def reach_outflow(storage):
+        ratio = reach_rate * jnp.power(storage, 2.0 / 3.0)
+        outflow = storage * ratio / (1.0 + ratio)
+        own_part = block_term(downstream, outflow, first_block, block_rows)
+        ahead_part = block_term(downstream, outflow, first_block + block_rows, SPAN)
+        return outflow, own_part, ahead_part
+
+    first_outflow = reach_outflow(storage)
+    ahead_rows = SPAN * reach_width // cell_cols
     depth = water_depth
     for step in range(STEPS):
         to_west, to_north, to_east, to_south = edges
         east_in = shifted(to_west, "gx", -1)
         south_in = shifted(to_north, "gy", -1)
-        west_in = shifted(to_east, "gx", 1)
+        if step == 0:
+            joined = shifted(
+                jnp.concatenate(
+                    [to_east, first_outflow[2].reshape(ahead_rows, cell_cols)], axis=0
+                ),
+                ("gy", "gx"),
+                1,
+            )
+            west_in = joined[: to_east.shape[0]]
+            first_ahead = joined[to_east.shape[0]:].reshape(SPAN, reach_width)
+        else:
+            west_in = shifted(to_east, "gx", 1)
         north_in = shifted(to_south, "gy", 1)
         last = step == STEPS - 1
         if last:
@@ -290,11 +321,14 @@
     ]
 
     for step in range(STEPS):
-        ratio = reach_rate * jnp.power(storage, 2.0 / 3.0)
-        outflow = storage * ratio / (1.0 + ratio)
-        own_part = block_term(downstream, outflow, first_block, block_rows)
-        ahead_part = block_term(downstream, outflow, first_block + block_rows, block_rows)
-        upstream = own_part + shifted(ahead_part, ("gy", "gx"), 1)
+        if step == 0:
+            outflow, own_part, _ = first_outflow
+            upstream = own_part + jnp.pad(first_ahead, ((0, block_rows - SPAN), (0, 0)))
+        else:
+            outflow, own_part, ahead_part = reach_outflow(storage)
+            upstream = own_part + jnp.pad(
+                shifted(ahead_part, ("gy", "gx"), 1), ((0, block_rows - SPAN), (0, 0))
+            )
         storage = storage - outflow + upstream + lateral_gain * laterals[step]
     return (depth, flux_east, flux_south, storage)
 

time: 83 us -> 80.3 us (0.967)
  starting transfers between devices: 49.3 us -> 46.1 us
  waiting for transfers between devices: 2.6 us -> 1.73 us
    ppermute x10 -> x9, starting transfers between devices: 28.1 us -> 24.8 us  [shifted(): lax.ppermute(value, axis, [(source, source + steps) for source in range(f...]
    all_to_all x0 -> x2, local copies, waits for them, and re-layouts: none -> 1.08 us  [body(): lax.all_to_all(start_lateral(tile_parts).reshape(device_count, first_rows...]
    concatenate x1 -> x0, local copies, waits for them, and re-layouts: 1 us -> none  [start_lateral(): return jnp.concatenate(packed + ([send_ids] if with_ids else []), axis=1)]
    ppermute x10 -> x9, waiting for transfers between devices: 2.6 us -> 1.64 us  [shifted(): lax.ppermute(value, axis, [(source, source + steps) for source in range(f...]
    unnamed x39 -> x41, local copies, waits for them, and re-layouts: 3.36 us -> 2.59 us
  transfers between devices with their start and end apart: 12 -> 11, of which waited for: 2 -> 2; matrix products, arithmetic and copies ran while one was open for 7% -> 7% of each run, Pallas kernels for 18% -> 19%
where the time goes in v9:
time: 80.3 us; the launch traced here: 79.6 us
  starting transfers between devices  46.1 us (57%)
  Pallas kernels  18.4 us (23%)
  local copies, waits for them, and re-layouts  6.95 us (9%)
  matrix products  3.27 us (4%)
  other arithmetic  1.94 us (2%)
  waiting for transfers between devices  1.73 us (2%)
  between operations  1.15 us (1%)
    ppermute x9, starting transfers between devices, shifted(): lax.ppermute(value, axis, [(source, source + steps) for source in range(f...  24.8 us
    pallas_call x2, Pallas kernels, body(): step_call(not last)  15.2 us
    all_to_all x1, starting transfers between devices, body(): lax.all_to_all(start_lateral(tile_parts).reshape(device_count, first_rows...  11.4 us
    all_to_all x1, starting transfers between devices, body(): got_second = lax.all_to_all(lateral_started, ('gy', 'gx'), 0, 0, tiled=True)  9.93 us
    pallas_call x1, Pallas kernels, body(): pl.pallas_call(edge_kernel, grid=(1,), out_shape=(tile_shape,) + edge_sha...  3.29 us
    unnamed x41, local copies, waits for them, and re-layouts  2.59 us
    ppermute x9, waiting for transfers between devices, shifted(): lax.ppermute(value, axis, [(source, source + steps) for source in range(f...  1.64 us
    dot_general x4, matrix products, block_term(): jnp.einsum('tb,tc->bc', onehot, values, precision=lax.Precision.HIGHEST)  1.61 us
  transfers between devices with their start and end apart: 11, of which 2 were waited for; matrix products, arithmetic and copies ran while one was open for 7% of the time, Pallas kernels for 19%

profile of v9, /device:TPU:1, one launch (start us, length us, event | category | flops | bytes accessed | tf_op | source)
XLA Modules:
  0.0 79.6 jit_solution(11981897021261132397)
XLA Ops:
  0.7 0.7 copy-done.7
  1.4 0.2 fusion.24
  1.6 0.7 add_convert_fusion.flags_ref
  2.3 3.3 %shard_map.129 = (f32[64,512]{1,0:T(8,128)}, f32[2,512]{1,0:T(2,128)}, f32[2,512]{1,0:T(2,128)}, f32[5,512]{1,0:T(8,128)}, f32[5,512]{1,0:T(8,128)}) custom-call(s32[3]{0:T(128)} %add_convert_fusion.flags_ref, f32[512,512]{1,0:T(8,128)} %d_ref.3, s32[512,512]{1,0:T(8,128)} %land_ref.5, f32[512,512]{1,0:T(8,128)} %bed_ref.3, f32[512,512]{1,0:T(8,128)} %bed_ref.3, ...), custom_call_target="tpu_custom_call" | custom-call | tf_op jit(solution)/shard_map/pallas_call | solution.py:204
  5.6 0.7 pad_maximum_fusion.1
  6.3 4.0 %collective-permute-start.2 = (f32[7,512]{1,0:T(8,128)S(1)}, f32[7,512]{1,0:T(8,128)S(1)}, u32[]{:S(2)}, u32[]{:S(2)}) collective-permute-start(f32[7,512]{1,0:T(8,128)S(1)} %pad_maximum_fusion.1), channel_id=1, source_target_pairs={{0,1},{1,2},{2,3},{3,4},{4,5},{5,6},{6,7},{7,8},{8,9},{9,10},{10,1... | collective-permute-start | bytes 43016 | tf_op jit(solution)/shard_map/ppermute | solution.py:26
  10.4 4.0 %collective-permute-start.3 = (f32[5,512]{1,0:T(8,128)S(1)}, f32[5,512]{1,0:T(8,128)S(1)}, u32[]{:S(2)}, u32[]{:S(2)}) collective-permute-start(f32[5,512]{1,0:T(8,128)S(1)} %copy-done.12), channel_id=1, source_target_pairs={{0,16},{16,32},{32,48},{48,64},{64,80},{80,96},{96,112},{1,17},{17... | collective-permute-start | bytes 30728 | tf_op jit(solution)/shard_map/ppermute | solution.py:26
  14.4 1.3 %collective-permute-start = (f32[2,512]{1,0:T(2,128)S(1)}, f32[2,512]{1,0:T(2,128)S(1)}, u32[]{:S(2)}, u32[]{:S(2)}) collective-permute-start(f32[2,512]{1,0:T(2,128)S(1)} %copy-done.16), channel_id=1, source_target_pairs={{1,0},{2,1},{3,2},{4,3},{5,4},{6,5},{7,6},{8,7},{9,8},{10,9},{11,1... | collective-permute-start | bytes 12296 | tf_op jit(solution)/shard_map/ppermute | solution.py:26
  15.7 1.9 %collective-permute-start.1 = (f32[2,512]{1,0:T(2,128)S(1)}, f32[2,512]{1,0:T(2,128)S(1)}, u32[]{:S(2)}, u32[]{:S(2)}) collective-permute-start(f32[2,512]{1,0:T(2,128)S(1)} %copy-done.15), channel_id=1, source_target_pairs={{16,0},{32,16},{48,32},{64,48},{80,64},{96,80},{112,96},{17,1},{33... | collective-permute-start | bytes 12296 | tf_op jit(solution)/shard_map/ppermute | solution.py:26
  18.3 0.7 copy-done
  19.0 0.3 fusion.4
  19.5 0.5 fusion
  20.1 0.9 %copy.32 = f32[128,1,640]{2,1,0:T(1,128)} copy(f32[128,1,640]{0,2,1:T(8,128)S(1)} %bitcast.38) | data formatting | bytes 655360 | tf_op jit(solution)/shard_map/all_to_all | solution.py:261
  21.0 11.4 %all-to-all-start = ((f32[128,1,640]{2,1,0:T(1,128)}), f32[128,1,640]{2,1,0:T(1,128)S(1)}, u32[]{:S(2)}, u32[]{:S(2)}) async-start(f32[128,1,640]{2,1,0:T(1,128)} %copy.32), calls=%async_computation | async-start | bytes 655360 | tf_op jit(solution)/shard_map/all_to_all | solution.py:261
  32.4 0.2 fusion.20
  32.8 0.5 copy-done.8
  33.3 7.8 %shard_map.130 = (f32[512,512]{1,0:T(8,128)}, f32[512,512]{1,0:T(8,128)}, f32[512,512]{1,0:T(8,128)}, f32[64,512]{1,0:T(8,128)}, f32[2,512]{1,0:T(2,128)}, /*ind...) custom-call(s32[3]{0:T(128)} %add_convert_fusion.flags_ref, f32[512,512]{1,0:T(8,128)} %d_ref.3, ...), custom_call_target="tpu_custom_call" | custom-call | tf_op jit(solution)/shard_map/pallas_call | solution.py:301
  41.1 0.9 %reshape.103 = f32[256,128,1]{1,0,2:T(8,128)S(1)} reshape(f32[64,512]{1,0:T(8,128)} %get-tuple-element.37) | data formatting | bytes 262144 | tf_op jit(solution)/shard_map/reshape;reshape | solution.py:247
  42.1 3.3 %collective-permute-start.6 = (f32[5,512]{1,0:T(8,128)S(1)}, f32[5,512]{1,0:T(8,128)S(1)}, u32[]{:S(2)}, u32[]{:S(2)}) collective-permute-start(f32[5,512]{1,0:T(8,128)S(1)} %copy-done.14), channel_id=1, source_target_pairs={{0,1},{1,2},{2,3},{3,4},{4,5},{5,6},{6,7},{7,8},{8,9},{9,10},{10,1... | collective-permute-start | bytes 30728 | tf_op jit(solution)/shard_map/ppermute | solution.py:26
  45.4 3.7 %collective-permute-start.7 = (f32[5,512]{1,0:T(8,128)S(1)}, f32[5,512]{1,0:T(8,128)S(1)}, u32[]{:S(2)}, u32[]{:S(2)}) collective-permute-start(f32[5,512]{1,0:T(8,128)S(1)} %copy-done.13), channel_id=1, source_target_pairs={{0,16},{16,32},{32,48},{48,64},{64,80},{80,96},{96,112},{1,17},{17... | collective-permute-start | bytes 30728 | tf_op jit(solution)/shard_map/ppermute | solution.py:26
  49.0 1.3 %collective-permute-start.4 = (f32[2,512]{1,0:T(2,128)S(1)}, f32[2,512]{1,0:T(2,128)S(1)}, u32[]{:S(2)}, u32[]{:S(2)}) collective-permute-start(f32[2,512]{1,0:T(2,128)S(1)} %copy-done.18), channel_id=1, source_target_pairs={{1,0},{2,1},{3,2},{4,3},{5,4},{6,5},{7,6},{8,7},{9,8},{10,9},{11,1... | collective-permute-start | bytes 12296 | tf_op jit(solution)/shard_map/ppermute | solution.py:26
  50.3 1.9 %collective-permute-start.5 = (f32[2,512]{1,0:T(2,128)S(1)}, f32[2,512]{1,0:T(2,128)S(1)}, u32[]{:S(2)}, u32[]{:S(2)}) collective-permute-start(f32[2,512]{1,0:T(2,128)S(1)} %copy-done.17), channel_id=1, source_target_pairs={{16,0},{32,16},{48,32},{64,48},{80,64},{96,80},{112,96},{17,1},{33... | collective-permute-start | bytes 12296 | tf_op jit(solution)/shard_map/ppermute | solution.py:26
  52.3 0.4 fusion.2
  52.7 0.7 slice.30
  53.6 1.6 %collective-permute-done.5.south_ref = f32[2,512]{1,0:T(2,128)S(1)} collective-permute-done((f32[2,512]{1,0:T(2,128)S(1)}, f32[2,512]{1,0:T(2,128)S(1)}, u32[]{:S(2)}, u32[]{:S(2)}) %collective-permute-start.5) | collective-permute-done | bytes 4128 | tf_op jit(solution)/shard_map/ppermute | solution.py:26
  55.3 0.5 copy-done.11
  56.3 0.9 %copy.36 = f32[128,4,128]{2,1,0:T(4,128)} copy(f32[128,4,128]{2,0,1:T(8,128)S(1)} %fusion.2) | data formatting | bytes 524288 | tf_op jit(solution)/shard_map/optimization_barrier | solution.py:297
  57.2 9.9 %all-to-all-start.1 = ((f32[128,4,128]{2,1,0:T(4,128)}), f32[128,4,128]{2,1,0:T(4,128)S(1)}, u32[]{:S(2)}, u32[]{:S(2)}) async-start(f32[128,4,128]{2,1,0:T(4,128)} %copy.36), calls=%async_computation.1 | async-start | bytes 524288 | tf_op jit(solution)/shard_map/all_to_all | solution.py:310
  67.3 0.3 fusion.22
  67.6 3.4 %collective-permute-start.8 = (f32[8,128]{1,0:T(8,128)S(1)}, f32[8,128]{1,0:T(8,128)S(1)}, u32[]{:S(2)}, u32[]{:S(2)}) collective-permute-start(f32[8,128]{1,0:T(8,128)S(1)} %fusion.22), channel_id=1, source_target_pairs={{0,1},{1,2},{2,3},{3,4},{4,5},{5,6},{6,7},{7,8},{8,9},{9,10},{10,1... | collective-permute-start | bytes 12296 | tf_op jit(solution)/shard_map/ppermute | solution.py:26
  71.0 7.4 %shard_map.131 = (f32[512,512]{1,0:T(8,128)}, f32[512,512]{1,0:T(8,128)}, f32[512,512]{1,0:T(8,128)}) custom-call(s32[3]{0:T(128)} %add_convert_fusion.flags_ref, f32[512,512]{1,0:T(8,128)} %get-tuple-element.30.d_ref, f32[512,512]{1,0:T(8,128)} %get-tuple-element.31.e_ref, f32[512,512]{1,0:T(8,128)} %get-tuple-element.32.s_ref, f32[512,512]{1,0:T(8,128)} %bed_ref.3, ...), custom_call_target="tpu_custom_call" | custom-call | tf_op jit(solution)/shard_map/pallas_call | solution.py:301
  78.7 0.9 %add_add_fusion = f32[16,128]{1,0:T(8,128)} fusion(f32[16,128]{1,0:T(8,128)S(1)} %convolution_multiply_fusion, f32[8,128]{1,0:T(8,128)S(1)} %collective-permute-done.8, f32[16,128]{1,0:T(8,128)S(1)} %add_add_fusion.1, s32[16]{0:T(128)S(1)} %iota_add_fusion, s32[16]{0:T(128)S(1)} %copy-done.19, f32[16,128]{1,0:T(8,128)S(1)} %copy-done.7), kind=kOutput, calls=%fused_computation.38 | convolution fusion | flops 418048 | bytes 36992 | tf_op jit(solution)/shard_map/tb,tc->bc/dot_general | solution.py:40
  (79 shorter events, 2.2 us)
Async XLA Ops:
  0.6 0.7 copy-start.7
  0.6 0.7 copy-start.6
  0.7 0.7 copy-start.19
  5.6 4.8 %copy-start.12 = (f32[5,512]{1,0:T(8,128)S(1)}, f32[5,512]{1,0:T(8,128)}, u32[]{:S(2)}) copy-start(f32[5,512]{1,0:T(8,128)} %get-tuple-element.29) | copy-start | bytes 30724
  5.6 8.8 %copy-start.16 = (f32[2,512]{1,0:T(2,128)S(1)}, f32[2,512]{1,0:T(2,128)}, u32[]{:S(2)}) copy-start(f32[2,512]{1,0:T(2,128)} %get-tuple-element.26) | copy-start | bytes 12292
  6.3 9.3 %copy-start.15 = (f32[2,512]{1,0:T(2,128)S(1)}, f32[2,512]{1,0:T(2,128)}, u32[]{:S(2)}) copy-start(f32[2,512]{1,0:T(2,128)} %get-tuple-element.27) | copy-start | bytes 12292
  6.3 26.4 %collective-permute-start.2 = (f32[7,512]{1,0:T(8,128)S(1)}, f32[7,512]{1,0:T(8,128)S(1)}, u32[]{:S(2)}, u32[]{:S(2)}) collective-permute-start(f32[7,512]{1,0:T(8,128)S(1)} %pad_maximum_fusion.1), channel_id=1, source_target_pairs={{0,1},{1,2},{2,3},{3,4},{4,5},{5,6},{6,7},{7,8},{8,9},{9,10},{10,1... | collective-permute-start | bytes 43016 | tf_op jit(solution)/shard_map/ppermute | solution.py:26
  10.4 22.3 %collective-permute-start.3 = (f32[5,512]{1,0:T(8,128)S(1)}, f32[5,512]{1,0:T(8,128)S(1)}, u32[]{:S(2)}, u32[]{:S(2)}) collective-permute-start(f32[5,512]{1,0:T(8,128)S(1)} %copy-done.12), channel_id=1, source_target_pairs={{0,16},{16,32},{32,48},{48,64},{64,80},{80,96},{96,112},{1,17},{17... | collective-permute-start | bytes 30728 | tf_op jit(solution)/shard_map/ppermute | solution.py:26
  14.4 3.3 %copy-start.5 = (s32[256]{0:T(256)S(1)}, s32[256]{0:T(256)}, u32[]{:S(2)}) copy-start(s32[256]{0:T(256)} %param.16) | copy-start | bytes 3076
  14.4 18.3 %collective-permute-start = (f32[2,512]{1,0:T(2,128)S(1)}, f32[2,512]{1,0:T(2,128)S(1)}, u32[]{:S(2)}, u32[]{:S(2)}) collective-permute-start(f32[2,512]{1,0:T(2,128)S(1)} %copy-done.16), channel_id=1, source_target_pairs={{1,0},{2,1},{3,2},{4,3},{5,4},{6,5},{7,6},{8,7},{9,8},{10,9},{11,1... | collective-permute-start | bytes 12296 | tf_op jit(solution)/shard_map/ppermute | solution.py:26
  15.7 17.0 %collective-permute-start.1 = (f32[2,512]{1,0:T(2,128)S(1)}, f32[2,512]{1,0:T(2,128)S(1)}, u32[]{:S(2)}, u32[]{:S(2)}) collective-permute-start(f32[2,512]{1,0:T(2,128)S(1)} %copy-done.15), channel_id=1, source_target_pairs={{16,0},{32,16},{48,32},{64,48},{80,64},{96,80},{112,96},{17,1},{33... | collective-permute-start | bytes 12296 | tf_op jit(solution)/shard_map/ppermute | solution.py:26
  18.1 0.9 %copy-start = (f32[64,512]{1,0:T(8,128)S(1)}, f32[64,512]{1,0:T(8,128)}, u32[]{:S(2)}) copy-start(f32[64,512]{1,0:T(8,128)} %get-tuple-element.38) | copy-start | bytes 393220
  21.0 32.4 %all-to-all-start = ((f32[128,1,640]{2,1,0:T(1,128)}), f32[128,1,640]{2,1,0:T(1,128)S(1)}, u32[]{:S(2)}, u32[]{:S(2)}) async-start(f32[128,1,640]{2,1,0:T(1,128)} %copy.32), calls=%async_computation | async-start | bytes 655360 | tf_op jit(solution)/shard_map/all_to_all | solution.py:261
  32.7 0.6 copy-start.8
  32.7 0.6 copy-start.9
  32.7 0.6 copy-start.2
  32.7 0.6 copy-start.1
  41.1 1.0 %copy-start.14 = (f32[5,512]{1,0:T(8,128)S(1)}, f32[5,512]{1,0:T(8,128)}, u32[]{:S(2)}) copy-start(f32[5,512]{1,0:T(8,128)} %get-tuple-element.35) | copy-start | bytes 30724
  41.1 4.2 %copy-start.13 = (f32[5,512]{1,0:T(8,128)S(1)}, f32[5,512]{1,0:T(8,128)}, u32[]{:S(2)}) copy-start(f32[5,512]{1,0:T(8,128)} %get-tuple-element.36) | copy-start | bytes 30724
  41.1 7.9 %copy-start.18 = (f32[2,512]{1,0:T(2,128)S(1)}, f32[2,512]{1,0:T(2,128)}, u32[]{:S(2)}) copy-start(f32[2,512]{1,0:T(2,128)} %get-tuple-element.33) | copy-start | bytes 12292
  42.1 8.3 %copy-start.17 = (f32[2,512]{1,0:T(2,128)S(1)}, f32[2,512]{1,0:T(2,128)}, u32[]{:S(2)}) copy-start(f32[2,512]{1,0:T(2,128)} %get-tuple-element.34) | copy-start | bytes 12292
  42.1 13.2 %collective-permute-start.6 = (f32[5,512]{1,0:T(8,128)S(1)}, f32[5,512]{1,0:T(8,128)S(1)}, u32[]{:S(2)}, u32[]{:S(2)}) collective-permute-start(f32[5,512]{1,0:T(8,128)S(1)} %copy-done.14), channel_id=1, source_target_pairs={{0,1},{1,2},{2,3},{3,4},{4,5},{5,6},{6,7},{7,8},{8,9},{9,10},{10,1... | collective-permute-start | bytes 30728 | tf_op jit(solution)/shard_map/ppermute | solution.py:26
  45.4 9.9 %collective-permute-start.7 = (f32[5,512]{1,0:T(8,128)S(1)}, f32[5,512]{1,0:T(8,128)S(1)}, u32[]{:S(2)}, u32[]{:S(2)}) collective-permute-start(f32[5,512]{1,0:T(8,128)S(1)} %copy-done.13), channel_id=1, source_target_pairs={{0,16},{16,32},{32,48},{48,64},{64,80},{80,96},{96,112},{1,17},{17... | collective-permute-start | bytes 30728 | tf_op jit(solution)/shard_map/ppermute | solution.py:26
  49.0 4.6 %collective-permute-start.4 = (f32[2,512]{1,0:T(2,128)S(1)}, f32[2,512]{1,0:T(2,128)S(1)}, u32[]{:S(2)}, u32[]{:S(2)}) collective-permute-start(f32[2,512]{1,0:T(2,128)S(1)} %copy-done.18), channel_id=1, source_target_pairs={{1,0},{2,1},{3,2},{4,3},{5,4},{6,5},{7,6},{8,7},{9,8},{10,9},{11,1... | collective-permute-start | bytes 12296 | tf_op jit(solution)/shard_map/ppermute | solution.py:26
  50.3 4.9 %collective-permute-start.5 = (f32[2,512]{1,0:T(2,128)S(1)}, f32[2,512]{1,0:T(2,128)S(1)}, u32[]{:S(2)}, u32[]{:S(2)}) collective-permute-start(f32[2,512]{1,0:T(2,128)S(1)} %copy-done.17), channel_id=1, source_target_pairs={{16,0},{32,16},{48,32},{64,48},{80,64},{96,80},{112,96},{17,1},{33... | collective-permute-start | bytes 12296 | tf_op jit(solution)/shard_map/ppermute | solution.py:26
  53.6 1.7 %copy-start.10 = (f32[2,512]{1,0:T(2,128)}, f32[2,512]{1,0:T(2,128)S(1)}, u32[]{:S(2)}) copy-start(f32[2,512]{1,0:T(2,128)S(1)} %collective-permute-done.4.east_ref) | copy-start | bytes 12292
  55.3 0.6 copy-start.11
  55.3 0.6 copy-start.3
  55.3 0.6 copy-start.4
  57.2 21.4 %all-to-all-start.1 = ((f32[128,4,128]{2,1,0:T(4,128)}), f32[128,4,128]{2,1,0:T(4,128)S(1)}, u32[]{:S(2)}, u32[]{:S(2)}) async-start(f32[128,4,128]{2,1,0:T(4,128)} %copy.36), calls=%async_computation.1 | async-start | bytes 524288 | tf_op jit(solution)/shard_map/all_to_all | solution.py:310
  67.6 11.2 %collective-permute-start.8 = (f32[8,128]{1,0:T(8,128)S(1)}, f32[8,128]{1,0:T(8,128)S(1)}, u32[]{:S(2)}, u32[]{:S(2)}) collective-permute-start(f32[8,128]{1,0:T(8,128)S(1)} %fusion.22), channel_id=1, source_target_pairs={{0,1},{1,2},{2,3},{3,4},{4,5},{5,6},{6,7},{7,8},{8,9},{9,10},{10,1... | collective-permute-start | bytes 12296 | tf_op jit(solution)/shard_map/ppermute | solution.py:26

commit v10 on v9

--- a/solution.py
+++ b/solution.py
@@ -257,11 +257,7 @@
         ]
         return jnp.concatenate(packed + ([send_ids] if with_ids else []), axis=1)
 
-    first_rows = slot_cap + id_rows
-    got_first = lax.all_to_all(
-        start_lateral(tile_parts).reshape(device_count, first_rows * reach_width),
-        ("gy", "gx"), 0, 0, tiled=True,
-    ).reshape(device_count, first_rows, reach_width)
+    message_rows = STEPS * slot_cap + id_rows
 
     def reach_outflow(storage):
         ratio = reach_rate * jnp.power(storage, 2.0 / 3.0)
@@ -292,11 +288,11 @@
         north_in = shifted(to_south, "gy", 1)
         last = step == STEPS - 1
         if last:
-            lateral_started = start_lateral(tile_parts[1:], False)
-            east_in, south_in, west_in, north_in, lateral_started, got_first = (
-                lax.optimization_barrier(
-                    (east_in, south_in, west_in, north_in, lateral_started, got_first)
-                )
+            lateral_started = start_lateral(tile_parts).reshape(
+                device_count, message_rows * reach_width
+            )
+            east_in, south_in, west_in, north_in, lateral_started = lax.optimization_barrier(
+                (east_in, south_in, west_in, north_in, lateral_started)
             )
         outs = step_call(not last)(
             flags, depth, flux_east, flux_south, bed_level, roughness, land_mask,
@@ -307,17 +303,19 @@
             tile_parts.append(outs[3])
             edges = outs[4:]
 
-    got_second = lax.all_to_all(lateral_started, ("gy", "gx"), 0, 0, tiled=True)
-    got_ids = got_first[:, slot_cap:].reshape(device_count, -1)[:, :slot_cap].reshape(-1)
+    got = lax.all_to_all(lateral_started, ("gy", "gx"), 0, 0, tiled=True).reshape(
+        device_count, message_rows, reach_width
+    )
+    got_ids = got[:, STEPS * slot_cap:].reshape(device_count, -1)[:, :slot_cap].reshape(-1)
     targets = lax.iota(f32, block_rows)
     scatter_onehot = (targets[:, None] == got_ids[None, :]).astype(f32)
     laterals = [
         jnp.dot(
             scatter_onehot,
-            got[:, :slot_cap].reshape(-1, reach_width),
+            got[:, step * slot_cap:(step + 1) * slot_cap].reshape(-1, reach_width),
             precision=lax.Precision.HIGHEST,
         )
-        for got in (got_first, got_second)
+        for step in range(STEPS)
     ]
 
     for step in range(STEPS):

time: 80.3 us -> 83.9 us (1.045)
  waiting for transfers between devices: 1.73 us -> 15.4 us
  starting transfers between devices: 46.1 us -> 36.3 us
    all_to_all x2 -> x1, starting transfers between devices: 21.4 us -> 12.2 us  [body(): lax.all_to_all(lateral_started, ('gy', 'gx'), 0, 0, tiled=True)]
    ppermute x9, waiting for transfers between devices: 1.64 us -> 9.09 us  [shifted(): lax.ppermute(value, axis, [(source, source + steps) for source in range(f...]
    all_to_all x2 -> x1, waiting for transfers between devices: 0.09 us -> 6.29 us  [body(): lax.all_to_all(lateral_started, ('gy', 'gx'), 0, 0, tiled=True)]
    optimization_barrier x1 -> x0, local copies, waits for them, and re-layouts: 0.9 us -> none  [body(): lax.optimization_barrier((east_in, south_in, west_in, north_in, lateral_s...]
  transfers between devices with their start and end apart: 11 -> 10, of which waited for: 2 -> 5; matrix products, arithmetic and copies ran while one was open for 7% -> 4% of each run, Pallas kernels for 19% -> 9%
where the time goes in v10:
time: 83.9 us; the launch traced here: 83.2 us
  starting transfers between devices  36.3 us (43%)
  Pallas kernels  18.4 us (22%)
  waiting for transfers between devices  15.4 us (18%)
  local copies, waits for them, and re-layouts  6.67 us (8%)
  matrix products  3.34 us (4%)
  other arithmetic  1.97 us (2%)
  between operations  1.11 us (1%)
    ppermute x9, starting transfers between devices, shifted(): lax.ppermute(value, axis, [(source, source + steps) for source in range(f...  24.1 us
    pallas_call x2, Pallas kernels, body(): step_call(not last)  15.2 us
    all_to_all x1, starting transfers between devices, body(): lax.all_to_all(lateral_started, ('gy', 'gx'), 0, 0, tiled=True)  12.2 us
    ppermute x9, waiting for transfers between devices, shifted(): lax.ppermute(value, axis, [(source, source + steps) for source in range(f...  9.09 us
    all_to_all x1, waiting for transfers between devices, body(): lax.all_to_all(lateral_started, ('gy', 'gx'), 0, 0, tiled=True)  6.29 us
    pallas_call x1, Pallas kernels, body(): pl.pallas_call(edge_kernel, grid=(1,), out_shape=(tile_shape,) + edge_sha...  3.29 us
    unnamed x41, local copies, waits for them, and re-layouts  2.22 us
    all_to_all x2, local copies, waits for them, and re-layouts, body(): lax.all_to_all(lateral_started, ('gy', 'gx'), 0, 0, tiled=True)  1.88 us
  transfers between devices with their start and end apart: 10, of which 5 were waited for; matrix products, arithmetic and copies ran while one was open for 4% of the time, Pallas kernels for 9%

profile of v10, /device:TPU:1, one launch (start us, length us, event | category | flops | bytes accessed | tf_op | source)
XLA Modules:
  0.0 83.2 jit_solution(1505405268705881946)
XLA Ops:
  0.7 0.7 copy-done.7
  1.6 0.7 add_convert_fusion.flags_ref
  2.3 3.3 %shard_map.129 = (f32[64,512]{1,0:T(8,128)}, f32[2,512]{1,0:T(2,128)}, f32[2,512]{1,0:T(2,128)}, f32[5,512]{1,0:T(8,128)}, f32[5,512]{1,0:T(8,128)}) custom-call(s32[3]{0:T(128)} %add_convert_fusion.flags_ref, f32[512,512]{1,0:T(8,128)} %d_ref.3, s32[512,512]{1,0:T(8,128)} %land_ref.5, f32[512,512]{1,0:T(8,128)} %bed_ref.3, f32[512,512]{1,0:T(8,128)} %bed_ref.3, ...), custom_call_target="tpu_custom_call" | custom-call | tf_op jit(solution)/shard_map/pallas_call | solution.py:204
  5.6 0.7 pad_maximum_fusion.1
  6.3 4.0 %collective-permute-start.2 = (f32[7,512]{1,0:T(8,128)S(1)}, f32[7,512]{1,0:T(8,128)S(1)}, u32[]{:S(2)}, u32[]{:S(2)}) collective-permute-start(f32[7,512]{1,0:T(8,128)S(1)} %pad_maximum_fusion.1), channel_id=1, source_target_pairs={{0,1},{1,2},{2,3},{3,4},{4,5},{5,6},{6,7},{7,8},{8,9},{9,10},{10,1... | collective-permute-start | bytes 43016 | tf_op jit(solution)/shard_map/ppermute | solution.py:26
  10.4 4.0 %collective-permute-start.3 = (f32[5,512]{1,0:T(8,128)S(1)}, f32[5,512]{1,0:T(8,128)S(1)}, u32[]{:S(2)}, u32[]{:S(2)}) collective-permute-start(f32[5,512]{1,0:T(8,128)S(1)} %copy-done.12), channel_id=1, source_target_pairs={{0,16},{16,32},{32,48},{48,64},{64,80},{80,96},{96,112},{1,17},{17... | collective-permute-start | bytes 30728 | tf_op jit(solution)/shard_map/ppermute | solution.py:26
  14.4 1.3 %collective-permute-start = (f32[2,512]{1,0:T(2,128)S(1)}, f32[2,512]{1,0:T(2,128)S(1)}, u32[]{:S(2)}, u32[]{:S(2)}) collective-permute-start(f32[2,512]{1,0:T(2,128)S(1)} %copy-done.16), channel_id=1, source_target_pairs={{1,0},{2,1},{3,2},{4,3},{5,4},{6,5},{7,6},{8,7},{9,8},{10,9},{11,1... | collective-permute-start | bytes 12296 | tf_op jit(solution)/shard_map/ppermute | solution.py:26
  15.7 1.9 %collective-permute-start.1 = (f32[2,512]{1,0:T(2,128)S(1)}, f32[2,512]{1,0:T(2,128)S(1)}, u32[]{:S(2)}, u32[]{:S(2)}) collective-permute-start(f32[2,512]{1,0:T(2,128)S(1)} %copy-done.15), channel_id=1, source_target_pairs={{16,0},{32,16},{48,32},{64,48},{80,64},{96,80},{112,96},{17,1},{33... | collective-permute-start | bytes 12296 | tf_op jit(solution)/shard_map/ppermute | solution.py:26
  18.3 0.7 copy-done
  19.0 0.3 fusion.4
  19.5 0.5 fusion.2
  20.1 0.5 collective-permute-done.1.south_ref
  20.7 0.5 copy-done.9
  21.2 7.8 %shard_map.130 = (f32[512,512]{1,0:T(8,128)}, f32[512,512]{1,0:T(8,128)}, f32[512,512]{1,0:T(8,128)}, f32[64,512]{1,0:T(8,128)}, f32[2,512]{1,0:T(2,128)}, /*ind...) custom-call(s32[3]{0:T(128)} %add_convert_fusion.flags_ref, f32[512,512]{1,0:T(8,128)} %d_ref.3, ...), custom_call_target="tpu_custom_call" | custom-call | tf_op jit(solution)/shard_map/pallas_call | solution.py:297
  29.0 0.9 %reshape_reshape.7 = f32[256,128]{1,0:T(8,128)S(1)} reshape(f32[64,512]{1,0:T(8,128)} %get-tuple-element.37) | data formatting | bytes 262144 | tf_op jit(solution)/shard_map/reshape;reshape | solution.py:247
  29.9 0.5 fusion
  30.6 4.0 %collective-permute-start.6 = (f32[5,512]{1,0:T(8,128)S(1)}, f32[5,512]{1,0:T(8,128)S(1)}, u32[]{:S(2)}, u32[]{:S(2)}) collective-permute-start(f32[5,512]{1,0:T(8,128)S(1)} %copy-done.14), channel_id=1, source_target_pairs={{0,1},{1,2},{2,3},{3,4},{4,5},{5,6},{6,7},{7,8},{8,9},{9,10},{10,1... | collective-permute-start | bytes 30728 | tf_op jit(solution)/shard_map/ppermute | solution.py:26
  34.6 3.4 %collective-permute-start.7 = (f32[5,512]{1,0:T(8,128)S(1)}, f32[5,512]{1,0:T(8,128)S(1)}, u32[]{:S(2)}, u32[]{:S(2)}) collective-permute-start(f32[5,512]{1,0:T(8,128)S(1)} %copy-done.13), channel_id=1, source_target_pairs={{0,16},{16,32},{32,48},{48,64},{64,80},{80,96},{96,112},{1,17},{17... | collective-permute-start | bytes 30728 | tf_op jit(solution)/shard_map/ppermute | solution.py:26
  38.1 1.3 %collective-permute-start.4 = (f32[2,512]{1,0:T(2,128)S(1)}, f32[2,512]{1,0:T(2,128)S(1)}, u32[]{:S(2)}, u32[]{:S(2)}) collective-permute-start(f32[2,512]{1,0:T(2,128)S(1)} %copy-done.18), channel_id=1, source_target_pairs={{1,0},{2,1},{3,2},{4,3},{5,4},{6,5},{7,6},{8,7},{9,8},{10,9},{11,1... | collective-permute-start | bytes 12296 | tf_op jit(solution)/shard_map/ppermute | solution.py:26
  39.4 1.9 %collective-permute-start.5 = (f32[2,512]{1,0:T(2,128)S(1)}, f32[2,512]{1,0:T(2,128)S(1)}, u32[]{:S(2)}, u32[]{:S(2)}) collective-permute-start(f32[2,512]{1,0:T(2,128)S(1)} %copy-done.17), channel_id=1, source_target_pairs={{16,0},{32,16},{48,32},{64,48},{80,64},{96,80},{112,96},{17,1},{33... | collective-permute-start | bytes 12296 | tf_op jit(solution)/shard_map/ppermute | solution.py:26
  41.4 1.1 %collective-permute-done.4.east_ref = f32[2,512]{1,0:T(2,128)S(1)} collective-permute-done((f32[2,512]{1,0:T(2,128)S(1)}, f32[2,512]{1,0:T(2,128)S(1)}, u32[]{:S(2)}, u32[]{:S(2)}) %collective-permute-start.4) | collective-permute-done | bytes 4128 | tf_op jit(solution)/shard_map/ppermute | solution.py:26
  42.4 1.9 %collective-permute-done.5.south_ref = f32[2,512]{1,0:T(2,128)S(1)} collective-permute-done((f32[2,512]{1,0:T(2,128)S(1)}, f32[2,512]{1,0:T(2,128)S(1)}, u32[]{:S(2)}, u32[]{:S(2)}) %collective-permute-start.5) | collective-permute-done | bytes 4128 | tf_op jit(solution)/shard_map/ppermute | solution.py:26
  44.3 1.2 %copy.44 = f32[128,1,1152]{2,1,0:T(1,128)} copy(f32[128,1,1152]{0,2,1:T(8,128)S(1)} %bitcast.39) | data formatting | bytes 1179648 | tf_op jit(solution)/shard_map/all_to_all | solution.py:306
  45.6 12.2 %all-to-all-start = ((f32[128,1,1152]{2,1,0:T(1,128)}), f32[128,1,1152]{2,1,0:T(1,128)S(1)}, u32[]{:S(2)}, u32[]{:S(2)}) async-start(f32[128,1,1152]{2,1,0:T(1,128)} %copy.44), calls=%async_computation | async-start | bytes 1179648 | tf_op jit(solution)/shard_map/all_to_all | solution.py:306
  58.1 0.7 slice.34
  58.8 7.4 %shard_map.131 = (f32[512,512]{1,0:T(8,128)}, f32[512,512]{1,0:T(8,128)}, f32[512,512]{1,0:T(8,128)}) custom-call(s32[3]{0:T(128)} %add_convert_fusion.flags_ref, f32[512,512]{1,0:T(8,128)} %get-tuple-element.29.d_ref, f32[512,512]{1,0:T(8,128)} %get-tuple-element.30.e_ref, f32[512,512]{1,0:T(8,128)} %get-tuple-element.31.s_ref, f32[512,512]{1,0:T(8,128)} %bed_ref.3, ...), custom_call_target="tpu_custom_call" | custom-call | tf_op jit(solution)/shard_map/pallas_call | solution.py:297
  66.2 6.3 %all-to-all-done = f32[128,1,1152]{2,1,0:T(1,128)S(1)} async-done(((f32[128,1,1152]{2,1,0:T(1,128)}), f32[128,1,1152]{2,1,0:T(1,128)S(1)}, u32[]{:S(2)}, u32[]{:S(2)}) %all-to-all-start) | async-done | bytes 589856 | tf_op jit(solution)/shard_map/all_to_all | solution.py:306
  72.5 0.7 copy.36
  73.8 0.3 fusion.23
  74.1 2.3 %collective-permute-start.8 = (f32[8,128]{1,0:T(8,128)S(1)}, f32[8,128]{1,0:T(8,128)S(1)}, u32[]{:S(2)}, u32[]{:S(2)}) collective-permute-start(f32[8,128]{1,0:T(8,128)S(1)} %fusion.23), channel_id=1, source_target_pairs={{0,1},{1,2},{2,3},{3,4},{4,5},{5,6},{6,7},{7,8},{8,9},{9,10},{10,1... | collective-permute-start | bytes 12296 | tf_op jit(solution)/shard_map/ppermute | solution.py:26
  76.7 5.6 %collective-permute-done.8 = f32[8,128]{1,0:T(8,128)S(1)} collective-permute-done((f32[8,128]{1,0:T(8,128)S(1)}, f32[8,128]{1,0:T(8,128)S(1)}, u32[]{:S(2)}, u32[]{:S(2)}) %collective-permute-start.8) | collective-permute-done | bytes 4128 | tf_op jit(solution)/shard_map/ppermute | solution.py:26
  82.3 0.9 %add_add_fusion = f32[16,128]{1,0:T(8,128)} fusion(f32[16,128]{1,0:T(8,128)S(1)} %convolution_multiply_fusion, f32[8,128]{1,0:T(8,128)S(1)} %collective-permute-done.8, f32[16,128]{1,0:T(8,128)S(1)} %add_add_fusion.1, s32[16]{0:T(128)S(1)} %iota_add_fusion, s32[16]{0:T(128)S(1)} %copy-done.19, f32[16,128]{1,0:T(8,128)S(1)} %copy-done.7), kind=kOutput, calls=%fused_computation.39 | convolution fusion | flops 418048 | bytes 36992 | tf_op jit(solution)/shard_map/tb,tc->bc/dot_general | solution.py:40
  (77 shorter events, 2.7 us)
Async XLA Ops:
  0.6 0.7 copy-start.7
  0.6 0.7 copy-start.6
  0.7 0.7 copy-start.19
  5.6 4.8 %copy-start.12 = (f32[5,512]{1,0:T(8,128)S(1)}, f32[5,512]{1,0:T(8,128)}, u32[]{:S(2)}) copy-start(f32[5,512]{1,0:T(8,128)} %get-tuple-element.28) | copy-start | bytes 30724
  5.6 8.8 %copy-start.16 = (f32[2,512]{1,0:T(2,128)S(1)}, f32[2,512]{1,0:T(2,128)}, u32[]{:S(2)}) copy-start(f32[2,512]{1,0:T(2,128)} %get-tuple-element.25) | copy-start | bytes 12292
  6.3 9.3 %copy-start.15 = (f32[2,512]{1,0:T(2,128)S(1)}, f32[2,512]{1,0:T(2,128)}, u32[]{:S(2)}) copy-start(f32[2,512]{1,0:T(2,128)} %get-tuple-element.26) | copy-start | bytes 12292
  6.3 14.3 %collective-permute-start.2 = (f32[7,512]{1,0:T(8,128)S(1)}, f32[7,512]{1,0:T(8,128)S(1)}, u32[]{:S(2)}, u32[]{:S(2)}) collective-permute-start(f32[7,512]{1,0:T(8,128)S(1)} %pad_maximum_fusion.1), channel_id=1, source_target_pairs={{0,1},{1,2},{2,3},{3,4},{4,5},{5,6},{6,7},{7,8},{8,9},{9,10},{10,1... | collective-permute-start | bytes 43016 | tf_op jit(solution)/shard_map/ppermute | solution.py:26
  10.4 10.2 %collective-permute-start.3 = (f32[5,512]{1,0:T(8,128)S(1)}, f32[5,512]{1,0:T(8,128)S(1)}, u32[]{:S(2)}, u32[]{:S(2)}) collective-permute-start(f32[5,512]{1,0:T(8,128)S(1)} %copy-done.12), channel_id=1, source_target_pairs={{0,16},{16,32},{32,48},{48,64},{64,80},{80,96},{96,112},{1,17},{17... | collective-permute-start | bytes 30728 | tf_op jit(solution)/shard_map/ppermute | solution.py:26
  14.4 3.3 %copy-start.5 = (s32[256]{0:T(256)S(1)}, s32[256]{0:T(256)}, u32[]{:S(2)}) copy-start(s32[256]{0:T(256)} %param.16) | copy-start | bytes 3076
  14.4 5.7 %collective-permute-start = (f32[2,512]{1,0:T(2,128)S(1)}, f32[2,512]{1,0:T(2,128)S(1)}, u32[]{:S(2)}, u32[]{:S(2)}) collective-permute-start(f32[2,512]{1,0:T(2,128)S(1)} %copy-done.16), channel_id=1, source_target_pairs={{1,0},{2,1},{3,2},{4,3},{5,4},{6,5},{7,6},{8,7},{9,8},{10,9},{11,1... | collective-permute-start | bytes 12296 | tf_op jit(solution)/shard_map/ppermute | solution.py:26
  15.7 4.9 %collective-permute-start.1 = (f32[2,512]{1,0:T(2,128)S(1)}, f32[2,512]{1,0:T(2,128)S(1)}, u32[]{:S(2)}, u32[]{:S(2)}) collective-permute-start(f32[2,512]{1,0:T(2,128)S(1)} %copy-done.15), channel_id=1, source_target_pairs={{16,0},{32,16},{48,32},{64,48},{80,64},{96,80},{112,96},{17,1},{33... | collective-permute-start | bytes 12296 | tf_op jit(solution)/shard_map/ppermute | solution.py:26
  18.1 0.9 %copy-start = (f32[64,512]{1,0:T(8,128)S(1)}, f32[64,512]{1,0:T(8,128)}, u32[]{:S(2)}) copy-start(f32[64,512]{1,0:T(8,128)} %get-tuple-element.36) | copy-start | bytes 393220
  20.1 0.6 copy-start.8
  20.6 0.6 copy-start.9
  20.6 0.6 copy-start.2
  20.6 0.6 copy-start.1
  29.9 0.7 copy-start.14
  29.9 4.7 %copy-start.13 = (f32[5,512]{1,0:T(8,128)S(1)}, f32[5,512]{1,0:T(8,128)}, u32[]{:S(2)}) copy-start(f32[5,512]{1,0:T(8,128)} %get-tuple-element.35) | copy-start | bytes 30724
  29.9 8.1 %copy-start.18 = (f32[2,512]{1,0:T(2,128)S(1)}, f32[2,512]{1,0:T(2,128)}, u32[]{:S(2)}) copy-start(f32[2,512]{1,0:T(2,128)} %get-tuple-element.32) | copy-start | bytes 12292
  30.4 9.0 %copy-start.17 = (f32[2,512]{1,0:T(2,128)S(1)}, f32[2,512]{1,0:T(2,128)}, u32[]{:S(2)}) copy-start(f32[2,512]{1,0:T(2,128)} %get-tuple-element.33) | copy-start | bytes 12292
  30.6 13.7 %collective-permute-start.6 = (f32[5,512]{1,0:T(8,128)S(1)}, f32[5,512]{1,0:T(8,128)S(1)}, u32[]{:S(2)}, u32[]{:S(2)}) collective-permute-start(f32[5,512]{1,0:T(8,128)S(1)} %copy-done.14), channel_id=1, source_target_pairs={{0,1},{1,2},{2,3},{3,4},{4,5},{5,6},{6,7},{7,8},{8,9},{9,10},{10,1... | collective-permute-start | bytes 30728 | tf_op jit(solution)/shard_map/ppermute | solution.py:26
  34.6 9.7 %collective-permute-start.7 = (f32[5,512]{1,0:T(8,128)S(1)}, f32[5,512]{1,0:T(8,128)S(1)}, u32[]{:S(2)}, u32[]{:S(2)}) collective-permute-start(f32[5,512]{1,0:T(8,128)S(1)} %copy-done.13), channel_id=1, source_target_pairs={{0,16},{16,32},{32,48},{48,64},{64,80},{80,96},{96,112},{1,17},{17... | collective-permute-start | bytes 30728 | tf_op jit(solution)/shard_map/ppermute | solution.py:26
  38.1 4.4 %collective-permute-start.4 = (f32[2,512]{1,0:T(2,128)S(1)}, f32[2,512]{1,0:T(2,128)S(1)}, u32[]{:S(2)}, u32[]{:S(2)}) collective-permute-start(f32[2,512]{1,0:T(2,128)S(1)} %copy-done.18), channel_id=1, source_target_pairs={{1,0},{2,1},{3,2},{4,3},{5,4},{6,5},{7,6},{8,7},{9,8},{10,9},{11,1... | collective-permute-start | bytes 12296 | tf_op jit(solution)/shard_map/ppermute | solution.py:26
  39.4 4.9 %collective-permute-start.5 = (f32[2,512]{1,0:T(2,128)S(1)}, f32[2,512]{1,0:T(2,128)S(1)}, u32[]{:S(2)}, u32[]{:S(2)}) collective-permute-start(f32[2,512]{1,0:T(2,128)S(1)} %copy-done.17), channel_id=1, source_target_pairs={{16,0},{32,16},{48,32},{64,48},{80,64},{96,80},{112,96},{17,1},{33... | collective-permute-start | bytes 12296 | tf_op jit(solution)/shard_map/ppermute | solution.py:26
  42.4 3.1 %copy-start.10 = (f32[2,512]{1,0:T(2,128)}, f32[2,512]{1,0:T(2,128)S(1)}, u32[]{:S(2)}) copy-start(f32[2,512]{1,0:T(2,128)S(1)} %collective-permute-done.4.east_ref) | copy-start | bytes 12292
  44.3 1.3 %copy-start.11 = (f32[2,512]{1,0:T(2,128)}, f32[2,512]{1,0:T(2,128)S(1)}, u32[]{:S(2)}) copy-start(f32[2,512]{1,0:T(2,128)S(1)} %collective-permute-done.5.south_ref) | copy-start | bytes 12292
  44.3 1.3 %copy-start.3 = (f32[5,512]{1,0:T(8,128)}, f32[5,512]{1,0:T(8,128)S(1)}, u32[]{:S(2)}) copy-start(f32[5,512]{1,0:T(8,128)S(1)} %collective-permute-done.6.west_ref) | copy-start | bytes 30724
  44.3 1.3 %copy-start.4 = (f32[5,512]{1,0:T(8,128)}, f32[5,512]{1,0:T(8,128)S(1)}, u32[]{:S(2)}) copy-start(f32[5,512]{1,0:T(8,128)S(1)} %collective-permute-done.7.north_ref) | copy-start | bytes 30724
  45.6 26.9 %all-to-all-start = ((f32[128,1,1152]{2,1,0:T(1,128)}), f32[128,1,1152]{2,1,0:T(1,128)S(1)}, u32[]{:S(2)}, u32[]{:S(2)}) async-start(f32[128,1,1152]{2,1,0:T(1,128)} %copy.44), calls=%async_computation | async-start | bytes 1179648 | tf_op jit(solution)/shard_map/all_to_all | solution.py:306
  74.1 8.2 %collective-permute-start.8 = (f32[8,128]{1,0:T(8,128)S(1)}, f32[8,128]{1,0:T(8,128)S(1)}, u32[]{:S(2)}, u32[]{:S(2)}) collective-permute-start(f32[8,128]{1,0:T(8,128)S(1)} %fusion.23), channel_id=1, source_target_pairs={{0,1},{1,2},{2,3},{3,4},{4,5},{5,6},{6,7},{7,8},{8,9},{9,10},{10,1... | collective-permute-start | bytes 12296 | tf_op jit(solution)/shard_map/ppermute | solution.py:26

commit v11 on v9

--- a/solution.py
+++ b/solution.py
@@ -72,6 +72,12 @@
     to_south[4:5, :] = sopen[-1:, :]
 
 
+def tile_rows(drained):
+    ny, nx = drained.shape
+    strips = drained.reshape(ny // STRIP, STRIP, nx).sum(axis=1)
+    return jnp.concatenate([strips[:, k * 128:(k + 1) * 128] for k in range(nx // 128)], axis=0)
+
+
 def open_masks(flags_ref, land):
     ny, nx = land.shape
     col = lax.broadcasted_iota(jnp.int32, (ny, nx), 1)
@@ -88,7 +94,7 @@
     depth = d_ref[...]
     land = land_ref[...].astype(jnp.float32)
     drained = drain_rate * land * jnp.abs(depth)
-    tile_out[...] = drained.reshape(ny // STRIP, STRIP, nx).sum(axis=1)
+    tile_out[...] = tile_rows(drained)
     _, _, eopen, sopen = open_masks(flags_ref, land)
     to_west[0:1, :] = first_col_row(bed_first_col[...] + depth[:, :128])
     to_west[1:2, :] = first_col_row(depth)
@@ -143,7 +149,7 @@
     if with_edges:
         tile_out, to_west, to_north, to_east, to_south = more
         next_drained = drain_rate * land * jnp.abs(new_depth)
-        tile_out[...] = next_drained.reshape(ny // STRIP, STRIP, nx).sum(axis=1)
+        tile_out[...] = tile_rows(next_drained)
         write_edges(bed + new_depth, new_depth, flux_e, flux_s, rough, eopen, sopen,
                     to_west, to_north, to_east, to_south)
 
@@ -200,7 +206,7 @@
     row_blocks = cell_rows // 8
     col_spec = lambda k: pl.BlockSpec((cell_rows, 128), lambda i: (0, k))
     row_spec = lambda k: pl.BlockSpec((8, cell_cols), lambda i: (k, 0))
-    tile_shape = jax.ShapeDtypeStruct((cell_rows // STRIP, cell_cols), f32)
+    tile_shape = jax.ShapeDtypeStruct((cell_rows // STRIP * cell_cols // 128, 128), f32)
     tiles, *edges = pl.pallas_call(
         edge_kernel,
         grid=(1,),
@@ -236,6 +242,11 @@
         lax.iota(jnp.int32, device_count * slot_cap)[:, None] == send_pos[None, :]
     ).astype(f32)
     send_ids = jnp.dot(gather_onehot, local_ids + 1.0, precision=lax.Precision.HIGHEST) - 1.0
+    lane_blocks = cell_cols // 128
+    row_pos = send_pos.reshape(cell_rows // STRIP, lane_blocks).T.reshape(-1)
+    row_onehot = (
+        lax.iota(jnp.int32, device_count * slot_cap)[:, None] == row_pos[None, :]
+    ).astype(f32)
     id_rows = -(-slot_cap // reach_width)
     send_ids = jnp.pad(
         send_ids.reshape(device_count, slot_cap),
@@ -243,14 +254,8 @@
         constant_values=-1.0,
     ).reshape(device_count, id_rows, reach_width)
     def start_lateral(parts, with_ids=True):
-        parts = [
-            part.reshape(cell_rows // STRIP, cell_cols // reach_width, reach_width).reshape(
-                -1, reach_width
-            )
-            for part in parts
-        ]
         packed = [
-            jnp.dot(gather_onehot, part, precision=lax.Precision.HIGHEST).reshape(
+            jnp.dot(row_onehot, part, precision=lax.Precision.HIGHEST).reshape(
                 device_count, slot_cap, reach_width
             )
             for part in parts

time: 80.3 us -> 79.2 us (0.986)
  local copies, waits for them, and re-layouts: 6.95 us -> 5.27 us
  waiting for transfers between devices: 1.73 us -> 0.16 us
  matrix products: 3.27 us -> 4.74 us
    ppermute x9, waiting for transfers between devices: 1.64 us -> 0.07 us  [shifted(): lax.ppermute(value, axis, [(source, source + steps) for source in range(f...]
    dot_general x2, matrix products: 0.92 us -> 2.38 us  [start_lateral(): jnp.dot(row_onehot, part, precision=lax.Precision.HIGHEST)]
    another operation x5 -> x3, local copies, waits for them, and re-layouts: 0.95 us -> 0.02 us  [the longest x2 0.93 us: start_lateral(): part.reshape(cell_rows // STRIP, cell_cols // reach_width, reach_width)]
    optimization_barrier x1 -> x0, local copies, waits for them, and re-layouts: 0.9 us -> none  [body(): lax.optimization_barrier((east_in, south_in, west_in, north_in, lateral_s...]
    all_to_all x1, starting transfers between devices: 9.93 us -> 10.8 us  [body(): got_second = lax.all_to_all(lateral_started, ('gy', 'gx'), 0, 0, tiled=True)]
    unnamed x41 -> x35, local copies, waits for them, and re-layouts: 2.59 us -> 2.31 us
  transfers between devices with their start and end apart: 11 -> 11, of which waited for: 2 -> 1; matrix products, arithmetic and copies ran while one was open for 7% -> 9% of each run, Pallas kernels for 19% -> 19%
where the time goes in v11:
time: 79.2 us; the launch traced here: 78.5 us
  starting transfers between devices  46.9 us (59%)
  Pallas kernels  18.4 us (23%)
  local copies, waits for them, and re-layouts  5.27 us (7%)
  matrix products  4.74 us (6%)
  other arithmetic  1.88 us (2%)
  between operations  1.1 us (1%)
    ppermute x9, starting transfers between devices, shifted(): lax.ppermute(value, axis, [(source, source + steps) for source in range(f...  24.8 us
    pallas_call x2, Pallas kernels, body(): step_call(not last)  15.2 us
    all_to_all x1, starting transfers between devices, body(): lax.all_to_all(start_lateral(tile_parts).reshape(device_count, first_rows...  11.4 us
    all_to_all x1, starting transfers between devices, body(): got_second = lax.all_to_all(lateral_started, ('gy', 'gx'), 0, 0, tiled=True)  10.8 us
    pallas_call x1, Pallas kernels, body(): pl.pallas_call(edge_kernel, grid=(1,), out_shape=(tile_shape,) + edge_sha...  3.29 us
    dot_general x2, matrix products, start_lateral(): jnp.dot(row_onehot, part, precision=lax.Precision.HIGHEST)  2.38 us
    unnamed x35, local copies, waits for them, and re-layouts  2.31 us
    dot_general x4, matrix products, block_term(): jnp.einsum('tb,tc->bc', onehot, values, precision=lax.Precision.HIGHEST)  1.61 us
  transfers between devices with their start and end apart: 11, of which 1 were waited for; matrix products, arithmetic and copies ran while one was open for 9% of the time, Pallas kernels for 19%

profile of v11, /device:TPU:1, one launch (start us, length us, event | category | flops | bytes accessed | tf_op | source)
XLA Modules:
  0.0 78.5 jit_solution(13117942435898534220)
XLA Ops:
  0.7 0.7 copy-done.7
  1.4 0.2 fusion.19
  1.6 0.6 add_convert_fusion.flags_ref
  2.2 3.3 %shard_map.129 = (f32[256,128]{1,0:T(8,128)}, f32[2,512]{1,0:T(2,128)}, f32[2,512]{1,0:T(2,128)}, f32[5,512]{1,0:T(8,128)}, f32[5,512]{1,0:T(8,128)}) custom-call(s32[3]{0:T(128)} %add_convert_fusion.flags_ref, f32[512,512]{1,0:T(8,128)} %d_ref.3, s32[512,512]{1,0:T(8,128)} %land_ref.5, f32[512,512]{1,0:T(8,128)} %bed_ref.3, f32[512,512]{1,0:T(8,128)} %bed_ref.3, ...), custom_call_target="tpu_custom_call" | custom-call | tf_op jit(solution)/shard_map/pallas_call | solution.py:210
  5.5 0.7 pad_maximum_fusion.1
  6.3 4.0 %collective-permute-start.2 = (f32[7,512]{1,0:T(8,128)S(1)}, f32[7,512]{1,0:T(8,128)S(1)}, u32[]{:S(2)}, u32[]{:S(2)}) collective-permute-start(f32[7,512]{1,0:T(8,128)S(1)} %pad_maximum_fusion.1), channel_id=1, source_target_pairs={{0,1},{1,2},{2,3},{3,4},{4,5},{5,6},{6,7},{7,8},{8,9},{9,10},{10,1... | collective-permute-start | bytes 43016 | tf_op jit(solution)/shard_map/ppermute | solution.py:26
  10.3 4.0 %collective-permute-start.3 = (f32[5,512]{1,0:T(8,128)S(1)}, f32[5,512]{1,0:T(8,128)S(1)}, u32[]{:S(2)}, u32[]{:S(2)}) collective-permute-start(f32[5,512]{1,0:T(8,128)S(1)} %copy-done.12), channel_id=1, source_target_pairs={{0,16},{16,32},{32,48},{48,64},{64,80},{80,96},{96,112},{1,17},{17... | collective-permute-start | bytes 30728 | tf_op jit(solution)/shard_map/ppermute | solution.py:26
  14.3 1.3 %collective-permute-start = (f32[2,512]{1,0:T(2,128)S(1)}, f32[2,512]{1,0:T(2,128)S(1)}, u32[]{:S(2)}, u32[]{:S(2)}) collective-permute-start(f32[2,512]{1,0:T(2,128)S(1)} %copy-done.14), channel_id=1, source_target_pairs={{1,0},{2,1},{3,2},{4,3},{5,4},{6,5},{7,6},{8,7},{9,8},{10,9},{11,1... | collective-permute-start | bytes 12296 | tf_op jit(solution)/shard_map/ppermute | solution.py:26
  15.6 1.9 %collective-permute-start.1 = (f32[2,512]{1,0:T(2,128)S(1)}, f32[2,512]{1,0:T(2,128)S(1)}, u32[]{:S(2)}, u32[]{:S(2)}) collective-permute-start(f32[2,512]{1,0:T(2,128)S(1)} %copy-done.13), channel_id=1, source_target_pairs={{16,0},{32,16},{48,32},{64,48},{80,64},{96,80},{112,96},{17,1},{33... | collective-permute-start | bytes 12296 | tf_op jit(solution)/shard_map/ppermute | solution.py:26
  17.7 0.2 fusion.6
  18.5 0.4 copy-done
  18.9 0.4 fusion
  19.5 0.3 fusion.2
  20.1 0.9 %copy.32 = f32[128,1,640]{2,1,0:T(1,128)} copy(f32[128,1,640]{0,2,1:T(8,128)S(1)} %bitcast.39) | data formatting | bytes 655360 | tf_op jit(solution)/shard_map/all_to_all | solution.py:266
  21.0 11.4 %all-to-all-start = ((f32[128,1,640]{2,1,0:T(1,128)}), f32[128,1,640]{2,1,0:T(1,128)S(1)}, u32[]{:S(2)}, u32[]{:S(2)}) async-start(f32[128,1,640]{2,1,0:T(1,128)} %copy.32), calls=%async_computation | async-start | bytes 655360 | tf_op jit(solution)/shard_map/all_to_all | solution.py:266
  32.4 0.2 fusion.15
  32.7 0.5 copy-done.8
  33.3 7.7 %shard_map.130 = (f32[512,512]{1,0:T(8,128)}, f32[512,512]{1,0:T(8,128)}, f32[512,512]{1,0:T(8,128)}, f32[256,128]{1,0:T(8,128)}, f32[2,512]{1,0:T(2,128)}, /*in...) custom-call(s32[3]{0:T(128)} %add_convert_fusion.flags_ref, f32[512,512]{1,0:T(8,128)} %d_ref.3, ...), custom_call_target="tpu_custom_call" | custom-call | tf_op jit(solution)/shard_map/pallas_call | solution.py:306
  41.1 3.3 %collective-permute-start.6 = (f32[5,512]{1,0:T(8,128)}, f32[5,512]{1,0:T(8,128)S(1)}, u32[]{:S(2)}, u32[]{:S(2)}) collective-permute-start(f32[5,512]{1,0:T(8,128)} %get-tuple-element.35), channel_id=1, source_target_pairs={{0,1},{1,2},{2,3},{3,4},{4,5},{5,6},{6,7},{7,8},{8,9},{9,10},{10,1... | collective-permute-start | bytes 30728 | tf_op jit(solution)/shard_map/ppermute | solution.py:26
  44.4 3.7 %collective-permute-start.7 = (f32[5,512]{1,0:T(8,128)}, f32[5,512]{1,0:T(8,128)S(1)}, u32[]{:S(2)}, u32[]{:S(2)}) collective-permute-start(f32[5,512]{1,0:T(8,128)} %get-tuple-element.36), channel_id=1, source_target_pairs={{0,16},{16,32},{32,48},{48,64},{64,80},{80,96},{96,112},{1,17},{17... | collective-permute-start | bytes 30728 | tf_op jit(solution)/shard_map/ppermute | solution.py:26
  48.0 1.3 %collective-permute-start.4 = (f32[2,512]{1,0:T(2,128)}, f32[2,512]{1,0:T(2,128)S(1)}, u32[]{:S(2)}, u32[]{:S(2)}) collective-permute-start(f32[2,512]{1,0:T(2,128)} %get-tuple-element.33), channel_id=1, source_target_pairs={{1,0},{2,1},{3,2},{4,3},{5,4},{6,5},{7,6},{8,7},{9,8},{10,9},{11,1... | collective-permute-start | bytes 12296 | tf_op jit(solution)/shard_map/ppermute | solution.py:26
  49.3 1.9 %collective-permute-start.5 = (f32[2,512]{1,0:T(2,128)S(1)}, f32[2,512]{1,0:T(2,128)S(1)}, u32[]{:S(2)}, u32[]{:S(2)}) collective-permute-start(f32[2,512]{1,0:T(2,128)S(1)} %copy-done.15), channel_id=1, source_target_pairs={{16,0},{32,16},{48,32},{64,48},{80,64},{96,80},{112,96},{17,1},{33... | collective-permute-start | bytes 12296 | tf_op jit(solution)/shard_map/ppermute | solution.py:26
  51.2 2.0 %fusion.1 = f32[512,128]{1,0:T(8,128)} fusion(f32[256,128]{1,0:T(8,128)} %get-tuple-element.37, s32[256]{0:T(256)S(1)} %eq.131), kind=kOutput, calls=%fused_computation.5 | convolution fusion | flops 201457664 | bytes 394240 | tf_op jit(solution)/shard_map/dot_general | solution.py:258
  53.2 0.7 slice.30
  54.3 0.5 copy-done.10
  55.3 10.8 %all-to-all-start.1 = ((f32[128,4,128]{2,1,0:T(4,128)}), f32[128,4,128]{2,1,0:T(4,128)S(1)}, u32[]{:S(2)}, u32[]{:S(2)}) async-start(f32[128,4,128]{2,1,0:T(4,128)} %bitcast.8), calls=%async_computation.1 | async-start | bytes 524288 | tf_op jit(solution)/shard_map/all_to_all | solution.py:315
  66.0 0.2 add_add_fusion.1
  66.2 0.3 fusion.17
  66.5 3.4 %collective-permute-start.8 = (f32[8,128]{1,0:T(8,128)S(1)}, f32[8,128]{1,0:T(8,128)S(1)}, u32[]{:S(2)}, u32[]{:S(2)}) collective-permute-start(f32[8,128]{1,0:T(8,128)S(1)} %fusion.17), channel_id=1, source_target_pairs={{0,1},{1,2},{2,3},{3,4},{4,5},{5,6},{6,7},{7,8},{8,9},{9,10},{10,1... | collective-permute-start | bytes 12296 | tf_op jit(solution)/shard_map/ppermute | solution.py:26
  69.9 7.4 %shard_map.131 = (f32[512,512]{1,0:T(8,128)}, f32[512,512]{1,0:T(8,128)}, f32[512,512]{1,0:T(8,128)}) custom-call(s32[3]{0:T(128)} %add_convert_fusion.flags_ref, f32[512,512]{1,0:T(8,128)} %get-tuple-element.30.d_ref, f32[512,512]{1,0:T(8,128)} %get-tuple-element.31.e_ref, f32[512,512]{1,0:T(8,128)} %get-tuple-element.32.s_ref, f32[512,512]{1,0:T(8,128)} %bed_ref.3, ...), custom_call_target="tpu_custom_call" | custom-call | tf_op jit(solution)/shard_map/pallas_call | solution.py:306
  77.4 0.2 convolution_multiply_fusion
  77.7 0.9 %add_add_fusion = f32[16,128]{1,0:T(8,128)} fusion(f32[16,128]{1,0:T(8,128)S(1)} %convolution_multiply_fusion, f32[8,128]{1,0:T(8,128)S(1)} %collective-permute-done.8, f32[16,128]{1,0:T(8,128)S(1)} %add_add_fusion.1, s32[16]{0:T(128)S(1)} %iota_add_fusion, s32[16]{0:T(128)S(1)} %copy-done.16, f32[16,128]{1,0:T(8,128)S(1)} %copy-done.7), kind=kOutput, calls=%fused_computation.34 | convolution fusion | flops 418048 | bytes 36992 | tf_op jit(solution)/shard_map/tb,tc->bc/dot_general | solution.py:40
  (73 shorter events, 2.0 us)
Async XLA Ops:
  0.6 0.7 copy-start.7
  0.6 0.7 copy-start.6
  0.7 0.7 copy-start.16
  5.5 4.8 %copy-start.12 = (f32[5,512]{1,0:T(8,128)S(1)}, f32[5,512]{1,0:T(8,128)}, u32[]{:S(2)}) copy-start(f32[5,512]{1,0:T(8,128)} %get-tuple-element.29) | copy-start | bytes 30724
  5.5 8.8 %copy-start.14 = (f32[2,512]{1,0:T(2,128)S(1)}, f32[2,512]{1,0:T(2,128)}, u32[]{:S(2)}) copy-start(f32[2,512]{1,0:T(2,128)} %get-tuple-element.26) | copy-start | bytes 12292
  6.3 9.3 %copy-start.13 = (f32[2,512]{1,0:T(2,128)S(1)}, f32[2,512]{1,0:T(2,128)}, u32[]{:S(2)}) copy-start(f32[2,512]{1,0:T(2,128)} %get-tuple-element.27) | copy-start | bytes 12292
  6.3 26.4 %collective-permute-start.2 = (f32[7,512]{1,0:T(8,128)S(1)}, f32[7,512]{1,0:T(8,128)S(1)}, u32[]{:S(2)}, u32[]{:S(2)}) collective-permute-start(f32[7,512]{1,0:T(8,128)S(1)} %pad_maximum_fusion.1), channel_id=1, source_target_pairs={{0,1},{1,2},{2,3},{3,4},{4,5},{5,6},{6,7},{7,8},{8,9},{9,10},{10,1... | collective-permute-start | bytes 43016 | tf_op jit(solution)/shard_map/ppermute | solution.py:26
  10.3 22.4 %collective-permute-start.3 = (f32[5,512]{1,0:T(8,128)S(1)}, f32[5,512]{1,0:T(8,128)S(1)}, u32[]{:S(2)}, u32[]{:S(2)}) collective-permute-start(f32[5,512]{1,0:T(8,128)S(1)} %copy-done.12), channel_id=1, source_target_pairs={{0,16},{16,32},{32,48},{48,64},{64,80},{80,96},{96,112},{1,17},{17... | collective-permute-start | bytes 30728 | tf_op jit(solution)/shard_map/ppermute | solution.py:26
  14.3 3.3 %copy-start.5 = (s32[256]{0:T(256)S(1)}, s32[256]{0:T(256)}, u32[]{:S(2)}) copy-start(s32[256]{0:T(256)} %param.16) | copy-start | bytes 3076
  14.3 18.3 %collective-permute-start = (f32[2,512]{1,0:T(2,128)S(1)}, f32[2,512]{1,0:T(2,128)S(1)}, u32[]{:S(2)}, u32[]{:S(2)}) collective-permute-start(f32[2,512]{1,0:T(2,128)S(1)} %copy-done.14), channel_id=1, source_target_pairs={{1,0},{2,1},{3,2},{4,3},{5,4},{6,5},{7,6},{8,7},{9,8},{10,9},{11,1... | collective-permute-start | bytes 12296 | tf_op jit(solution)/shard_map/ppermute | solution.py:26
  15.6 17.0 %collective-permute-start.1 = (f32[2,512]{1,0:T(2,128)S(1)}, f32[2,512]{1,0:T(2,128)S(1)}, u32[]{:S(2)}, u32[]{:S(2)}) collective-permute-start(f32[2,512]{1,0:T(2,128)S(1)} %copy-done.13), channel_id=1, source_target_pairs={{16,0},{32,16},{48,32},{64,48},{80,64},{96,80},{112,96},{17,1},{33... | collective-permute-start | bytes 12296 | tf_op jit(solution)/shard_map/ppermute | solution.py:26
  18.0 0.9 %copy-start = (f32[256,128]{1,0:T(8,128)S(1)}, f32[256,128]{1,0:T(8,128)}, u32[]{:S(2)}) copy-start(f32[256,128]{1,0:T(8,128)} %get-tuple-element.38) | copy-start | bytes 393220
  21.0 33.0 %all-to-all-start = ((f32[128,1,640]{2,1,0:T(1,128)}), f32[128,1,640]{2,1,0:T(1,128)S(1)}, u32[]{:S(2)}, u32[]{:S(2)}) async-start(f32[128,1,640]{2,1,0:T(1,128)} %copy.32), calls=%async_computation | async-start | bytes 655360 | tf_op jit(solution)/shard_map/all_to_all | solution.py:266
  32.7 0.6 copy-start.8
  32.7 0.6 copy-start.9
  32.7 0.6 copy-start.2
  32.7 0.6 copy-start.1
  41.1 8.2 %copy-start.15 = (f32[2,512]{1,0:T(2,128)S(1)}, f32[2,512]{1,0:T(2,128)}, u32[]{:S(2)}) copy-start(f32[2,512]{1,0:T(2,128)} %get-tuple-element.34) | copy-start | bytes 12292
  41.1 13.2 %collective-permute-start.6 = (f32[5,512]{1,0:T(8,128)}, f32[5,512]{1,0:T(8,128)S(1)}, u32[]{:S(2)}, u32[]{:S(2)}) collective-permute-start(f32[5,512]{1,0:T(8,128)} %get-tuple-element.35), channel_id=1, source_target_pairs={{0,1},{1,2},{2,3},{3,4},{4,5},{5,6},{6,7},{7,8},{8,9},{9,10},{10,1... | collective-permute-start | bytes 30728 | tf_op jit(solution)/shard_map/ppermute | solution.py:26
  44.4 9.9 %collective-permute-start.7 = (f32[5,512]{1,0:T(8,128)}, f32[5,512]{1,0:T(8,128)S(1)}, u32[]{:S(2)}, u32[]{:S(2)}) collective-permute-start(f32[5,512]{1,0:T(8,128)} %get-tuple-element.36), channel_id=1, source_target_pairs={{0,16},{16,32},{32,48},{48,64},{64,80},{80,96},{96,112},{1,17},{17... | collective-permute-start | bytes 30728 | tf_op jit(solution)/shard_map/ppermute | solution.py:26
  48.0 6.2 %collective-permute-start.4 = (f32[2,512]{1,0:T(2,128)}, f32[2,512]{1,0:T(2,128)S(1)}, u32[]{:S(2)}, u32[]{:S(2)}) collective-permute-start(f32[2,512]{1,0:T(2,128)} %get-tuple-element.33), channel_id=1, source_target_pairs={{1,0},{2,1},{3,2},{4,3},{5,4},{6,5},{7,6},{8,7},{9,8},{10,9},{11,1... | collective-permute-start | bytes 12296 | tf_op jit(solution)/shard_map/ppermute | solution.py:26
  49.3 4.9 %collective-permute-start.5 = (f32[2,512]{1,0:T(2,128)S(1)}, f32[2,512]{1,0:T(2,128)S(1)}, u32[]{:S(2)}, u32[]{:S(2)}) collective-permute-start(f32[2,512]{1,0:T(2,128)S(1)} %copy-done.15), channel_id=1, source_target_pairs={{16,0},{32,16},{48,32},{64,48},{80,64},{96,80},{112,96},{17,1},{33... | collective-permute-start | bytes 12296 | tf_op jit(solution)/shard_map/ppermute | solution.py:26
  54.2 0.6 copy-start.10
  54.2 0.6 copy-start.11
  54.3 0.6 copy-start.3
  54.3 0.6 copy-start.4
  55.3 22.2 %all-to-all-start.1 = ((f32[128,4,128]{2,1,0:T(4,128)}), f32[128,4,128]{2,1,0:T(4,128)S(1)}, u32[]{:S(2)}, u32[]{:S(2)}) async-start(f32[128,4,128]{2,1,0:T(4,128)} %bitcast.8), calls=%async_computation.1 | async-start | bytes 524288 | tf_op jit(solution)/shard_map/all_to_all | solution.py:315
  66.5 11.2 %collective-permute-start.8 = (f32[8,128]{1,0:T(8,128)S(1)}, f32[8,128]{1,0:T(8,128)S(1)}, u32[]{:S(2)}, u32[]{:S(2)}) collective-permute-start(f32[8,128]{1,0:T(8,128)S(1)} %fusion.17), channel_id=1, source_target_pairs={{0,1},{1,2},{2,3},{3,4},{4,5},{5,6},{6,7},{7,8},{8,9},{9,10},{10,1... | collective-permute-start | bytes 12296 | tf_op jit(solution)/shard_map/ppermute | solution.py:26

commit v12 on v11

--- a/solution.py
+++ b/solution.py
@@ -78,6 +78,16 @@
     return jnp.concatenate([strips[:, k * 128:(k + 1) * 128] for k in range(nx // 128)], axis=0)
 
 
+def pack_slots(slot_ref, tile_out, packed_out):
+    packed_out[...] = jnp.zeros(packed_out.shape, jnp.float32)
+
+    def place(row, carry):
+        packed_out[pl.ds(slot_ref[row], 1), :] = tile_out[pl.ds(row, 1), :]
+        return carry
+
+    lax.fori_loop(0, tile_out.shape[0], place, 0)
+
+
 def open_masks(flags_ref, land):
     ny, nx = land.shape
     col = lax.broadcasted_iota(jnp.int32, (ny, nx), 1)
@@ -87,14 +97,15 @@
     return col, row, eopen, sopen
 
 
-def edge_kernel(flags_ref, d_ref, land_ref, bed_first_col, bed_last_col, bed_first_row,
+def edge_kernel(flags_ref, slot_ref, d_ref, land_ref, bed_first_col, bed_last_col, bed_first_row,
                 bed_last_row, e_ref, s_ref, r_col, r_row,
-                tile_out, to_west, to_north, to_east, to_south):
+                tile_out, packed_out, to_west, to_north, to_east, to_south):
     ny, nx = d_ref.shape
     depth = d_ref[...]
     land = land_ref[...].astype(jnp.float32)
     drained = drain_rate * land * jnp.abs(depth)
     tile_out[...] = tile_rows(drained)
+    pack_slots(slot_ref, tile_out, packed_out)
     _, _, eopen, sopen = open_masks(flags_ref, land)
     to_west[0:1, :] = first_col_row(bed_first_col[...] + depth[:, :128])
     to_west[1:2, :] = first_col_row(depth)
@@ -112,7 +123,7 @@
     to_south[4:5, :] = sopen[-1:, :]
 
 
-def step_kernel(with_edges, flags_ref, d_ref, e_ref, s_ref, bed_ref, r_ref, land_ref,
+def step_kernel(with_edges, flags_ref, slot_ref, d_ref, e_ref, s_ref, bed_ref, r_ref, land_ref,
                 east_ref, south_ref, west_ref, north_ref,
                 d_out, e_out, s_out, *more):
     ny, nx = d_ref.shape
@@ -147,9 +158,10 @@
     e_out[...] = flux_e
     s_out[...] = flux_s
     if with_edges:
-        tile_out, to_west, to_north, to_east, to_south = more
+        tile_out, packed_out, to_west, to_north, to_east, to_south = more
         next_drained = drain_rate * land * jnp.abs(new_depth)
         tile_out[...] = tile_rows(next_drained)
+        pack_slots(slot_ref, tile_out, packed_out)
         write_edges(bed + new_depth, new_depth, flux_e, flux_s, rough, eopen, sopen,
                     to_west, to_north, to_east, to_south)
 
@@ -202,35 +214,6 @@
     grid_shape = jax.ShapeDtypeStruct((cell_rows, cell_cols), f32)
     smem_spec = pl.BlockSpec(memory_space=pltpu.SMEM)
 
-    col_blocks = cell_cols // 128
-    row_blocks = cell_rows // 8
-    col_spec = lambda k: pl.BlockSpec((cell_rows, 128), lambda i: (0, k))
-    row_spec = lambda k: pl.BlockSpec((8, cell_cols), lambda i: (k, 0))
-    tile_shape = jax.ShapeDtypeStruct((cell_rows // STRIP * cell_cols // 128, 128), f32)
-    tiles, *edges = pl.pallas_call(
-        edge_kernel,
-        grid=(1,),
-        out_shape=(tile_shape,) + edge_shapes(cell_rows, cell_cols),
-        in_specs=[smem_spec] + vmem_specs(2)
-        + [col_spec(0), col_spec(col_blocks - 1), row_spec(0), row_spec(row_blocks - 1),
-           col_spec(col_blocks - 1), row_spec(row_blocks - 1),
-           col_spec(col_blocks - 1), row_spec(row_blocks - 1)],
-        out_specs=vmem_specs(5),
-    )(flags, water_depth, land_mask, bed_level, bed_level, bed_level, bed_level,
-      flux_east, flux_south, roughness, roughness)
-    tile_parts = [tiles]
-
-    def step_call(with_edges):
-        outs = (grid_shape, grid_shape, grid_shape)
-        if with_edges:
-            outs = outs + (tile_shape,) + edge_shapes(cell_rows, cell_cols)
-        return pl.pallas_call(
-            functools.partial(step_kernel, with_edges),
-            out_shape=outs,
-            in_specs=[smem_spec] + vmem_specs(10),
-            out_specs=vmem_specs(len(outs)),
-        )
-
     tile_owner = tile_block // block_rows
     owner_hits = (tile_owner[:, None] == lax.iota(jnp.int32, device_count)[None, :]).astype(
         jnp.int32
@@ -244,20 +227,45 @@
     send_ids = jnp.dot(gather_onehot, local_ids + 1.0, precision=lax.Precision.HIGHEST) - 1.0
     lane_blocks = cell_cols // 128
     row_pos = send_pos.reshape(cell_rows // STRIP, lane_blocks).T.reshape(-1)
-    row_onehot = (
-        lax.iota(jnp.int32, device_count * slot_cap)[:, None] == row_pos[None, :]
-    ).astype(f32)
     id_rows = -(-slot_cap // reach_width)
     send_ids = jnp.pad(
         send_ids.reshape(device_count, slot_cap),
         ((0, 0), (0, id_rows * reach_width - slot_cap)),
         constant_values=-1.0,
     ).reshape(device_count, id_rows, reach_width)
+    col_blocks = cell_cols // 128
+    row_blocks = cell_rows // 8
+    col_spec = lambda k: pl.BlockSpec((cell_rows, 128), lambda i: (0, k))
+    row_spec = lambda k: pl.BlockSpec((8, cell_cols), lambda i: (k, 0))
+    tile_shape = jax.ShapeDtypeStruct((cell_rows // STRIP * cell_cols // 128, 128), f32)
+    slot_shape = jax.ShapeDtypeStruct((device_count * slot_cap, reach_width), f32)
+    _, slots, *edges = pl.pallas_call(
+        edge_kernel,
+        grid=(1,),
+        out_shape=(tile_shape, slot_shape) + edge_shapes(cell_rows, cell_cols),
+        in_specs=[smem_spec, smem_spec] + vmem_specs(2)
+        + [col_spec(0), col_spec(col_blocks - 1), row_spec(0), row_spec(row_blocks - 1),
+           col_spec(col_blocks - 1), row_spec(row_blocks - 1),
+           col_spec(col_blocks - 1), row_spec(row_blocks - 1)],
+        out_specs=vmem_specs(6),
+    )(flags, row_pos, water_depth, land_mask, bed_level, bed_level, bed_level, bed_level,
+      flux_east, flux_south, roughness, roughness)
+    tile_parts = [slots]
+
+    def step_call(with_edges):
+        outs = (grid_shape, grid_shape, grid_shape)
+        if with_edges:
+            outs = outs + (tile_shape, slot_shape) + edge_shapes(cell_rows, cell_cols)
+        return pl.pallas_call(
+            functools.partial(step_kernel, with_edges),
+            out_shape=outs,
+            in_specs=[smem_spec, smem_spec] + vmem_specs(10),
+            out_specs=vmem_specs(len(outs)),
+        )
+
     def start_lateral(parts, with_ids=True):
         packed = [
-            jnp.dot(row_onehot, part, precision=lax.Precision.HIGHEST).reshape(
-                device_count, slot_cap, reach_width
-            )
+            part.reshape(device_count, slot_cap, reach_width)
             for part in parts
         ]
         return jnp.concatenate(packed + ([send_ids] if with_ids else []), axis=1)
@@ -304,13 +312,13 @@
                 )
             )
         outs = step_call(not last)(
-            flags, depth, flux_east, flux_south, bed_level, roughness, land_mask,
+            flags, row_pos, depth, flux_east, flux_south, bed_level, roughness, land_mask,
             east_in, south_in, west_in, north_in,
         )
         depth, flux_east, flux_south = outs[:3]
         if not last:
-            tile_parts.append(outs[3])
-            edges = outs[4:]
+            tile_parts.append(outs[4])
+            edges = outs[5:]
 
     got_second = lax.all_to_all(lateral_started, ("gy", "gx"), 0, 0, tiled=True)
     got_ids = got_first[:, slot_cap:].reshape(device_count, -1)[:, :slot_cap].reshape(-1)

time: 79.2 us -> 83.4 us (1.053)
  Pallas kernels: 18.4 us -> 22.3 us
  matrix products: 4.74 us -> 2.36 us
  local copies, waits for them, and re-layouts: 5.27 us -> 7.03 us
  waiting for transfers between devices: 0.16 us -> 1.91 us
    dot_general x2 -> x0, matrix products: 2.38 us -> none  [start_lateral(): jnp.dot(row_onehot, part, precision=lax.Precision.HIGHEST)]
    pallas_call x2, Pallas kernels: 15.2 us -> 17.2 us  [body(): step_call(not last)]
    pallas_call x1, Pallas kernels: 3.29 us -> 5.08 us  [body(): pl.pallas_call(edge_kernel, grid=(1,), out_shape=(tile_shape, slot_shape)...]
    ppermute x9, waiting for transfers between devices: 0.07 us -> 1.82 us  [shifted(): lax.ppermute(value, axis, [(source, source + steps) for source in range(f...]
    reshape x1, local copies, waits for them, and re-layouts: 0.13 us -> 1.07 us  [start_lateral(): part.reshape(device_count, slot_cap, reach_width)]
    unnamed x35 -> x33, local copies, waits for them, and re-layouts: 2.31 us -> 2.51 us
  transfers between devices with their start and end apart: 11 -> 11, of which waited for: 1 -> 3; matrix products, arithmetic and copies ran while one was open for 9% -> 5% of each run, Pallas kernels for 19% -> 21%
where the time goes in v12:
time: 83.4 us; the launch traced here: 82.7 us
  starting transfers between devices  46.1 us (55%)
  Pallas kernels  22.3 us (27%)
  local copies, waits for them, and re-layouts  7.03 us (8%)
  matrix products  2.36 us (3%)
  other arithmetic  1.93 us (2%)
  waiting for transfers between devices  1.91 us (2%)
  between operations  1.04 us (1%)
    ppermute x9, starting transfers between devices, shifted(): lax.ppermute(value, axis, [(source, source + steps) for source in range(f...  24.8 us
    pallas_call x2, Pallas kernels, body(): step_call(not last)  17.2 us
    all_to_all x1, starting transfers between devices, body(): lax.all_to_all(start_lateral(tile_parts).reshape(device_count, first_rows...  11.4 us
    all_to_all x1, starting transfers between devices, body(): got_second = lax.all_to_all(lateral_started, ('gy', 'gx'), 0, 0, tiled=True)  9.94 us
    pallas_call x1, Pallas kernels, body(): pl.pallas_call(edge_kernel, grid=(1,), out_shape=(tile_shape, slot_shape)...  5.08 us
    unnamed x33, local copies, waits for them, and re-layouts  2.51 us
    ppermute x9, waiting for transfers between devices, shifted(): lax.ppermute(value, axis, [(source, source + steps) for source in range(f...  1.82 us
  transfers between devices with their start and end apart: 11, of which 3 were waited for; matrix products, arithmetic and copies ran while one was open for 5% of the time, Pallas kernels for 21%

profile of v12, /device:TPU:1, one launch (start us, length us, event | category | flops | bytes accessed | tf_op | source)
XLA Modules:
  0.0 82.7 jit_solution(11635536414584595096)
XLA Ops:
  0.6 0.7 copy-done.4
  2.2 0.7 reshape.78.slot_ref
  2.9 0.6 copy-done.15
  3.5 0.2 fusion.15
  3.8 0.7 add_convert_fusion.flags_ref
  4.4 5.1 %shard_map.129 = (f32[256,128]{1,0:T(8,128)}, f32[512,128]{1,0:T(8,128)}, f32[2,512]{1,0:T(2,128)}, f32[2,512]{1,0:T(2,128)}, f32[5,512]{1,0:T(8,128)}, /*index=5*/f32[5,512]{1,0:T(8,128)}) custom-call(s32[3]{0:T(128)} %add_convert_fusion.flags_ref, s32[256]{0:T(256)} %reshape.78.slot_ref, f32[512,512]{1,0:T(8,128)} %d_ref.3, s32[512,512]{1,0:T(8,128)} %land_ref.5, ...), custom_call_target="tpu_custom_call" | custom-call | tf_op jit(solution)/shard_map/pallas_call | solution.py:242
  9.5 0.7 pad_maximum_fusion.1
  10.3 4.0 %collective-permute-start.2 = (f32[7,512]{1,0:T(8,128)S(1)}, f32[7,512]{1,0:T(8,128)S(1)}, u32[]{:S(2)}, u32[]{:S(2)}) collective-permute-start(f32[7,512]{1,0:T(8,128)S(1)} %pad_maximum_fusion.1), channel_id=1, source_target_pairs={{0,1},{1,2},{2,3},{3,4},{4,5},{5,6},{6,7},{7,8},{8,9},{9,10},{10,1... | collective-permute-start | bytes 43016 | tf_op jit(solution)/shard_map/ppermute | solution.py:26
  14.3 4.0 %collective-permute-start.3 = (f32[5,512]{1,0:T(8,128)S(1)}, f32[5,512]{1,0:T(8,128)S(1)}, u32[]{:S(2)}, u32[]{:S(2)}) collective-permute-start(f32[5,512]{1,0:T(8,128)S(1)} %copy-done.11), channel_id=1, source_target_pairs={{0,16},{16,32},{32,48},{48,64},{64,80},{80,96},{96,112},{1,17},{17... | collective-permute-start | bytes 30728 | tf_op jit(solution)/shard_map/ppermute | solution.py:26
  18.3 1.3 %collective-permute-start = (f32[2,512]{1,0:T(2,128)S(1)}, f32[2,512]{1,0:T(2,128)S(1)}, u32[]{:S(2)}, u32[]{:S(2)}) collective-permute-start(f32[2,512]{1,0:T(2,128)S(1)} %copy-done.13), channel_id=1, source_target_pairs={{1,0},{2,1},{3,2},{4,3},{5,4},{6,5},{7,6},{8,7},{9,8},{10,9},{11,1... | collective-permute-start | bytes 12296 | tf_op jit(solution)/shard_map/ppermute | solution.py:26
  19.6 1.9 %collective-permute-start.1 = (f32[2,512]{1,0:T(2,128)S(1)}, f32[2,512]{1,0:T(2,128)S(1)}, u32[]{:S(2)}, u32[]{:S(2)}) collective-permute-start(f32[2,512]{1,0:T(2,128)S(1)} %copy-done.12), channel_id=1, source_target_pairs={{16,0},{32,16},{48,32},{64,48},{80,64},{96,80},{112,96},{17,1},{33... | collective-permute-start | bytes 12296 | tf_op jit(solution)/shard_map/ppermute | solution.py:26
  21.5 1.1 %copy.30 = f32[128,4,128]{0,2,1:T(8,128)S(1)} copy(f32[128,4,128]{2,1,0:T(4,128)} %bitcast.42) | data formatting | bytes 524288 | tf_op jit(solution)/shard_map/reshape | solution.py:268
  22.6 0.3 fusion
  23.2 0.9 %copy.32 = f32[128,1,640]{2,1,0:T(1,128)} copy(f32[128,1,640]{0,2,1:T(8,128)S(1)} %bitcast.37) | data formatting | bytes 655360 | tf_op jit(solution)/shard_map/all_to_all | solution.py:274
  24.1 11.4 %all-to-all-start = ((f32[128,1,640]{2,1,0:T(1,128)}), f32[128,1,640]{2,1,0:T(1,128)S(1)}, u32[]{:S(2)}, u32[]{:S(2)}) async-start(f32[128,1,640]{2,1,0:T(1,128)} %copy.32), calls=%async_computation | async-start | bytes 655360 | tf_op jit(solution)/shard_map/all_to_all | solution.py:274
  35.7 0.5 copy-done.9
  36.3 9.8 %shard_map.130 = (f32[512,512]{1,0:T(8,128)}, f32[512,512]{1,0:T(8,128)}, f32[512,512]{1,0:T(8,128)}, f32[256,128]{1,0:T(8,128)}, f32[512,128]{1,0:T(8,128)}, /*...) custom-call(s32[3]{0:T(128)} %add_convert_fusion.flags_ref, s32[256]{0:T(256)} %reshape.78.slot_ref, ...), custom_call_target="tpu_custom_call" | custom-call | tf_op jit(solution)/shard_map/pallas_call | solution.py:314
  46.1 3.3 %collective-permute-start.6 = (f32[5,512]{1,0:T(8,128)}, f32[5,512]{1,0:T(8,128)S(1)}, u32[]{:S(2)}, u32[]{:S(2)}) collective-permute-start(f32[5,512]{1,0:T(8,128)} %get-tuple-element.35), channel_id=1, source_target_pairs={{0,1},{1,2},{2,3},{3,4},{4,5},{5,6},{6,7},{7,8},{8,9},{9,10},{10,1... | collective-permute-start | bytes 30728 | tf_op jit(solution)/shard_map/ppermute | solution.py:26
  49.3 3.7 %collective-permute-start.7 = (f32[5,512]{1,0:T(8,128)}, f32[5,512]{1,0:T(8,128)S(1)}, u32[]{:S(2)}, u32[]{:S(2)}) collective-permute-start(f32[5,512]{1,0:T(8,128)} %get-tuple-element.36), channel_id=1, source_target_pairs={{0,16},{16,32},{32,48},{48,64},{64,80},{80,96},{96,112},{1,17},{17... | collective-permute-start | bytes 30728 | tf_op jit(solution)/shard_map/ppermute | solution.py:26
  53.0 1.3 %collective-permute-start.4 = (f32[2,512]{1,0:T(2,128)}, f32[2,512]{1,0:T(2,128)S(1)}, u32[]{:S(2)}, u32[]{:S(2)}) collective-permute-start(f32[2,512]{1,0:T(2,128)} %get-tuple-element.33), channel_id=1, source_target_pairs={{1,0},{2,1},{3,2},{4,3},{5,4},{6,5},{7,6},{8,7},{9,8},{10,9},{11,1... | collective-permute-start | bytes 12296 | tf_op jit(solution)/shard_map/ppermute | solution.py:26
  54.3 1.9 %collective-permute-start.5 = (f32[2,512]{1,0:T(2,128)S(1)}, f32[2,512]{1,0:T(2,128)S(1)}, u32[]{:S(2)}, u32[]{:S(2)}) collective-permute-start(f32[2,512]{1,0:T(2,128)S(1)} %copy-done.14), channel_id=1, source_target_pairs={{16,0},{32,16},{48,32},{64,48},{80,64},{96,80},{112,96},{17,1},{33... | collective-permute-start | bytes 12296 | tf_op jit(solution)/shard_map/ppermute | solution.py:26
  56.2 0.2 fusion.11
  56.5 0.7 slice.30
  57.6 1.7 %collective-permute-done.5.south_ref = f32[2,512]{1,0:T(2,128)S(1)} collective-permute-done((f32[2,512]{1,0:T(2,128)S(1)}, f32[2,512]{1,0:T(2,128)S(1)}, u32[]{:S(2)}, u32[]{:S(2)}) %collective-permute-start.5) | collective-permute-done | bytes 4128 | tf_op jit(solution)/shard_map/ppermute | solution.py:26
  59.3 0.5 copy-done.8
  60.2 9.9 %all-to-all-start.1 = ((f32[128,4,128]{2,1,0:T(4,128)}), f32[128,4,128]{2,1,0:T(4,128)S(1)}, u32[]{:S(2)}, u32[]{:S(2)}) async-start(f32[128,4,128]{2,1,0:T(4,128)} %bitcast.8), calls=%async_computation.1 | async-start | bytes 524288 | tf_op jit(solution)/shard_map/all_to_all | solution.py:323
  70.2 0.2 add_add_fusion.1
  70.4 0.3 fusion.13
  70.7 3.4 %collective-permute-start.8 = (f32[8,128]{1,0:T(8,128)S(1)}, f32[8,128]{1,0:T(8,128)S(1)}, u32[]{:S(2)}, u32[]{:S(2)}) collective-permute-start(f32[8,128]{1,0:T(8,128)S(1)} %fusion.13), channel_id=1, source_target_pairs={{0,1},{1,2},{2,3},{3,4},{4,5},{5,6},{6,7},{7,8},{8,9},{9,10},{10,1... | collective-permute-start | bytes 12296 | tf_op jit(solution)/shard_map/ppermute | solution.py:26
  74.1 7.4 %shard_map.131 = (f32[512,512]{1,0:T(8,128)}, f32[512,512]{1,0:T(8,128)}, f32[512,512]{1,0:T(8,128)}) custom-call(s32[3]{0:T(128)} %add_convert_fusion.flags_ref, s32[256]{0:T(256)} %reshape.78.slot_ref, f32[512,512]{1,0:T(8,128)} %get-tuple-element.30.d_ref, f32[512,512]{1,0:T(8,128)} %get-tuple-element.31.e_ref, f32[512,512]{1,0:T(8,128)} %get-tuple-element.32.s_ref, ...), custom_call_target="tpu_custom_call" | custom-call | tf_op jit(solution)/shard_map/pallas_call | solution.py:314
  81.6 0.2 convolution_multiply_fusion
  81.8 0.9 %add_add_fusion = f32[16,128]{1,0:T(8,128)} fusion(f32[16,128]{1,0:T(8,128)S(1)} %convolution_multiply_fusion, f32[8,128]{1,0:T(8,128)S(1)} %collective-permute-done.8, f32[16,128]{1,0:T(8,128)S(1)} %add_add_fusion.1, s32[16]{0:T(128)S(1)} %iota_add_fusion, s32[16]{0:T(128)S(1)} %copy-done.15, f32[16,128]{1,0:T(8,128)S(1)} %copy-done.6), kind=kOutput, calls=%fused_computation.29 | convolution fusion | flops 418048 | bytes 36992 | tf_op jit(solution)/shard_map/tb,tc->bc/dot_general | solution.py:40
  (69 shorter events, 2.0 us)
Async XLA Ops:
  0.6 0.7 copy-start.4
  2.1 0.8 copy-start.6
  2.2 0.7 copy-start.5
  2.8 0.7 copy-start.15
  9.5 4.8 %copy-start.11 = (f32[5,512]{1,0:T(8,128)S(1)}, f32[5,512]{1,0:T(8,128)}, u32[]{:S(2)}) copy-start(f32[5,512]{1,0:T(8,128)} %get-tuple-element.29) | copy-start | bytes 30724
  9.5 8.8 %copy-start.13 = (f32[2,512]{1,0:T(2,128)S(1)}, f32[2,512]{1,0:T(2,128)}, u32[]{:S(2)}) copy-start(f32[2,512]{1,0:T(2,128)} %get-tuple-element.26) | copy-start | bytes 12292
  10.3 9.3 %copy-start.12 = (f32[2,512]{1,0:T(2,128)S(1)}, f32[2,512]{1,0:T(2,128)}, u32[]{:S(2)}) copy-start(f32[2,512]{1,0:T(2,128)} %get-tuple-element.27) | copy-start | bytes 12292
  10.3 25.4 %collective-permute-start.2 = (f32[7,512]{1,0:T(8,128)S(1)}, f32[7,512]{1,0:T(8,128)S(1)}, u32[]{:S(2)}, u32[]{:S(2)}) collective-permute-start(f32[7,512]{1,0:T(8,128)S(1)} %pad_maximum_fusion.1), channel_id=1, source_target_pairs={{0,1},{1,2},{2,3},{3,4},{4,5},{5,6},{6,7},{7,8},{8,9},{9,10},{10,1... | collective-permute-start | bytes 43016 | tf_op jit(solution)/shard_map/ppermute | solution.py:26
  14.3 21.3 %collective-permute-start.3 = (f32[5,512]{1,0:T(8,128)S(1)}, f32[5,512]{1,0:T(8,128)S(1)}, u32[]{:S(2)}, u32[]{:S(2)}) collective-permute-start(f32[5,512]{1,0:T(8,128)S(1)} %copy-done.11), channel_id=1, source_target_pairs={{0,16},{16,32},{32,48},{48,64},{64,80},{80,96},{96,112},{1,17},{17... | collective-permute-start | bytes 30728 | tf_op jit(solution)/shard_map/ppermute | solution.py:26
  18.3 17.3 %collective-permute-start = (f32[2,512]{1,0:T(2,128)S(1)}, f32[2,512]{1,0:T(2,128)S(1)}, u32[]{:S(2)}, u32[]{:S(2)}) collective-permute-start(f32[2,512]{1,0:T(2,128)S(1)} %copy-done.13), channel_id=1, source_target_pairs={{1,0},{2,1},{3,2},{4,3},{5,4},{6,5},{7,6},{8,7},{9,8},{10,9},{11,1... | collective-permute-start | bytes 12296 | tf_op jit(solution)/shard_map/ppermute | solution.py:26
  19.6 16.0 %collective-permute-start.1 = (f32[2,512]{1,0:T(2,128)S(1)}, f32[2,512]{1,0:T(2,128)S(1)}, u32[]{:S(2)}, u32[]{:S(2)}) collective-permute-start(f32[2,512]{1,0:T(2,128)S(1)} %copy-done.12), channel_id=1, source_target_pairs={{16,0},{32,16},{48,32},{64,48},{80,64},{96,80},{112,96},{17,1},{33... | collective-permute-start | bytes 12296 | tf_op jit(solution)/shard_map/ppermute | solution.py:26
  24.1 33.1 %all-to-all-start = ((f32[128,1,640]{2,1,0:T(1,128)}), f32[128,1,640]{2,1,0:T(1,128)S(1)}, u32[]{:S(2)}, u32[]{:S(2)}) async-start(f32[128,1,640]{2,1,0:T(1,128)} %copy.32), calls=%async_computation | async-start | bytes 655360 | tf_op jit(solution)/shard_map/all_to_all | solution.py:274
  35.6 0.6 copy-start.9
  35.6 0.6 copy-start.10
  35.6 0.6 copy-start.3
  35.6 0.6 copy-start
  46.1 8.2 %copy-start.14 = (f32[2,512]{1,0:T(2,128)S(1)}, f32[2,512]{1,0:T(2,128)}, u32[]{:S(2)}) copy-start(f32[2,512]{1,0:T(2,128)} %get-tuple-element.34) | copy-start | bytes 12292
  46.1 13.2 %collective-permute-start.6 = (f32[5,512]{1,0:T(8,128)}, f32[5,512]{1,0:T(8,128)S(1)}, u32[]{:S(2)}, u32[]{:S(2)}) collective-permute-start(f32[5,512]{1,0:T(8,128)} %get-tuple-element.35), channel_id=1, source_target_pairs={{0,1},{1,2},{2,3},{3,4},{4,5},{5,6},{6,7},{7,8},{8,9},{9,10},{10,1... | collective-permute-start | bytes 30728 | tf_op jit(solution)/shard_map/ppermute | solution.py:26
  49.3 9.9 %collective-permute-start.7 = (f32[5,512]{1,0:T(8,128)}, f32[5,512]{1,0:T(8,128)S(1)}, u32[]{:S(2)}, u32[]{:S(2)}) collective-permute-start(f32[5,512]{1,0:T(8,128)} %get-tuple-element.36), channel_id=1, source_target_pairs={{0,16},{16,32},{32,48},{48,64},{64,80},{80,96},{96,112},{1,17},{17... | collective-permute-start | bytes 30728 | tf_op jit(solution)/shard_map/ppermute | solution.py:26
  53.0 4.6 %collective-permute-start.4 = (f32[2,512]{1,0:T(2,128)}, f32[2,512]{1,0:T(2,128)S(1)}, u32[]{:S(2)}, u32[]{:S(2)}) collective-permute-start(f32[2,512]{1,0:T(2,128)} %get-tuple-element.33), channel_id=1, source_target_pairs={{1,0},{2,1},{3,2},{4,3},{5,4},{6,5},{7,6},{8,7},{9,8},{10,9},{11,1... | collective-permute-start | bytes 12296 | tf_op jit(solution)/shard_map/ppermute | solution.py:26
  54.3 4.9 %collective-permute-start.5 = (f32[2,512]{1,0:T(2,128)S(1)}, f32[2,512]{1,0:T(2,128)S(1)}, u32[]{:S(2)}, u32[]{:S(2)}) collective-permute-start(f32[2,512]{1,0:T(2,128)S(1)} %copy-done.14), channel_id=1, source_target_pairs={{16,0},{32,16},{48,32},{64,48},{80,64},{96,80},{112,96},{17,1},{33... | collective-permute-start | bytes 12296 | tf_op jit(solution)/shard_map/ppermute | solution.py:26
  57.6 1.7 %copy-start.7 = (f32[2,512]{1,0:T(2,128)}, f32[2,512]{1,0:T(2,128)S(1)}, u32[]{:S(2)}) copy-start(f32[2,512]{1,0:T(2,128)S(1)} %collective-permute-done.4.east_ref) | copy-start | bytes 12292
  59.2 0.6 copy-start.8
  59.2 0.6 copy-start.1
  59.3 0.6 copy-start.2
  60.2 21.4 %all-to-all-start.1 = ((f32[128,4,128]{2,1,0:T(4,128)}), f32[128,4,128]{2,1,0:T(4,128)S(1)}, u32[]{:S(2)}, u32[]{:S(2)}) async-start(f32[128,4,128]{2,1,0:T(4,128)} %bitcast.8), calls=%async_computation.1 | async-start | bytes 524288 | tf_op jit(solution)/shard_map/all_to_all | solution.py:323
  70.7 11.2 %collective-permute-start.8 = (f32[8,128]{1,0:T(8,128)S(1)}, f32[8,128]{1,0:T(8,128)S(1)}, u32[]{:S(2)}, u32[]{:S(2)}) collective-permute-start(f32[8,128]{1,0:T(8,128)S(1)} %fusion.13), channel_id=1, source_target_pairs={{0,1},{1,2},{2,3},{3,4},{4,5},{5,6},{6,7},{7,8},{8,9},{9,10},{10,1... | collective-permute-start | bytes 12296 | tf_op jit(solution)/shard_map/ppermute | solution.py:26

commit v13 on v11

--- a/solution.py
+++ b/solution.py
@@ -241,7 +241,7 @@
     gather_onehot = (
         lax.iota(jnp.int32, device_count * slot_cap)[:, None] == send_pos[None, :]
     ).astype(f32)
-    send_ids = jnp.dot(gather_onehot, local_ids + 1.0, precision=lax.Precision.HIGHEST) - 1.0
+    send_ids = jnp.dot(gather_onehot, local_ids + 1.0, precision=lax.Precision.DEFAULT) - 1.0
     lane_blocks = cell_cols // 128
     row_pos = send_pos.reshape(cell_rows // STRIP, lane_blocks).T.reshape(-1)
     row_onehot = (
@@ -255,7 +255,7 @@
     ).reshape(device_count, id_rows, reach_width)
     def start_lateral(parts, with_ids=True):
         packed = [
-            jnp.dot(row_onehot, part, precision=lax.Precision.HIGHEST).reshape(
+            jnp.dot(row_onehot, part, precision=lax.Precision.HIGH).reshape(
                 device_count, slot_cap, reach_width
             )
             for part in parts

time: 79.2 us -> 78.9 us (level)
  transfers between devices with their start and end apart: 11 -> 11, of which waited for: 1 -> 2; matrix products, arithmetic and copies ran while one was open for 9% -> 8% of each run, Pallas kernels for 19% -> 19%
where the time goes in v13:
time: 78.9 us; the launch traced here: 78.2 us
  starting transfers between devices  46.9 us (59%)
  Pallas kernels  18.4 us (23%)
  local copies, waits for them, and re-layouts  5.26 us (7%)
  matrix products  4.46 us (6%)
  other arithmetic  1.88 us (2%)
  between operations  1.1 us (1%)
    ppermute x9, starting transfers between devices, shifted(): lax.ppermute(value, axis, [(source, source + steps) for source in range(f...  24.8 us
    pallas_call x2, Pallas kernels, body(): step_call(not last)  15.2 us
    all_to_all x1, starting transfers between devices, body(): lax.all_to_all(start_lateral(tile_parts).reshape(device_count, first_rows...  11.4 us
    all_to_all x1, starting transfers between devices, body(): got_second = lax.all_to_all(lateral_started, ('gy', 'gx'), 0, 0, tiled=True)  10.7 us
    pallas_call x1, Pallas kernels, body(): pl.pallas_call(edge_kernel, grid=(1,), out_shape=(tile_shape,) + edge_sha...  3.29 us
    unnamed x35, local copies, waits for them, and re-layouts  2.31 us
    dot_general x2, matrix products, start_lateral(): jnp.dot(row_onehot, part, precision=lax.Precision.HIGH)  2.23 us
    dot_general x4, matrix products, block_term(): jnp.einsum('tb,tc->bc', onehot, values, precision=lax.Precision.HIGHEST)  1.61 us
  transfers between devices with their start and end apart: 11, of which 2 were waited for; matrix products, arithmetic and copies ran while one was open for 8% of the time, Pallas kernels for 19%

profile of v13, /device:TPU:1, one launch (start us, length us, event | category | flops | bytes accessed | tf_op | source)
XLA Modules:
  0.0 78.2 jit_solution(10109965779021906985)
XLA Ops:
  0.7 0.7 copy-done.7
  1.4 0.2 fusion.19
  1.6 0.6 add_convert_fusion.flags_ref
  2.2 3.3 %shard_map.129 = (f32[256,128]{1,0:T(8,128)}, f32[2,512]{1,0:T(2,128)}, f32[2,512]{1,0:T(2,128)}, f32[5,512]{1,0:T(8,128)}, f32[5,512]{1,0:T(8,128)}) custom-call(s32[3]{0:T(128)} %add_convert_fusion.flags_ref, f32[512,512]{1,0:T(8,128)} %d_ref.3, s32[512,512]{1,0:T(8,128)} %land_ref.5, f32[512,512]{1,0:T(8,128)} %bed_ref.3, f32[512,512]{1,0:T(8,128)} %bed_ref.3, ...), custom_call_target="tpu_custom_call" | custom-call | tf_op jit(solution)/shard_map/pallas_call | solution.py:210
  5.5 0.7 pad_maximum_fusion.1
  6.3 4.0 %collective-permute-start.2 = (f32[7,512]{1,0:T(8,128)S(1)}, f32[7,512]{1,0:T(8,128)S(1)}, u32[]{:S(2)}, u32[]{:S(2)}) collective-permute-start(f32[7,512]{1,0:T(8,128)S(1)} %pad_maximum_fusion.1), channel_id=1, source_target_pairs={{0,1},{1,2},{2,3},{3,4},{4,5},{5,6},{6,7},{7,8},{8,9},{9,10},{10,1... | collective-permute-start | bytes 43016 | tf_op jit(solution)/shard_map/ppermute | solution.py:26
  10.3 4.0 %collective-permute-start.3 = (f32[5,512]{1,0:T(8,128)S(1)}, f32[5,512]{1,0:T(8,128)S(1)}, u32[]{:S(2)}, u32[]{:S(2)}) collective-permute-start(f32[5,512]{1,0:T(8,128)S(1)} %copy-done.12), channel_id=1, source_target_pairs={{0,16},{16,32},{32,48},{48,64},{64,80},{80,96},{96,112},{1,17},{17... | collective-permute-start | bytes 30728 | tf_op jit(solution)/shard_map/ppermute | solution.py:26
  14.3 1.3 %collective-permute-start = (f32[2,512]{1,0:T(2,128)S(1)}, f32[2,512]{1,0:T(2,128)S(1)}, u32[]{:S(2)}, u32[]{:S(2)}) collective-permute-start(f32[2,512]{1,0:T(2,128)S(1)} %copy-done.14), channel_id=1, source_target_pairs={{1,0},{2,1},{3,2},{4,3},{5,4},{6,5},{7,6},{8,7},{9,8},{10,9},{11,1... | collective-permute-start | bytes 12296 | tf_op jit(solution)/shard_map/ppermute | solution.py:26
  15.6 1.9 %collective-permute-start.1 = (f32[2,512]{1,0:T(2,128)S(1)}, f32[2,512]{1,0:T(2,128)S(1)}, u32[]{:S(2)}, u32[]{:S(2)}) collective-permute-start(f32[2,512]{1,0:T(2,128)S(1)} %copy-done.13), channel_id=1, source_target_pairs={{16,0},{32,16},{48,32},{64,48},{80,64},{96,80},{112,96},{17,1},{33... | collective-permute-start | bytes 12296 | tf_op jit(solution)/shard_map/ppermute | solution.py:26
  17.7 0.2 fusion.6
  18.5 0.4 copy-done
  18.9 0.3 fusion
  19.4 0.2 fusion.2
  19.9 0.9 %copy.32 = f32[128,1,640]{2,1,0:T(1,128)} copy(f32[128,1,640]{0,2,1:T(8,128)S(1)} %bitcast.39) | data formatting | bytes 655360 | tf_op jit(solution)/shard_map/all_to_all | solution.py:266
  20.8 11.4 %all-to-all-start = ((f32[128,1,640]{2,1,0:T(1,128)}), f32[128,1,640]{2,1,0:T(1,128)S(1)}, u32[]{:S(2)}, u32[]{:S(2)}) async-start(f32[128,1,640]{2,1,0:T(1,128)} %copy.32), calls=%async_computation | async-start | bytes 655360 | tf_op jit(solution)/shard_map/all_to_all | solution.py:266
  32.2 0.2 fusion.15
  32.5 0.5 copy-done.8
  33.1 7.7 %shard_map.130 = (f32[512,512]{1,0:T(8,128)}, f32[512,512]{1,0:T(8,128)}, f32[512,512]{1,0:T(8,128)}, f32[256,128]{1,0:T(8,128)}, f32[2,512]{1,0:T(2,128)}, /*in...) custom-call(s32[3]{0:T(128)} %add_convert_fusion.flags_ref, f32[512,512]{1,0:T(8,128)} %d_ref.3, ...), custom_call_target="tpu_custom_call" | custom-call | tf_op jit(solution)/shard_map/pallas_call | solution.py:306
  40.9 3.3 %collective-permute-start.6 = (f32[5,512]{1,0:T(8,128)}, f32[5,512]{1,0:T(8,128)S(1)}, u32[]{:S(2)}, u32[]{:S(2)}) collective-permute-start(f32[5,512]{1,0:T(8,128)} %get-tuple-element.35), channel_id=1, source_target_pairs={{0,1},{1,2},{2,3},{3,4},{4,5},{5,6},{6,7},{7,8},{8,9},{9,10},{10,1... | collective-permute-start | bytes 30728 | tf_op jit(solution)/shard_map/ppermute | solution.py:26
  44.1 3.7 %collective-permute-start.7 = (f32[5,512]{1,0:T(8,128)}, f32[5,512]{1,0:T(8,128)S(1)}, u32[]{:S(2)}, u32[]{:S(2)}) collective-permute-start(f32[5,512]{1,0:T(8,128)} %get-tuple-element.36), channel_id=1, source_target_pairs={{0,16},{16,32},{32,48},{48,64},{64,80},{80,96},{96,112},{1,17},{17... | collective-permute-start | bytes 30728 | tf_op jit(solution)/shard_map/ppermute | solution.py:26
  47.8 1.3 %collective-permute-start.4 = (f32[2,512]{1,0:T(2,128)}, f32[2,512]{1,0:T(2,128)S(1)}, u32[]{:S(2)}, u32[]{:S(2)}) collective-permute-start(f32[2,512]{1,0:T(2,128)} %get-tuple-element.33), channel_id=1, source_target_pairs={{1,0},{2,1},{3,2},{4,3},{5,4},{6,5},{7,6},{8,7},{9,8},{10,9},{11,1... | collective-permute-start | bytes 12296 | tf_op jit(solution)/shard_map/ppermute | solution.py:26
  49.1 1.9 %collective-permute-start.5 = (f32[2,512]{1,0:T(2,128)S(1)}, f32[2,512]{1,0:T(2,128)S(1)}, u32[]{:S(2)}, u32[]{:S(2)}) collective-permute-start(f32[2,512]{1,0:T(2,128)S(1)} %copy-done.15), channel_id=1, source_target_pairs={{16,0},{32,16},{48,32},{64,48},{80,64},{96,80},{112,96},{17,1},{33... | collective-permute-start | bytes 12296 | tf_op jit(solution)/shard_map/ppermute | solution.py:26
  51.0 1.9 %fusion.1 = f32[512,128]{1,0:T(8,128)} fusion(f32[256,128]{1,0:T(8,128)} %get-tuple-element.37, s32[256]{0:T(256)S(1)} %eq.131), kind=kOutput, calls=%fused_computation.5 | convolution fusion | flops 100794368 | bytes 394240 | tf_op jit(solution)/shard_map/dot_general | solution.py:258
  53.0 0.7 slice.30
  54.1 0.4 copy-done.10
  55.0 10.7 %all-to-all-start.1 = ((f32[128,4,128]{2,1,0:T(4,128)}), f32[128,4,128]{2,1,0:T(4,128)S(1)}, u32[]{:S(2)}, u32[]{:S(2)}) async-start(f32[128,4,128]{2,1,0:T(4,128)} %bitcast.8), calls=%async_computation.1 | async-start | bytes 524288 | tf_op jit(solution)/shard_map/all_to_all | solution.py:315
  65.7 0.2 add_add_fusion.1
  65.9 0.3 fusion.17
  66.2 3.4 %collective-permute-start.8 = (f32[8,128]{1,0:T(8,128)S(1)}, f32[8,128]{1,0:T(8,128)S(1)}, u32[]{:S(2)}, u32[]{:S(2)}) collective-permute-start(f32[8,128]{1,0:T(8,128)S(1)} %fusion.17), channel_id=1, source_target_pairs={{0,1},{1,2},{2,3},{3,4},{4,5},{5,6},{6,7},{7,8},{8,9},{9,10},{10,1... | collective-permute-start | bytes 12296 | tf_op jit(solution)/shard_map/ppermute | solution.py:26
  69.7 7.4 %shard_map.131 = (f32[512,512]{1,0:T(8,128)}, f32[512,512]{1,0:T(8,128)}, f32[512,512]{1,0:T(8,128)}) custom-call(s32[3]{0:T(128)} %add_convert_fusion.flags_ref, f32[512,512]{1,0:T(8,128)} %get-tuple-element.30.d_ref, f32[512,512]{1,0:T(8,128)} %get-tuple-element.31.e_ref, f32[512,512]{1,0:T(8,128)} %get-tuple-element.32.s_ref, f32[512,512]{1,0:T(8,128)} %bed_ref.3, ...), custom_call_target="tpu_custom_call" | custom-call | tf_op jit(solution)/shard_map/pallas_call | solution.py:306
  77.2 0.2 convolution_multiply_fusion
  77.4 0.9 %add_add_fusion = f32[16,128]{1,0:T(8,128)} fusion(f32[16,128]{1,0:T(8,128)S(1)} %convolution_multiply_fusion, f32[8,128]{1,0:T(8,128)S(1)} %collective-permute-done.8, f32[16,128]{1,0:T(8,128)S(1)} %add_add_fusion.1, s32[16]{0:T(128)S(1)} %iota_add_fusion, s32[16]{0:T(128)S(1)} %copy-done.16, f32[16,128]{1,0:T(8,128)S(1)} %copy-done.7), kind=kOutput, calls=%fused_computation.34 | convolution fusion | flops 418048 | bytes 36992 | tf_op jit(solution)/shard_map/tb,tc->bc/dot_general | solution.py:40
  (73 shorter events, 2.2 us)
Async XLA Ops:
  0.6 0.7 copy-start.7
  0.6 0.7 copy-start.6
  0.7 0.7 copy-start.16
  5.5 4.8 %copy-start.12 = (f32[5,512]{1,0:T(8,128)S(1)}, f32[5,512]{1,0:T(8,128)}, u32[]{:S(2)}) copy-start(f32[5,512]{1,0:T(8,128)} %get-tuple-element.29) | copy-start | bytes 30724
  5.5 8.8 %copy-start.14 = (f32[2,512]{1,0:T(2,128)S(1)}, f32[2,512]{1,0:T(2,128)}, u32[]{:S(2)}) copy-start(f32[2,512]{1,0:T(2,128)} %get-tuple-element.26) | copy-start | bytes 12292
  6.3 9.3 %copy-start.13 = (f32[2,512]{1,0:T(2,128)S(1)}, f32[2,512]{1,0:T(2,128)}, u32[]{:S(2)}) copy-start(f32[2,512]{1,0:T(2,128)} %get-tuple-element.27) | copy-start | bytes 12292
  6.3 26.2 %collective-permute-start.2 = (f32[7,512]{1,0:T(8,128)S(1)}, f32[7,512]{1,0:T(8,128)S(1)}, u32[]{:S(2)}, u32[]{:S(2)}) collective-permute-start(f32[7,512]{1,0:T(8,128)S(1)} %pad_maximum_fusion.1), channel_id=1, source_target_pairs={{0,1},{1,2},{2,3},{3,4},{4,5},{5,6},{6,7},{7,8},{8,9},{9,10},{10,1... | collective-permute-start | bytes 43016 | tf_op jit(solution)/shard_map/ppermute | solution.py:26
  10.3 22.2 %collective-permute-start.3 = (f32[5,512]{1,0:T(8,128)S(1)}, f32[5,512]{1,0:T(8,128)S(1)}, u32[]{:S(2)}, u32[]{:S(2)}) collective-permute-start(f32[5,512]{1,0:T(8,128)S(1)} %copy-done.12), channel_id=1, source_target_pairs={{0,16},{16,32},{32,48},{48,64},{64,80},{80,96},{96,112},{1,17},{17... | collective-permute-start | bytes 30728 | tf_op jit(solution)/shard_map/ppermute | solution.py:26
  14.3 3.3 %copy-start.5 = (s32[256]{0:T(256)S(1)}, s32[256]{0:T(256)}, u32[]{:S(2)}) copy-start(s32[256]{0:T(256)} %param.16) | copy-start | bytes 3076
  14.3 18.1 %collective-permute-start = (f32[2,512]{1,0:T(2,128)S(1)}, f32[2,512]{1,0:T(2,128)S(1)}, u32[]{:S(2)}, u32[]{:S(2)}) collective-permute-start(f32[2,512]{1,0:T(2,128)S(1)} %copy-done.14), channel_id=1, source_target_pairs={{1,0},{2,1},{3,2},{4,3},{5,4},{6,5},{7,6},{8,7},{9,8},{10,9},{11,1... | collective-permute-start | bytes 12296 | tf_op jit(solution)/shard_map/ppermute | solution.py:26
  15.6 16.8 %collective-permute-start.1 = (f32[2,512]{1,0:T(2,128)S(1)}, f32[2,512]{1,0:T(2,128)S(1)}, u32[]{:S(2)}, u32[]{:S(2)}) collective-permute-start(f32[2,512]{1,0:T(2,128)S(1)} %copy-done.13), channel_id=1, source_target_pairs={{16,0},{32,16},{48,32},{64,48},{80,64},{96,80},{112,96},{17,1},{33... | collective-permute-start | bytes 12296 | tf_op jit(solution)/shard_map/ppermute | solution.py:26
  18.0 0.9 %copy-start = (f32[256,128]{1,0:T(8,128)S(1)}, f32[256,128]{1,0:T(8,128)}, u32[]{:S(2)}) copy-start(f32[256,128]{1,0:T(8,128)} %get-tuple-element.38) | copy-start | bytes 393220
  20.8 32.9 %all-to-all-start = ((f32[128,1,640]{2,1,0:T(1,128)}), f32[128,1,640]{2,1,0:T(1,128)S(1)}, u32[]{:S(2)}, u32[]{:S(2)}) async-start(f32[128,1,640]{2,1,0:T(1,128)} %copy.32), calls=%async_computation | async-start | bytes 655360 | tf_op jit(solution)/shard_map/all_to_all | solution.py:266
  32.5 0.6 copy-start.8
  32.5 0.6 copy-start.9
  32.5 0.6 copy-start.2
  32.5 0.6 copy-start.1
  40.9 8.2 %copy-start.15 = (f32[2,512]{1,0:T(2,128)S(1)}, f32[2,512]{1,0:T(2,128)}, u32[]{:S(2)}) copy-start(f32[2,512]{1,0:T(2,128)} %get-tuple-element.34) | copy-start | bytes 12292
  40.9 13.2 %collective-permute-start.6 = (f32[5,512]{1,0:T(8,128)}, f32[5,512]{1,0:T(8,128)S(1)}, u32[]{:S(2)}, u32[]{:S(2)}) collective-permute-start(f32[5,512]{1,0:T(8,128)} %get-tuple-element.35), channel_id=1, source_target_pairs={{0,1},{1,2},{2,3},{3,4},{4,5},{5,6},{6,7},{7,8},{8,9},{9,10},{10,1... | collective-permute-start | bytes 30728 | tf_op jit(solution)/shard_map/ppermute | solution.py:26
  44.1 9.9 %collective-permute-start.7 = (f32[5,512]{1,0:T(8,128)}, f32[5,512]{1,0:T(8,128)S(1)}, u32[]{:S(2)}, u32[]{:S(2)}) collective-permute-start(f32[5,512]{1,0:T(8,128)} %get-tuple-element.36), channel_id=1, source_target_pairs={{0,16},{16,32},{32,48},{48,64},{64,80},{80,96},{96,112},{1,17},{17... | collective-permute-start | bytes 30728 | tf_op jit(solution)/shard_map/ppermute | solution.py:26
  47.8 6.1 %collective-permute-start.4 = (f32[2,512]{1,0:T(2,128)}, f32[2,512]{1,0:T(2,128)S(1)}, u32[]{:S(2)}, u32[]{:S(2)}) collective-permute-start(f32[2,512]{1,0:T(2,128)} %get-tuple-element.33), channel_id=1, source_target_pairs={{1,0},{2,1},{3,2},{4,3},{5,4},{6,5},{7,6},{8,7},{9,8},{10,9},{11,1... | collective-permute-start | bytes 12296 | tf_op jit(solution)/shard_map/ppermute | solution.py:26
  49.1 4.9 %collective-permute-start.5 = (f32[2,512]{1,0:T(2,128)S(1)}, f32[2,512]{1,0:T(2,128)S(1)}, u32[]{:S(2)}, u32[]{:S(2)}) collective-permute-start(f32[2,512]{1,0:T(2,128)S(1)} %copy-done.15), channel_id=1, source_target_pairs={{16,0},{32,16},{48,32},{64,48},{80,64},{96,80},{112,96},{17,1},{33... | collective-permute-start | bytes 12296 | tf_op jit(solution)/shard_map/ppermute | solution.py:26
  53.9 0.6 copy-start.10
  54.0 0.6 copy-start.11
  54.0 0.6 copy-start.3
  54.1 0.6 copy-start.4
  55.0 22.1 %all-to-all-start.1 = ((f32[128,4,128]{2,1,0:T(4,128)}), f32[128,4,128]{2,1,0:T(4,128)S(1)}, u32[]{:S(2)}, u32[]{:S(2)}) async-start(f32[128,4,128]{2,1,0:T(4,128)} %bitcast.8), calls=%async_computation.1 | async-start | bytes 524288 | tf_op jit(solution)/shard_map/all_to_all | solution.py:315
  66.2 11.2 %collective-permute-start.8 = (f32[8,128]{1,0:T(8,128)S(1)}, f32[8,128]{1,0:T(8,128)S(1)}, u32[]{:S(2)}, u32[]{:S(2)}) collective-permute-start(f32[8,128]{1,0:T(8,128)S(1)} %fusion.17), channel_id=1, source_target_pairs={{0,1},{1,2},{2,3},{3,4},{4,5},{5,6},{6,7},{7,8},{8,9},{9,10},{10,1... | collective-permute-start | bytes 12296 | tf_op jit(solution)/shard_map/ppermute | solution.py:26

commit v14 on v13

--- a/solution.py
+++ b/solution.py
@@ -88,7 +88,7 @@
 
 
 def edge_kernel(flags_ref, d_ref, land_ref, bed_first_col, bed_last_col, bed_first_row,
-                bed_last_row, e_ref, s_ref, r_col, r_row,
+                bed_last_row, e_ref, s_ref, r_col, r_row, ahead_ref,
                 tile_out, to_west, to_north, to_east, to_south):
     ny, nx = d_ref.shape
     depth = d_ref[...]
@@ -105,6 +105,12 @@
     to_east[2:3, :] = last_col_row(depth)
     to_east[3:4, :] = last_col_row(r_col[...])
     to_east[4:5, :] = last_col_row(eopen)
+    ahead = ahead_ref[...]
+    per_row = ny // ahead.shape[1]
+    for j in range(ahead.shape[0] // per_row):
+        to_east[5 + j:6 + j, :] = jnp.concatenate(
+            [ahead[j * per_row + m:j * per_row + m + 1, :] for m in range(per_row)], axis=1
+        )
     to_south[0:1, :] = s_ref[-1:, :]
     to_south[1:2, :] = bed_last_row[-1:, :] + depth[-1:, :]
     to_south[2:3, :] = depth[-1:, :]
@@ -202,22 +208,33 @@
     grid_shape = jax.ShapeDtypeStruct((cell_rows, cell_cols), f32)
     smem_spec = pl.BlockSpec(memory_space=pltpu.SMEM)
 
+    def reach_outflow(storage):
+        ratio = reach_rate * jnp.power(storage, 2.0 / 3.0)
+        outflow = storage * ratio / (1.0 + ratio)
+        own_part = block_term(downstream, outflow, first_block, block_rows)
+        ahead_part = block_term(downstream, outflow, first_block + block_rows, SPAN)
+        return outflow, own_part, ahead_part
+
+    first_outflow = reach_outflow(storage)
+    ahead_rows = SPAN * reach_width // cell_cols
     col_blocks = cell_cols // 128
     row_blocks = cell_rows // 8
     col_spec = lambda k: pl.BlockSpec((cell_rows, 128), lambda i: (0, k))
     row_spec = lambda k: pl.BlockSpec((8, cell_cols), lambda i: (k, 0))
     tile_shape = jax.ShapeDtypeStruct((cell_rows // STRIP * cell_cols // 128, 128), f32)
+    first_shapes = list(edge_shapes(cell_rows, cell_cols))
+    first_shapes[2] = jax.ShapeDtypeStruct((5 + ahead_rows, cell_rows), f32)
     tiles, *edges = pl.pallas_call(
         edge_kernel,
         grid=(1,),
-        out_shape=(tile_shape,) + edge_shapes(cell_rows, cell_cols),
+        out_shape=(tile_shape,) + tuple(first_shapes),
         in_specs=[smem_spec] + vmem_specs(2)
         + [col_spec(0), col_spec(col_blocks - 1), row_spec(0), row_spec(row_blocks - 1),
            col_spec(col_blocks - 1), row_spec(row_blocks - 1),
-           col_spec(col_blocks - 1), row_spec(row_blocks - 1)],
+           col_spec(col_blocks - 1), row_spec(row_blocks - 1)] + vmem_specs(1),
         out_specs=vmem_specs(5),
     )(flags, water_depth, land_mask, bed_level, bed_level, bed_level, bed_level,
-      flux_east, flux_south, roughness, roughness)
+      flux_east, flux_south, roughness, roughness, first_outflow[2])
     tile_parts = [tiles]
 
     def step_call(with_edges):
@@ -268,30 +285,14 @@
         ("gy", "gx"), 0, 0, tiled=True,
     ).reshape(device_count, first_rows, reach_width)
 
-    def reach_outflow(storage):
-        ratio = reach_rate * jnp.power(storage, 2.0 / 3.0)
-        outflow = storage * ratio / (1.0 + ratio)
-        own_part = block_term(downstream, outflow, first_block, block_rows)
-        ahead_part = block_term(downstream, outflow, first_block + block_rows, SPAN)
-        return outflow, own_part, ahead_part
-
-    first_outflow = reach_outflow(storage)
-    ahead_rows = SPAN * reach_width // cell_cols
     depth = water_depth
     for step in range(STEPS):
         to_west, to_north, to_east, to_south = edges
         east_in = shifted(to_west, "gx", -1)
         south_in = shifted(to_north, "gy", -1)
         if step == 0:
-            joined = shifted(
-                jnp.concatenate(
-                    [to_east, first_outflow[2].reshape(ahead_rows, cell_cols)], axis=0
-                ),
-                ("gy", "gx"),
-                1,
-            )
-            west_in = joined[: to_east.shape[0]]
-            first_ahead = joined[to_east.shape[0]:].reshape(SPAN, reach_width)
+            west_in = shifted(to_east, ("gy", "gx"), 1)
+            first_ahead = west_in[5:].reshape(SPAN, reach_width)
         else:
             west_in = shifted(to_east, "gx", 1)
         north_in = shifted(to_south, "gy", 1)

time: 78.9 us -> 78.6 us (level)
    unnamed x35 -> x31, local copies, waits for them, and re-layouts: 2.31 us -> 2.22 us
where the time goes in v14:
time: 78.6 us; the launch traced here: 78 us
  starting transfers between devices  46.8 us (60%)
  Pallas kernels  18.4 us (23%)
  local copies, waits for them, and re-layouts  5.16 us (7%)
  matrix products  5.05 us (6%)
  other arithmetic  1.19 us (2%)
  between operations  1.07 us (1%)
    ppermute x9, starting transfers between devices, shifted(): lax.ppermute(value, axis, [(source, source + steps) for source in range(f...  24.8 us
    pallas_call x2, Pallas kernels, body(): step_call(not last)  15.2 us
    all_to_all x1, starting transfers between devices, body(): lax.all_to_all(start_lateral(tile_parts).reshape(device_count, first_rows...  11.4 us
    all_to_all x1, starting transfers between devices, body(): got_second = lax.all_to_all(lateral_started, ('gy', 'gx'), 0, 0, tiled=True)  10.7 us
    pallas_call x1, Pallas kernels, body(): pl.pallas_call(edge_kernel, grid=(1,), out_shape=(tile_shape,) + tuple(fi...  3.29 us
    unnamed x31, local copies, waits for them, and re-layouts  2.22 us
    dot_general x4, matrix products, block_term(): jnp.einsum('tb,tc->bc', onehot, values, precision=lax.Precision.HIGHEST)  2.22 us
    dot_general x2, matrix products, start_lateral(): jnp.dot(row_onehot, part, precision=lax.Precision.HIGH)  2.21 us
  transfers between devices with their start and end apart: 11, of which 2 were waited for; matrix products, arithmetic and copies ran while one was open for 8% of the time, Pallas kernels for 19%

profile of v14, /device:TPU:1, one launch (start us, length us, event | category | flops | bytes accessed | tf_op | source)
XLA Modules:
  0.0 78.0 jit_solution(11274163811490891522)
XLA Ops:
  0.7 0.7 add_convert_fusion.flags_ref
  1.4 0.9 %fusion.19.ahead_ref = f32[8,128]{1,0:T(8,128)} fusion(s32[8]{0:T(128)S(1)} %iota_add_fusion.1, s32[16]{0:T(128)S(1)} %copy-done.14, f32[16,128]{1,0:T(8,128)S(1)} %copy-done.6, f32[16,128]{1,0:T(8,128)S(1)} %copy-done.7), kind=kOutput, calls=%fused_computation.31 | convolution fusion | flops 204928 | bytes 20576 | tf_op jit(solution)/shard_map/tb,tc->bc/dot_general | solution.py:40
  2.2 3.3 %shard_map.129 = (f32[256,128]{1,0:T(8,128)}, f32[2,512]{1,0:T(2,128)}, f32[2,512]{1,0:T(2,128)}, f32[7,512]{1,0:T(8,128)}, f32[5,512]{1,0:T(8,128)}) custom-call(s32[3]{0:T(128)} %add_convert_fusion.flags_ref, f32[512,512]{1,0:T(8,128)} %d_ref.3, s32[512,512]{1,0:T(8,128)} %land_ref.5, f32[512,512]{1,0:T(8,128)} %bed_ref.3, f32[512,512]{1,0:T(8,128)} %bed_ref.3, ...), custom_call_target="tpu_custom_call" | custom-call | tf_op jit(solution)/shard_map/pallas_call | solution.py:227
  5.5 4.0 %collective-permute-start.2 = (f32[7,512]{1,0:T(8,128)}, f32[7,512]{1,0:T(8,128)S(1)}, u32[]{:S(2)}, u32[]{:S(2)}) collective-permute-start(f32[7,512]{1,0:T(8,128)} %get-tuple-element.28), channel_id=1, source_target_pairs={{0,1},{1,2},{2,3},{3,4},{4,5},{5,6},{6,7},{7,8},{8,9},{9,10},{10,1... | collective-permute-start | bytes 43016 | tf_op jit(solution)/shard_map/ppermute | solution.py:26
  9.5 4.0 %collective-permute-start.3 = (f32[5,512]{1,0:T(8,128)}, f32[5,512]{1,0:T(8,128)S(1)}, u32[]{:S(2)}, u32[]{:S(2)}) collective-permute-start(f32[5,512]{1,0:T(8,128)} %get-tuple-element.29), channel_id=1, source_target_pairs={{0,16},{16,32},{32,48},{48,64},{64,80},{80,96},{96,112},{1,17},{17... | collective-permute-start | bytes 30728 | tf_op jit(solution)/shard_map/ppermute | solution.py:26
  13.5 1.3 %collective-permute-start = (f32[2,512]{1,0:T(2,128)}, f32[2,512]{1,0:T(2,128)S(1)}, u32[]{:S(2)}, u32[]{:S(2)}) collective-permute-start(f32[2,512]{1,0:T(2,128)} %get-tuple-element.26), channel_id=1, source_target_pairs={{1,0},{2,1},{3,2},{4,3},{5,4},{6,5},{7,6},{8,7},{9,8},{10,9},{11,1... | collective-permute-start | bytes 12296 | tf_op jit(solution)/shard_map/ppermute | solution.py:26
  14.8 1.9 %collective-permute-start.1 = (f32[2,512]{1,0:T(2,128)S(1)}, f32[2,512]{1,0:T(2,128)S(1)}, u32[]{:S(2)}, u32[]{:S(2)}) collective-permute-start(f32[2,512]{1,0:T(2,128)S(1)} %copy-done.12), channel_id=1, source_target_pairs={{16,0},{32,16},{48,32},{64,48},{80,64},{96,80},{112,96},{17,1},{33... | collective-permute-start | bytes 12296 | tf_op jit(solution)/shard_map/ppermute | solution.py:26
  16.9 0.2 fusion.6
  17.7 0.4 copy-done
  18.1 0.3 fusion
  18.6 0.2 fusion.2
  19.1 0.9 %copy.32 = f32[128,1,640]{2,1,0:T(1,128)} copy(f32[128,1,640]{0,2,1:T(8,128)S(1)} %bitcast.38) | data formatting | bytes 655360 | tf_op jit(solution)/shard_map/all_to_all | solution.py:283
  20.0 11.4 %all-to-all-start = ((f32[128,1,640]{2,1,0:T(1,128)}), f32[128,1,640]{2,1,0:T(1,128)S(1)}, u32[]{:S(2)}, u32[]{:S(2)}) async-start(f32[128,1,640]{2,1,0:T(1,128)} %copy.32), calls=%async_computation | async-start | bytes 655360 | tf_op jit(solution)/shard_map/all_to_all | solution.py:283
  31.4 0.2 fusion.15
  31.7 0.5 copy-done.8
  32.3 0.6 copy-done.1
  32.9 7.7 %shard_map.130 = (f32[512,512]{1,0:T(8,128)}, f32[512,512]{1,0:T(8,128)}, f32[512,512]{1,0:T(8,128)}, f32[256,128]{1,0:T(8,128)}, f32[2,512]{1,0:T(2,128)}, /*in...) custom-call(s32[3]{0:T(128)} %add_convert_fusion.flags_ref, f32[512,512]{1,0:T(8,128)} %d_ref.3, ...), custom_call_target="tpu_custom_call" | custom-call | tf_op jit(solution)/shard_map/pallas_call | solution.py:307
  40.7 3.3 %collective-permute-start.6 = (f32[5,512]{1,0:T(8,128)}, f32[5,512]{1,0:T(8,128)S(1)}, u32[]{:S(2)}, u32[]{:S(2)}) collective-permute-start(f32[5,512]{1,0:T(8,128)} %get-tuple-element.35), channel_id=1, source_target_pairs={{0,1},{1,2},{2,3},{3,4},{4,5},{5,6},{6,7},{7,8},{8,9},{9,10},{10,1... | collective-permute-start | bytes 30728 | tf_op jit(solution)/shard_map/ppermute | solution.py:26
  43.9 3.7 %collective-permute-start.7 = (f32[5,512]{1,0:T(8,128)}, f32[5,512]{1,0:T(8,128)S(1)}, u32[]{:S(2)}, u32[]{:S(2)}) collective-permute-start(f32[5,512]{1,0:T(8,128)} %get-tuple-element.36), channel_id=1, source_target_pairs={{0,16},{16,32},{32,48},{48,64},{64,80},{80,96},{96,112},{1,17},{17... | collective-permute-start | bytes 30728 | tf_op jit(solution)/shard_map/ppermute | solution.py:26
  47.6 1.3 %collective-permute-start.4 = (f32[2,512]{1,0:T(2,128)}, f32[2,512]{1,0:T(2,128)S(1)}, u32[]{:S(2)}, u32[]{:S(2)}) collective-permute-start(f32[2,512]{1,0:T(2,128)} %get-tuple-element.33), channel_id=1, source_target_pairs={{1,0},{2,1},{3,2},{4,3},{5,4},{6,5},{7,6},{8,7},{9,8},{10,9},{11,1... | collective-permute-start | bytes 12296 | tf_op jit(solution)/shard_map/ppermute | solution.py:26
  48.9 1.9 %collective-permute-start.5 = (f32[2,512]{1,0:T(2,128)S(1)}, f32[2,512]{1,0:T(2,128)S(1)}, u32[]{:S(2)}, u32[]{:S(2)}) collective-permute-start(f32[2,512]{1,0:T(2,128)S(1)} %copy-done.13), channel_id=1, source_target_pairs={{16,0},{32,16},{48,32},{64,48},{80,64},{96,80},{112,96},{17,1},{33... | collective-permute-start | bytes 12296 | tf_op jit(solution)/shard_map/ppermute | solution.py:26
  50.8 1.9 %fusion.1 = f32[512,128]{1,0:T(8,128)} fusion(f32[256,128]{1,0:T(8,128)} %get-tuple-element.37, s32[256]{0:T(256)S(1)} %eq.131), kind=kOutput, calls=%fused_computation.5 | convolution fusion | flops 100794368 | bytes 394240 | tf_op jit(solution)/shard_map/dot_general | solution.py:275
  52.7 0.7 slice.25
  53.5 0.2 copy.33
  53.9 0.4 copy-done.10
  54.8 10.7 %all-to-all-start.1 = ((f32[128,4,128]{2,1,0:T(4,128)}), f32[128,4,128]{2,1,0:T(4,128)S(1)}, u32[]{:S(2)}, u32[]{:S(2)}) async-start(f32[128,4,128]{2,1,0:T(4,128)} %bitcast.8), calls=%async_computation.1 | async-start | bytes 524288 | tf_op jit(solution)/shard_map/all_to_all | solution.py:316
  65.5 0.2 add_add_fusion.1
  65.7 0.3 fusion.17
  66.0 3.4 %collective-permute-start.8 = (f32[8,128]{1,0:T(8,128)S(1)}, f32[8,128]{1,0:T(8,128)S(1)}, u32[]{:S(2)}, u32[]{:S(2)}) collective-permute-start(f32[8,128]{1,0:T(8,128)S(1)} %fusion.17), channel_id=1, source_target_pairs={{0,1},{1,2},{2,3},{3,4},{4,5},{5,6},{6,7},{7,8},{8,9},{9,10},{10,1... | collective-permute-start | bytes 12296 | tf_op jit(solution)/shard_map/ppermute | solution.py:26
  69.4 7.4 %shard_map.131 = (f32[512,512]{1,0:T(8,128)}, f32[512,512]{1,0:T(8,128)}, f32[512,512]{1,0:T(8,128)}) custom-call(s32[3]{0:T(128)} %add_convert_fusion.flags_ref, f32[512,512]{1,0:T(8,128)} %get-tuple-element.30.d_ref, f32[512,512]{1,0:T(8,128)} %get-tuple-element.31.e_ref, f32[512,512]{1,0:T(8,128)} %get-tuple-element.32.s_ref, f32[512,512]{1,0:T(8,128)} %bed_ref.3, ...), custom_call_target="tpu_custom_call" | custom-call | tf_op jit(solution)/shard_map/pallas_call | solution.py:307
  76.9 0.2 convolution_multiply_fusion
  77.1 0.9 %add_add_fusion = f32[16,128]{1,0:T(8,128)} fusion(f32[16,128]{1,0:T(8,128)S(1)} %convolution_multiply_fusion, f32[8,128]{1,0:T(8,128)S(1)} %collective-permute-done.8, f32[16,128]{1,0:T(8,128)S(1)} %add_add_fusion.1, s32[16]{0:T(128)S(1)} %iota_add_fusion, s32[16]{0:T(128)S(1)} %copy-done.14, f32[16,128]{1,0:T(8,128)S(1)} %copy-done.7), kind=kOutput, calls=%fused_computation.33 | convolution fusion | flops 418048 | bytes 36992 | tf_op jit(solution)/shard_map/tb,tc->bc/dot_general | solution.py:40
  (67 shorter events, 2.0 us)
Async XLA Ops:
  0.6 0.7 copy-start.7
  0.7 0.7 copy-start.6
  0.7 0.7 copy-start.14
  5.5 9.3 %copy-start.12 = (f32[2,512]{1,0:T(2,128)S(1)}, f32[2,512]{1,0:T(2,128)}, u32[]{:S(2)}) copy-start(f32[2,512]{1,0:T(2,128)} %get-tuple-element.27) | copy-start | bytes 12292
  5.5 26.2 %collective-permute-start.2 = (f32[7,512]{1,0:T(8,128)}, f32[7,512]{1,0:T(8,128)S(1)}, u32[]{:S(2)}, u32[]{:S(2)}) collective-permute-start(f32[7,512]{1,0:T(8,128)} %get-tuple-element.28), channel_id=1, source_target_pairs={{0,1},{1,2},{2,3},{3,4},{4,5},{5,6},{6,7},{7,8},{8,9},{9,10},{10,1... | collective-permute-start | bytes 43016 | tf_op jit(solution)/shard_map/ppermute | solution.py:26
  9.5 22.1 %collective-permute-start.3 = (f32[5,512]{1,0:T(8,128)}, f32[5,512]{1,0:T(8,128)S(1)}, u32[]{:S(2)}, u32[]{:S(2)}) collective-permute-start(f32[5,512]{1,0:T(8,128)} %get-tuple-element.29), channel_id=1, source_target_pairs={{0,16},{16,32},{32,48},{48,64},{64,80},{80,96},{96,112},{1,17},{17... | collective-permute-start | bytes 30728 | tf_op jit(solution)/shard_map/ppermute | solution.py:26
  13.5 3.3 %copy-start.5 = (s32[256]{0:T(256)S(1)}, s32[256]{0:T(256)}, u32[]{:S(2)}) copy-start(s32[256]{0:T(256)} %param.16) | copy-start | bytes 3076
  13.5 18.1 %collective-permute-start = (f32[2,512]{1,0:T(2,128)}, f32[2,512]{1,0:T(2,128)S(1)}, u32[]{:S(2)}, u32[]{:S(2)}) collective-permute-start(f32[2,512]{1,0:T(2,128)} %get-tuple-element.26), channel_id=1, source_target_pairs={{1,0},{2,1},{3,2},{4,3},{5,4},{6,5},{7,6},{8,7},{9,8},{10,9},{11,1... | collective-permute-start | bytes 12296 | tf_op jit(solution)/shard_map/ppermute | solution.py:26
  14.8 16.8 %collective-permute-start.1 = (f32[2,512]{1,0:T(2,128)S(1)}, f32[2,512]{1,0:T(2,128)S(1)}, u32[]{:S(2)}, u32[]{:S(2)}) collective-permute-start(f32[2,512]{1,0:T(2,128)S(1)} %copy-done.12), channel_id=1, source_target_pairs={{16,0},{32,16},{48,32},{64,48},{80,64},{96,80},{112,96},{17,1},{33... | collective-permute-start | bytes 12296 | tf_op jit(solution)/shard_map/ppermute | solution.py:26
  17.2 0.9 %copy-start = (f32[256,128]{1,0:T(8,128)S(1)}, f32[256,128]{1,0:T(8,128)}, u32[]{:S(2)}) copy-start(f32[256,128]{1,0:T(8,128)} %get-tuple-element.38) | copy-start | bytes 393220
  20.0 33.5 %all-to-all-start = ((f32[128,1,640]{2,1,0:T(1,128)}), f32[128,1,640]{2,1,0:T(1,128)S(1)}, u32[]{:S(2)}, u32[]{:S(2)}) async-start(f32[128,1,640]{2,1,0:T(1,128)} %copy.32), calls=%async_computation | async-start | bytes 655360 | tf_op jit(solution)/shard_map/all_to_all | solution.py:283
  31.7 0.6 copy-start.8
  31.7 0.6 copy-start.9
  31.7 0.6 copy-start.2
  32.3 0.6 copy-start.1
  40.6 8.2 %copy-start.13 = (f32[2,512]{1,0:T(2,128)S(1)}, f32[2,512]{1,0:T(2,128)}, u32[]{:S(2)}) copy-start(f32[2,512]{1,0:T(2,128)} %get-tuple-element.34) | copy-start | bytes 12292
  40.7 13.2 %collective-permute-start.6 = (f32[5,512]{1,0:T(8,128)}, f32[5,512]{1,0:T(8,128)S(1)}, u32[]{:S(2)}, u32[]{:S(2)}) collective-permute-start(f32[5,512]{1,0:T(8,128)} %get-tuple-element.35), channel_id=1, source_target_pairs={{0,1},{1,2},{2,3},{3,4},{4,5},{5,6},{6,7},{7,8},{8,9},{9,10},{10,1... | collective-permute-start | bytes 30728 | tf_op jit(solution)/shard_map/ppermute | solution.py:26
  43.9 9.9 %collective-permute-start.7 = (f32[5,512]{1,0:T(8,128)}, f32[5,512]{1,0:T(8,128)S(1)}, u32[]{:S(2)}, u32[]{:S(2)}) collective-permute-start(f32[5,512]{1,0:T(8,128)} %get-tuple-element.36), channel_id=1, source_target_pairs={{0,16},{16,32},{32,48},{48,64},{64,80},{80,96},{96,112},{1,17},{17... | collective-permute-start | bytes 30728 | tf_op jit(solution)/shard_map/ppermute | solution.py:26
  47.6 6.1 %collective-permute-start.4 = (f32[2,512]{1,0:T(2,128)}, f32[2,512]{1,0:T(2,128)S(1)}, u32[]{:S(2)}, u32[]{:S(2)}) collective-permute-start(f32[2,512]{1,0:T(2,128)} %get-tuple-element.33), channel_id=1, source_target_pairs={{1,0},{2,1},{3,2},{4,3},{5,4},{6,5},{7,6},{8,7},{9,8},{10,9},{11,1... | collective-permute-start | bytes 12296 | tf_op jit(solution)/shard_map/ppermute | solution.py:26
  48.9 4.9 %collective-permute-start.5 = (f32[2,512]{1,0:T(2,128)S(1)}, f32[2,512]{1,0:T(2,128)S(1)}, u32[]{:S(2)}, u32[]{:S(2)}) collective-permute-start(f32[2,512]{1,0:T(2,128)S(1)} %copy-done.13), channel_id=1, source_target_pairs={{16,0},{32,16},{48,32},{64,48},{80,64},{96,80},{112,96},{17,1},{33... | collective-permute-start | bytes 12296 | tf_op jit(solution)/shard_map/ppermute | solution.py:26
  53.7 0.6 copy-start.10
  53.8 0.6 copy-start.11
  53.8 0.6 copy-start.3
  53.8 0.6 copy-start.4
  54.8 22.1 %all-to-all-start.1 = ((f32[128,4,128]{2,1,0:T(4,128)}), f32[128,4,128]{2,1,0:T(4,128)S(1)}, u32[]{:S(2)}, u32[]{:S(2)}) async-start(f32[128,4,128]{2,1,0:T(4,128)} %bitcast.8), calls=%async_computation.1 | async-start | bytes 524288 | tf_op jit(solution)/shard_map/all_to_all | solution.py:316
  66.0 11.2 %collective-permute-start.8 = (f32[8,128]{1,0:T(8,128)S(1)}, f32[8,128]{1,0:T(8,128)S(1)}, u32[]{:S(2)}, u32[]{:S(2)}) collective-permute-start(f32[8,128]{1,0:T(8,128)S(1)} %fusion.17), channel_id=1, source_target_pairs={{0,1},{1,2},{2,3},{3,4},{4,5},{5,6},{6,7},{7,8},{8,9},{9,10},{10,1... | collective-permute-start | bytes 12296 | tf_op jit(solution)/shard_map/ppermute | solution.py:26

commit v15 on v14

--- a/solution.py
+++ b/solution.py
@@ -76,6 +76,15 @@
     ny, nx = drained.shape
     strips = drained.reshape(ny // STRIP, STRIP, nx).sum(axis=1)
     return jnp.concatenate([strips[:, k * 128:(k + 1) * 128] for k in range(nx // 128)], axis=0)
+
+
+def write_ahead(ahead_ref, to_east):
+    ahead = ahead_ref[...]
+    per_row = to_east.shape[1] // ahead.shape[1]
+    for j in range(ahead.shape[0] // per_row):
+        to_east[5 + j:6 + j, :] = jnp.concatenate(
+            [ahead[j * per_row + m:j * per_row + m + 1, :] for m in range(per_row)], axis=1
+        )
 
 
 def open_masks(flags_ref, land):
@@ -105,12 +114,7 @@
     to_east[2:3, :] = last_col_row(depth)
     to_east[3:4, :] = last_col_row(r_col[...])
     to_east[4:5, :] = last_col_row(eopen)
-    ahead = ahead_ref[...]
-    per_row = ny // ahead.shape[1]
-    for j in range(ahead.shape[0] // per_row):
-        to_east[5 + j:6 + j, :] = jnp.concatenate(
-            [ahead[j * per_row + m:j * per_row + m + 1, :] for m in range(per_row)], axis=1
-        )
+    write_ahead(ahead_ref, to_east)
     to_south[0:1, :] = s_ref[-1:, :]
     to_south[1:2, :] = bed_last_row[-1:, :] + depth[-1:, :]
     to_south[2:3, :] = depth[-1:, :]
@@ -119,8 +123,11 @@
 
 
 def step_kernel(with_edges, flags_ref, d_ref, e_ref, s_ref, bed_ref, r_ref, land_ref,
-                east_ref, south_ref, west_ref, north_ref,
-                d_out, e_out, s_out, *more):
+                east_ref, south_ref, west_ref, north_ref, *rest):
+    if with_edges:
+        ahead_ref, d_out, e_out, s_out, tile_out, to_west, to_north, to_east, to_south = rest
+    else:
+        d_out, e_out, s_out = rest
     ny, nx = d_ref.shape
     depth = d_ref[...]
     bed = bed_ref[...]
@@ -153,7 +160,7 @@
     e_out[...] = flux_e
     s_out[...] = flux_s
     if with_edges:
-        tile_out, to_west, to_north, to_east, to_south = more
+        write_ahead(ahead_ref, to_east)
         next_drained = drain_rate * land * jnp.abs(new_depth)
         tile_out[...] = tile_rows(next_drained)
         write_edges(bed + new_depth, new_depth, flux_e, flux_s, rough, eopen, sopen,
@@ -240,11 +247,11 @@
     def step_call(with_edges):
         outs = (grid_shape, grid_shape, grid_shape)
         if with_edges:
-            outs = outs + (tile_shape,) + edge_shapes(cell_rows, cell_cols)
+            outs = outs + (tile_shape,) + tuple(first_shapes)
         return pl.pallas_call(
             functools.partial(step_kernel, with_edges),
             out_shape=outs,
-            in_specs=[smem_spec] + vmem_specs(10),
+            in_specs=[smem_spec] + vmem_specs(11 if with_edges else 10),
             out_specs=vmem_specs(len(outs)),
         )
 
@@ -285,28 +292,45 @@
         ("gy", "gx"), 0, 0, tiled=True,
     ).reshape(device_count, first_rows, reach_width)
 
+    got_ids = got_first[:, slot_cap:].reshape(device_count, -1)[:, :slot_cap].reshape(-1)
+    targets = lax.iota(f32, block_rows)
+    scatter_onehot = (targets[:, None] == got_ids[None, :]).astype(f32)
+
+    def lateral_from(got):
+        return jnp.dot(
+            scatter_onehot,
+            got[:, :slot_cap].reshape(-1, reach_width),
+            precision=lax.Precision.HIGHEST,
+        )
+
+    def with_upstream(storage, outflow_parts, ahead, lateral):
+        outflow, own_part, _ = outflow_parts
+        upstream = own_part + jnp.pad(ahead, ((0, block_rows - SPAN), (0, 0)))
+        return storage - outflow + upstream + lateral_gain * lateral
+
     depth = water_depth
     for step in range(STEPS):
         to_west, to_north, to_east, to_south = edges
         east_in = shifted(to_west, "gx", -1)
         south_in = shifted(to_north, "gy", -1)
-        if step == 0:
-            west_in = shifted(to_east, ("gy", "gx"), 1)
-            first_ahead = west_in[5:].reshape(SPAN, reach_width)
-        else:
-            west_in = shifted(to_east, "gx", 1)
+        west_in = shifted(to_east, ("gy", "gx"), 1)
+        ahead_in = west_in[5:].reshape(SPAN, reach_width)
         north_in = shifted(to_south, "gy", 1)
         last = step == STEPS - 1
+        extra = ()
+        if step == 0:
+            storage = with_upstream(storage, first_outflow, ahead_in, lateral_from(got_first))
+            second_outflow = reach_outflow(storage)
+            extra = (second_outflow[2],)
         if last:
+            second_ahead = ahead_in
             lateral_started = start_lateral(tile_parts[1:], False)
-            east_in, south_in, west_in, north_in, lateral_started, got_first = (
-                lax.optimization_barrier(
-                    (east_in, south_in, west_in, north_in, lateral_started, got_first)
-                )
+            east_in, south_in, west_in, north_in, lateral_started = lax.optimization_barrier(
+                (east_in, south_in, west_in, north_in, lateral_started)
             )
         outs = step_call(not last)(
             flags, depth, flux_east, flux_south, bed_level, roughness, land_mask,
-            east_in, south_in, west_in, north_in,
+            east_in, south_in, west_in, north_in, *extra,
         )
         depth, flux_east, flux_south = outs[:3]
         if not last:
@@ -314,28 +338,7 @@
             edges = outs[4:]
 
     got_second = lax.all_to_all(lateral_started, ("gy", "gx"), 0, 0, tiled=True)
-    got_ids = got_first[:, slot_cap:].reshape(device_count, -1)[:, :slot_cap].reshape(-1)
-    targets = lax.iota(f32, block_rows)
-    scatter_onehot = (targets[:, None] == got_ids[None, :]).astype(f32)
-    laterals = [
-        jnp.dot(
-            scatter_onehot,
-            got[:, :slot_cap].reshape(-1, reach_width),
-            precision=lax.Precision.HIGHEST,
-        )
-        for got in (got_first, got_second)
-    ]
-
-    for step in range(STEPS):
-        if step == 0:
-            outflow, own_part, _ = first_outflow
-            upstream = own_part + jnp.pad(first_ahead, ((0, block_rows - SPAN), (0, 0)))
-        else:
-            outflow, own_part, ahead_part = reach_outflow(storage)
-            upstream = own_part + jnp.pad(
-                shifted(ahead_part, ("gy", "gx"), 1), ((0, block_rows - SPAN), (0, 0))
-            )
-        storage = storage - outflow + upstream + lateral_gain * laterals[step]
+    storage = with_upstream(storage, second_outflow, second_ahead, lateral_from(got_second))
     return (depth, flux_east, flux_south, storage)
 
 

time: 78.6 us -> 82.4 us (1.048)
  waiting for transfers between devices: 0.25 us -> 6.64 us
  starting transfers between devices: 46.8 us -> 43.2 us
  matrix products: 5.05 us -> 6.55 us
    ppermute x9 -> x8, starting transfers between devices: 24.8 us -> 20.1 us  [shifted(): lax.ppermute(value, axis, [(source, source + steps) for source in range(f...]
    all_to_all x1, waiting for transfers between devices: 0.09 us -> 3.96 us  [body(): got_second = lax.all_to_all(lateral_started, ('gy', 'gx'), 0, 0, tiled=True)]
    all_to_all x1, waiting for transfers between devices: 0.01 us -> 1.56 us  [body(): lax.all_to_all(start_lateral(tile_parts).reshape(device_count, first_rows...]
    all_to_all x1, starting transfers between devices: 10.7 us -> 11.6 us  [body(): got_second = lax.all_to_all(lateral_started, ('gy', 'gx'), 0, 0, tiled=True)]
    ppermute x9 -> x8, waiting for transfers between devices: 0.16 us -> 1.11 us  [shifted(): lax.ppermute(value, axis, [(source, source + steps) for source in range(f...]
    dot_general x2, matrix products: 2.21 us -> 3.11 us  [start_lateral(): jnp.dot(row_onehot, part, precision=lax.Precision.HIGH)]
    unnamed x31 -> x35, local copies, waits for them, and re-layouts: 2.22 us -> 2.53 us
  transfers between devices with their start and end apart: 11 -> 10, of which waited for: 2 -> 3; matrix products, arithmetic and copies ran while one was open for 8% -> 5% of each run, Pallas kernels for 19% -> 9%
where the time goes in v15:
time: 82.4 us; the launch traced here: 81.8 us
  starting transfers between devices  43.2 us (52%)
  Pallas kernels  18.5 us (22%)
  waiting for transfers between devices  6.64 us (8%)
  matrix products  6.55 us (8%)
  local copies, waits for them, and re-layouts  4.77 us (6%)
  other arithmetic  1.12 us (1%)
  between operations  1.07 us (1%)
    ppermute x8, starting transfers between devices, shifted(): lax.ppermute(value, axis, [(source, source + steps) for source in range(f...  20.1 us
    pallas_call x2, Pallas kernels, body(): step_call(not last)  15.2 us
    all_to_all x1, starting transfers between devices, body(): got_second = lax.all_to_all(lateral_started, ('gy', 'gx'), 0, 0, tiled=True)  11.6 us
    all_to_all x1, starting transfers between devices, body(): lax.all_to_all(start_lateral(tile_parts).reshape(device_count, first_rows...  11.5 us
    all_to_all x1, waiting for transfers between devices, body(): got_second = lax.all_to_all(lateral_started, ('gy', 'gx'), 0, 0, tiled=True)  3.96 us
    pallas_call x1, Pallas kernels, body(): pl.pallas_call(edge_kernel, grid=(1,), out_shape=(tile_shape,) + tuple(fi...  3.29 us
    dot_general x2, matrix products, start_lateral(): jnp.dot(row_onehot, part, precision=lax.Precision.HIGH)  3.11 us
    dot_general x4, matrix products, block_term(): jnp.einsum('tb,tc->bc', onehot, values, precision=lax.Precision.HIGHEST)  2.82 us
  transfers between devices with their start and end apart: 10, of which 3 were waited for; matrix products, arithmetic and copies ran while one was open for 5% of the time, Pallas kernels for 9%

profile of v15, /device:TPU:1, one launch (start us, length us, event | category | flops | bytes accessed | tf_op | source)
XLA Modules:
  0.0 81.8 jit_solution(5886145183837980658)
XLA Ops:
  0.6 0.7 copy-done.4
  1.5 0.2 fusion.6
  2.3 0.6 add_convert_fusion.flags_ref
  2.9 0.8 %fusion.19.ahead_ref = f32[8,128]{1,0:T(8,128)} fusion(s32[8]{0:T(128)S(1)} %iota_add_fusion.1, s32[16]{0:T(128)S(1)} %copy-done.16, f32[16,128]{1,0:T(8,128)S(1)} %copy-done.5, f32[16,128]{1,0:T(8,128)S(1)} %copy-done.6), kind=kOutput, calls=%fused_computation.31 | convolution fusion | flops 204928 | bytes 20576 | tf_op jit(solution)/shard_map/tb,tc->bc/dot_general | solution.py:40
  3.8 3.3 %shard_map.129 = (f32[256,128]{1,0:T(8,128)}, f32[2,512]{1,0:T(2,128)}, f32[2,512]{1,0:T(2,128)}, f32[7,512]{1,0:T(8,128)}, f32[5,512]{1,0:T(8,128)}) custom-call(s32[3]{0:T(128)} %add_convert_fusion.flags_ref, f32[512,512]{1,0:T(8,128)} %d_ref.3, s32[512,512]{1,0:T(8,128)} %land_ref.5, f32[512,512]{1,0:T(8,128)} %bed_ref.3, f32[512,512]{1,0:T(8,128)} %bed_ref.3, ...), custom_call_target="tpu_custom_call" | custom-call | tf_op jit(solution)/shard_map/pallas_call | solution.py:234
  7.1 1.2 %fusion.1 = f32[512,128]{1,0:T(8,128)S(1)} fusion(f32[256,128]{1,0:T(8,128)} %get-tuple-element.29, s32[256]{0:T(256)S(1)} %eq.135), kind=kOutput, calls=%fused_computation.5 | convolution fusion | flops 100794368 | bytes 394240 | tf_op jit(solution)/shard_map/dot_general | solution.py:282
  8.4 0.2 fusion.2
  8.9 0.9 %copy.32 = f32[128,1,640]{2,1,0:T(1,128)} copy(f32[128,1,640]{0,2,1:T(8,128)S(1)} %bitcast.36) | data formatting | bytes 655360 | tf_op jit(solution)/shard_map/all_to_all | solution.py:290
  9.8 11.5 %all-to-all-start = ((f32[128,1,640]{2,1,0:T(1,128)}), f32[128,1,640]{2,1,0:T(1,128)S(1)}, u32[]{:S(2)}, u32[]{:S(2)}) async-start(f32[128,1,640]{2,1,0:T(1,128)} %copy.32), calls=%async_computation | async-start | bytes 655360 | tf_op jit(solution)/shard_map/all_to_all | solution.py:290
  21.3 3.3 %collective-permute-start.2 = (f32[7,512]{1,0:T(8,128)S(1)}, f32[7,512]{1,0:T(8,128)S(1)}, u32[]{:S(2)}, u32[]{:S(2)}) collective-permute-start(f32[7,512]{1,0:T(8,128)S(1)} %copy-done.12), channel_id=1, source_target_pairs={{0,1},{1,2},{2,3},{3,4},{4,5},{5,6},{6,7},{7,8},{8,9},{9,10},{10,1... | collective-permute-start | bytes 43016 | tf_op jit(solution)/shard_map/ppermute | solution.py:26
  24.6 3.7 %collective-permute-start.3 = (f32[5,512]{1,0:T(8,128)S(1)}, f32[5,512]{1,0:T(8,128)S(1)}, u32[]{:S(2)}, u32[]{:S(2)}) collective-permute-start(f32[5,512]{1,0:T(8,128)S(1)} %copy-done.11), channel_id=1, source_target_pairs={{0,16},{16,32},{32,48},{48,64},{64,80},{80,96},{96,112},{1,17},{17... | collective-permute-start | bytes 30728 | tf_op jit(solution)/shard_map/ppermute | solution.py:26
  28.3 1.3 %collective-permute-start = (f32[2,512]{1,0:T(2,128)S(1)}, f32[2,512]{1,0:T(2,128)S(1)}, u32[]{:S(2)}, u32[]{:S(2)}) collective-permute-start(f32[2,512]{1,0:T(2,128)S(1)} %copy-done.14), channel_id=1, source_target_pairs={{1,0},{2,1},{3,2},{4,3},{5,4},{6,5},{7,6},{8,7},{9,8},{10,9},{11,1... | collective-permute-start | bytes 12296 | tf_op jit(solution)/shard_map/ppermute | solution.py:26
  29.6 1.9 %collective-permute-start.1 = (f32[2,512]{1,0:T(2,128)S(1)}, f32[2,512]{1,0:T(2,128)S(1)}, u32[]{:S(2)}, u32[]{:S(2)}) collective-permute-start(f32[2,512]{1,0:T(2,128)S(1)} %copy-done.13), channel_id=1, source_target_pairs={{16,0},{32,16},{48,32},{64,48},{80,64},{96,80},{112,96},{17,1},{33... | collective-permute-start | bytes 12296 | tf_op jit(solution)/shard_map/ppermute | solution.py:26
  31.5 0.2 fusion.15
  31.8 1.6 %all-to-all-done = f32[128,1,640]{2,1,0:T(1,128)S(1)} async-done(((f32[128,1,640]{2,1,0:T(1,128)}), f32[128,1,640]{2,1,0:T(1,128)S(1)}, u32[]{:S(2)}, u32[]{:S(2)}) %all-to-all-start) | async-done | bytes 327712 | tf_op jit(solution)/shard_map/all_to_all | solution.py:290
  34.0 0.2 add_add_fusion.1
  34.2 0.9 %fusion.17.rest_0_ = f32[8,128]{1,0:T(8,128)} fusion(s32[8]{0:T(128)S(1)} %iota_add_fusion.1, s32[16]{0:T(128)S(1)} %copy-done.16, f32[16,128]{1,0:T(8,128)S(1)} %add_add_fusion.1, f32[16,128]{1,0:T(8,128)S(1)} %copy-done.6), kind=kOutput, calls=%fused_computation.29 | convolution fusion | flops 204928 | bytes 20576 | tf_op jit(solution)/shard_map/tb,tc->bc/dot_general | solution.py:40
  35.1 0.6 copy-done.9
  35.7 0.6 copy-done.2
  36.3 7.8 %shard_map.130 = (f32[512,512]{1,0:T(8,128)}, f32[512,512]{1,0:T(8,128)}, f32[512,512]{1,0:T(8,128)}, f32[256,128]{1,0:T(8,128)}, f32[2,512]{1,0:T(2,128)}, /*in...) custom-call(s32[3]{0:T(128)} %add_convert_fusion.flags_ref, f32[512,512]{1,0:T(8,128)} %d_ref.3, ...), custom_call_target="tpu_custom_call" | custom-call | tf_op jit(solution)/shard_map/pallas_call | solution.py:331
  44.1 3.4 %collective-permute-start.6 = (f32[7,512]{1,0:T(8,128)}, f32[7,512]{1,0:T(8,128)S(1)}, u32[]{:S(2)}, u32[]{:S(2)}) collective-permute-start(f32[7,512]{1,0:T(8,128)} %get-tuple-element.35), channel_id=1, source_target_pairs={{0,1},{1,2},{2,3},{3,4},{4,5},{5,6},{6,7},{7,8},{8,9},{9,10},{10,1... | collective-permute-start | bytes 43016 | tf_op jit(solution)/shard_map/ppermute | solution.py:26
  47.5 3.3 %collective-permute-start.7 = (f32[5,512]{1,0:T(8,128)}, f32[5,512]{1,0:T(8,128)S(1)}, u32[]{:S(2)}, u32[]{:S(2)}) collective-permute-start(f32[5,512]{1,0:T(8,128)} %get-tuple-element.36), channel_id=1, source_target_pairs={{0,16},{16,32},{32,48},{48,64},{64,80},{80,96},{96,112},{1,17},{17... | collective-permute-start | bytes 30728 | tf_op jit(solution)/shard_map/ppermute | solution.py:26
  50.8 1.3 %collective-permute-start.4 = (f32[2,512]{1,0:T(2,128)}, f32[2,512]{1,0:T(2,128)S(1)}, u32[]{:S(2)}, u32[]{:S(2)}) collective-permute-start(f32[2,512]{1,0:T(2,128)} %get-tuple-element.33), channel_id=1, source_target_pairs={{1,0},{2,1},{3,2},{4,3},{5,4},{6,5},{7,6},{8,7},{9,8},{10,9},{11,1... | collective-permute-start | bytes 12296 | tf_op jit(solution)/shard_map/ppermute | solution.py:26
  52.1 1.9 %collective-permute-start.5 = (f32[2,512]{1,0:T(2,128)S(1)}, f32[2,512]{1,0:T(2,128)S(1)}, u32[]{:S(2)}, u32[]{:S(2)}) collective-permute-start(f32[2,512]{1,0:T(2,128)S(1)} %copy-done.15), channel_id=1, source_target_pairs={{16,0},{32,16},{48,32},{64,48},{80,64},{96,80},{112,96},{17,1},{33... | collective-permute-start | bytes 12296 | tf_op jit(solution)/shard_map/ppermute | solution.py:26
  54.1 1.9 %fusion = f32[512,128]{1,0:T(8,128)} fusion(f32[256,128]{1,0:T(8,128)} %get-tuple-element.37, s32[256]{0:T(256)S(1)} %eq.135), kind=kOutput, calls=%fused_computation.4 | convolution fusion | flops 100794368 | bytes 394240 | tf_op jit(solution)/shard_map/dot_general | solution.py:282
  56.0 1.1 %collective-permute-done.5.south_ref = f32[2,512]{1,0:T(2,128)S(1)} collective-permute-done((f32[2,512]{1,0:T(2,128)S(1)}, f32[2,512]{1,0:T(2,128)S(1)}, u32[]{:S(2)}, u32[]{:S(2)}) %collective-permute-start.5) | collective-permute-done | bytes 4128 | tf_op jit(solution)/shard_map/ppermute | solution.py:26
  57.1 0.6 copy-done.8
  57.7 11.6 %all-to-all-start.1 = ((f32[128,4,128]{2,1,0:T(4,128)}), f32[128,4,128]{2,1,0:T(4,128)S(1)}, u32[]{:S(2)}, u32[]{:S(2)}) async-start(f32[128,4,128]{2,1,0:T(4,128)} %bitcast.16), calls=%async_computation.1 | async-start | bytes 524288 | tf_op jit(solution)/shard_map/all_to_all | solution.py:340
  69.3 7.4 %shard_map.131 = (f32[512,512]{1,0:T(8,128)}, f32[512,512]{1,0:T(8,128)}, f32[512,512]{1,0:T(8,128)}) custom-call(s32[3]{0:T(128)} %add_convert_fusion.flags_ref, f32[512,512]{1,0:T(8,128)} %get-tuple-element.30.d_ref, f32[512,512]{1,0:T(8,128)} %get-tuple-element.31.e_ref, f32[512,512]{1,0:T(8,128)} %get-tuple-element.32.s_ref, f32[512,512]{1,0:T(8,128)} %bed_ref.3, ...), custom_call_target="tpu_custom_call" | custom-call | tf_op jit(solution)/shard_map/pallas_call | solution.py:331
  76.7 4.0 %all-to-all-done.1 = f32[128,4,128]{2,1,0:T(4,128)S(1)} async-done(((f32[128,4,128]{2,1,0:T(4,128)}), f32[128,4,128]{2,1,0:T(4,128)S(1)}, u32[]{:S(2)}, u32[]{:S(2)}) %all-to-all-start.1) | async-done | bytes 262176 | tf_op jit(solution)/shard_map/all_to_all | solution.py:340
  80.7 0.2 convolution_multiply_fusion
  80.9 0.9 %add_add_fusion = f32[16,128]{1,0:T(8,128)} fusion(f32[16,128]{1,0:T(8,128)S(1)} %convolution_multiply_fusion, f32[8,128]{1,0:T(8,128)S(1)} %reshape.84, f32[16,128]{1,0:T(8,128)S(1)} %add_add_fusion.1, s32[16]{0:T(128)S(1)} %iota_add_fusion, s32[16]{0:T(128)S(1)} %copy-done.16, f32[16,128]{1,0:T(8,128)S(1)} %copy-done.6), kind=kOutput, calls=%fused_computation.33 | convolution fusion | flops 418048 | bytes 36992 | tf_op jit(solution)/shard_map/tb,tc->bc/dot_general | solution.py:40
  (71 shorter events, 1.8 us)
Async XLA Ops:
  0.6 0.7 copy-start.4
  2.1 0.8 copy-start.6
  2.2 0.7 copy-start.5
  2.3 0.7 copy-start.16
  9.8 11.5 %copy-start.12 = (f32[7,512]{1,0:T(8,128)S(1)}, f32[7,512]{1,0:T(8,128)}, u32[]{:S(2)}) copy-start(f32[7,512]{1,0:T(8,128)} %get-tuple-element.27) | copy-start | bytes 43012
  9.8 14.8 %copy-start.11 = (f32[5,512]{1,0:T(8,128)S(1)}, f32[5,512]{1,0:T(8,128)}, u32[]{:S(2)}) copy-start(f32[5,512]{1,0:T(8,128)} %get-tuple-element.28) | copy-start | bytes 30724
  9.8 18.5 %copy-start.14 = (f32[2,512]{1,0:T(2,128)S(1)}, f32[2,512]{1,0:T(2,128)}, u32[]{:S(2)}) copy-start(f32[2,512]{1,0:T(2,128)} %get-tuple-element.25) | copy-start | bytes 12292
  9.8 23.6 %all-to-all-start = ((f32[128,1,640]{2,1,0:T(1,128)}), f32[128,1,640]{2,1,0:T(1,128)S(1)}, u32[]{:S(2)}, u32[]{:S(2)}) async-start(f32[128,1,640]{2,1,0:T(1,128)} %copy.32), calls=%async_computation | async-start | bytes 655360 | tf_op jit(solution)/shard_map/all_to_all | solution.py:290
  21.3 8.3 %copy-start.13 = (f32[2,512]{1,0:T(2,128)S(1)}, f32[2,512]{1,0:T(2,128)}, u32[]{:S(2)}) copy-start(f32[2,512]{1,0:T(2,128)} %get-tuple-element.26) | copy-start | bytes 12292
  21.3 10.5 %collective-permute-start.2 = (f32[7,512]{1,0:T(8,128)S(1)}, f32[7,512]{1,0:T(8,128)S(1)}, u32[]{:S(2)}, u32[]{:S(2)}) collective-permute-start(f32[7,512]{1,0:T(8,128)S(1)} %copy-done.12), channel_id=1, source_target_pairs={{0,1},{1,2},{2,3},{3,4},{4,5},{5,6},{6,7},{7,8},{8,9},{9,10},{10,1... | collective-permute-start | bytes 43016 | tf_op jit(solution)/shard_map/ppermute | solution.py:26
  24.6 10.5 %collective-permute-start.3 = (f32[5,512]{1,0:T(8,128)S(1)}, f32[5,512]{1,0:T(8,128)S(1)}, u32[]{:S(2)}, u32[]{:S(2)}) collective-permute-start(f32[5,512]{1,0:T(8,128)S(1)} %copy-done.11), channel_id=1, source_target_pairs={{0,16},{16,32},{32,48},{48,64},{64,80},{80,96},{96,112},{1,17},{17... | collective-permute-start | bytes 30728 | tf_op jit(solution)/shard_map/ppermute | solution.py:26
  28.3 6.8 %collective-permute-start = (f32[2,512]{1,0:T(2,128)S(1)}, f32[2,512]{1,0:T(2,128)S(1)}, u32[]{:S(2)}, u32[]{:S(2)}) collective-permute-start(f32[2,512]{1,0:T(2,128)S(1)} %copy-done.14), channel_id=1, source_target_pairs={{1,0},{2,1},{3,2},{4,3},{5,4},{6,5},{7,6},{8,7},{9,8},{10,9},{11,1... | collective-permute-start | bytes 12296 | tf_op jit(solution)/shard_map/ppermute | solution.py:26
  29.6 5.5 %collective-permute-start.1 = (f32[2,512]{1,0:T(2,128)S(1)}, f32[2,512]{1,0:T(2,128)S(1)}, u32[]{:S(2)}, u32[]{:S(2)}) collective-permute-start(f32[2,512]{1,0:T(2,128)S(1)} %copy-done.13), channel_id=1, source_target_pairs={{16,0},{32,16},{48,32},{64,48},{80,64},{96,80},{112,96},{17,1},{33... | collective-permute-start | bytes 12296 | tf_op jit(solution)/shard_map/ppermute | solution.py:26
  31.8 1.8 %copy-start = (f32[7,512]{1,0:T(8,128)}, f32[7,512]{1,0:T(8,128)S(1)}, u32[]{:S(2)}) copy-start(f32[7,512]{1,0:T(8,128)S(1)} %collective-permute-done.2.west_ref) | copy-start | bytes 43012
  35.1 0.6 copy-start.9
  35.1 0.6 copy-start.10
  35.7 0.6 copy-start.2
  44.1 8.0 %copy-start.15 = (f32[2,512]{1,0:T(2,128)S(1)}, f32[2,512]{1,0:T(2,128)}, u32[]{:S(2)}) copy-start(f32[2,512]{1,0:T(2,128)} %get-tuple-element.34) | copy-start | bytes 12292
  44.1 13.0 %collective-permute-start.6 = (f32[7,512]{1,0:T(8,128)}, f32[7,512]{1,0:T(8,128)S(1)}, u32[]{:S(2)}, u32[]{:S(2)}) collective-permute-start(f32[7,512]{1,0:T(8,128)} %get-tuple-element.35), channel_id=1, source_target_pairs={{0,1},{1,2},{2,3},{3,4},{4,5},{5,6},{6,7},{7,8},{8,9},{9,10},{10,1... | collective-permute-start | bytes 43016 | tf_op jit(solution)/shard_map/ppermute | solution.py:26
  47.5 9.6 %collective-permute-start.7 = (f32[5,512]{1,0:T(8,128)}, f32[5,512]{1,0:T(8,128)S(1)}, u32[]{:S(2)}, u32[]{:S(2)}) collective-permute-start(f32[5,512]{1,0:T(8,128)} %get-tuple-element.36), channel_id=1, source_target_pairs={{0,16},{16,32},{32,48},{48,64},{64,80},{80,96},{96,112},{1,17},{17... | collective-permute-start | bytes 30728 | tf_op jit(solution)/shard_map/ppermute | solution.py:26
  50.8 5.1 %collective-permute-start.4 = (f32[2,512]{1,0:T(2,128)}, f32[2,512]{1,0:T(2,128)S(1)}, u32[]{:S(2)}, u32[]{:S(2)}) collective-permute-start(f32[2,512]{1,0:T(2,128)} %get-tuple-element.33), channel_id=1, source_target_pairs={{1,0},{2,1},{3,2},{4,3},{5,4},{6,5},{7,6},{8,7},{9,8},{10,9},{11,1... | collective-permute-start | bytes 12296 | tf_op jit(solution)/shard_map/ppermute | solution.py:26
  52.1 4.9 %collective-permute-start.5 = (f32[2,512]{1,0:T(2,128)S(1)}, f32[2,512]{1,0:T(2,128)S(1)}, u32[]{:S(2)}, u32[]{:S(2)}) collective-permute-start(f32[2,512]{1,0:T(2,128)S(1)} %copy-done.15), channel_id=1, source_target_pairs={{16,0},{32,16},{48,32},{64,48},{80,64},{96,80},{112,96},{17,1},{33... | collective-permute-start | bytes 12296 | tf_op jit(solution)/shard_map/ppermute | solution.py:26
  56.0 1.1 %copy-start.7 = (f32[2,512]{1,0:T(2,128)}, f32[2,512]{1,0:T(2,128)S(1)}, u32[]{:S(2)}) copy-start(f32[2,512]{1,0:T(2,128)S(1)} %collective-permute-done.4.east_ref) | copy-start | bytes 12292
  57.1 0.6 copy-start.8
  57.1 0.6 copy-start.3
  57.1 12.2 %copy-start.1 = (f32[7,512]{1,0:T(8,128)}, f32[7,512]{1,0:T(8,128)S(1)}, u32[]{:S(2)}) copy-start(f32[7,512]{1,0:T(8,128)S(1)} %collective-permute-done.6.west_ref) | copy-start | bytes 43012
  57.7 23.0 %all-to-all-start.1 = ((f32[128,4,128]{2,1,0:T(4,128)}), f32[128,4,128]{2,1,0:T(4,128)S(1)}, u32[]{:S(2)}, u32[]{:S(2)}) async-start(f32[128,4,128]{2,1,0:T(4,128)} %bitcast.16), calls=%async_computation.1 | async-start | bytes 524288 | tf_op jit(solution)/shard_map/all_to_all | solution.py:340

commit v16 on v15

--- a/solution.py
+++ b/solution.py
@@ -287,14 +287,8 @@
         return jnp.concatenate(packed + ([send_ids] if with_ids else []), axis=1)
 
     first_rows = slot_cap + id_rows
-    got_first = lax.all_to_all(
-        start_lateral(tile_parts).reshape(device_count, first_rows * reach_width),
-        ("gy", "gx"), 0, 0, tiled=True,
-    ).reshape(device_count, first_rows, reach_width)
-
-    got_ids = got_first[:, slot_cap:].reshape(device_count, -1)[:, :slot_cap].reshape(-1)
-    targets = lax.iota(f32, block_rows)
-    scatter_onehot = (targets[:, None] == got_ids[None, :]).astype(f32)
+    first_message = start_lateral(tile_parts).reshape(device_count, first_rows * reach_width)
+
 
     def lateral_from(got):
         return jnp.dot(
@@ -319,6 +313,16 @@
         last = step == STEPS - 1
         extra = ()
         if step == 0:
+            east_in, south_in, west_in, north_in, first_message = lax.optimization_barrier(
+                (east_in, south_in, west_in, north_in, first_message)
+            )
+            ahead_in = west_in[5:].reshape(SPAN, reach_width)
+            got_first = lax.all_to_all(
+                first_message, ("gy", "gx"), 0, 0, tiled=True
+            ).reshape(device_count, first_rows, reach_width)
+            got_ids = got_first[:, slot_cap:].reshape(device_count, -1)[:, :slot_cap].reshape(-1)
+            targets = lax.iota(f32, block_rows)
+            scatter_onehot = (targets[:, None] == got_ids[None, :]).astype(f32)
             storage = with_upstream(storage, first_outflow, ahead_in, lateral_from(got_first))
             second_outflow = reach_outflow(storage)
             extra = (second_outflow[2],)

time: 82.4 us -> 85.1 us (1.033)
  waiting for transfers between devices: 6.64 us -> 17.3 us
  starting transfers between devices: 43.2 us -> 37.6 us
  local copies, waits for them, and re-layouts: 4.77 us -> 3.38 us
  matrix products: 6.55 us -> 5.65 us
    all_to_all x1, waiting for transfers between devices: 1.56 us -> 11.8 us  [body(): lax.all_to_all(first_message, ('gy', 'gx'), 0, 0, tiled=True)]
    all_to_all x1, starting transfers between devices: 11.6 us -> 7.25 us  [body(): got_second = lax.all_to_all(lateral_started, ('gy', 'gx'), 0, 0, tiled=True)]
    unnamed x35 -> x31, local copies, waits for them, and re-layouts: 2.53 us -> 1.14 us
    dot_general x2, matrix products: 3.11 us -> 2.21 us  [start_lateral(): jnp.dot(row_onehot, part, precision=lax.Precision.HIGH)]
  transfers between devices with their start and end apart: 10 -> 10, of which waited for: 3 -> 4; matrix products, arithmetic and copies ran while one was open for 5% -> 5% of each run, Pallas kernels for 9% -> 9%
where the time goes in v16:
time: 85.1 us; the launch traced here: 84.6 us
  starting transfers between devices  37.6 us (44%)
  Pallas kernels  18.5 us (22%)
  waiting for transfers between devices  17.3 us (20%)
  matrix products  5.65 us (7%)
  local copies, waits for them, and re-layouts  3.38 us (4%)
  other arithmetic  1.11 us (1%)
  between operations  1.06 us (1%)
    ppermute x8, starting transfers between devices, shifted(): lax.ppermute(value, axis, [(source, source + steps) for source in range(f...  19.6 us
    pallas_call x2, Pallas kernels, body(): step_call(not last)  15.2 us
    all_to_all x1, waiting for transfers between devices, body(): lax.all_to_all(first_message, ('gy', 'gx'), 0, 0, tiled=True)  11.8 us
    all_to_all x1, starting transfers between devices, body(): lax.all_to_all(first_message, ('gy', 'gx'), 0, 0, tiled=True)  10.8 us
    all_to_all x1, starting transfers between devices, body(): got_second = lax.all_to_all(lateral_started, ('gy', 'gx'), 0, 0, tiled=True)  7.25 us
    all_to_all x1, waiting for transfers between devices, body(): got_second = lax.all_to_all(lateral_started, ('gy', 'gx'), 0, 0, tiled=True)  3.71 us
    pallas_call x1, Pallas kernels, body(): pl.pallas_call(edge_kernel, grid=(1,), out_shape=(tile_shape,) + tuple(fi...  3.29 us
    dot_general x2, matrix products, start_lateral(): jnp.dot(row_onehot, part, precision=lax.Precision.HIGH)  2.21 us
  transfers between devices with their start and end apart: 10, of which 4 were waited for; matrix products, arithmetic and copies ran while one was open for 5% of the time, Pallas kernels for 9%

profile of v16, /device:TPU:1, one launch (start us, length us, event | category | flops | bytes accessed | tf_op | source)
XLA Modules:
  0.0 84.6 jit_solution(17129292038484115607)
XLA Ops:
  0.7 0.6 add_convert_fusion.flags_ref
  1.4 0.8 %fusion.20.ahead_ref = f32[8,128]{1,0:T(8,128)} fusion(s32[8]{0:T(128)S(1)} %iota_add_fusion.1, s32[16]{0:T(128)S(1)} %copy-done.14, f32[16,128]{1,0:T(8,128)S(1)} %copy-done.11, f32[16,128]{1,0:T(8,128)S(1)} %copy-done.6), kind=kOutput, calls=%fused_computation.33 | convolution fusion | flops 204928 | bytes 20576 | tf_op jit(solution)/shard_map/tb,tc->bc/dot_general | solution.py:40
  2.2 3.3 %shard_map.129 = (f32[256,128]{1,0:T(8,128)}, f32[2,512]{1,0:T(2,128)}, f32[2,512]{1,0:T(2,128)}, f32[7,512]{1,0:T(8,128)}, f32[5,512]{1,0:T(8,128)}) custom-call(s32[3]{0:T(128)} %add_convert_fusion.flags_ref, f32[512,512]{1,0:T(8,128)} %d_ref.3, s32[512,512]{1,0:T(8,128)} %land_ref.5, f32[512,512]{1,0:T(8,128)} %bed_ref.3, f32[512,512]{1,0:T(8,128)} %bed_ref.3, ...), custom_call_target="tpu_custom_call" | custom-call | tf_op jit(solution)/shard_map/pallas_call | solution.py:234
  5.5 4.0 %collective-permute-start.2 = (f32[7,512]{1,0:T(8,128)}, f32[7,512]{1,0:T(8,128)S(1)}, u32[]{:S(2)}, u32[]{:S(2)}) collective-permute-start(f32[7,512]{1,0:T(8,128)} %get-tuple-element.32), channel_id=1, source_target_pairs={{0,1},{1,2},{2,3},{3,4},{4,5},{5,6},{6,7},{7,8},{8,9},{9,10},{10,1... | collective-permute-start | bytes 43016 | tf_op jit(solution)/shard_map/ppermute | solution.py:26
  9.5 4.0 %collective-permute-start.3 = (f32[5,512]{1,0:T(8,128)}, f32[5,512]{1,0:T(8,128)S(1)}, u32[]{:S(2)}, u32[]{:S(2)}) collective-permute-start(f32[5,512]{1,0:T(8,128)} %get-tuple-element.33), channel_id=1, source_target_pairs={{0,16},{16,32},{32,48},{48,64},{64,80},{80,96},{96,112},{1,17},{17... | collective-permute-start | bytes 30728 | tf_op jit(solution)/shard_map/ppermute | solution.py:26
  13.5 1.3 %collective-permute-start = (f32[2,512]{1,0:T(2,128)}, f32[2,512]{1,0:T(2,128)S(1)}, u32[]{:S(2)}, u32[]{:S(2)}) collective-permute-start(f32[2,512]{1,0:T(2,128)} %get-tuple-element.30), channel_id=1, source_target_pairs={{1,0},{2,1},{3,2},{4,3},{5,4},{6,5},{7,6},{8,7},{9,8},{10,9},{11,1... | collective-permute-start | bytes 12296 | tf_op jit(solution)/shard_map/ppermute | solution.py:26
  14.8 1.9 %collective-permute-start.1 = (f32[2,512]{1,0:T(2,128)S(1)}, f32[2,512]{1,0:T(2,128)S(1)}, u32[]{:S(2)}, u32[]{:S(2)}) collective-permute-start(f32[2,512]{1,0:T(2,128)S(1)} %copy-done.12), channel_id=1, source_target_pairs={{16,0},{32,16},{48,32},{64,48},{80,64},{96,80},{112,96},{17,1},{33... | collective-permute-start | bytes 12296 | tf_op jit(solution)/shard_map/ppermute | solution.py:26
  16.9 0.2 fusion.8
  17.7 0.4 copy-done
  18.1 0.3 fusion.3
  18.6 0.2 fusion.4
  19.1 0.7 collective-permute-done.1.south_ref
  19.8 0.9 %copy.32 = f32[128,1,640]{2,1,0:T(1,128)} copy(f32[128,1,640]{0,2,1:T(8,128)S(1)} %bitcast.37) | data formatting | bytes 655360 | tf_op jit(solution)/shard_map/all_to_all | solution.py:320
  20.7 10.8 %all-to-all-start = ((f32[128,1,640]{2,1,0:T(1,128)}), f32[128,1,640]{2,1,0:T(1,128)S(1)}, u32[]{:S(2)}, u32[]{:S(2)}) async-start(f32[128,1,640]{2,1,0:T(1,128)} %copy.32), calls=%async_computation | async-start | bytes 655360 | tf_op jit(solution)/shard_map/all_to_all | solution.py:320
  31.5 0.3 fusion.1
  31.8 11.8 %all-to-all-done = f32[128,1,640]{2,1,0:T(1,128)S(1)} async-done(((f32[128,1,640]{2,1,0:T(1,128)}), f32[128,1,640]{2,1,0:T(1,128)S(1)}, u32[]{:S(2)}, u32[]{:S(2)}) %all-to-all-start) | async-done | bytes 327712 | tf_op jit(solution)/shard_map/all_to_all | solution.py:320
  43.6 0.2 copy.33
  44.2 0.2 fusion
  44.4 0.9 %fusion.18.rest_0_ = f32[8,128]{1,0:T(8,128)} fusion(s32[8]{0:T(128)S(1)} %iota_add_fusion.1, s32[16]{0:T(128)S(1)} %copy-done.14, f32[16,128]{1,0:T(8,128)S(1)} %fusion, f32[16,128]{1,0:T(8,128)S(1)} %copy-done.6), kind=kOutput, calls=%fused_computation.31 | convolution fusion | flops 204928 | bytes 20576 | tf_op jit(solution)/shard_map/tb,tc->bc/dot_general | solution.py:40
  45.3 7.8 %shard_map.130 = (f32[512,512]{1,0:T(8,128)}, f32[512,512]{1,0:T(8,128)}, f32[512,512]{1,0:T(8,128)}, f32[256,128]{1,0:T(8,128)}, f32[2,512]{1,0:T(2,128)}, /*in...) custom-call(s32[3]{0:T(128)} %add_convert_fusion.flags_ref, f32[512,512]{1,0:T(8,128)} %d_ref.3, ...), custom_call_target="tpu_custom_call" | custom-call | tf_op jit(solution)/shard_map/pallas_call | solution.py:335
  53.0 2.3 %collective-permute-start.6 = (f32[7,512]{1,0:T(8,128)}, f32[7,512]{1,0:T(8,128)S(1)}, u32[]{:S(2)}, u32[]{:S(2)}) collective-permute-start(f32[7,512]{1,0:T(8,128)} %get-tuple-element.45), channel_id=1, source_target_pairs={{0,1},{1,2},{2,3},{3,4},{4,5},{5,6},{6,7},{7,8},{8,9},{9,10},{10,1... | collective-permute-start | bytes 43016 | tf_op jit(solution)/shard_map/ppermute | solution.py:26
  55.3 2.9 %collective-permute-start.7 = (f32[5,512]{1,0:T(8,128)}, f32[5,512]{1,0:T(8,128)S(1)}, u32[]{:S(2)}, u32[]{:S(2)}) collective-permute-start(f32[5,512]{1,0:T(8,128)} %get-tuple-element.46), channel_id=1, source_target_pairs={{0,16},{16,32},{32,48},{48,64},{64,80},{80,96},{96,112},{1,17},{17... | collective-permute-start | bytes 30728 | tf_op jit(solution)/shard_map/ppermute | solution.py:26
  58.3 1.3 %collective-permute-start.4 = (f32[2,512]{1,0:T(2,128)}, f32[2,512]{1,0:T(2,128)S(1)}, u32[]{:S(2)}, u32[]{:S(2)}) collective-permute-start(f32[2,512]{1,0:T(2,128)} %get-tuple-element.43), channel_id=1, source_target_pairs={{1,0},{2,1},{3,2},{4,3},{5,4},{6,5},{7,6},{8,7},{9,8},{10,9},{11,1... | collective-permute-start | bytes 12296 | tf_op jit(solution)/shard_map/ppermute | solution.py:26
  59.6 1.9 %collective-permute-start.5 = (f32[2,512]{1,0:T(2,128)S(1)}, f32[2,512]{1,0:T(2,128)S(1)}, u32[]{:S(2)}, u32[]{:S(2)}) collective-permute-start(f32[2,512]{1,0:T(2,128)S(1)} %copy-done.13), channel_id=1, source_target_pairs={{16,0},{32,16},{48,32},{64,48},{80,64},{96,80},{112,96},{17,1},{33... | collective-permute-start | bytes 12296 | tf_op jit(solution)/shard_map/ppermute | solution.py:26
  61.5 1.9 %fusion.2 = f32[512,128]{1,0:T(8,128)} fusion(f32[256,128]{1,0:T(8,128)} %get-tuple-element.47, s32[256]{0:T(256)S(1)} %eq.131), kind=kOutput, calls=%fused_computation.7 | convolution fusion | flops 100794368 | bytes 394240 | tf_op jit(solution)/shard_map/dot_general | solution.py:282
  63.4 1.1 %collective-permute-done.5.south_ref = f32[2,512]{1,0:T(2,128)S(1)} collective-permute-done((f32[2,512]{1,0:T(2,128)S(1)}, f32[2,512]{1,0:T(2,128)S(1)}, u32[]{:S(2)}, u32[]{:S(2)}) %collective-permute-start.5) | collective-permute-done | bytes 4128 | tf_op jit(solution)/shard_map/ppermute | solution.py:26
  64.5 0.6 copy-done.8
  65.1 7.3 %all-to-all-start.1 = ((f32[128,4,128]{2,1,0:T(4,128)}), f32[128,4,128]{2,1,0:T(4,128)S(1)}, u32[]{:S(2)}, u32[]{:S(2)}) async-start(f32[128,4,128]{2,1,0:T(4,128)} %bitcast.17), calls=%async_computation.1 | async-start | bytes 524288 | tf_op jit(solution)/shard_map/all_to_all | solution.py:344
  72.4 0.2 fusion.15
  72.6 7.4 %shard_map.131 = (f32[512,512]{1,0:T(8,128)}, f32[512,512]{1,0:T(8,128)}, f32[512,512]{1,0:T(8,128)}) custom-call(s32[3]{0:T(128)} %add_convert_fusion.flags_ref, f32[512,512]{1,0:T(8,128)} %get-tuple-element.40.d_ref, f32[512,512]{1,0:T(8,128)} %get-tuple-element.41.e_ref, f32[512,512]{1,0:T(8,128)} %get-tuple-element.42.s_ref, f32[512,512]{1,0:T(8,128)} %bed_ref.3, ...), custom_call_target="tpu_custom_call" | custom-call | tf_op jit(solution)/shard_map/pallas_call | solution.py:335
  80.1 3.7 %all-to-all-done.1 = f32[128,4,128]{2,1,0:T(4,128)S(1)} async-done(((f32[128,4,128]{2,1,0:T(4,128)}), f32[128,4,128]{2,1,0:T(4,128)S(1)}, u32[]{:S(2)}, u32[]{:S(2)}) %all-to-all-start.1) | async-done | bytes 262176 | tf_op jit(solution)/shard_map/all_to_all | solution.py:344
  83.8 0.8 add_add_fusion
  (67 shorter events, 1.6 us)
Async XLA Ops:
  0.6 0.7 copy-start.11
  0.7 0.7 copy-start.6
  0.7 0.7 copy-start.14
  5.5 9.3 %copy-start.12 = (f32[2,512]{1,0:T(2,128)S(1)}, f32[2,512]{1,0:T(2,128)}, u32[]{:S(2)}) copy-start(f32[2,512]{1,0:T(2,128)} %get-tuple-element.31) | copy-start | bytes 12292
  5.5 14.3 %collective-permute-start.2 = (f32[7,512]{1,0:T(8,128)}, f32[7,512]{1,0:T(8,128)S(1)}, u32[]{:S(2)}, u32[]{:S(2)}) collective-permute-start(f32[7,512]{1,0:T(8,128)} %get-tuple-element.32), channel_id=1, source_target_pairs={{0,1},{1,2},{2,3},{3,4},{4,5},{5,6},{6,7},{7,8},{8,9},{9,10},{10,1... | collective-permute-start | bytes 43016 | tf_op jit(solution)/shard_map/ppermute | solution.py:26
  9.5 10.2 %collective-permute-start.3 = (f32[5,512]{1,0:T(8,128)}, f32[5,512]{1,0:T(8,128)S(1)}, u32[]{:S(2)}, u32[]{:S(2)}) collective-permute-start(f32[5,512]{1,0:T(8,128)} %get-tuple-element.33), channel_id=1, source_target_pairs={{0,16},{16,32},{32,48},{48,64},{64,80},{80,96},{96,112},{1,17},{17... | collective-permute-start | bytes 30728 | tf_op jit(solution)/shard_map/ppermute | solution.py:26
  13.5 3.3 %copy-start.5 = (s32[256]{0:T(256)S(1)}, s32[256]{0:T(256)}, u32[]{:S(2)}) copy-start(s32[256]{0:T(256)} %param.16) | copy-start | bytes 3076
  13.5 5.6 %collective-permute-start = (f32[2,512]{1,0:T(2,128)}, f32[2,512]{1,0:T(2,128)S(1)}, u32[]{:S(2)}, u32[]{:S(2)}) collective-permute-start(f32[2,512]{1,0:T(2,128)} %get-tuple-element.30), channel_id=1, source_target_pairs={{1,0},{2,1},{3,2},{4,3},{5,4},{6,5},{7,6},{8,7},{9,8},{10,9},{11,1... | collective-permute-start | bytes 12296 | tf_op jit(solution)/shard_map/ppermute | solution.py:26
  14.8 4.9 %collective-permute-start.1 = (f32[2,512]{1,0:T(2,128)S(1)}, f32[2,512]{1,0:T(2,128)S(1)}, u32[]{:S(2)}, u32[]{:S(2)}) collective-permute-start(f32[2,512]{1,0:T(2,128)S(1)} %copy-done.12), channel_id=1, source_target_pairs={{16,0},{32,16},{48,32},{64,48},{80,64},{96,80},{112,96},{17,1},{33... | collective-permute-start | bytes 12296 | tf_op jit(solution)/shard_map/ppermute | solution.py:26
  17.2 0.9 %copy-start = (f32[256,128]{1,0:T(8,128)S(1)}, f32[256,128]{1,0:T(8,128)}, u32[]{:S(2)}) copy-start(f32[256,128]{1,0:T(8,128)} %get-tuple-element.34) | copy-start | bytes 393220
  19.1 1.6 %copy-start.9 = (f32[2,512]{1,0:T(2,128)}, f32[2,512]{1,0:T(2,128)S(1)}, u32[]{:S(2)}) copy-start(f32[2,512]{1,0:T(2,128)S(1)} %collective-permute-done.east_ref) | copy-start | bytes 12292
  19.8 0.9 %copy-start.10 = (f32[2,512]{1,0:T(2,128)}, f32[2,512]{1,0:T(2,128)S(1)}, u32[]{:S(2)}) copy-start(f32[2,512]{1,0:T(2,128)S(1)} %collective-permute-done.1.south_ref) | copy-start | bytes 12292
  19.8 0.9 %copy-start.3 = (f32[5,512]{1,0:T(8,128)}, f32[5,512]{1,0:T(8,128)S(1)}, u32[]{:S(2)}) copy-start(f32[5,512]{1,0:T(8,128)S(1)} %collective-permute-done.3.north_ref) | copy-start | bytes 30724
  19.8 11.7 %copy-start.1 = (f32[7,512]{1,0:T(8,128)}, f32[7,512]{1,0:T(8,128)S(1)}, u32[]{:S(2)}) copy-start(f32[7,512]{1,0:T(8,128)S(1)} %collective-permute-done.2.west_ref) | copy-start | bytes 43012
  20.7 22.9 %all-to-all-start = ((f32[128,1,640]{2,1,0:T(1,128)}), f32[128,1,640]{2,1,0:T(1,128)S(1)}, u32[]{:S(2)}, u32[]{:S(2)}) async-start(f32[128,1,640]{2,1,0:T(1,128)} %copy.32), calls=%async_computation | async-start | bytes 655360 | tf_op jit(solution)/shard_map/all_to_all | solution.py:320
  53.0 6.5 %copy-start.13 = (f32[2,512]{1,0:T(2,128)S(1)}, f32[2,512]{1,0:T(2,128)}, u32[]{:S(2)}) copy-start(f32[2,512]{1,0:T(2,128)} %get-tuple-element.44) | copy-start | bytes 12292
  53.0 11.5 %collective-permute-start.6 = (f32[7,512]{1,0:T(8,128)}, f32[7,512]{1,0:T(8,128)S(1)}, u32[]{:S(2)}, u32[]{:S(2)}) collective-permute-start(f32[7,512]{1,0:T(8,128)} %get-tuple-element.45), channel_id=1, source_target_pairs={{0,1},{1,2},{2,3},{3,4},{4,5},{5,6},{6,7},{7,8},{8,9},{9,10},{10,1... | collective-permute-start | bytes 43016 | tf_op jit(solution)/shard_map/ppermute | solution.py:26
  55.3 9.2 %collective-permute-start.7 = (f32[5,512]{1,0:T(8,128)}, f32[5,512]{1,0:T(8,128)S(1)}, u32[]{:S(2)}, u32[]{:S(2)}) collective-permute-start(f32[5,512]{1,0:T(8,128)} %get-tuple-element.46), channel_id=1, source_target_pairs={{0,16},{16,32},{32,48},{48,64},{64,80},{80,96},{96,112},{1,17},{17... | collective-permute-start | bytes 30728 | tf_op jit(solution)/shard_map/ppermute | solution.py:26
  58.3 5.1 %collective-permute-start.4 = (f32[2,512]{1,0:T(2,128)}, f32[2,512]{1,0:T(2,128)S(1)}, u32[]{:S(2)}, u32[]{:S(2)}) collective-permute-start(f32[2,512]{1,0:T(2,128)} %get-tuple-element.43), channel_id=1, source_target_pairs={{1,0},{2,1},{3,2},{4,3},{5,4},{6,5},{7,6},{8,7},{9,8},{10,9},{11,1... | collective-permute-start | bytes 12296 | tf_op jit(solution)/shard_map/ppermute | solution.py:26
  59.6 4.9 %collective-permute-start.5 = (f32[2,512]{1,0:T(2,128)S(1)}, f32[2,512]{1,0:T(2,128)S(1)}, u32[]{:S(2)}, u32[]{:S(2)}) collective-permute-start(f32[2,512]{1,0:T(2,128)S(1)} %copy-done.13), channel_id=1, source_target_pairs={{16,0},{32,16},{48,32},{64,48},{80,64},{96,80},{112,96},{17,1},{33... | collective-permute-start | bytes 12296 | tf_op jit(solution)/shard_map/ppermute | solution.py:26
  63.4 1.1 %copy-start.7 = (f32[2,512]{1,0:T(2,128)}, f32[2,512]{1,0:T(2,128)S(1)}, u32[]{:S(2)}) copy-start(f32[2,512]{1,0:T(2,128)S(1)} %collective-permute-done.4.east_ref) | copy-start | bytes 12292
  64.5 0.6 copy-start.8
  64.5 0.6 copy-start.4
  64.5 8.1 %copy-start.2 = (f32[7,512]{1,0:T(8,128)}, f32[7,512]{1,0:T(8,128)S(1)}, u32[]{:S(2)}) copy-start(f32[7,512]{1,0:T(8,128)S(1)} %collective-permute-done.6.west_ref) | copy-start | bytes 43012
  65.1 18.7 %all-to-all-start.1 = ((f32[128,4,128]{2,1,0:T(4,128)}), f32[128,4,128]{2,1,0:T(4,128)S(1)}, u32[]{:S(2)}, u32[]{:S(2)}) async-start(f32[128,4,128]{2,1,0:T(4,128)} %bitcast.17), calls=%async_computation.1 | async-start | bytes 524288 | tf_op jit(solution)/shard_map/all_to_all | solution.py:344

commit v17 on v13

--- a/solution.py
+++ b/solution.py
@@ -80,11 +80,11 @@
 
 def open_masks(flags_ref, land):
     ny, nx = land.shape
-    col = lax.broadcasted_iota(jnp.int32, (ny, nx), 1)
-    row = lax.broadcasted_iota(jnp.int32, (ny, nx), 0)
-    eopen = jnp.where((col == nx - 1) & (flags_ref[0] == 1), 0.0, land)
-    sopen = jnp.where((row == ny - 1) & (flags_ref[1] == 1), 0.0, land)
-    return col, row, eopen, sopen
+    col = lax.broadcasted_iota(jnp.int32, (1, nx), 1)
+    row = lax.broadcasted_iota(jnp.int32, (ny, 1), 0)
+    east_keep = jnp.where((col == nx - 1) & (flags_ref[0] == 1), 0.0, 1.0)
+    south_keep = jnp.where((row == ny - 1) & (flags_ref[1] == 1), 0.0, 1.0)
+    return col, row, land * east_keep, land * south_keep
 
 
 def edge_kernel(flags_ref, d_ref, land_ref, bed_first_col, bed_last_col, bed_first_row,

time: 78.9 us -> 78.9 us (level)
  no operation moved by 1% of the time
where the time goes in v17:
time: 78.9 us; the launch traced here: 78.2 us
  starting transfers between devices  46.9 us (59%)
  Pallas kernels  18.5 us (23%)
  local copies, waits for them, and re-layouts  5.26 us (7%)
  matrix products  4.47 us (6%)
  other arithmetic  1.88 us (2%)
  between operations  1.1 us (1%)
    ppermute x9, starting transfers between devices, shifted(): lax.ppermute(value, axis, [(source, source + steps) for source in range(f...  24.8 us
    pallas_call x2, Pallas kernels, body(): step_call(not last)  15.2 us
    all_to_all x1, starting transfers between devices, body(): lax.all_to_all(start_lateral(tile_parts).reshape(device_count, first_rows...  11.4 us
    all_to_all x1, starting transfers between devices, body(): got_second = lax.all_to_all(lateral_started, ('gy', 'gx'), 0, 0, tiled=True)  10.7 us
    pallas_call x1, Pallas kernels, body(): pl.pallas_call(edge_kernel, grid=(1,), out_shape=(tile_shape,) + edge_sha...  3.28 us
    unnamed x35, local copies, waits for them, and re-layouts  2.31 us
    dot_general x2, matrix products, start_lateral(): jnp.dot(row_onehot, part, precision=lax.Precision.HIGH)  2.23 us
    dot_general x4, matrix products, block_term(): jnp.einsum('tb,tc->bc', onehot, values, precision=lax.Precision.HIGHEST)  1.61 us
  transfers between devices with their start and end apart: 11, of which 2 were waited for; matrix products, arithmetic and copies ran while one was open for 8% of the time, Pallas kernels for 19%

profile of v17, /device:TPU:1, one launch (start us, length us, event | category | flops | bytes accessed | tf_op | source)
XLA Modules:
  0.0 78.2 jit_solution(7609249476338138911)
XLA Ops:
  0.7 0.7 copy-done.7
  1.4 0.2 fusion.19
  1.6 0.6 add_convert_fusion.flags_ref
  2.2 3.3 %shard_map.129 = (f32[256,128]{1,0:T(8,128)}, f32[2,512]{1,0:T(2,128)}, f32[2,512]{1,0:T(2,128)}, f32[5,512]{1,0:T(8,128)}, f32[5,512]{1,0:T(8,128)}) custom-call(s32[3]{0:T(128)} %add_convert_fusion.flags_ref, f32[512,512]{1,0:T(8,128)} %d_ref.3, s32[512,512]{1,0:T(8,128)} %land_ref.5, f32[512,512]{1,0:T(8,128)} %bed_ref.3, f32[512,512]{1,0:T(8,128)} %bed_ref.3, ...), custom_call_target="tpu_custom_call" | custom-call | tf_op jit(solution)/shard_map/pallas_call | solution.py:210
  5.5 0.7 pad_maximum_fusion.1
  6.3 4.0 %collective-permute-start.2 = (f32[7,512]{1,0:T(8,128)S(1)}, f32[7,512]{1,0:T(8,128)S(1)}, u32[]{:S(2)}, u32[]{:S(2)}) collective-permute-start(f32[7,512]{1,0:T(8,128)S(1)} %pad_maximum_fusion.1), channel_id=1, source_target_pairs={{0,1},{1,2},{2,3},{3,4},{4,5},{5,6},{6,7},{7,8},{8,9},{9,10},{10,1... | collective-permute-start | bytes 43016 | tf_op jit(solution)/shard_map/ppermute | solution.py:26
  10.3 4.0 %collective-permute-start.3 = (f32[5,512]{1,0:T(8,128)S(1)}, f32[5,512]{1,0:T(8,128)S(1)}, u32[]{:S(2)}, u32[]{:S(2)}) collective-permute-start(f32[5,512]{1,0:T(8,128)S(1)} %copy-done.12), channel_id=1, source_target_pairs={{0,16},{16,32},{32,48},{48,64},{64,80},{80,96},{96,112},{1,17},{17... | collective-permute-start | bytes 30728 | tf_op jit(solution)/shard_map/ppermute | solution.py:26
  14.3 1.3 %collective-permute-start = (f32[2,512]{1,0:T(2,128)S(1)}, f32[2,512]{1,0:T(2,128)S(1)}, u32[]{:S(2)}, u32[]{:S(2)}) collective-permute-start(f32[2,512]{1,0:T(2,128)S(1)} %copy-done.14), channel_id=1, source_target_pairs={{1,0},{2,1},{3,2},{4,3},{5,4},{6,5},{7,6},{8,7},{9,8},{10,9},{11,1... | collective-permute-start | bytes 12296 | tf_op jit(solution)/shard_map/ppermute | solution.py:26
  15.6 1.9 %collective-permute-start.1 = (f32[2,512]{1,0:T(2,128)S(1)}, f32[2,512]{1,0:T(2,128)S(1)}, u32[]{:S(2)}, u32[]{:S(2)}) collective-permute-start(f32[2,512]{1,0:T(2,128)S(1)} %copy-done.13), channel_id=1, source_target_pairs={{16,0},{32,16},{48,32},{64,48},{80,64},{96,80},{112,96},{17,1},{33... | collective-permute-start | bytes 12296 | tf_op jit(solution)/shard_map/ppermute | solution.py:26
  17.7 0.2 fusion.6
  18.5 0.4 copy-done
  18.9 0.3 fusion
  19.4 0.2 fusion.2
  19.9 0.9 %copy.32 = f32[128,1,640]{2,1,0:T(1,128)} copy(f32[128,1,640]{0,2,1:T(8,128)S(1)} %bitcast.39) | data formatting | bytes 655360 | tf_op jit(solution)/shard_map/all_to_all | solution.py:266
  20.8 11.4 %all-to-all-start = ((f32[128,1,640]{2,1,0:T(1,128)}), f32[128,1,640]{2,1,0:T(1,128)S(1)}, u32[]{:S(2)}, u32[]{:S(2)}) async-start(f32[128,1,640]{2,1,0:T(1,128)} %copy.32), calls=%async_computation | async-start | bytes 655360 | tf_op jit(solution)/shard_map/all_to_all | solution.py:266
  32.2 0.2 fusion.15
  32.5 0.5 copy-done.8
  33.1 7.8 %shard_map.130 = (f32[512,512]{1,0:T(8,128)}, f32[512,512]{1,0:T(8,128)}, f32[512,512]{1,0:T(8,128)}, f32[256,128]{1,0:T(8,128)}, f32[2,512]{1,0:T(2,128)}, /*in...) custom-call(s32[3]{0:T(128)} %add_convert_fusion.flags_ref, f32[512,512]{1,0:T(8,128)} %d_ref.3, ...), custom_call_target="tpu_custom_call" | custom-call | tf_op jit(solution)/shard_map/pallas_call | solution.py:306
  40.9 3.3 %collective-permute-start.6 = (f32[5,512]{1,0:T(8,128)}, f32[5,512]{1,0:T(8,128)S(1)}, u32[]{:S(2)}, u32[]{:S(2)}) collective-permute-start(f32[5,512]{1,0:T(8,128)} %get-tuple-element.35), channel_id=1, source_target_pairs={{0,1},{1,2},{2,3},{3,4},{4,5},{5,6},{6,7},{7,8},{8,9},{9,10},{10,1... | collective-permute-start | bytes 30728 | tf_op jit(solution)/shard_map/ppermute | solution.py:26
  44.1 3.7 %collective-permute-start.7 = (f32[5,512]{1,0:T(8,128)}, f32[5,512]{1,0:T(8,128)S(1)}, u32[]{:S(2)}, u32[]{:S(2)}) collective-permute-start(f32[5,512]{1,0:T(8,128)} %get-tuple-element.36), channel_id=1, source_target_pairs={{0,16},{16,32},{32,48},{48,64},{64,80},{80,96},{96,112},{1,17},{17... | collective-permute-start | bytes 30728 | tf_op jit(solution)/shard_map/ppermute | solution.py:26
  47.8 1.3 %collective-permute-start.4 = (f32[2,512]{1,0:T(2,128)}, f32[2,512]{1,0:T(2,128)S(1)}, u32[]{:S(2)}, u32[]{:S(2)}) collective-permute-start(f32[2,512]{1,0:T(2,128)} %get-tuple-element.33), channel_id=1, source_target_pairs={{1,0},{2,1},{3,2},{4,3},{5,4},{6,5},{7,6},{8,7},{9,8},{10,9},{11,1... | collective-permute-start | bytes 12296 | tf_op jit(solution)/shard_map/ppermute | solution.py:26
  49.1 1.9 %collective-permute-start.5 = (f32[2,512]{1,0:T(2,128)S(1)}, f32[2,512]{1,0:T(2,128)S(1)}, u32[]{:S(2)}, u32[]{:S(2)}) collective-permute-start(f32[2,512]{1,0:T(2,128)S(1)} %copy-done.15), channel_id=1, source_target_pairs={{16,0},{32,16},{48,32},{64,48},{80,64},{96,80},{112,96},{17,1},{33... | collective-permute-start | bytes 12296 | tf_op jit(solution)/shard_map/ppermute | solution.py:26
  51.0 1.9 %fusion.1 = f32[512,128]{1,0:T(8,128)} fusion(f32[256,128]{1,0:T(8,128)} %get-tuple-element.37, s32[256]{0:T(256)S(1)} %eq.131), kind=kOutput, calls=%fused_computation.5 | convolution fusion | flops 100794368 | bytes 394240 | tf_op jit(solution)/shard_map/dot_general | solution.py:258
  53.0 0.7 slice.30
  54.1 0.4 copy-done.10
  55.1 10.7 %all-to-all-start.1 = ((f32[128,4,128]{2,1,0:T(4,128)}), f32[128,4,128]{2,1,0:T(4,128)S(1)}, u32[]{:S(2)}, u32[]{:S(2)}) async-start(f32[128,4,128]{2,1,0:T(4,128)} %bitcast.8), calls=%async_computation.1 | async-start | bytes 524288 | tf_op jit(solution)/shard_map/all_to_all | solution.py:315
  65.7 0.2 add_add_fusion.1
  66.0 0.3 fusion.17
  66.2 3.4 %collective-permute-start.8 = (f32[8,128]{1,0:T(8,128)S(1)}, f32[8,128]{1,0:T(8,128)S(1)}, u32[]{:S(2)}, u32[]{:S(2)}) collective-permute-start(f32[8,128]{1,0:T(8,128)S(1)} %fusion.17), channel_id=1, source_target_pairs={{0,1},{1,2},{2,3},{3,4},{4,5},{5,6},{6,7},{7,8},{8,9},{9,10},{10,1... | collective-permute-start | bytes 12296 | tf_op jit(solution)/shard_map/ppermute | solution.py:26
  69.7 7.4 %shard_map.131 = (f32[512,512]{1,0:T(8,128)}, f32[512,512]{1,0:T(8,128)}, f32[512,512]{1,0:T(8,128)}) custom-call(s32[3]{0:T(128)} %add_convert_fusion.flags_ref, f32[512,512]{1,0:T(8,128)} %get-tuple-element.30.d_ref, f32[512,512]{1,0:T(8,128)} %get-tuple-element.31.e_ref, f32[512,512]{1,0:T(8,128)} %get-tuple-element.32.s_ref, f32[512,512]{1,0:T(8,128)} %bed_ref.3, ...), custom_call_target="tpu_custom_call" | custom-call | tf_op jit(solution)/shard_map/pallas_call | solution.py:306
  77.2 0.2 convolution_multiply_fusion
  77.4 0.9 %add_add_fusion = f32[16,128]{1,0:T(8,128)} fusion(f32[16,128]{1,0:T(8,128)S(1)} %convolution_multiply_fusion, f32[8,128]{1,0:T(8,128)S(1)} %collective-permute-done.8, f32[16,128]{1,0:T(8,128)S(1)} %add_add_fusion.1, s32[16]{0:T(128)S(1)} %iota_add_fusion, s32[16]{0:T(128)S(1)} %copy-done.16, f32[16,128]{1,0:T(8,128)S(1)} %copy-done.7), kind=kOutput, calls=%fused_computation.34 | convolution fusion | flops 418048 | bytes 36992 | tf_op jit(solution)/shard_map/tb,tc->bc/dot_general | solution.py:40
  (73 shorter events, 2.2 us)
Async XLA Ops:
  0.6 0.7 copy-start.7
  0.6 0.7 copy-start.6
  0.7 0.7 copy-start.16
  5.5 4.8 %copy-start.12 = (f32[5,512]{1,0:T(8,128)S(1)}, f32[5,512]{1,0:T(8,128)}, u32[]{:S(2)}) copy-start(f32[5,512]{1,0:T(8,128)} %get-tuple-element.29) | copy-start | bytes 30724
  5.5 8.8 %copy-start.14 = (f32[2,512]{1,0:T(2,128)S(1)}, f32[2,512]{1,0:T(2,128)}, u32[]{:S(2)}) copy-start(f32[2,512]{1,0:T(2,128)} %get-tuple-element.26) | copy-start | bytes 12292
  6.3 9.3 %copy-start.13 = (f32[2,512]{1,0:T(2,128)S(1)}, f32[2,512]{1,0:T(2,128)}, u32[]{:S(2)}) copy-start(f32[2,512]{1,0:T(2,128)} %get-tuple-element.27) | copy-start | bytes 12292
  6.3 26.2 %collective-permute-start.2 = (f32[7,512]{1,0:T(8,128)S(1)}, f32[7,512]{1,0:T(8,128)S(1)}, u32[]{:S(2)}, u32[]{:S(2)}) collective-permute-start(f32[7,512]{1,0:T(8,128)S(1)} %pad_maximum_fusion.1), channel_id=1, source_target_pairs={{0,1},{1,2},{2,3},{3,4},{4,5},{5,6},{6,7},{7,8},{8,9},{9,10},{10,1... | collective-permute-start | bytes 43016 | tf_op jit(solution)/shard_map/ppermute | solution.py:26
  10.3 22.2 %collective-permute-start.3 = (f32[5,512]{1,0:T(8,128)S(1)}, f32[5,512]{1,0:T(8,128)S(1)}, u32[]{:S(2)}, u32[]{:S(2)}) collective-permute-start(f32[5,512]{1,0:T(8,128)S(1)} %copy-done.12), channel_id=1, source_target_pairs={{0,16},{16,32},{32,48},{48,64},{64,80},{80,96},{96,112},{1,17},{17... | collective-permute-start | bytes 30728 | tf_op jit(solution)/shard_map/ppermute | solution.py:26
  14.3 3.3 %copy-start.5 = (s32[256]{0:T(256)S(1)}, s32[256]{0:T(256)}, u32[]{:S(2)}) copy-start(s32[256]{0:T(256)} %param.16) | copy-start | bytes 3076
  14.3 18.1 %collective-permute-start = (f32[2,512]{1,0:T(2,128)S(1)}, f32[2,512]{1,0:T(2,128)S(1)}, u32[]{:S(2)}, u32[]{:S(2)}) collective-permute-start(f32[2,512]{1,0:T(2,128)S(1)} %copy-done.14), channel_id=1, source_target_pairs={{1,0},{2,1},{3,2},{4,3},{5,4},{6,5},{7,6},{8,7},{9,8},{10,9},{11,1... | collective-permute-start | bytes 12296 | tf_op jit(solution)/shard_map/ppermute | solution.py:26
  15.6 16.8 %collective-permute-start.1 = (f32[2,512]{1,0:T(2,128)S(1)}, f32[2,512]{1,0:T(2,128)S(1)}, u32[]{:S(2)}, u32[]{:S(2)}) collective-permute-start(f32[2,512]{1,0:T(2,128)S(1)} %copy-done.13), channel_id=1, source_target_pairs={{16,0},{32,16},{48,32},{64,48},{80,64},{96,80},{112,96},{17,1},{33... | collective-permute-start | bytes 12296 | tf_op jit(solution)/shard_map/ppermute | solution.py:26
  18.0 0.9 %copy-start = (f32[256,128]{1,0:T(8,128)S(1)}, f32[256,128]{1,0:T(8,128)}, u32[]{:S(2)}) copy-start(f32[256,128]{1,0:T(8,128)} %get-tuple-element.38) | copy-start | bytes 393220
  20.8 33.0 %all-to-all-start = ((f32[128,1,640]{2,1,0:T(1,128)}), f32[128,1,640]{2,1,0:T(1,128)S(1)}, u32[]{:S(2)}, u32[]{:S(2)}) async-start(f32[128,1,640]{2,1,0:T(1,128)} %copy.32), calls=%async_computation | async-start | bytes 655360 | tf_op jit(solution)/shard_map/all_to_all | solution.py:266
  32.4 0.6 copy-start.8
  32.5 0.6 copy-start.9
  32.5 0.6 copy-start.2
  32.5 0.6 copy-start.1
  40.9 8.2 %copy-start.15 = (f32[2,512]{1,0:T(2,128)S(1)}, f32[2,512]{1,0:T(2,128)}, u32[]{:S(2)}) copy-start(f32[2,512]{1,0:T(2,128)} %get-tuple-element.34) | copy-start | bytes 12292
  40.9 13.2 %collective-permute-start.6 = (f32[5,512]{1,0:T(8,128)}, f32[5,512]{1,0:T(8,128)S(1)}, u32[]{:S(2)}, u32[]{:S(2)}) collective-permute-start(f32[5,512]{1,0:T(8,128)} %get-tuple-element.35), channel_id=1, source_target_pairs={{0,1},{1,2},{2,3},{3,4},{4,5},{5,6},{6,7},{7,8},{8,9},{9,10},{10,1... | collective-permute-start | bytes 30728 | tf_op jit(solution)/shard_map/ppermute | solution.py:26
  44.1 9.9 %collective-permute-start.7 = (f32[5,512]{1,0:T(8,128)}, f32[5,512]{1,0:T(8,128)S(1)}, u32[]{:S(2)}, u32[]{:S(2)}) collective-permute-start(f32[5,512]{1,0:T(8,128)} %get-tuple-element.36), channel_id=1, source_target_pairs={{0,16},{16,32},{32,48},{48,64},{64,80},{80,96},{96,112},{1,17},{17... | collective-permute-start | bytes 30728 | tf_op jit(solution)/shard_map/ppermute | solution.py:26
  47.8 6.1 %collective-permute-start.4 = (f32[2,512]{1,0:T(2,128)}, f32[2,512]{1,0:T(2,128)S(1)}, u32[]{:S(2)}, u32[]{:S(2)}) collective-permute-start(f32[2,512]{1,0:T(2,128)} %get-tuple-element.33), channel_id=1, source_target_pairs={{1,0},{2,1},{3,2},{4,3},{5,4},{6,5},{7,6},{8,7},{9,8},{10,9},{11,1... | collective-permute-start | bytes 12296 | tf_op jit(solution)/shard_map/ppermute | solution.py:26
  49.1 4.9 %collective-permute-start.5 = (f32[2,512]{1,0:T(2,128)S(1)}, f32[2,512]{1,0:T(2,128)S(1)}, u32[]{:S(2)}, u32[]{:S(2)}) collective-permute-start(f32[2,512]{1,0:T(2,128)S(1)} %copy-done.15), channel_id=1, source_target_pairs={{16,0},{32,16},{48,32},{64,48},{80,64},{96,80},{112,96},{17,1},{33... | collective-permute-start | bytes 12296 | tf_op jit(solution)/shard_map/ppermute | solution.py:26
  53.9 0.6 copy-start.10
  54.0 0.6 copy-start.11
  54.1 0.6 copy-start.3
  54.1 0.6 copy-start.4
  55.1 22.1 %all-to-all-start.1 = ((f32[128,4,128]{2,1,0:T(4,128)}), f32[128,4,128]{2,1,0:T(4,128)S(1)}, u32[]{:S(2)}, u32[]{:S(2)}) async-start(f32[128,4,128]{2,1,0:T(4,128)} %bitcast.8), calls=%async_computation.1 | async-start | bytes 524288 | tf_op jit(solution)/shard_map/all_to_all | solution.py:315
  66.2 11.2 %collective-permute-start.8 = (f32[8,128]{1,0:T(8,128)S(1)}, f32[8,128]{1,0:T(8,128)S(1)}, u32[]{:S(2)}, u32[]{:S(2)}) collective-permute-start(f32[8,128]{1,0:T(8,128)S(1)} %fusion.17), channel_id=1, source_target_pairs={{0,1},{1,2},{2,3},{3,4},{4,5},{5,6},{6,7},{7,8},{8,9},{9,10},{10,1... | collective-permute-start | bytes 12296 | tf_op jit(solution)/shard_map/ppermute | solution.py:26

commit v18 on v13

--- a/solution.py
+++ b/solution.py
@@ -152,6 +152,57 @@
         tile_out[...] = tile_rows(next_drained)
         write_edges(bed + new_depth, new_depth, flux_e, flux_s, rough, eopen, sopen,
                     to_west, to_north, to_east, to_south)
+
+
+def last_step_kernel(total_rows, flags_ref, d_ref, e_ref, s_ref, bed_ref, r_ref, land_ref,
+                     d_up, s_up, bed_up, r_up, land_up, d_dn, bed_dn,
+                     east_ref, south_ref, west_ref, north_ref, d_out, e_out, s_out):
+    block = pl.program_id(0)
+    blocks = pl.num_programs(0)
+    tr, nx = d_ref.shape
+    depth = d_ref[...]
+    bed = bed_ref[...]
+    land = land_ref[...].astype(jnp.float32)
+    rough = r_ref[...]
+    level = bed + depth
+    col = lax.broadcasted_iota(jnp.int32, (1, nx), 1)
+    row = lax.broadcasted_iota(jnp.int32, (tr, 1), 0)
+    eopen = land * jnp.where((col == nx - 1) & (flags_ref[0] == 1), 0.0, 1.0)
+    sopen = land * jnp.where(
+        (block * tr + row == total_rows - 1) & (flags_ref[1] == 1), 0.0, 1.0
+    )
+    east = rows_as_cols(east_ref[...])
+    west = rows_as_cols(west_ref[...])
+    level_e = jnp.where(col == nx - 1, east[:, 0:1], pltpu.roll(level, nx - 1, 1))
+    depth_e = jnp.where(col == nx - 1, east[:, 1:2], pltpu.roll(depth, nx - 1, 1))
+    at_bottom = block == blocks - 1
+    below_depth = jnp.where(at_bottom, south_ref[1:2, :], d_dn[0:1, :])
+    below_level = jnp.where(at_bottom, south_ref[0:1, :], bed_dn[0:1, :] + d_dn[0:1, :])
+    level_s = jnp.where(row == tr - 1, below_level, pltpu.roll(level, tr - 1, 0))
+    depth_s = jnp.where(row == tr - 1, below_depth, pltpu.roll(depth, tr - 1, 0))
+    flux_e = face_update(e_ref[...], level, level_e, depth, depth_e, rough, eopen)
+    flux_s = face_update(s_ref[...], level, level_s, depth, depth_s, rough, sopen)
+    west_edge = face_update(
+        west[:, 0:1], west[:, 1:2], level[:, 0:1], west[:, 2:3], depth[:, 0:1],
+        west[:, 3:4], west[:, 4:5],
+    )
+    west_edge = jnp.where(flags_ref[2] == 1, 0.0, west_edge)
+    outer_north = face_update(
+        north_ref[0:1, :], north_ref[1:2, :], level[0:1, :], north_ref[2:3, :], depth[0:1, :],
+        north_ref[3:4, :], north_ref[4:5, :],
+    )
+    up_depth = d_up[7:8, :]
+    inner_north = face_update(
+        s_up[7:8, :], bed_up[7:8, :] + up_depth, level[0:1, :], up_depth, depth[0:1, :],
+        r_up[7:8, :], land_up[7:8, :].astype(jnp.float32),
+    )
+    north_edge = jnp.where(block == 0, outer_north, inner_north)
+    west_flux = jnp.where(col == 0, west_edge, pltpu.roll(flux_e, 1, 1))
+    north_flux = jnp.where(row == 0, north_edge, pltpu.roll(flux_s, 1, 0))
+    drained = drain_rate * land * jnp.abs(depth)
+    d_out[...] = depth - mass_gain * (flux_e - west_flux + (flux_s - north_flux)) - drained
+    e_out[...] = flux_e
+    s_out[...] = flux_s
 
 
 def edge_shapes(ny, nx):
@@ -277,6 +328,27 @@
 
     first_outflow = reach_outflow(storage)
     ahead_rows = SPAN * reach_width // cell_cols
+    tr = 128
+    nblk = cell_rows // tr
+    main_spec = pl.BlockSpec((tr, cell_cols), lambda i: (i, 0))
+    up_spec = pl.BlockSpec((8, cell_cols), lambda i: (jnp.maximum(i * (tr // 8) - 1, 0), 0))
+    dn_spec = pl.BlockSpec(
+        (8, cell_cols), lambda i: (jnp.minimum((i + 1) * (tr // 8), cell_rows // 8 - 1), 0)
+    )
+    last_call = pl.pallas_call(
+        functools.partial(last_step_kernel, cell_rows),
+        grid=(nblk,),
+        out_shape=(grid_shape, grid_shape, grid_shape),
+        in_specs=[smem_spec] + [main_spec] * 6 + [up_spec] * 5 + [dn_spec] * 2
+        + [
+            pl.BlockSpec((2, tr), lambda i: (0, i)),
+            pl.BlockSpec((2, cell_cols), lambda i: (0, 0)),
+            pl.BlockSpec((5, tr), lambda i: (0, i)),
+            pl.BlockSpec((5, cell_cols), lambda i: (0, 0)),
+        ],
+        out_specs=[main_spec] * 3,
+    )
+
     depth = water_depth
     for step in range(STEPS):
         to_west, to_north, to_east, to_south = edges
@@ -303,10 +375,17 @@
                     (east_in, south_in, west_in, north_in, lateral_started, got_first)
                 )
             )
-        outs = step_call(not last)(
-            flags, depth, flux_east, flux_south, bed_level, roughness, land_mask,
-            east_in, south_in, west_in, north_in,
-        )
+        if last:
+            outs = last_call(
+                flags, depth, flux_east, flux_south, bed_level, roughness, land_mask,
+                depth, flux_south, bed_level, roughness, land_mask, depth, bed_level,
+                east_in, south_in, west_in, north_in,
+            )
+        else:
+            outs = step_call(True)(
+                flags, depth, flux_east, flux_south, bed_level, roughness, land_mask,
+                east_in, south_in, west_in, north_in,
+            )
         depth, flux_east, flux_south = outs[:3]
         if not last:
             tile_parts.append(outs[3])

time: 78.9 us -> 79 us (level)
  no operation moved by 1% of the time
where the time goes in v18:
time: 79 us; the launch traced here: 78.2 us
  starting transfers between devices  46.7 us (59%)
  Pallas kernels  18.3 us (23%)
  local copies, waits for them, and re-layouts  5.26 us (7%)
  matrix products  4.46 us (6%)
  other arithmetic  1.88 us (2%)
  between operations  1.11 us (1%)
    ppermute x9, starting transfers between devices, shifted(): lax.ppermute(value, axis, [(source, source + steps) for source in range(f...  24.6 us
    all_to_all x1, starting transfers between devices, body(): lax.all_to_all(start_lateral(tile_parts).reshape(device_count, first_rows...  11.4 us
    all_to_all x1, starting transfers between devices, body(): got_second = lax.all_to_all(lateral_started, ('gy', 'gx'), 0, 0, tiled=True)  10.7 us
    pallas_call x1, Pallas kernels, body(): step_call(True)  7.74 us
    pallas_call x1, Pallas kernels, body(): last_call(flags, depth, flux_east, flux_south, bed_level, roughness, land...  7.26 us
    pallas_call x1, Pallas kernels, body(): pl.pallas_call(edge_kernel, grid=(1,), out_shape=(tile_shape,) + edge_sha...  3.29 us
    unnamed x35, local copies, waits for them, and re-layouts  2.31 us
    dot_general x2, matrix products, start_lateral(): jnp.dot(row_onehot, part, precision=lax.Precision.HIGH)  2.23 us
  transfers between devices with their start and end apart: 11, of which 2 were waited for; matrix products, arithmetic and copies ran while one was open for 8% of the time, Pallas kernels for 19%

profile of v18, /device:TPU:1, one launch (start us, length us, event | category | flops | bytes accessed | tf_op | source)
XLA Modules:
  0.0 78.2 jit_solution(3121357150649227587)
XLA Ops:
  0.7 0.7 copy-done.7
  1.4 0.2 fusion.19
  1.6 0.6 add_convert_fusion.flags_ref
  2.2 3.3 %shard_map.129 = (f32[256,128]{1,0:T(8,128)}, f32[2,512]{1,0:T(2,128)}, f32[2,512]{1,0:T(2,128)}, f32[5,512]{1,0:T(8,128)}, f32[5,512]{1,0:T(8,128)}) custom-call(s32[3]{0:T(128)} %add_convert_fusion.flags_ref, f32[512,512]{1,0:T(8,128)} %d_ref.3, s32[512,512]{1,0:T(8,128)} %land_up.1, f32[512,512]{1,0:T(8,128)} %bed_dn.1, f32[512,512]{1,0:T(8,128)} %bed_dn.1, ...), custom_call_target="tpu_custom_call" | custom-call | tf_op jit(solution)/shard_map/pallas_call | solution.py:261
  5.5 0.7 pad_maximum_fusion.1
  6.3 4.0 %collective-permute-start.2 = (f32[7,512]{1,0:T(8,128)S(1)}, f32[7,512]{1,0:T(8,128)S(1)}, u32[]{:S(2)}, u32[]{:S(2)}) collective-permute-start(f32[7,512]{1,0:T(8,128)S(1)} %pad_maximum_fusion.1), channel_id=1, source_target_pairs={{0,1},{1,2},{2,3},{3,4},{4,5},{5,6},{6,7},{7,8},{8,9},{9,10},{10,1... | collective-permute-start | bytes 43016 | tf_op jit(solution)/shard_map/ppermute | solution.py:26
  10.3 4.0 %collective-permute-start.3 = (f32[5,512]{1,0:T(8,128)S(1)}, f32[5,512]{1,0:T(8,128)S(1)}, u32[]{:S(2)}, u32[]{:S(2)}) collective-permute-start(f32[5,512]{1,0:T(8,128)S(1)} %copy-done.12), channel_id=1, source_target_pairs={{0,16},{16,32},{32,48},{48,64},{64,80},{80,96},{96,112},{1,17},{17... | collective-permute-start | bytes 30728 | tf_op jit(solution)/shard_map/ppermute | solution.py:26
  14.3 1.3 %collective-permute-start = (f32[2,512]{1,0:T(2,128)S(1)}, f32[2,512]{1,0:T(2,128)S(1)}, u32[]{:S(2)}, u32[]{:S(2)}) collective-permute-start(f32[2,512]{1,0:T(2,128)S(1)} %copy-done.14), channel_id=1, source_target_pairs={{1,0},{2,1},{3,2},{4,3},{5,4},{6,5},{7,6},{8,7},{9,8},{10,9},{11,1... | collective-permute-start | bytes 12296 | tf_op jit(solution)/shard_map/ppermute | solution.py:26
  15.6 1.9 %collective-permute-start.1 = (f32[2,512]{1,0:T(2,128)S(1)}, f32[2,512]{1,0:T(2,128)S(1)}, u32[]{:S(2)}, u32[]{:S(2)}) collective-permute-start(f32[2,512]{1,0:T(2,128)S(1)} %copy-done.13), channel_id=1, source_target_pairs={{16,0},{32,16},{48,32},{64,48},{80,64},{96,80},{112,96},{17,1},{33... | collective-permute-start | bytes 12296 | tf_op jit(solution)/shard_map/ppermute | solution.py:26
  18.5 0.4 copy-done
  18.9 0.3 fusion
  19.4 0.2 fusion.2
  19.9 0.9 %copy.32 = f32[128,1,640]{2,1,0:T(1,128)} copy(f32[128,1,640]{0,2,1:T(8,128)S(1)} %bitcast.39) | data formatting | bytes 655360 | tf_op jit(solution)/shard_map/all_to_all | solution.py:317
  20.8 11.4 %all-to-all-start = ((f32[128,1,640]{2,1,0:T(1,128)}), f32[128,1,640]{2,1,0:T(1,128)S(1)}, u32[]{:S(2)}, u32[]{:S(2)}) async-start(f32[128,1,640]{2,1,0:T(1,128)} %copy.32), calls=%async_computation | async-start | bytes 655360 | tf_op jit(solution)/shard_map/all_to_all | solution.py:317
  32.2 0.2 fusion.15
  32.5 0.5 copy-done.8
  33.1 7.7 %shard_map.130 = (f32[512,512]{1,0:T(8,128)}, f32[512,512]{1,0:T(8,128)}, f32[512,512]{1,0:T(8,128)}, f32[256,128]{1,0:T(8,128)}, f32[2,512]{1,0:T(2,128)}, /*in...) custom-call(s32[3]{0:T(128)} %add_convert_fusion.flags_ref, f32[512,512]{1,0:T(8,128)} %d_ref.3, ...), custom_call_target="tpu_custom_call" | custom-call | tf_op jit(solution)/shard_map/pallas_call | solution.py:385
  40.9 3.3 %collective-permute-start.6 = (f32[5,512]{1,0:T(8,128)}, f32[5,512]{1,0:T(8,128)S(1)}, u32[]{:S(2)}, u32[]{:S(2)}) collective-permute-start(f32[5,512]{1,0:T(8,128)} %get-tuple-element.35), channel_id=1, source_target_pairs={{0,1},{1,2},{2,3},{3,4},{4,5},{5,6},{6,7},{7,8},{8,9},{9,10},{10,1... | collective-permute-start | bytes 30728 | tf_op jit(solution)/shard_map/ppermute | solution.py:26
  44.1 3.7 %collective-permute-start.7 = (f32[5,512]{1,0:T(8,128)}, f32[5,512]{1,0:T(8,128)S(1)}, u32[]{:S(2)}, u32[]{:S(2)}) collective-permute-start(f32[5,512]{1,0:T(8,128)} %get-tuple-element.36), channel_id=1, source_target_pairs={{0,16},{16,32},{32,48},{48,64},{64,80},{80,96},{96,112},{1,17},{17... | collective-permute-start | bytes 30728 | tf_op jit(solution)/shard_map/ppermute | solution.py:26
  47.8 1.3 %collective-permute-start.4 = (f32[2,512]{1,0:T(2,128)}, f32[2,512]{1,0:T(2,128)S(1)}, u32[]{:S(2)}, u32[]{:S(2)}) collective-permute-start(f32[2,512]{1,0:T(2,128)} %get-tuple-element.33), channel_id=1, source_target_pairs={{1,0},{2,1},{3,2},{4,3},{5,4},{6,5},{7,6},{8,7},{9,8},{10,9},{11,1... | collective-permute-start | bytes 12296 | tf_op jit(solution)/shard_map/ppermute | solution.py:26
  49.1 1.9 %collective-permute-start.5 = (f32[2,512]{1,0:T(2,128)S(1)}, f32[2,512]{1,0:T(2,128)S(1)}, u32[]{:S(2)}, u32[]{:S(2)}) collective-permute-start(f32[2,512]{1,0:T(2,128)S(1)} %copy-done.15), channel_id=1, source_target_pairs={{16,0},{32,16},{48,32},{64,48},{80,64},{96,80},{112,96},{17,1},{33... | collective-permute-start | bytes 12296 | tf_op jit(solution)/shard_map/ppermute | solution.py:26
  51.0 1.9 %fusion.1 = f32[512,128]{1,0:T(8,128)} fusion(f32[256,128]{1,0:T(8,128)} %get-tuple-element.37, s32[256]{0:T(256)S(1)} %eq.131), kind=kOutput, calls=%fused_computation.5 | convolution fusion | flops 100794368 | bytes 394240 | tf_op jit(solution)/shard_map/dot_general | solution.py:309
  53.0 0.7 slice.30
  54.1 0.4 copy-done.10
  55.0 10.7 %all-to-all-start.1 = ((f32[128,4,128]{2,1,0:T(4,128)}), f32[128,4,128]{2,1,0:T(4,128)S(1)}, u32[]{:S(2)}, u32[]{:S(2)}) async-start(f32[128,4,128]{2,1,0:T(4,128)} %bitcast.8), calls=%async_computation.1 | async-start | bytes 524288 | tf_op jit(solution)/shard_map/all_to_all | solution.py:394
  65.7 0.2 add_add_fusion.1
  65.9 0.3 fusion.17
  66.2 3.3 %collective-permute-start.8 = (f32[8,128]{1,0:T(8,128)S(1)}, f32[8,128]{1,0:T(8,128)S(1)}, u32[]{:S(2)}, u32[]{:S(2)}) collective-permute-start(f32[8,128]{1,0:T(8,128)S(1)} %fusion.17), channel_id=1, source_target_pairs={{0,1},{1,2},{2,3},{3,4},{4,5},{5,6},{6,7},{7,8},{8,9},{9,10},{10,1... | collective-permute-start | bytes 12296 | tf_op jit(solution)/shard_map/ppermute | solution.py:26
  69.5 7.3 %shard_map.131 = (f32[512,512]{1,0:T(8,128)}, f32[512,512]{1,0:T(8,128)}, f32[512,512]{1,0:T(8,128)}) custom-call(s32[3]{0:T(128)} %add_convert_fusion.flags_ref, f32[512,512]{1,0:T(8,128)} %get-tuple-element.30.d_ref.d_up.d_dn, f32[512,512]{1,0:T(8,128)} %get-tuple-element.31.e_ref, f32[512,512]{1,0:T(8,128)} %get-tuple-element.32.s_ref.s_up, ...), custom_call_target="tpu_custom_call" | custom-call | tf_op jit(solution)/shard_map/pallas_call | solution.py:379
  76.7 0.4 all-to-all-done.1
  77.2 0.2 convolution_multiply_fusion
  77.4 0.9 %add_add_fusion = f32[16,128]{1,0:T(8,128)} fusion(f32[16,128]{1,0:T(8,128)S(1)} %convolution_multiply_fusion, f32[8,128]{1,0:T(8,128)S(1)} %collective-permute-done.8, f32[16,128]{1,0:T(8,128)S(1)} %add_add_fusion.1, s32[16]{0:T(128)S(1)} %iota_add_fusion, s32[16]{0:T(128)S(1)} %copy-done.16, f32[16,128]{1,0:T(8,128)S(1)} %copy-done.7), kind=kOutput, calls=%fused_computation.34 | convolution fusion | flops 418048 | bytes 36992 | tf_op jit(solution)/shard_map/tb,tc->bc/dot_general | solution.py:40
  (73 shorter events, 2.3 us)
Async XLA Ops:
  0.6 0.7 copy-start.7
  0.6 0.7 copy-start.6
  0.7 0.7 copy-start.16
  5.5 4.8 %copy-start.12 = (f32[5,512]{1,0:T(8,128)S(1)}, f32[5,512]{1,0:T(8,128)}, u32[]{:S(2)}) copy-start(f32[5,512]{1,0:T(8,128)} %get-tuple-element.29) | copy-start | bytes 30724
  5.5 8.8 %copy-start.14 = (f32[2,512]{1,0:T(2,128)S(1)}, f32[2,512]{1,0:T(2,128)}, u32[]{:S(2)}) copy-start(f32[2,512]{1,0:T(2,128)} %get-tuple-element.26) | copy-start | bytes 12292
  6.3 9.3 %copy-start.13 = (f32[2,512]{1,0:T(2,128)S(1)}, f32[2,512]{1,0:T(2,128)}, u32[]{:S(2)}) copy-start(f32[2,512]{1,0:T(2,128)} %get-tuple-element.27) | copy-start | bytes 12292
  6.3 26.2 %collective-permute-start.2 = (f32[7,512]{1,0:T(8,128)S(1)}, f32[7,512]{1,0:T(8,128)S(1)}, u32[]{:S(2)}, u32[]{:S(2)}) collective-permute-start(f32[7,512]{1,0:T(8,128)S(1)} %pad_maximum_fusion.1), channel_id=1, source_target_pairs={{0,1},{1,2},{2,3},{3,4},{4,5},{5,6},{6,7},{7,8},{8,9},{9,10},{10,1... | collective-permute-start | bytes 43016 | tf_op jit(solution)/shard_map/ppermute | solution.py:26
  10.3 22.2 %collective-permute-start.3 = (f32[5,512]{1,0:T(8,128)S(1)}, f32[5,512]{1,0:T(8,128)S(1)}, u32[]{:S(2)}, u32[]{:S(2)}) collective-permute-start(f32[5,512]{1,0:T(8,128)S(1)} %copy-done.12), channel_id=1, source_target_pairs={{0,16},{16,32},{32,48},{48,64},{64,80},{80,96},{96,112},{1,17},{17... | collective-permute-start | bytes 30728 | tf_op jit(solution)/shard_map/ppermute | solution.py:26
  14.3 3.3 %copy-start.5 = (s32[256]{0:T(256)S(1)}, s32[256]{0:T(256)}, u32[]{:S(2)}) copy-start(s32[256]{0:T(256)} %param.16) | copy-start | bytes 3076
  14.3 18.1 %collective-permute-start = (f32[2,512]{1,0:T(2,128)S(1)}, f32[2,512]{1,0:T(2,128)S(1)}, u32[]{:S(2)}, u32[]{:S(2)}) collective-permute-start(f32[2,512]{1,0:T(2,128)S(1)} %copy-done.14), channel_id=1, source_target_pairs={{1,0},{2,1},{3,2},{4,3},{5,4},{6,5},{7,6},{8,7},{9,8},{10,9},{11,1... | collective-permute-start | bytes 12296 | tf_op jit(solution)/shard_map/ppermute | solution.py:26
  15.6 16.8 %collective-permute-start.1 = (f32[2,512]{1,0:T(2,128)S(1)}, f32[2,512]{1,0:T(2,128)S(1)}, u32[]{:S(2)}, u32[]{:S(2)}) collective-permute-start(f32[2,512]{1,0:T(2,128)S(1)} %copy-done.13), channel_id=1, source_target_pairs={{16,0},{32,16},{48,32},{64,48},{80,64},{96,80},{112,96},{17,1},{33... | collective-permute-start | bytes 12296 | tf_op jit(solution)/shard_map/ppermute | solution.py:26
  18.0 0.9 %copy-start = (f32[256,128]{1,0:T(8,128)S(1)}, f32[256,128]{1,0:T(8,128)}, u32[]{:S(2)}) copy-start(f32[256,128]{1,0:T(8,128)} %get-tuple-element.38) | copy-start | bytes 393220
  20.8 32.9 %all-to-all-start = ((f32[128,1,640]{2,1,0:T(1,128)}), f32[128,1,640]{2,1,0:T(1,128)S(1)}, u32[]{:S(2)}, u32[]{:S(2)}) async-start(f32[128,1,640]{2,1,0:T(1,128)} %copy.32), calls=%async_computation | async-start | bytes 655360 | tf_op jit(solution)/shard_map/all_to_all | solution.py:317
  32.5 0.6 copy-start.8
  32.5 0.6 copy-start.9
  32.5 0.6 copy-start.2
  32.5 0.6 copy-start.1
  40.9 8.2 %copy-start.15 = (f32[2,512]{1,0:T(2,128)S(1)}, f32[2,512]{1,0:T(2,128)}, u32[]{:S(2)}) copy-start(f32[2,512]{1,0:T(2,128)} %get-tuple-element.34) | copy-start | bytes 12292
  40.9 13.2 %collective-permute-start.6 = (f32[5,512]{1,0:T(8,128)}, f32[5,512]{1,0:T(8,128)S(1)}, u32[]{:S(2)}, u32[]{:S(2)}) collective-permute-start(f32[5,512]{1,0:T(8,128)} %get-tuple-element.35), channel_id=1, source_target_pairs={{0,1},{1,2},{2,3},{3,4},{4,5},{5,6},{6,7},{7,8},{8,9},{9,10},{10,1... | collective-permute-start | bytes 30728 | tf_op jit(solution)/shard_map/ppermute | solution.py:26
  44.1 9.9 %collective-permute-start.7 = (f32[5,512]{1,0:T(8,128)}, f32[5,512]{1,0:T(8,128)S(1)}, u32[]{:S(2)}, u32[]{:S(2)}) collective-permute-start(f32[5,512]{1,0:T(8,128)} %get-tuple-element.36), channel_id=1, source_target_pairs={{0,16},{16,32},{32,48},{48,64},{64,80},{80,96},{96,112},{1,17},{17... | collective-permute-start | bytes 30728 | tf_op jit(solution)/shard_map/ppermute | solution.py:26
  47.8 6.1 %collective-permute-start.4 = (f32[2,512]{1,0:T(2,128)}, f32[2,512]{1,0:T(2,128)S(1)}, u32[]{:S(2)}, u32[]{:S(2)}) collective-permute-start(f32[2,512]{1,0:T(2,128)} %get-tuple-element.33), channel_id=1, source_target_pairs={{1,0},{2,1},{3,2},{4,3},{5,4},{6,5},{7,6},{8,7},{9,8},{10,9},{11,1... | collective-permute-start | bytes 12296 | tf_op jit(solution)/shard_map/ppermute | solution.py:26
  49.1 4.9 %collective-permute-start.5 = (f32[2,512]{1,0:T(2,128)S(1)}, f32[2,512]{1,0:T(2,128)S(1)}, u32[]{:S(2)}, u32[]{:S(2)}) collective-permute-start(f32[2,512]{1,0:T(2,128)S(1)} %copy-done.15), channel_id=1, source_target_pairs={{16,0},{32,16},{48,32},{64,48},{80,64},{96,80},{112,96},{17,1},{33... | collective-permute-start | bytes 12296 | tf_op jit(solution)/shard_map/ppermute | solution.py:26
  53.9 0.6 copy-start.10
  54.0 0.6 copy-start.11
  54.0 0.6 copy-start.3
  54.1 0.6 copy-start.4
  55.0 22.1 %all-to-all-start.1 = ((f32[128,4,128]{2,1,0:T(4,128)}), f32[128,4,128]{2,1,0:T(4,128)S(1)}, u32[]{:S(2)}, u32[]{:S(2)}) async-start(f32[128,4,128]{2,1,0:T(4,128)} %bitcast.8), calls=%async_computation.1 | async-start | bytes 524288 | tf_op jit(solution)/shard_map/all_to_all | solution.py:394
  66.2 11.2 %collective-permute-start.8 = (f32[8,128]{1,0:T(8,128)S(1)}, f32[8,128]{1,0:T(8,128)S(1)}, u32[]{:S(2)}, u32[]{:S(2)}) collective-permute-start(f32[8,128]{1,0:T(8,128)S(1)} %fusion.17), channel_id=1, source_target_pairs={{0,1},{1,2},{2,3},{3,4},{4,5},{5,6},{6,7},{7,8},{8,9},{9,10},{10,1... | collective-permute-start | bytes 12296 | tf_op jit(solution)/shard_map/ppermute | solution.py:26

commit v19 on v18

--- a/solution.py
+++ b/solution.py
@@ -156,7 +156,8 @@
 
 def last_step_kernel(total_rows, flags_ref, d_ref, e_ref, s_ref, bed_ref, r_ref, land_ref,
                      d_up, s_up, bed_up, r_up, land_up, d_dn, bed_dn,
-                     east_ref, south_ref, west_ref, north_ref, d_out, e_out, s_out):
+                     east_ref, south_ref, west_ref, north_ref, d_out, e_out, s_out,
+                     east_cols, west_cols):
     block = pl.program_id(0)
     blocks = pl.num_programs(0)
     tr, nx = d_ref.shape
@@ -171,8 +172,11 @@
     sopen = land * jnp.where(
         (block * tr + row == total_rows - 1) & (flags_ref[1] == 1), 0.0, 1.0
     )
-    east = rows_as_cols(east_ref[...])
-    west = rows_as_cols(west_ref[...])
+    east_cols[...] = rows_as_cols(east_ref[...])
+    west_cols[...] = rows_as_cols(west_ref[...])
+    start = pl.multiple_of(block * tr, 8)
+    east = east_cols[pl.ds(start, tr), :]
+    west = west_cols[pl.ds(start, tr), :]
     level_e = jnp.where(col == nx - 1, east[:, 0:1], pltpu.roll(level, nx - 1, 1))
     depth_e = jnp.where(col == nx - 1, east[:, 1:2], pltpu.roll(depth, nx - 1, 1))
     at_bottom = block == blocks - 1
@@ -328,7 +332,7 @@
 
     first_outflow = reach_outflow(storage)
     ahead_rows = SPAN * reach_width // cell_cols
-    tr = 128
+    tr = 64
     nblk = cell_rows // tr
     main_spec = pl.BlockSpec((tr, cell_cols), lambda i: (i, 0))
     up_spec = pl.BlockSpec((8, cell_cols), lambda i: (jnp.maximum(i * (tr // 8) - 1, 0), 0))
@@ -341,12 +345,13 @@
         out_shape=(grid_shape, grid_shape, grid_shape),
         in_specs=[smem_spec] + [main_spec] * 6 + [up_spec] * 5 + [dn_spec] * 2
         + [
-            pl.BlockSpec((2, tr), lambda i: (0, i)),
+            pl.BlockSpec((2, cell_rows), lambda i: (0, 0)),
             pl.BlockSpec((2, cell_cols), lambda i: (0, 0)),
-            pl.BlockSpec((5, tr), lambda i: (0, i)),
+            pl.BlockSpec((5, cell_rows), lambda i: (0, 0)),
             pl.BlockSpec((5, cell_cols), lambda i: (0, 0)),
         ],
         out_specs=[main_spec] * 3,
+        scratch_shapes=[pltpu.VMEM((cell_rows, 128), f32), pltpu.VMEM((cell_rows, 128), f32)],
     )
 
     depth = water_depth

time: 79 us -> 81 us (1.025)
  Pallas kernels: 18.3 us -> 20.6 us
    pallas_call x1, Pallas kernels: 7.26 us -> 9.57 us  [body(): last_call(flags, depth, flux_east, flux_south, bed_level, roughness, land...]
  transfers between devices with their start and end apart: 11 -> 11, of which waited for: 2 -> 1; matrix products, arithmetic and copies ran while one was open for 8% -> 8% of each run, Pallas kernels for 19% -> 22%
where the time goes in v19:
time: 81 us; the launch traced here: 80.1 us
  starting transfers between devices  46.7 us (58%)
  Pallas kernels  20.6 us (25%)
  local copies, waits for them, and re-layouts  5.26 us (6%)
  matrix products  4.46 us (6%)
  other arithmetic  1.88 us (2%)
  between operations  1.11 us (1%)
    ppermute x9, starting transfers between devices, shifted(): lax.ppermute(value, axis, [(source, source + steps) for source in range(f...  24.6 us
    all_to_all x1, starting transfers between devices, body(): lax.all_to_all(start_lateral(tile_parts).reshape(device_count, first_rows...  11.4 us
    all_to_all x1, starting transfers between devices, body(): got_second = lax.all_to_all(lateral_started, ('gy', 'gx'), 0, 0, tiled=True)  10.7 us
    pallas_call x1, Pallas kernels, body(): last_call(flags, depth, flux_east, flux_south, bed_level, roughness, land...  9.57 us
    pallas_call x1, Pallas kernels, body(): step_call(True)  7.74 us
    pallas_call x1, Pallas kernels, body(): pl.pallas_call(edge_kernel, grid=(1,), out_shape=(tile_shape,) + edge_sha...  3.29 us
    unnamed x35, local copies, waits for them, and re-layouts  2.31 us
    dot_general x2, matrix products, start_lateral(): jnp.dot(row_onehot, part, precision=lax.Precision.HIGH)  2.23 us
  transfers between devices with their start and end apart: 11, of which 1 were waited for; matrix products, arithmetic and copies ran while one was open for 8% of the time, Pallas kernels for 22%

profile of v19, /device:TPU:1, one launch (start us, length us, event | category | flops | bytes accessed | tf_op | source)
XLA Modules:
  0.0 80.1 jit_solution(3725437796396882684)
XLA Ops:
  0.7 0.7 copy-done.7
  1.4 0.2 fusion.19
  1.6 0.6 add_convert_fusion.flags_ref
  2.2 3.3 %shard_map.129 = (f32[256,128]{1,0:T(8,128)}, f32[2,512]{1,0:T(2,128)}, f32[2,512]{1,0:T(2,128)}, f32[5,512]{1,0:T(8,128)}, f32[5,512]{1,0:T(8,128)}) custom-call(s32[3]{0:T(128)} %add_convert_fusion.flags_ref, f32[512,512]{1,0:T(8,128)} %d_ref.3, s32[512,512]{1,0:T(8,128)} %land_up.1, f32[512,512]{1,0:T(8,128)} %bed_dn.1, f32[512,512]{1,0:T(8,128)} %bed_dn.1, ...), custom_call_target="tpu_custom_call" | custom-call | tf_op jit(solution)/shard_map/pallas_call | solution.py:265
  5.5 0.7 pad_maximum_fusion.1
  6.3 4.0 %collective-permute-start.2 = (f32[7,512]{1,0:T(8,128)S(1)}, f32[7,512]{1,0:T(8,128)S(1)}, u32[]{:S(2)}, u32[]{:S(2)}) collective-permute-start(f32[7,512]{1,0:T(8,128)S(1)} %pad_maximum_fusion.1), channel_id=1, source_target_pairs={{0,1},{1,2},{2,3},{3,4},{4,5},{5,6},{6,7},{7,8},{8,9},{9,10},{10,1... | collective-permute-start | bytes 43016 | tf_op jit(solution)/shard_map/ppermute | solution.py:26
  10.3 4.0 %collective-permute-start.3 = (f32[5,512]{1,0:T(8,128)S(1)}, f32[5,512]{1,0:T(8,128)S(1)}, u32[]{:S(2)}, u32[]{:S(2)}) collective-permute-start(f32[5,512]{1,0:T(8,128)S(1)} %copy-done.12), channel_id=1, source_target_pairs={{0,16},{16,32},{32,48},{48,64},{64,80},{80,96},{96,112},{1,17},{17... | collective-permute-start | bytes 30728 | tf_op jit(solution)/shard_map/ppermute | solution.py:26
  14.3 1.3 %collective-permute-start = (f32[2,512]{1,0:T(2,128)S(1)}, f32[2,512]{1,0:T(2,128)S(1)}, u32[]{:S(2)}, u32[]{:S(2)}) collective-permute-start(f32[2,512]{1,0:T(2,128)S(1)} %copy-done.14), channel_id=1, source_target_pairs={{1,0},{2,1},{3,2},{4,3},{5,4},{6,5},{7,6},{8,7},{9,8},{10,9},{11,1... | collective-permute-start | bytes 12296 | tf_op jit(solution)/shard_map/ppermute | solution.py:26
  15.6 1.9 %collective-permute-start.1 = (f32[2,512]{1,0:T(2,128)S(1)}, f32[2,512]{1,0:T(2,128)S(1)}, u32[]{:S(2)}, u32[]{:S(2)}) collective-permute-start(f32[2,512]{1,0:T(2,128)S(1)} %copy-done.13), channel_id=1, source_target_pairs={{16,0},{32,16},{48,32},{64,48},{80,64},{96,80},{112,96},{17,1},{33... | collective-permute-start | bytes 12296 | tf_op jit(solution)/shard_map/ppermute | solution.py:26
  17.7 0.2 fusion.6
  18.5 0.4 copy-done
  18.9 0.3 fusion
  19.4 0.2 fusion.2
  19.9 0.9 %copy.32 = f32[128,1,640]{2,1,0:T(1,128)} copy(f32[128,1,640]{0,2,1:T(8,128)S(1)} %bitcast.39) | data formatting | bytes 655360 | tf_op jit(solution)/shard_map/all_to_all | solution.py:321
  20.8 11.4 %all-to-all-start = ((f32[128,1,640]{2,1,0:T(1,128)}), f32[128,1,640]{2,1,0:T(1,128)S(1)}, u32[]{:S(2)}, u32[]{:S(2)}) async-start(f32[128,1,640]{2,1,0:T(1,128)} %copy.32), calls=%async_computation | async-start | bytes 655360 | tf_op jit(solution)/shard_map/all_to_all | solution.py:321
  32.2 0.2 fusion.15
  32.5 0.5 copy-done.8
  33.1 7.7 %shard_map.130 = (f32[512,512]{1,0:T(8,128)}, f32[512,512]{1,0:T(8,128)}, f32[512,512]{1,0:T(8,128)}, f32[256,128]{1,0:T(8,128)}, f32[2,512]{1,0:T(2,128)}, /*in...) custom-call(s32[3]{0:T(128)} %add_convert_fusion.flags_ref, f32[512,512]{1,0:T(8,128)} %d_ref.3, ...), custom_call_target="tpu_custom_call" | custom-call | tf_op jit(solution)/shard_map/pallas_call | solution.py:390
  40.9 3.3 %collective-permute-start.6 = (f32[5,512]{1,0:T(8,128)}, f32[5,512]{1,0:T(8,128)S(1)}, u32[]{:S(2)}, u32[]{:S(2)}) collective-permute-start(f32[5,512]{1,0:T(8,128)} %get-tuple-element.35), channel_id=1, source_target_pairs={{0,1},{1,2},{2,3},{3,4},{4,5},{5,6},{6,7},{7,8},{8,9},{9,10},{10,1... | collective-permute-start | bytes 30728 | tf_op jit(solution)/shard_map/ppermute | solution.py:26
  44.1 3.7 %collective-permute-start.7 = (f32[5,512]{1,0:T(8,128)}, f32[5,512]{1,0:T(8,128)S(1)}, u32[]{:S(2)}, u32[]{:S(2)}) collective-permute-start(f32[5,512]{1,0:T(8,128)} %get-tuple-element.36), channel_id=1, source_target_pairs={{0,16},{16,32},{32,48},{48,64},{64,80},{80,96},{96,112},{1,17},{17... | collective-permute-start | bytes 30728 | tf_op jit(solution)/shard_map/ppermute | solution.py:26
  47.8 1.3 %collective-permute-start.4 = (f32[2,512]{1,0:T(2,128)}, f32[2,512]{1,0:T(2,128)S(1)}, u32[]{:S(2)}, u32[]{:S(2)}) collective-permute-start(f32[2,512]{1,0:T(2,128)} %get-tuple-element.33), channel_id=1, source_target_pairs={{1,0},{2,1},{3,2},{4,3},{5,4},{6,5},{7,6},{8,7},{9,8},{10,9},{11,1... | collective-permute-start | bytes 12296 | tf_op jit(solution)/shard_map/ppermute | solution.py:26
  49.1 1.9 %collective-permute-start.5 = (f32[2,512]{1,0:T(2,128)S(1)}, f32[2,512]{1,0:T(2,128)S(1)}, u32[]{:S(2)}, u32[]{:S(2)}) collective-permute-start(f32[2,512]{1,0:T(2,128)S(1)} %copy-done.15), channel_id=1, source_target_pairs={{16,0},{32,16},{48,32},{64,48},{80,64},{96,80},{112,96},{17,1},{33... | collective-permute-start | bytes 12296 | tf_op jit(solution)/shard_map/ppermute | solution.py:26
  51.0 1.9 %fusion.1 = f32[512,128]{1,0:T(8,128)} fusion(f32[256,128]{1,0:T(8,128)} %get-tuple-element.37, s32[256]{0:T(256)S(1)} %eq.131), kind=kOutput, calls=%fused_computation.5 | convolution fusion | flops 100794368 | bytes 394240 | tf_op jit(solution)/shard_map/dot_general | solution.py:313
  53.0 0.7 slice.30
  54.1 0.4 copy-done.10
  55.0 10.7 %all-to-all-start.1 = ((f32[128,4,128]{2,1,0:T(4,128)}), f32[128,4,128]{2,1,0:T(4,128)S(1)}, u32[]{:S(2)}, u32[]{:S(2)}) async-start(f32[128,4,128]{2,1,0:T(4,128)} %bitcast.8), calls=%async_computation.1 | async-start | bytes 524288 | tf_op jit(solution)/shard_map/all_to_all | solution.py:399
  65.7 0.2 add_add_fusion.1
  65.9 0.3 fusion.17
  66.2 3.3 %collective-permute-start.8 = (f32[8,128]{1,0:T(8,128)S(1)}, f32[8,128]{1,0:T(8,128)S(1)}, u32[]{:S(2)}, u32[]{:S(2)}) collective-permute-start(f32[8,128]{1,0:T(8,128)S(1)} %fusion.17), channel_id=1, source_target_pairs={{0,1},{1,2},{2,3},{3,4},{4,5},{5,6},{6,7},{7,8},{8,9},{9,10},{10,1... | collective-permute-start | bytes 12296 | tf_op jit(solution)/shard_map/ppermute | solution.py:26
  69.5 9.6 %shard_map.131 = (f32[512,512]{1,0:T(8,128)}, f32[512,512]{1,0:T(8,128)}, f32[512,512]{1,0:T(8,128)}) custom-call(s32[3]{0:T(128)} %add_convert_fusion.flags_ref, f32[512,512]{1,0:T(8,128)} %get-tuple-element.30.d_ref.d_up.d_dn, f32[512,512]{1,0:T(8,128)} %get-tuple-element.31.e_ref, f32[512,512]{1,0:T(8,128)} %get-tuple-element.32.s_ref.s_up, ...), custom_call_target="tpu_custom_call" | custom-call | tf_op jit(solution)/shard_map/pallas_call | solution.py:384
  79.1 0.2 convolution_multiply_fusion
  79.3 0.9 %add_add_fusion = f32[16,128]{1,0:T(8,128)} fusion(f32[16,128]{1,0:T(8,128)S(1)} %convolution_multiply_fusion, f32[8,128]{1,0:T(8,128)S(1)} %collective-permute-done.8, f32[16,128]{1,0:T(8,128)S(1)} %add_add_fusion.1, s32[16]{0:T(128)S(1)} %iota_add_fusion, s32[16]{0:T(128)S(1)} %copy-done.16, f32[16,128]{1,0:T(8,128)S(1)} %copy-done.7), kind=kOutput, calls=%fused_computation.34 | convolution fusion | flops 418048 | bytes 36992 | tf_op jit(solution)/shard_map/tb,tc->bc/dot_general | solution.py:40
  (73 shorter events, 2.1 us)
Async XLA Ops:
  0.6 0.7 copy-start.7
  0.6 0.7 copy-start.6
  0.7 0.7 copy-start.16
  5.5 4.8 %copy-start.12 = (f32[5,512]{1,0:T(8,128)S(1)}, f32[5,512]{1,0:T(8,128)}, u32[]{:S(2)}) copy-start(f32[5,512]{1,0:T(8,128)} %get-tuple-element.29) | copy-start | bytes 30724
  5.5 8.8 %copy-start.14 = (f32[2,512]{1,0:T(2,128)S(1)}, f32[2,512]{1,0:T(2,128)}, u32[]{:S(2)}) copy-start(f32[2,512]{1,0:T(2,128)} %get-tuple-element.26) | copy-start | bytes 12292
  6.3 9.3 %copy-start.13 = (f32[2,512]{1,0:T(2,128)S(1)}, f32[2,512]{1,0:T(2,128)}, u32[]{:S(2)}) copy-start(f32[2,512]{1,0:T(2,128)} %get-tuple-element.27) | copy-start | bytes 12292
  6.3 26.2 %collective-permute-start.2 = (f32[7,512]{1,0:T(8,128)S(1)}, f32[7,512]{1,0:T(8,128)S(1)}, u32[]{:S(2)}, u32[]{:S(2)}) collective-permute-start(f32[7,512]{1,0:T(8,128)S(1)} %pad_maximum_fusion.1), channel_id=1, source_target_pairs={{0,1},{1,2},{2,3},{3,4},{4,5},{5,6},{6,7},{7,8},{8,9},{9,10},{10,1... | collective-permute-start | bytes 43016 | tf_op jit(solution)/shard_map/ppermute | solution.py:26
  10.3 22.2 %collective-permute-start.3 = (f32[5,512]{1,0:T(8,128)S(1)}, f32[5,512]{1,0:T(8,128)S(1)}, u32[]{:S(2)}, u32[]{:S(2)}) collective-permute-start(f32[5,512]{1,0:T(8,128)S(1)} %copy-done.12), channel_id=1, source_target_pairs={{0,16},{16,32},{32,48},{48,64},{64,80},{80,96},{96,112},{1,17},{17... | collective-permute-start | bytes 30728 | tf_op jit(solution)/shard_map/ppermute | solution.py:26
  14.3 3.3 %copy-start.5 = (s32[256]{0:T(256)S(1)}, s32[256]{0:T(256)}, u32[]{:S(2)}) copy-start(s32[256]{0:T(256)} %param.16) | copy-start | bytes 3076
  14.3 18.1 %collective-permute-start = (f32[2,512]{1,0:T(2,128)S(1)}, f32[2,512]{1,0:T(2,128)S(1)}, u32[]{:S(2)}, u32[]{:S(2)}) collective-permute-start(f32[2,512]{1,0:T(2,128)S(1)} %copy-done.14), channel_id=1, source_target_pairs={{1,0},{2,1},{3,2},{4,3},{5,4},{6,5},{7,6},{8,7},{9,8},{10,9},{11,1... | collective-permute-start | bytes 12296 | tf_op jit(solution)/shard_map/ppermute | solution.py:26
  15.6 16.8 %collective-permute-start.1 = (f32[2,512]{1,0:T(2,128)S(1)}, f32[2,512]{1,0:T(2,128)S(1)}, u32[]{:S(2)}, u32[]{:S(2)}) collective-permute-start(f32[2,512]{1,0:T(2,128)S(1)} %copy-done.13), channel_id=1, source_target_pairs={{16,0},{32,16},{48,32},{64,48},{80,64},{96,80},{112,96},{17,1},{33... | collective-permute-start | bytes 12296 | tf_op jit(solution)/shard_map/ppermute | solution.py:26
  18.0 0.9 %copy-start = (f32[256,128]{1,0:T(8,128)S(1)}, f32[256,128]{1,0:T(8,128)}, u32[]{:S(2)}) copy-start(f32[256,128]{1,0:T(8,128)} %get-tuple-element.38) | copy-start | bytes 393220
  20.8 32.9 %all-to-all-start = ((f32[128,1,640]{2,1,0:T(1,128)}), f32[128,1,640]{2,1,0:T(1,128)S(1)}, u32[]{:S(2)}, u32[]{:S(2)}) async-start(f32[128,1,640]{2,1,0:T(1,128)} %copy.32), calls=%async_computation | async-start | bytes 655360 | tf_op jit(solution)/shard_map/all_to_all | solution.py:321
  32.5 0.6 copy-start.8
  32.5 0.6 copy-start.9
  32.5 0.6 copy-start.2
  32.5 0.6 copy-start.1
  40.9 8.2 %copy-start.15 = (f32[2,512]{1,0:T(2,128)S(1)}, f32[2,512]{1,0:T(2,128)}, u32[]{:S(2)}) copy-start(f32[2,512]{1,0:T(2,128)} %get-tuple-element.34) | copy-start | bytes 12292
  40.9 13.2 %collective-permute-start.6 = (f32[5,512]{1,0:T(8,128)}, f32[5,512]{1,0:T(8,128)S(1)}, u32[]{:S(2)}, u32[]{:S(2)}) collective-permute-start(f32[5,512]{1,0:T(8,128)} %get-tuple-element.35), channel_id=1, source_target_pairs={{0,1},{1,2},{2,3},{3,4},{4,5},{5,6},{6,7},{7,8},{8,9},{9,10},{10,1... | collective-permute-start | bytes 30728 | tf_op jit(solution)/shard_map/ppermute | solution.py:26
  44.1 9.9 %collective-permute-start.7 = (f32[5,512]{1,0:T(8,128)}, f32[5,512]{1,0:T(8,128)S(1)}, u32[]{:S(2)}, u32[]{:S(2)}) collective-permute-start(f32[5,512]{1,0:T(8,128)} %get-tuple-element.36), channel_id=1, source_target_pairs={{0,16},{16,32},{32,48},{48,64},{64,80},{80,96},{96,112},{1,17},{17... | collective-permute-start | bytes 30728 | tf_op jit(solution)/shard_map/ppermute | solution.py:26
  47.8 6.1 %collective-permute-start.4 = (f32[2,512]{1,0:T(2,128)}, f32[2,512]{1,0:T(2,128)S(1)}, u32[]{:S(2)}, u32[]{:S(2)}) collective-permute-start(f32[2,512]{1,0:T(2,128)} %get-tuple-element.33), channel_id=1, source_target_pairs={{1,0},{2,1},{3,2},{4,3},{5,4},{6,5},{7,6},{8,7},{9,8},{10,9},{11,1... | collective-permute-start | bytes 12296 | tf_op jit(solution)/shard_map/ppermute | solution.py:26
  49.1 4.9 %collective-permute-start.5 = (f32[2,512]{1,0:T(2,128)S(1)}, f32[2,512]{1,0:T(2,128)S(1)}, u32[]{:S(2)}, u32[]{:S(2)}) collective-permute-start(f32[2,512]{1,0:T(2,128)S(1)} %copy-done.15), channel_id=1, source_target_pairs={{16,0},{32,16},{48,32},{64,48},{80,64},{96,80},{112,96},{17,1},{33... | collective-permute-start | bytes 12296 | tf_op jit(solution)/shard_map/ppermute | solution.py:26
  53.9 0.6 copy-start.10
  54.0 0.6 copy-start.11
  54.0 0.6 copy-start.3
  54.1 0.6 copy-start.4
  55.0 24.0 %all-to-all-start.1 = ((f32[128,4,128]{2,1,0:T(4,128)}), f32[128,4,128]{2,1,0:T(4,128)S(1)}, u32[]{:S(2)}, u32[]{:S(2)}) async-start(f32[128,4,128]{2,1,0:T(4,128)} %bitcast.8), calls=%async_computation.1 | async-start | bytes 524288 | tf_op jit(solution)/shard_map/all_to_all | solution.py:399
  66.2 13.1 %collective-permute-start.8 = (f32[8,128]{1,0:T(8,128)S(1)}, f32[8,128]{1,0:T(8,128)S(1)}, u32[]{:S(2)}, u32[]{:S(2)}) collective-permute-start(f32[8,128]{1,0:T(8,128)S(1)} %fusion.17), channel_id=1, source_target_pairs={{0,1},{1,2},{2,3},{3,4},{4,5},{5,6},{6,7},{7,8},{8,9},{9,10},{10,1... | collective-permute-start | bytes 12296 | tf_op jit(solution)/shard_map/ppermute | solution.py:26

commit v20 on v18

--- a/solution.py
+++ b/solution.py
@@ -328,7 +328,7 @@
 
     first_outflow = reach_outflow(storage)
     ahead_rows = SPAN * reach_width // cell_cols
-    tr = 128
+    tr = 256
     nblk = cell_rows // tr
     main_spec = pl.BlockSpec((tr, cell_cols), lambda i: (i, 0))
     up_spec = pl.BlockSpec((8, cell_cols), lambda i: (jnp.maximum(i * (tr // 8) - 1, 0), 0))

time: 79 us -> 78.9 us (level)
  no operation moved by 1% of the time
where the time goes in v20:
time: 78.9 us; the launch traced here: 78.2 us
  starting transfers between devices  46.7 us (59%)
  Pallas kernels  18.2 us (23%)
  local copies, waits for them, and re-layouts  5.26 us (7%)
  matrix products  4.46 us (6%)
  other arithmetic  1.88 us (2%)
  between operations  1.11 us (1%)
    ppermute x9, starting transfers between devices, shifted(): lax.ppermute(value, axis, [(source, source + steps) for source in range(f...  24.6 us
    all_to_all x1, starting transfers between devices, body(): lax.all_to_all(start_lateral(tile_parts).reshape(device_count, first_rows...  11.4 us
    all_to_all x1, starting transfers between devices, body(): got_second = lax.all_to_all(lateral_started, ('gy', 'gx'), 0, 0, tiled=True)  10.7 us
    pallas_call x1, Pallas kernels, body(): step_call(True)  7.74 us
    pallas_call x1, Pallas kernels, body(): last_call(flags, depth, flux_east, flux_south, bed_level, roughness, land...  7.19 us
    pallas_call x1, Pallas kernels, body(): pl.pallas_call(edge_kernel, grid=(1,), out_shape=(tile_shape,) + edge_sha...  3.29 us
    unnamed x35, local copies, waits for them, and re-layouts  2.31 us
    dot_general x2, matrix products, start_lateral(): jnp.dot(row_onehot, part, precision=lax.Precision.HIGH)  2.23 us
  transfers between devices with their start and end apart: 11, of which 2 were waited for; matrix products, arithmetic and copies ran while one was open for 8% of the time, Pallas kernels for 19%

profile of v20, /device:TPU:1, one launch (start us, length us, event | category | flops | bytes accessed | tf_op | source)
XLA Modules:
  0.0 78.2 jit_solution(9867250817144326914)
XLA Ops:
  0.7 0.7 copy-done.7
  1.4 0.2 fusion.19
  1.6 0.6 add_convert_fusion.flags_ref
  2.2 3.3 %shard_map.129 = (f32[256,128]{1,0:T(8,128)}, f32[2,512]{1,0:T(2,128)}, f32[2,512]{1,0:T(2,128)}, f32[5,512]{1,0:T(8,128)}, f32[5,512]{1,0:T(8,128)}) custom-call(s32[3]{0:T(128)} %add_convert_fusion.flags_ref, f32[512,512]{1,0:T(8,128)} %d_ref.3, s32[512,512]{1,0:T(8,128)} %land_up.1, f32[512,512]{1,0:T(8,128)} %bed_dn.1, f32[512,512]{1,0:T(8,128)} %bed_dn.1, ...), custom_call_target="tpu_custom_call" | custom-call | tf_op jit(solution)/shard_map/pallas_call | solution.py:261
  5.5 0.7 pad_maximum_fusion.1
  6.3 4.0 %collective-permute-start.2 = (f32[7,512]{1,0:T(8,128)S(1)}, f32[7,512]{1,0:T(8,128)S(1)}, u32[]{:S(2)}, u32[]{:S(2)}) collective-permute-start(f32[7,512]{1,0:T(8,128)S(1)} %pad_maximum_fusion.1), channel_id=1, source_target_pairs={{0,1},{1,2},{2,3},{3,4},{4,5},{5,6},{6,7},{7,8},{8,9},{9,10},{10,1... | collective-permute-start | bytes 43016 | tf_op jit(solution)/shard_map/ppermute | solution.py:26
  10.3 4.0 %collective-permute-start.3 = (f32[5,512]{1,0:T(8,128)S(1)}, f32[5,512]{1,0:T(8,128)S(1)}, u32[]{:S(2)}, u32[]{:S(2)}) collective-permute-start(f32[5,512]{1,0:T(8,128)S(1)} %copy-done.12), channel_id=1, source_target_pairs={{0,16},{16,32},{32,48},{48,64},{64,80},{80,96},{96,112},{1,17},{17... | collective-permute-start | bytes 30728 | tf_op jit(solution)/shard_map/ppermute | solution.py:26
  14.3 1.3 %collective-permute-start = (f32[2,512]{1,0:T(2,128)S(1)}, f32[2,512]{1,0:T(2,128)S(1)}, u32[]{:S(2)}, u32[]{:S(2)}) collective-permute-start(f32[2,512]{1,0:T(2,128)S(1)} %copy-done.14), channel_id=1, source_target_pairs={{1,0},{2,1},{3,2},{4,3},{5,4},{6,5},{7,6},{8,7},{9,8},{10,9},{11,1... | collective-permute-start | bytes 12296 | tf_op jit(solution)/shard_map/ppermute | solution.py:26
  15.6 1.9 %collective-permute-start.1 = (f32[2,512]{1,0:T(2,128)S(1)}, f32[2,512]{1,0:T(2,128)S(1)}, u32[]{:S(2)}, u32[]{:S(2)}) collective-permute-start(f32[2,512]{1,0:T(2,128)S(1)} %copy-done.13), channel_id=1, source_target_pairs={{16,0},{32,16},{48,32},{64,48},{80,64},{96,80},{112,96},{17,1},{33... | collective-permute-start | bytes 12296 | tf_op jit(solution)/shard_map/ppermute | solution.py:26
  18.5 0.4 copy-done
  18.9 0.3 fusion
  19.4 0.2 fusion.2
  19.9 0.9 %copy.32 = f32[128,1,640]{2,1,0:T(1,128)} copy(f32[128,1,640]{0,2,1:T(8,128)S(1)} %bitcast.39) | data formatting | bytes 655360 | tf_op jit(solution)/shard_map/all_to_all | solution.py:317
  20.8 11.4 %all-to-all-start = ((f32[128,1,640]{2,1,0:T(1,128)}), f32[128,1,640]{2,1,0:T(1,128)S(1)}, u32[]{:S(2)}, u32[]{:S(2)}) async-start(f32[128,1,640]{2,1,0:T(1,128)} %copy.32), calls=%async_computation | async-start | bytes 655360 | tf_op jit(solution)/shard_map/all_to_all | solution.py:317
  32.2 0.2 fusion.15
  32.5 0.5 copy-done.8
  33.1 7.7 %shard_map.130 = (f32[512,512]{1,0:T(8,128)}, f32[512,512]{1,0:T(8,128)}, f32[512,512]{1,0:T(8,128)}, f32[256,128]{1,0:T(8,128)}, f32[2,512]{1,0:T(2,128)}, /*in...) custom-call(s32[3]{0:T(128)} %add_convert_fusion.flags_ref, f32[512,512]{1,0:T(8,128)} %d_ref.3, ...), custom_call_target="tpu_custom_call" | custom-call | tf_op jit(solution)/shard_map/pallas_call | solution.py:385
  40.9 3.3 %collective-permute-start.6 = (f32[5,512]{1,0:T(8,128)}, f32[5,512]{1,0:T(8,128)S(1)}, u32[]{:S(2)}, u32[]{:S(2)}) collective-permute-start(f32[5,512]{1,0:T(8,128)} %get-tuple-element.35), channel_id=1, source_target_pairs={{0,1},{1,2},{2,3},{3,4},{4,5},{5,6},{6,7},{7,8},{8,9},{9,10},{10,1... | collective-permute-start | bytes 30728 | tf_op jit(solution)/shard_map/ppermute | solution.py:26
  44.1 3.7 %collective-permute-start.7 = (f32[5,512]{1,0:T(8,128)}, f32[5,512]{1,0:T(8,128)S(1)}, u32[]{:S(2)}, u32[]{:S(2)}) collective-permute-start(f32[5,512]{1,0:T(8,128)} %get-tuple-element.36), channel_id=1, source_target_pairs={{0,16},{16,32},{32,48},{48,64},{64,80},{80,96},{96,112},{1,17},{17... | collective-permute-start | bytes 30728 | tf_op jit(solution)/shard_map/ppermute | solution.py:26
  47.8 1.3 %collective-permute-start.4 = (f32[2,512]{1,0:T(2,128)}, f32[2,512]{1,0:T(2,128)S(1)}, u32[]{:S(2)}, u32[]{:S(2)}) collective-permute-start(f32[2,512]{1,0:T(2,128)} %get-tuple-element.33), channel_id=1, source_target_pairs={{1,0},{2,1},{3,2},{4,3},{5,4},{6,5},{7,6},{8,7},{9,8},{10,9},{11,1... | collective-permute-start | bytes 12296 | tf_op jit(solution)/shard_map/ppermute | solution.py:26
  49.1 1.9 %collective-permute-start.5 = (f32[2,512]{1,0:T(2,128)S(1)}, f32[2,512]{1,0:T(2,128)S(1)}, u32[]{:S(2)}, u32[]{:S(2)}) collective-permute-start(f32[2,512]{1,0:T(2,128)S(1)} %copy-done.15), channel_id=1, source_target_pairs={{16,0},{32,16},{48,32},{64,48},{80,64},{96,80},{112,96},{17,1},{33... | collective-permute-start | bytes 12296 | tf_op jit(solution)/shard_map/ppermute | solution.py:26
  51.0 1.9 %fusion.1 = f32[512,128]{1,0:T(8,128)} fusion(f32[256,128]{1,0:T(8,128)} %get-tuple-element.37, s32[256]{0:T(256)S(1)} %eq.131), kind=kOutput, calls=%fused_computation.5 | convolution fusion | flops 100794368 | bytes 394240 | tf_op jit(solution)/shard_map/dot_general | solution.py:309
  53.0 0.7 slice.30
  54.1 0.4 copy-done.10
  55.0 10.7 %all-to-all-start.1 = ((f32[128,4,128]{2,1,0:T(4,128)}), f32[128,4,128]{2,1,0:T(4,128)S(1)}, u32[]{:S(2)}, u32[]{:S(2)}) async-start(f32[128,4,128]{2,1,0:T(4,128)} %bitcast.8), calls=%async_computation.1 | async-start | bytes 524288 | tf_op jit(solution)/shard_map/all_to_all | solution.py:394
  65.7 0.2 add_add_fusion.1
  65.9 0.3 fusion.17
  66.2 3.3 %collective-permute-start.8 = (f32[8,128]{1,0:T(8,128)S(1)}, f32[8,128]{1,0:T(8,128)S(1)}, u32[]{:S(2)}, u32[]{:S(2)}) collective-permute-start(f32[8,128]{1,0:T(8,128)S(1)} %fusion.17), channel_id=1, source_target_pairs={{0,1},{1,2},{2,3},{3,4},{4,5},{5,6},{6,7},{7,8},{8,9},{9,10},{10,1... | collective-permute-start | bytes 12296 | tf_op jit(solution)/shard_map/ppermute | solution.py:26
  69.5 7.2 %shard_map.131 = (f32[512,512]{1,0:T(8,128)}, f32[512,512]{1,0:T(8,128)}, f32[512,512]{1,0:T(8,128)}) custom-call(s32[3]{0:T(128)} %add_convert_fusion.flags_ref, f32[512,512]{1,0:T(8,128)} %get-tuple-element.30.d_ref.d_up.d_dn, f32[512,512]{1,0:T(8,128)} %get-tuple-element.31.e_ref, f32[512,512]{1,0:T(8,128)} %get-tuple-element.32.s_ref.s_up, ...), custom_call_target="tpu_custom_call" | custom-call | tf_op jit(solution)/shard_map/pallas_call | solution.py:379
  76.7 0.5 all-to-all-done.1
  77.2 0.2 convolution_multiply_fusion
  77.4 0.9 %add_add_fusion = f32[16,128]{1,0:T(8,128)} fusion(f32[16,128]{1,0:T(8,128)S(1)} %convolution_multiply_fusion, f32[8,128]{1,0:T(8,128)S(1)} %collective-permute-done.8, f32[16,128]{1,0:T(8,128)S(1)} %add_add_fusion.1, s32[16]{0:T(128)S(1)} %iota_add_fusion, s32[16]{0:T(128)S(1)} %copy-done.16, f32[16,128]{1,0:T(8,128)S(1)} %copy-done.7), kind=kOutput, calls=%fused_computation.34 | convolution fusion | flops 418048 | bytes 36992 | tf_op jit(solution)/shard_map/tb,tc->bc/dot_general | solution.py:40
  (73 shorter events, 2.3 us)
Async XLA Ops:
  0.6 0.7 copy-start.7
  0.6 0.7 copy-start.6
  0.7 0.7 copy-start.16
  5.5 4.8 %copy-start.12 = (f32[5,512]{1,0:T(8,128)S(1)}, f32[5,512]{1,0:T(8,128)}, u32[]{:S(2)}) copy-start(f32[5,512]{1,0:T(8,128)} %get-tuple-element.29) | copy-start | bytes 30724
  5.5 8.8 %copy-start.14 = (f32[2,512]{1,0:T(2,128)S(1)}, f32[2,512]{1,0:T(2,128)}, u32[]{:S(2)}) copy-start(f32[2,512]{1,0:T(2,128)} %get-tuple-element.26) | copy-start | bytes 12292
  6.3 9.3 %copy-start.13 = (f32[2,512]{1,0:T(2,128)S(1)}, f32[2,512]{1,0:T(2,128)}, u32[]{:S(2)}) copy-start(f32[2,512]{1,0:T(2,128)} %get-tuple-element.27) | copy-start | bytes 12292
  6.3 26.2 %collective-permute-start.2 = (f32[7,512]{1,0:T(8,128)S(1)}, f32[7,512]{1,0:T(8,128)S(1)}, u32[]{:S(2)}, u32[]{:S(2)}) collective-permute-start(f32[7,512]{1,0:T(8,128)S(1)} %pad_maximum_fusion.1), channel_id=1, source_target_pairs={{0,1},{1,2},{2,3},{3,4},{4,5},{5,6},{6,7},{7,8},{8,9},{9,10},{10,1... | collective-permute-start | bytes 43016 | tf_op jit(solution)/shard_map/ppermute | solution.py:26
  10.3 22.2 %collective-permute-start.3 = (f32[5,512]{1,0:T(8,128)S(1)}, f32[5,512]{1,0:T(8,128)S(1)}, u32[]{:S(2)}, u32[]{:S(2)}) collective-permute-start(f32[5,512]{1,0:T(8,128)S(1)} %copy-done.12), channel_id=1, source_target_pairs={{0,16},{16,32},{32,48},{48,64},{64,80},{80,96},{96,112},{1,17},{17... | collective-permute-start | bytes 30728 | tf_op jit(solution)/shard_map/ppermute | solution.py:26
  14.3 3.3 %copy-start.5 = (s32[256]{0:T(256)S(1)}, s32[256]{0:T(256)}, u32[]{:S(2)}) copy-start(s32[256]{0:T(256)} %param.16) | copy-start | bytes 3076
  14.3 18.1 %collective-permute-start = (f32[2,512]{1,0:T(2,128)S(1)}, f32[2,512]{1,0:T(2,128)S(1)}, u32[]{:S(2)}, u32[]{:S(2)}) collective-permute-start(f32[2,512]{1,0:T(2,128)S(1)} %copy-done.14), channel_id=1, source_target_pairs={{1,0},{2,1},{3,2},{4,3},{5,4},{6,5},{7,6},{8,7},{9,8},{10,9},{11,1... | collective-permute-start | bytes 12296 | tf_op jit(solution)/shard_map/ppermute | solution.py:26
  15.6 16.8 %collective-permute-start.1 = (f32[2,512]{1,0:T(2,128)S(1)}, f32[2,512]{1,0:T(2,128)S(1)}, u32[]{:S(2)}, u32[]{:S(2)}) collective-permute-start(f32[2,512]{1,0:T(2,128)S(1)} %copy-done.13), channel_id=1, source_target_pairs={{16,0},{32,16},{48,32},{64,48},{80,64},{96,80},{112,96},{17,1},{33... | collective-permute-start | bytes 12296 | tf_op jit(solution)/shard_map/ppermute | solution.py:26
  18.0 0.9 %copy-start = (f32[256,128]{1,0:T(8,128)S(1)}, f32[256,128]{1,0:T(8,128)}, u32[]{:S(2)}) copy-start(f32[256,128]{1,0:T(8,128)} %get-tuple-element.38) | copy-start | bytes 393220
  20.8 32.9 %all-to-all-start = ((f32[128,1,640]{2,1,0:T(1,128)}), f32[128,1,640]{2,1,0:T(1,128)S(1)}, u32[]{:S(2)}, u32[]{:S(2)}) async-start(f32[128,1,640]{2,1,0:T(1,128)} %copy.32), calls=%async_computation | async-start | bytes 655360 | tf_op jit(solution)/shard_map/all_to_all | solution.py:317
  32.5 0.6 copy-start.8
  32.5 0.6 copy-start.9
  32.5 0.6 copy-start.2
  32.5 0.6 copy-start.1
  40.9 8.2 %copy-start.15 = (f32[2,512]{1,0:T(2,128)S(1)}, f32[2,512]{1,0:T(2,128)}, u32[]{:S(2)}) copy-start(f32[2,512]{1,0:T(2,128)} %get-tuple-element.34) | copy-start | bytes 12292
  40.9 13.2 %collective-permute-start.6 = (f32[5,512]{1,0:T(8,128)}, f32[5,512]{1,0:T(8,128)S(1)}, u32[]{:S(2)}, u32[]{:S(2)}) collective-permute-start(f32[5,512]{1,0:T(8,128)} %get-tuple-element.35), channel_id=1, source_target_pairs={{0,1},{1,2},{2,3},{3,4},{4,5},{5,6},{6,7},{7,8},{8,9},{9,10},{10,1... | collective-permute-start | bytes 30728 | tf_op jit(solution)/shard_map/ppermute | solution.py:26
  44.1 9.9 %collective-permute-start.7 = (f32[5,512]{1,0:T(8,128)}, f32[5,512]{1,0:T(8,128)S(1)}, u32[]{:S(2)}, u32[]{:S(2)}) collective-permute-start(f32[5,512]{1,0:T(8,128)} %get-tuple-element.36), channel_id=1, source_target_pairs={{0,16},{16,32},{32,48},{48,64},{64,80},{80,96},{96,112},{1,17},{17... | collective-permute-start | bytes 30728 | tf_op jit(solution)/shard_map/ppermute | solution.py:26
  47.8 6.1 %collective-permute-start.4 = (f32[2,512]{1,0:T(2,128)}, f32[2,512]{1,0:T(2,128)S(1)}, u32[]{:S(2)}, u32[]{:S(2)}) collective-permute-start(f32[2,512]{1,0:T(2,128)} %get-tuple-element.33), channel_id=1, source_target_pairs={{1,0},{2,1},{3,2},{4,3},{5,4},{6,5},{7,6},{8,7},{9,8},{10,9},{11,1... | collective-permute-start | bytes 12296 | tf_op jit(solution)/shard_map/ppermute | solution.py:26
  49.1 4.9 %collective-permute-start.5 = (f32[2,512]{1,0:T(2,128)S(1)}, f32[2,512]{1,0:T(2,128)S(1)}, u32[]{:S(2)}, u32[]{:S(2)}) collective-permute-start(f32[2,512]{1,0:T(2,128)S(1)} %copy-done.15), channel_id=1, source_target_pairs={{16,0},{32,16},{48,32},{64,48},{80,64},{96,80},{112,96},{17,1},{33... | collective-permute-start | bytes 12296 | tf_op jit(solution)/shard_map/ppermute | solution.py:26
  53.9 0.6 copy-start.10
  54.0 0.6 copy-start.11
  54.0 0.6 copy-start.3
  54.1 0.6 copy-start.4
  55.0 22.1 %all-to-all-start.1 = ((f32[128,4,128]{2,1,0:T(4,128)}), f32[128,4,128]{2,1,0:T(4,128)S(1)}, u32[]{:S(2)}, u32[]{:S(2)}) async-start(f32[128,4,128]{2,1,0:T(4,128)} %bitcast.8), calls=%async_computation.1 | async-start | bytes 524288 | tf_op jit(solution)/shard_map/all_to_all | solution.py:394
  66.2 11.2 %collective-permute-start.8 = (f32[8,128]{1,0:T(8,128)S(1)}, f32[8,128]{1,0:T(8,128)S(1)}, u32[]{:S(2)}, u32[]{:S(2)}) collective-permute-start(f32[8,128]{1,0:T(8,128)S(1)} %fusion.17), channel_id=1, source_target_pairs={{0,1},{1,2},{2,3},{3,4},{4,5},{5,6},{6,7},{7,8},{8,9},{9,10},{10,1... | collective-permute-start | bytes 12296 | tf_op jit(solution)/shard_map/ppermute | solution.py:26

commit v21 on v13

--- a/solution.py
+++ b/solution.py
@@ -320,7 +320,7 @@
         jnp.dot(
             scatter_onehot,
             got[:, :slot_cap].reshape(-1, reach_width),
-            precision=lax.Precision.HIGHEST,
+            precision=lax.Precision.HIGH,
         )
         for got in (got_first, got_second)
     ]

time: 78.9 us -> 78.8 us (level)
  no operation moved by 1% of the time
where the time goes in v21:
time: 78.8 us; the launch traced here: 78.2 us
  starting transfers between devices  46.9 us (60%)
  Pallas kernels  18.4 us (23%)
  local copies, waits for them, and re-layouts  5.26 us (7%)
  matrix products  4.38 us (6%)
  other arithmetic  1.88 us (2%)
  between operations  1.09 us (1%)
    ppermute x9, starting transfers between devices, shifted(): lax.ppermute(value, axis, [(source, source + steps) for source in range(f...  24.8 us
    pallas_call x2, Pallas kernels, body(): step_call(not last)  15.2 us
    all_to_all x1, starting transfers between devices, body(): lax.all_to_all(start_lateral(tile_parts).reshape(device_count, first_rows...  11.4 us
    all_to_all x1, starting transfers between devices, body(): got_second = lax.all_to_all(lateral_started, ('gy', 'gx'), 0, 0, tiled=True)  10.7 us
    pallas_call x1, Pallas kernels, body(): pl.pallas_call(edge_kernel, grid=(1,), out_shape=(tile_shape,) + edge_sha...  3.29 us
    unnamed x35, local copies, waits for them, and re-layouts  2.31 us
    dot_general x2, matrix products, start_lateral(): jnp.dot(row_onehot, part, precision=lax.Precision.HIGH)  2.23 us
    dot_general x4, matrix products, block_term(): jnp.einsum('tb,tc->bc', onehot, values, precision=lax.Precision.HIGHEST)  1.62 us
  transfers between devices with their start and end apart: 11, of which 2 were waited for; matrix products, arithmetic and copies ran while one was open for 8% of the time, Pallas kernels for 19%

profile of v21, /device:TPU:1, one launch (start us, length us, event | category | flops | bytes accessed | tf_op | source)
XLA Modules:
  0.0 78.2 jit_solution(5775649125313587859)
XLA Ops:
  0.7 0.7 copy-done.7
  1.4 0.2 fusion.19
  1.6 0.6 add_convert_fusion.flags_ref
  2.2 3.3 %shard_map.129 = (f32[256,128]{1,0:T(8,128)}, f32[2,512]{1,0:T(2,128)}, f32[2,512]{1,0:T(2,128)}, f32[5,512]{1,0:T(8,128)}, f32[5,512]{1,0:T(8,128)}) custom-call(s32[3]{0:T(128)} %add_convert_fusion.flags_ref, f32[512,512]{1,0:T(8,128)} %d_ref.3, s32[512,512]{1,0:T(8,128)} %land_ref.5, f32[512,512]{1,0:T(8,128)} %bed_ref.3, f32[512,512]{1,0:T(8,128)} %bed_ref.3, ...), custom_call_target="tpu_custom_call" | custom-call | tf_op jit(solution)/shard_map/pallas_call | solution.py:210
  5.5 0.7 pad_maximum_fusion.1
  6.3 4.0 %collective-permute-start.2 = (f32[7,512]{1,0:T(8,128)S(1)}, f32[7,512]{1,0:T(8,128)S(1)}, u32[]{:S(2)}, u32[]{:S(2)}) collective-permute-start(f32[7,512]{1,0:T(8,128)S(1)} %pad_maximum_fusion.1), channel_id=1, source_target_pairs={{0,1},{1,2},{2,3},{3,4},{4,5},{5,6},{6,7},{7,8},{8,9},{9,10},{10,1... | collective-permute-start | bytes 43016 | tf_op jit(solution)/shard_map/ppermute | solution.py:26
  10.3 4.0 %collective-permute-start.3 = (f32[5,512]{1,0:T(8,128)S(1)}, f32[5,512]{1,0:T(8,128)S(1)}, u32[]{:S(2)}, u32[]{:S(2)}) collective-permute-start(f32[5,512]{1,0:T(8,128)S(1)} %copy-done.12), channel_id=1, source_target_pairs={{0,16},{16,32},{32,48},{48,64},{64,80},{80,96},{96,112},{1,17},{17... | collective-permute-start | bytes 30728 | tf_op jit(solution)/shard_map/ppermute | solution.py:26
  14.3 1.3 %collective-permute-start = (f32[2,512]{1,0:T(2,128)S(1)}, f32[2,512]{1,0:T(2,128)S(1)}, u32[]{:S(2)}, u32[]{:S(2)}) collective-permute-start(f32[2,512]{1,0:T(2,128)S(1)} %copy-done.14), channel_id=1, source_target_pairs={{1,0},{2,1},{3,2},{4,3},{5,4},{6,5},{7,6},{8,7},{9,8},{10,9},{11,1... | collective-permute-start | bytes 12296 | tf_op jit(solution)/shard_map/ppermute | solution.py:26
  15.6 1.9 %collective-permute-start.1 = (f32[2,512]{1,0:T(2,128)S(1)}, f32[2,512]{1,0:T(2,128)S(1)}, u32[]{:S(2)}, u32[]{:S(2)}) collective-permute-start(f32[2,512]{1,0:T(2,128)S(1)} %copy-done.13), channel_id=1, source_target_pairs={{16,0},{32,16},{48,32},{64,48},{80,64},{96,80},{112,96},{17,1},{33... | collective-permute-start | bytes 12296 | tf_op jit(solution)/shard_map/ppermute | solution.py:26
  17.7 0.2 fusion.6
  18.0 0.2 fusion.8
  18.5 0.4 copy-done
  18.9 0.3 fusion
  19.4 0.2 fusion.2
  19.9 0.9 %copy.32 = f32[128,1,640]{2,1,0:T(1,128)} copy(f32[128,1,640]{0,2,1:T(8,128)S(1)} %bitcast.39) | data formatting | bytes 655360 | tf_op jit(solution)/shard_map/all_to_all | solution.py:266
  20.8 11.4 %all-to-all-start = ((f32[128,1,640]{2,1,0:T(1,128)}), f32[128,1,640]{2,1,0:T(1,128)S(1)}, u32[]{:S(2)}, u32[]{:S(2)}) async-start(f32[128,1,640]{2,1,0:T(1,128)} %copy.32), calls=%async_computation | async-start | bytes 655360 | tf_op jit(solution)/shard_map/all_to_all | solution.py:266
  32.2 0.2 fusion.15
  32.5 0.5 copy-done.8
  33.1 7.7 %shard_map.130 = (f32[512,512]{1,0:T(8,128)}, f32[512,512]{1,0:T(8,128)}, f32[512,512]{1,0:T(8,128)}, f32[256,128]{1,0:T(8,128)}, f32[2,512]{1,0:T(2,128)}, /*in...) custom-call(s32[3]{0:T(128)} %add_convert_fusion.flags_ref, f32[512,512]{1,0:T(8,128)} %d_ref.3, ...), custom_call_target="tpu_custom_call" | custom-call | tf_op jit(solution)/shard_map/pallas_call | solution.py:306
  40.9 3.3 %collective-permute-start.6 = (f32[5,512]{1,0:T(8,128)}, f32[5,512]{1,0:T(8,128)S(1)}, u32[]{:S(2)}, u32[]{:S(2)}) collective-permute-start(f32[5,512]{1,0:T(8,128)} %get-tuple-element.35), channel_id=1, source_target_pairs={{0,1},{1,2},{2,3},{3,4},{4,5},{5,6},{6,7},{7,8},{8,9},{9,10},{10,1... | collective-permute-start | bytes 30728 | tf_op jit(solution)/shard_map/ppermute | solution.py:26
  44.1 3.7 %collective-permute-start.7 = (f32[5,512]{1,0:T(8,128)}, f32[5,512]{1,0:T(8,128)S(1)}, u32[]{:S(2)}, u32[]{:S(2)}) collective-permute-start(f32[5,512]{1,0:T(8,128)} %get-tuple-element.36), channel_id=1, source_target_pairs={{0,16},{16,32},{32,48},{48,64},{64,80},{80,96},{96,112},{1,17},{17... | collective-permute-start | bytes 30728 | tf_op jit(solution)/shard_map/ppermute | solution.py:26
  47.8 1.3 %collective-permute-start.4 = (f32[2,512]{1,0:T(2,128)}, f32[2,512]{1,0:T(2,128)S(1)}, u32[]{:S(2)}, u32[]{:S(2)}) collective-permute-start(f32[2,512]{1,0:T(2,128)} %get-tuple-element.33), channel_id=1, source_target_pairs={{1,0},{2,1},{3,2},{4,3},{5,4},{6,5},{7,6},{8,7},{9,8},{10,9},{11,1... | collective-permute-start | bytes 12296 | tf_op jit(solution)/shard_map/ppermute | solution.py:26
  49.1 1.9 %collective-permute-start.5 = (f32[2,512]{1,0:T(2,128)S(1)}, f32[2,512]{1,0:T(2,128)S(1)}, u32[]{:S(2)}, u32[]{:S(2)}) collective-permute-start(f32[2,512]{1,0:T(2,128)S(1)} %copy-done.15), channel_id=1, source_target_pairs={{16,0},{32,16},{48,32},{64,48},{80,64},{96,80},{112,96},{17,1},{33... | collective-permute-start | bytes 12296 | tf_op jit(solution)/shard_map/ppermute | solution.py:26
  51.0 1.9 %fusion.1 = f32[512,128]{1,0:T(8,128)} fusion(f32[256,128]{1,0:T(8,128)} %get-tuple-element.37, s32[256]{0:T(256)S(1)} %eq.131), kind=kOutput, calls=%fused_computation.5 | convolution fusion | flops 100794368 | bytes 394240 | tf_op jit(solution)/shard_map/dot_general | solution.py:258
  53.0 0.7 slice.30
  53.7 0.2 copy.33
  54.1 0.4 copy-done.10
  55.0 10.7 %all-to-all-start.1 = ((f32[128,4,128]{2,1,0:T(4,128)}), f32[128,4,128]{2,1,0:T(4,128)S(1)}, u32[]{:S(2)}, u32[]{:S(2)}) async-start(f32[128,4,128]{2,1,0:T(4,128)} %bitcast.8), calls=%async_computation.1 | async-start | bytes 524288 | tf_op jit(solution)/shard_map/all_to_all | solution.py:315
  65.9 0.3 fusion.17
  66.2 3.4 %collective-permute-start.8 = (f32[8,128]{1,0:T(8,128)S(1)}, f32[8,128]{1,0:T(8,128)S(1)}, u32[]{:S(2)}, u32[]{:S(2)}) collective-permute-start(f32[8,128]{1,0:T(8,128)S(1)} %fusion.17), channel_id=1, source_target_pairs={{0,1},{1,2},{2,3},{3,4},{4,5},{5,6},{6,7},{7,8},{8,9},{9,10},{10,1... | collective-permute-start | bytes 12296 | tf_op jit(solution)/shard_map/ppermute | solution.py:26
  69.6 7.4 %shard_map.131 = (f32[512,512]{1,0:T(8,128)}, f32[512,512]{1,0:T(8,128)}, f32[512,512]{1,0:T(8,128)}) custom-call(s32[3]{0:T(128)} %add_convert_fusion.flags_ref, f32[512,512]{1,0:T(8,128)} %get-tuple-element.30.d_ref, f32[512,512]{1,0:T(8,128)} %get-tuple-element.31.e_ref, f32[512,512]{1,0:T(8,128)} %get-tuple-element.32.s_ref, f32[512,512]{1,0:T(8,128)} %bed_ref.3, ...), custom_call_target="tpu_custom_call" | custom-call | tf_op jit(solution)/shard_map/pallas_call | solution.py:306
  77.3 0.9 %add_add_fusion = f32[16,128]{1,0:T(8,128)} fusion(f32[16,128]{1,0:T(8,128)S(1)} %convolution_multiply_fusion, f32[8,128]{1,0:T(8,128)S(1)} %collective-permute-done.8, f32[16,128]{1,0:T(8,128)S(1)} %add_add_fusion.1, s32[16]{0:T(128)S(1)} %iota_add_fusion, s32[16]{0:T(128)S(1)} %copy-done.16, f32[16,128]{1,0:T(8,128)S(1)} %copy-done.7), kind=kOutput, calls=%fused_computation.34 | convolution fusion | flops 418048 | bytes 36992 | tf_op jit(solution)/shard_map/tb,tc->bc/dot_general | solution.py:40
  (73 shorter events, 2.2 us)
Async XLA Ops:
  0.6 0.7 copy-start.7
  0.6 0.7 copy-start.6
  0.7 0.7 copy-start.16
  5.5 4.8 %copy-start.12 = (f32[5,512]{1,0:T(8,128)S(1)}, f32[5,512]{1,0:T(8,128)}, u32[]{:S(2)}) copy-start(f32[5,512]{1,0:T(8,128)} %get-tuple-element.29) | copy-start | bytes 30724
  5.5 8.8 %copy-start.14 = (f32[2,512]{1,0:T(2,128)S(1)}, f32[2,512]{1,0:T(2,128)}, u32[]{:S(2)}) copy-start(f32[2,512]{1,0:T(2,128)} %get-tuple-element.26) | copy-start | bytes 12292
  6.3 9.3 %copy-start.13 = (f32[2,512]{1,0:T(2,128)S(1)}, f32[2,512]{1,0:T(2,128)}, u32[]{:S(2)}) copy-start(f32[2,512]{1,0:T(2,128)} %get-tuple-element.27) | copy-start | bytes 12292
  6.3 26.2 %collective-permute-start.2 = (f32[7,512]{1,0:T(8,128)S(1)}, f32[7,512]{1,0:T(8,128)S(1)}, u32[]{:S(2)}, u32[]{:S(2)}) collective-permute-start(f32[7,512]{1,0:T(8,128)S(1)} %pad_maximum_fusion.1), channel_id=1, source_target_pairs={{0,1},{1,2},{2,3},{3,4},{4,5},{5,6},{6,7},{7,8},{8,9},{9,10},{10,1... | collective-permute-start | bytes 43016 | tf_op jit(solution)/shard_map/ppermute | solution.py:26
  10.3 22.2 %collective-permute-start.3 = (f32[5,512]{1,0:T(8,128)S(1)}, f32[5,512]{1,0:T(8,128)S(1)}, u32[]{:S(2)}, u32[]{:S(2)}) collective-permute-start(f32[5,512]{1,0:T(8,128)S(1)} %copy-done.12), channel_id=1, source_target_pairs={{0,16},{16,32},{32,48},{48,64},{64,80},{80,96},{96,112},{1,17},{17... | collective-permute-start | bytes 30728 | tf_op jit(solution)/shard_map/ppermute | solution.py:26
  14.3 3.3 %copy-start.5 = (s32[256]{0:T(256)S(1)}, s32[256]{0:T(256)}, u32[]{:S(2)}) copy-start(s32[256]{0:T(256)} %param.16) | copy-start | bytes 3076
  14.3 18.1 %collective-permute-start = (f32[2,512]{1,0:T(2,128)S(1)}, f32[2,512]{1,0:T(2,128)S(1)}, u32[]{:S(2)}, u32[]{:S(2)}) collective-permute-start(f32[2,512]{1,0:T(2,128)S(1)} %copy-done.14), channel_id=1, source_target_pairs={{1,0},{2,1},{3,2},{4,3},{5,4},{6,5},{7,6},{8,7},{9,8},{10,9},{11,1... | collective-permute-start | bytes 12296 | tf_op jit(solution)/shard_map/ppermute | solution.py:26
  15.6 16.8 %collective-permute-start.1 = (f32[2,512]{1,0:T(2,128)S(1)}, f32[2,512]{1,0:T(2,128)S(1)}, u32[]{:S(2)}, u32[]{:S(2)}) collective-permute-start(f32[2,512]{1,0:T(2,128)S(1)} %copy-done.13), channel_id=1, source_target_pairs={{16,0},{32,16},{48,32},{64,48},{80,64},{96,80},{112,96},{17,1},{33... | collective-permute-start | bytes 12296 | tf_op jit(solution)/shard_map/ppermute | solution.py:26
  18.0 0.9 %copy-start = (f32[256,128]{1,0:T(8,128)S(1)}, f32[256,128]{1,0:T(8,128)}, u32[]{:S(2)}) copy-start(f32[256,128]{1,0:T(8,128)} %get-tuple-element.38) | copy-start | bytes 393220
  20.8 32.9 %all-to-all-start = ((f32[128,1,640]{2,1,0:T(1,128)}), f32[128,1,640]{2,1,0:T(1,128)S(1)}, u32[]{:S(2)}, u32[]{:S(2)}) async-start(f32[128,1,640]{2,1,0:T(1,128)} %copy.32), calls=%async_computation | async-start | bytes 655360 | tf_op jit(solution)/shard_map/all_to_all | solution.py:266
  32.5 0.6 copy-start.8
  32.5 0.6 copy-start.9
  32.5 0.6 copy-start.2
  32.5 0.6 copy-start.1
  40.9 8.2 %copy-start.15 = (f32[2,512]{1,0:T(2,128)S(1)}, f32[2,512]{1,0:T(2,128)}, u32[]{:S(2)}) copy-start(f32[2,512]{1,0:T(2,128)} %get-tuple-element.34) | copy-start | bytes 12292
  40.9 13.2 %collective-permute-start.6 = (f32[5,512]{1,0:T(8,128)}, f32[5,512]{1,0:T(8,128)S(1)}, u32[]{:S(2)}, u32[]{:S(2)}) collective-permute-start(f32[5,512]{1,0:T(8,128)} %get-tuple-element.35), channel_id=1, source_target_pairs={{0,1},{1,2},{2,3},{3,4},{4,5},{5,6},{6,7},{7,8},{8,9},{9,10},{10,1... | collective-permute-start | bytes 30728 | tf_op jit(solution)/shard_map/ppermute | solution.py:26
  44.1 9.9 %collective-permute-start.7 = (f32[5,512]{1,0:T(8,128)}, f32[5,512]{1,0:T(8,128)S(1)}, u32[]{:S(2)}, u32[]{:S(2)}) collective-permute-start(f32[5,512]{1,0:T(8,128)} %get-tuple-element.36), channel_id=1, source_target_pairs={{0,16},{16,32},{32,48},{48,64},{64,80},{80,96},{96,112},{1,17},{17... | collective-permute-start | bytes 30728 | tf_op jit(solution)/shard_map/ppermute | solution.py:26
  47.8 6.1 %collective-permute-start.4 = (f32[2,512]{1,0:T(2,128)}, f32[2,512]{1,0:T(2,128)S(1)}, u32[]{:S(2)}, u32[]{:S(2)}) collective-permute-start(f32[2,512]{1,0:T(2,128)} %get-tuple-element.33), channel_id=1, source_target_pairs={{1,0},{2,1},{3,2},{4,3},{5,4},{6,5},{7,6},{8,7},{9,8},{10,9},{11,1... | collective-permute-start | bytes 12296 | tf_op jit(solution)/shard_map/ppermute | solution.py:26
  49.1 4.9 %collective-permute-start.5 = (f32[2,512]{1,0:T(2,128)S(1)}, f32[2,512]{1,0:T(2,128)S(1)}, u32[]{:S(2)}, u32[]{:S(2)}) collective-permute-start(f32[2,512]{1,0:T(2,128)S(1)} %copy-done.15), channel_id=1, source_target_pairs={{16,0},{32,16},{48,32},{64,48},{80,64},{96,80},{112,96},{17,1},{33... | collective-permute-start | bytes 12296 | tf_op jit(solution)/shard_map/ppermute | solution.py:26
  53.9 0.6 copy-start.10
  54.0 0.6 copy-start.11
  54.0 0.6 copy-start.3
  54.1 0.6 copy-start.4
  55.0 22.1 %all-to-all-start.1 = ((f32[128,4,128]{2,1,0:T(4,128)}), f32[128,4,128]{2,1,0:T(4,128)S(1)}, u32[]{:S(2)}, u32[]{:S(2)}) async-start(f32[128,4,128]{2,1,0:T(4,128)} %bitcast.8), calls=%async_computation.1 | async-start | bytes 524288 | tf_op jit(solution)/shard_map/all_to_all | solution.py:315
  66.2 11.2 %collective-permute-start.8 = (f32[8,128]{1,0:T(8,128)S(1)}, f32[8,128]{1,0:T(8,128)S(1)}, u32[]{:S(2)}, u32[]{:S(2)}) collective-permute-start(f32[8,128]{1,0:T(8,128)S(1)} %fusion.17), channel_id=1, source_target_pairs={{0,1},{1,2},{2,3},{3,4},{4,5},{5,6},{6,7},{7,8},{8,9},{9,10},{10,1... | collective-permute-start | bytes 12296 | tf_op jit(solution)/shard_map/ppermute | solution.py:26
